TPU v7x, 32 devices: a whole 2x2x4 slice. The times are simulated.
32 devices in a mesh: day: 8 (over z, x), pt: 4 (over y, core).
Axes of the slice: x: 2, y: 2, z: 4, core: 2. Of those that a mesh axis runs over, the one named last changes fastest.
Arguments:
- points: bfloat16 [8, 64, 2048], P('day', None, 'pt'), may hold values from -0.45 to 0.45
- cells: bfloat16 [8, 64, 8192], P('day', None, 'pt'), may hold values from -0.44921875 to 0.44921875
- clone_weight: float32 [8, 64, 2048], P('day', None, 'pt'), may hold values from 0.1 to 1
- potential: float32 [8, 2048], P('day', 'pt'), may hold values from 0.2 to 5
- support_count: int32 [8], P('day'), may hold values from 512 to 2048, as said below
- cell_count: int32 [8], P('day'), may hold values from 2048 to 8192, as said below
Outputs:
- forward_message: float32 [8, 64, 2048], P('day', None, 'pt')
- backward_message: float32 [8, 64, 2048], P('day', None, 'pt')
- fit_ratio: float32 [8, 2048], P('day', 'pt')
Inputs may be any that keep to these rules, and one draw needn't show every extreme that they name: Live support points of a day are its first support_count slots; some day has all 2048 slots live and some day has 512. Observed cells of a day are its first cell_count slots; some day fills all 8192 slots and some day has 2048.
All inputs are finite; a program needn't handle non-finite values.
Results may differ from a plain program's by a relative error of at most 0.0003.
Values may be sent and summed in bfloat16 or wider, within the bound.
No kernel may reach another device: no remote copies, remote signals or barrier semaphores. Data moves between devices by JAX's collectives and lax.ppermute only.
A program may use at most 64 MiB of HBM per device.

v0:
```python
import jax
import jax.numpy as jnp
from jax import lax
from jax.sharding import PartitionSpec as P


def with_halo(cells, sides, width):
    for axis, dim in sides:
        count = lax.axis_size(axis)
        ends = count - 1
        head = lax.slice_in_dim(cells, 0, width, axis=dim)
        tail = lax.slice_in_dim(cells, cells.shape[dim] - width, cells.shape[dim], axis=dim)
        cells = jnp.concatenate(
            [
                lax.ppermute(tail, axis, [(i, (i + 1) % count) for i in range(ends)]),
                cells,
                lax.ppermute(head, axis, [((i + 1) % count, i) for i in range(ends)]),
            ],
            axis=dim,
        )
    return cells


def shifted(block, axis, distance):
    devices = range(lax.axis_size(axis))
    route = [(i - distance, i) for i in devices if i - distance in devices]
    return lax.ppermute(block, axis, route)


def norm_of(coords):
    wide = coords.astype(jnp.float32)
    return jnp.sum(wide * wide, axis=0)


def squared_dist(left_pts, left_norm, right_pts, right_norm):
    inner = lax.dot_general(
        left_pts, right_pts, (((0,), (0,)), ((), ())), preferred_element_type=jnp.float32
    )
    return left_norm[:, None] + right_norm[None, :] - 2.0 * inner


def shards(points, cells, clone_weight, potential, support_count, cell_count):
    pt_rank = lax.axis_index("pt")
    day_index = lax.axis_index("day")
    day_count = lax.axis_size("day")
    full_pts, full_clone, full_pot = (
        lax.all_gather(points.astype(jnp.float32), "pt", axis=2, tiled=True).astype(points.dtype),
        lax.all_gather(clone_weight, "pt", axis=2, tiled=True),
        lax.all_gather(potential, "pt", axis=1, tiled=True),
    )
    beside_all = with_halo(full_pts, (("day", 0),), 1)
    before_day = beside_all[0]
    after_day = beside_all[2]
    own_pts = points[0]
    per_device = own_pts.shape[1]
    support_total = full_pts.shape[2]
    clones = clone_weight.shape[1]
    weight = full_clone[0] * full_pot
    live_total = support_count[0].astype(jnp.float32)
    live_all = (jnp.arange(support_total, dtype=jnp.int32) < support_count[0]).astype(jnp.float32)
    live_own = lax.dynamic_slice_in_dim(live_all, pt_rank * per_device, per_device)
    own_norm = norm_of(own_pts)
    before_norm = norm_of(before_day)
    after_norm = norm_of(after_day)
    row_span = 512
    span_count = support_total // row_span

    def kernel_rows(source_pts, source_norm, block_index):
        offset = block_index * row_span
        source_rows = lax.dynamic_slice_in_dim(source_pts, offset, row_span, 1)
        norm_rows = lax.dynamic_slice_in_dim(source_norm, offset, row_span, 0)
        return jnp.exp(-squared_dist(source_rows, norm_rows, own_pts, own_norm)).astype(
            jnp.bfloat16
        )

    def contract(sent_rows, source_pts, source_norm):

        def add_rows(block_index, result):
            sent_part = lax.dynamic_slice_in_dim(sent_rows, block_index * row_span, row_span, 1)
            return result + jnp.dot(
                sent_part,
                kernel_rows(source_pts, source_norm, block_index),
                preferred_element_type=jnp.float32,
            )

        return lax.fori_loop(
            0, span_count, add_rows, jnp.zeros((sent_rows.shape[0], per_device), jnp.float32)
        )

    block_count = 4
    block_rows = clones // block_count
    steps_total = day_count + block_count - 1
    empty_rows = jnp.zeros((block_rows, per_device), jnp.float32)
    seed_rows = jnp.broadcast_to(live_own[None, :], (block_rows, per_device))

    def settle(piece_rows, full_rows, valid):
        column_sums = jnp.sum(full_rows * live_all[None, :], axis=1, keepdims=True)
        column_sums = jnp.where(valid, column_sums, 1.0)
        own_part = piece_rows * live_own[None, :] * live_total / column_sums
        whole_part = full_rows * live_all[None, :] * live_total / column_sums
        return (own_part, whole_part)

    def one_step(step_index, carried):
        forward_in, backward_in, forward_out, backward_out = carried
        forward_at = step_index - day_index
        forward_ok = (forward_at >= 0) & (forward_at < block_count)
        forward_block = jnp.clip(forward_at, 0, block_count - 1)
        backward_at = step_index - (day_count - 1 - day_index)
        backward_ok = (backward_at >= 0) & (backward_at < block_count)
        backward_block = jnp.clip(backward_at, 0, block_count - 1)
        forward_got = lax.cond(
            forward_ok & (day_index > 0),
            lambda: contract(forward_in, before_day, before_norm),
            lambda: empty_rows,
        )
        forward_piece = jnp.where(day_index == 0, seed_rows, forward_got)
        backward_got = lax.cond(
            backward_ok & (day_index < day_count - 1),
            lambda: contract(backward_in, after_day, after_norm),
            lambda: empty_rows,
        )
        backward_piece = jnp.where(day_index == day_count - 1, seed_rows, backward_got)
        forward_full, backward_full = (
            lax.all_gather(forward_piece, "pt", axis=1, tiled=True),
            lax.all_gather(backward_piece, "pt", axis=1, tiled=True),
        )
        forward_own, forward_all = settle(forward_piece, forward_full, forward_ok)
        backward_own, backward_all = settle(backward_piece, backward_full, backward_ok)
        forward_out = jnp.where(
            forward_ok,
            lax.dynamic_update_slice_in_dim(
                forward_out, forward_own, forward_block * block_rows, 0
            ),
            forward_out,
        )
        backward_out = jnp.where(
            backward_ok,
            lax.dynamic_update_slice_in_dim(
                backward_out, backward_own, backward_block * block_rows, 0
            ),
            backward_out,
        )
        forward_sent = (
            forward_all
            * lax.dynamic_slice_in_dim(weight, forward_block * block_rows, block_rows, 0)
        ).astype(jnp.bfloat16)
        backward_sent = (
            backward_all
            * lax.dynamic_slice_in_dim(weight, backward_block * block_rows, block_rows, 0)
        ).astype(jnp.bfloat16)
        forward_in = shifted(forward_sent, "day", 1)
        backward_in = shifted(backward_sent, "day", -1)
        return (forward_in, backward_in, forward_out, backward_out)

    start_in = jnp.zeros((block_rows, support_total), jnp.bfloat16)
    start_out = jnp.zeros((clones, per_device), jnp.float32)
    carried = lax.fori_loop(0, steps_total, one_step, (start_in, start_in, start_out, start_out))
    forward_out = carried[2]
    backward_out = carried[3]
    mass_own = (
        live_own * potential[0] * jnp.sum(forward_out * clone_weight[0] * backward_out, axis=0)
    )
    cell_total = cell_count[0]
    cell_total_f = cell_total.astype(jnp.float32)
    full_mass = lax.all_gather(mass_own, "pt", axis=0, tiled=True)
    mass_total = jnp.sum(full_mass)
    own_cells = cells[0]
    cell_norm = norm_of(own_cells)
    own_slots = own_cells.shape[1]
    day_pts = full_pts[0]
    day_norm = norm_of(day_pts)
    fit_span = 256
    fit_blocks = support_total // fit_span

    def fit_rows(block_index):
        offset = block_index * fit_span
        chosen = lax.dynamic_slice_in_dim(day_pts, offset, fit_span, 1)
        chosen_norm = lax.dynamic_slice_in_dim(day_norm, offset, fit_span, 0)
        return jnp.exp(-squared_dist(chosen, chosen_norm, own_cells, cell_norm))

    def density_part(block_index):
        chosen_mass = lax.dynamic_slice_in_dim(full_mass, block_index * fit_span, fit_span, 0)
        return jnp.dot(chosen_mass, fit_rows(block_index), precision=lax.Precision.HIGHEST)

    density = jnp.sum(lax.map(density_part, jnp.arange(fit_blocks)), axis=0) / mass_total
    cell_live = (pt_rank * own_slots + jnp.arange(own_slots, dtype=jnp.int32) < cell_total).astype(
        jnp.float32
    )
    inverse = cell_live / density

    def ratio_part(block_index):
        return jnp.dot(fit_rows(block_index), inverse, precision=lax.Precision.HIGHEST)

    ratio_rows = lax.map(ratio_part, jnp.arange(fit_blocks)).reshape(support_total)
    summed = lax.psum_scatter(ratio_rows, "pt", scatter_dimension=0, tiled=True)
    fit_rows_out = live_own / cell_total_f * summed
    return (forward_out[None], backward_out[None], fit_rows_out[None])


def solution(mesh):
    in_specs = (
        P("day", None, "pt"),
        P("day", None, "pt"),
        P("day", None, "pt"),
        P("day", "pt"),
        P("day"),
        P("day"),
    )
    out_specs = (P("day", None, "pt"), P("day", None, "pt"), P("day", "pt"))
    return jax.shard_map(shards, mesh=mesh, in_specs=in_specs, out_specs=out_specs, check_vma=False)
```

profile of v0, /device:TPU:0, one launch (start us, length us, event | category | flops | bytes accessed | tf_op | source)
XLA Modules:
  0.0 437.7 jit_solution(1554293441669828181)
XLA Ops:
  0.7 7.6 %all_gather.28 = bf16[1,64,2048]{2,1,0:T(8,128)(2,1)S(1)} all-gather(bf16[1,64,512]{2,1,0:T(8,128)(2,1)} %param.20), channel_id=1, replica_groups=mesh['day'=8,'pt'=4] {'pt'}, dimensions={2}, use_global_device_ids=true | all-gather | bytes 327680 | tf_op jit(solution)/shard_map/all_gather | solution.py:47
  14.2 7.4 %all_gather.29 = f32[1,64,2048]{2,1,0:T(8,128)S(1)} all-gather(f32[1,64,512]{2,1,0:T(8,128)} %param.22), channel_id=1, replica_groups=mesh['day'=8,'pt'=4] {'pt'}, dimensions={2}, use_global_device_ids=true | all-gather | bytes 655360 | tf_op jit(solution)/shard_map/all_gather | solution.py:48
  30.0 338.5 %while.72 = (s32[]{:T(128)}, bf16[16,2048]{1,0:T(8,128)(2,1)S(1)}, bf16[16,2048]{1,0:T(8,128)(2,1)S(1)}, f32[64,512]{1,0:T(8,128)S(1)}, f32[64,512]{1,0:T(8,128)...) while((s32[]{:T(128)}, bf16[16,2048]{1,0:T(8,128)(2,1)S(1)}, ...), condition=%wide.region_14.15_spmd.clone.clone, body=%wide.region_3.14_spmd.clone.clone.sunk | while | flops 87085088 | bytes 2573997 | solution.py:157
  32.0 5.4 %all_gather.38 = f32[16,2048]{1,0:T(8,128)S(1)} all-gather(f32[16,512]{1,0:T(8,128)S(1)} %get-tuple-element.1308), channel_id=1, replica_groups=mesh['day'=8,'pt'=4] {'pt'}, dimensions={1}, use_global_device_ids=true | all-gather | bytes 163840 | tf_op jit(solution)/shard_map/while/body/eval_jaxpr/all_gather | solution.py:125
  56.2 5.4 %all_gather.38 = f32[16,2048]{1,0:T(8,128)S(1)} all-gather(f32[16,512]{1,0:T(8,128)S(1)} %get-tuple-element.1308), channel_id=1, replica_groups=mesh['day'=8,'pt'=4] {'pt'}, dimensions={1}, use_global_device_ids=true | all-gather | bytes 163840 | tf_op jit(solution)/shard_map/while/body/eval_jaxpr/all_gather | solution.py:125
  68.0 9.9 %collective-permute-start = (bf16[16,2048]{1,0:T(8,128)(2,1)S(1)}, bf16[16,2048]{1,0:T(8,128)(2,1)S(1)}, u32[]{:S(2)}, u32[]{:S(2)}) collective-permute-start(bf16[16,2048]{1,0:T(8,128)(2,1)S(1)} %get-tuple-element.1314), channel_id=1, source_target_pairs={{0,4},{4,8},{8,12},{12,16},{16,20},{20,24},{24,28},{1,5},{5,9},{9,... | collective-permute-start | bytes 196616 | tf_op jit(solution)/shard_map/while/body/eval_jaxpr/ppermute | solution.py:27
  86.0 5.4 %all_gather.38 = f32[16,2048]{1,0:T(8,128)S(1)} all-gather(f32[16,512]{1,0:T(8,128)S(1)} %get-tuple-element.1308), channel_id=1, replica_groups=mesh['day'=8,'pt'=4] {'pt'}, dimensions={1}, use_global_device_ids=true | all-gather | bytes 163840 | tf_op jit(solution)/shard_map/while/body/eval_jaxpr/all_gather | solution.py:125
  97.8 9.3 %collective-permute-start = (bf16[16,2048]{1,0:T(8,128)(2,1)S(1)}, bf16[16,2048]{1,0:T(8,128)(2,1)S(1)}, u32[]{:S(2)}, u32[]{:S(2)}) collective-permute-start(bf16[16,2048]{1,0:T(8,128)(2,1)S(1)} %get-tuple-element.1314), channel_id=1, source_target_pairs={{0,4},{4,8},{8,12},{12,16},{16,20},{20,24},{24,28},{1,5},{5,9},{9,... | collective-permute-start | bytes 196616 | tf_op jit(solution)/shard_map/while/body/eval_jaxpr/ppermute | solution.py:27
  115.3 5.4 %all_gather.38 = f32[16,2048]{1,0:T(8,128)S(1)} all-gather(f32[16,512]{1,0:T(8,128)S(1)} %get-tuple-element.1308), channel_id=1, replica_groups=mesh['day'=8,'pt'=4] {'pt'}, dimensions={1}, use_global_device_ids=true | all-gather | bytes 163840 | tf_op jit(solution)/shard_map/while/body/eval_jaxpr/all_gather | solution.py:125
  127.0 9.3 %collective-permute-start = (bf16[16,2048]{1,0:T(8,128)(2,1)S(1)}, bf16[16,2048]{1,0:T(8,128)(2,1)S(1)}, u32[]{:S(2)}, u32[]{:S(2)}) collective-permute-start(bf16[16,2048]{1,0:T(8,128)(2,1)S(1)} %get-tuple-element.1314), channel_id=1, source_target_pairs={{0,4},{4,8},{8,12},{12,16},{16,20},{20,24},{24,28},{1,5},{5,9},{9,... | collective-permute-start | bytes 196616 | tf_op jit(solution)/shard_map/while/body/eval_jaxpr/ppermute | solution.py:27
  144.5 5.4 %all_gather.38 = f32[16,2048]{1,0:T(8,128)S(1)} all-gather(f32[16,512]{1,0:T(8,128)S(1)} %get-tuple-element.1308), channel_id=1, replica_groups=mesh['day'=8,'pt'=4] {'pt'}, dimensions={1}, use_global_device_ids=true | all-gather | bytes 163840 | tf_op jit(solution)/shard_map/while/body/eval_jaxpr/all_gather | solution.py:125
  156.3 9.3 %collective-permute-start = (bf16[16,2048]{1,0:T(8,128)(2,1)S(1)}, bf16[16,2048]{1,0:T(8,128)(2,1)S(1)}, u32[]{:S(2)}, u32[]{:S(2)}) collective-permute-start(bf16[16,2048]{1,0:T(8,128)(2,1)S(1)} %get-tuple-element.1314), channel_id=1, source_target_pairs={{0,4},{4,8},{8,12},{12,16},{16,20},{20,24},{24,28},{1,5},{5,9},{9,... | collective-permute-start | bytes 196616 | tf_op jit(solution)/shard_map/while/body/eval_jaxpr/ppermute | solution.py:27
  173.8 5.4 %all_gather.38 = f32[16,2048]{1,0:T(8,128)S(1)} all-gather(f32[16,512]{1,0:T(8,128)S(1)} %get-tuple-element.1308), channel_id=1, replica_groups=mesh['day'=8,'pt'=4] {'pt'}, dimensions={1}, use_global_device_ids=true | all-gather | bytes 163840 | tf_op jit(solution)/shard_map/while/body/eval_jaxpr/all_gather | solution.py:125
  185.5 11.0 %collective-permute-start = (bf16[16,2048]{1,0:T(8,128)(2,1)S(1)}, bf16[16,2048]{1,0:T(8,128)(2,1)S(1)}, u32[]{:S(2)}, u32[]{:S(2)}) collective-permute-start(bf16[16,2048]{1,0:T(8,128)(2,1)S(1)} %get-tuple-element.1314), channel_id=1, source_target_pairs={{0,4},{4,8},{8,12},{12,16},{16,20},{20,24},{24,28},{1,5},{5,9},{9,... | collective-permute-start | bytes 196616 | tf_op jit(solution)/shard_map/while/body/eval_jaxpr/ppermute | solution.py:27
  198.4 17.1 %collective-permute-done.1 = bf16[16,2048]{1,0:T(8,128)(2,1)S(1)} collective-permute-done((bf16[16,2048]{1,0:T(8,128)(2,1)S(1)}, bf16[16,2048]{1,0:T(8,128)(2,1)S(1)}, u32[]{:S(2)}, u32[]{:S(2)}) %collective-permute-start.1) | collective-permute-done | bytes 65568 | tf_op jit(solution)/shard_map/while/body/eval_jaxpr/ppermute | solution.py:27
  217.6 5.4 %all_gather.38 = f32[16,2048]{1,0:T(8,128)S(1)} all-gather(f32[16,512]{1,0:T(8,128)S(1)} %get-tuple-element.1308), channel_id=1, replica_groups=mesh['day'=8,'pt'=4] {'pt'}, dimensions={1}, use_global_device_ids=true | all-gather | bytes 163840 | tf_op jit(solution)/shard_map/while/body/eval_jaxpr/all_gather | solution.py:125
  229.3 11.2 %collective-permute-start = (bf16[16,2048]{1,0:T(8,128)(2,1)S(1)}, bf16[16,2048]{1,0:T(8,128)(2,1)S(1)}, u32[]{:S(2)}, u32[]{:S(2)}) collective-permute-start(bf16[16,2048]{1,0:T(8,128)(2,1)S(1)} %get-tuple-element.1314), channel_id=1, source_target_pairs={{0,4},{4,8},{8,12},{12,16},{16,20},{20,24},{24,28},{1,5},{5,9},{9,... | collective-permute-start | bytes 196616 | tf_op jit(solution)/shard_map/while/body/eval_jaxpr/ppermute | solution.py:27
  246.6 7.0 %conditional.8 = (f32[16,512]{1,0:T(8,128)}) conditional(s32[]{:T(128)} %convert_element_type.133, () %tuple.157, (bf16[16,2048]{1,0:T(8,128)(2,1)S(1)}, f32[2048]{0:T(1024)S(1)}, f32[512]{0:T(512)S(1)}, bf16[64,2048]{1,0:T(8,128)(2,1)S(1)}, bf16[64,512]{1,0:T(8,128)(2,1)S(1)}) %tuple.158), branch_computations={%region_9.9_spmd, %region_10.12_spmd} | conditional | flops 43270152 | bytes 222992 | solution.py:117
  246.6 7.0 %while.69 = (s32[]{:T(128)}, f32[16,512]{1,0:T(8,128)}, bf16[16,2048]{1,0:T(8,128)(2,1)S(1)}, f32[2048]{0:T(1024)S(1)}, f32[512]{0:T(512)S(1)}, /*index=5*/bf16[...) while((s32[]{:T(128)}, f32[16,512]{1,0:T(8,128)}, ...), condition=%wide.region_12.11_spmd.clone, body=%wide.region_11.10_spmd.clone.sunk | while | flops 43270152 | bytes 222888 | solution.py:86
  255.1 5.4 %all_gather.38 = f32[16,2048]{1,0:T(8,128)S(1)} all-gather(f32[16,512]{1,0:T(8,128)S(1)} %get-tuple-element.1308), channel_id=1, replica_groups=mesh['day'=8,'pt'=4] {'pt'}, dimensions={1}, use_global_device_ids=true | all-gather | bytes 163840 | tf_op jit(solution)/shard_map/while/body/eval_jaxpr/all_gather | solution.py:125
  266.8 7.5 %collective-permute-start = (bf16[16,2048]{1,0:T(8,128)(2,1)S(1)}, bf16[16,2048]{1,0:T(8,128)(2,1)S(1)}, u32[]{:S(2)}, u32[]{:S(2)}) collective-permute-start(bf16[16,2048]{1,0:T(8,128)(2,1)S(1)} %get-tuple-element.1314), channel_id=1, source_target_pairs={{0,4},{4,8},{8,12},{12,16},{16,20},{20,24},{24,28},{1,5},{5,9},{9,... | collective-permute-start | bytes 196616 | tf_op jit(solution)/shard_map/while/body/eval_jaxpr/ppermute | solution.py:27
  280.5 7.0 %conditional.8 = (f32[16,512]{1,0:T(8,128)}) conditional(s32[]{:T(128)} %convert_element_type.133, () %tuple.157, (bf16[16,2048]{1,0:T(8,128)(2,1)S(1)}, f32[2048]{0:T(1024)S(1)}, f32[512]{0:T(512)S(1)}, bf16[64,2048]{1,0:T(8,128)(2,1)S(1)}, bf16[64,512]{1,0:T(8,128)(2,1)S(1)}) %tuple.158), branch_computations={%region_9.9_spmd, %region_10.12_spmd} | conditional | flops 43270152 | bytes 222992 | solution.py:117
  280.5 7.0 %while.69 = (s32[]{:T(128)}, f32[16,512]{1,0:T(8,128)}, bf16[16,2048]{1,0:T(8,128)(2,1)S(1)}, f32[2048]{0:T(1024)S(1)}, f32[512]{0:T(512)S(1)}, /*index=5*/bf16[...) while((s32[]{:T(128)}, f32[16,512]{1,0:T(8,128)}, ...), condition=%wide.region_12.11_spmd.clone, body=%wide.region_11.10_spmd.clone.sunk | while | flops 43270152 | bytes 222888 | solution.py:86
  311.6 7.0 %conditional.8 = (f32[16,512]{1,0:T(8,128)}) conditional(s32[]{:T(128)} %convert_element_type.133, () %tuple.157, (bf16[16,2048]{1,0:T(8,128)(2,1)S(1)}, f32[2048]{0:T(1024)S(1)}, f32[512]{0:T(512)S(1)}, bf16[64,2048]{1,0:T(8,128)(2,1)S(1)}, bf16[64,512]{1,0:T(8,128)(2,1)S(1)}) %tuple.158), branch_computations={%region_9.9_spmd, %region_10.12_spmd} | conditional | flops 43270152 | bytes 222992 | solution.py:117
  311.6 7.0 %while.69 = (s32[]{:T(128)}, f32[16,512]{1,0:T(8,128)}, bf16[16,2048]{1,0:T(8,128)(2,1)S(1)}, f32[2048]{0:T(1024)S(1)}, f32[512]{0:T(512)S(1)}, /*index=5*/bf16[...) while((s32[]{:T(128)}, f32[16,512]{1,0:T(8,128)}, ...), condition=%wide.region_12.11_spmd.clone, body=%wide.region_11.10_spmd.clone.sunk | while | flops 43270152 | bytes 222888 | solution.py:86
  320.0 5.4 %all_gather.38 = f32[16,2048]{1,0:T(8,128)S(1)} all-gather(f32[16,512]{1,0:T(8,128)S(1)} %get-tuple-element.1308), channel_id=1, replica_groups=mesh['day'=8,'pt'=4] {'pt'}, dimensions={1}, use_global_device_ids=true | all-gather | bytes 163840 | tf_op jit(solution)/shard_map/while/body/eval_jaxpr/all_gather | solution.py:125
  340.8 7.0 %conditional.8 = (f32[16,512]{1,0:T(8,128)}) conditional(s32[]{:T(128)} %convert_element_type.133, () %tuple.157, (bf16[16,2048]{1,0:T(8,128)(2,1)S(1)}, f32[2048]{0:T(1024)S(1)}, f32[512]{0:T(512)S(1)}, bf16[64,2048]{1,0:T(8,128)(2,1)S(1)}, bf16[64,512]{1,0:T(8,128)(2,1)S(1)}) %tuple.158), branch_computations={%region_9.9_spmd, %region_10.12_spmd} | conditional | flops 43270152 | bytes 222992 | solution.py:117
  340.8 7.0 %while.69 = (s32[]{:T(128)}, f32[16,512]{1,0:T(8,128)}, bf16[16,2048]{1,0:T(8,128)(2,1)S(1)}, f32[2048]{0:T(1024)S(1)}, f32[512]{0:T(512)S(1)}, /*index=5*/bf16[...) while((s32[]{:T(128)}, f32[16,512]{1,0:T(8,128)}, ...), condition=%wide.region_12.11_spmd.clone, body=%wide.region_11.10_spmd.clone.sunk | while | flops 43270152 | bytes 222888 | solution.py:86
  349.2 5.4 %all_gather.38 = f32[16,2048]{1,0:T(8,128)S(1)} all-gather(f32[16,512]{1,0:T(8,128)S(1)} %get-tuple-element.1308), channel_id=1, replica_groups=mesh['day'=8,'pt'=4] {'pt'}, dimensions={1}, use_global_device_ids=true | all-gather | bytes 163840 | tf_op jit(solution)/shard_map/while/body/eval_jaxpr/all_gather | solution.py:125
  373.8 25.9 %while.70 = (s32[]{:T(128)}, f32[8,2048]{1,0:T(8,128)S(1)}, s32[8]{0:T(128)S(1)}, f32[2048]{0:T(1024)S(1)}, f32[2048]{0:T(1024)S(1)}, /*index=5*/f32[2048]{0:T(1...) while((s32[]{:T(128)}, f32[8,2048]{1,0:T(8,128)S(1)}, ...), condition=%wide.region_20.21_spmd, body=%wide.region_19.20_spmd.sunk | while | flops 75497480 | bytes 4528319 | solution.py:185
  401.0 29.2 %while.71 = (s32[]{:T(128)}, f32[8,256]{1,0:T(8,128)S(1)}, s32[8]{0:T(128)S(1)}, f32[2048]{0:T(1024)S(1)}, f32[2048]{0:T(1024)S(1)}, /*index=5*/bf16[64,2048]{1,...) while((s32[]{:T(128)}, f32[8,256]{1,0:T(8,128)S(1)}, ...), condition=%wide.region_23.24_spmd, body=%wide.region_22.23_spmd.sunk | while | flops 75497480 | bytes 4511931 | solution.py:194
  430.2 6.8 %all-reduce = f32[2048]{0:T(1024)S(1)} all-reduce(f32[2048]{0:T(1024)S(1)} %bitcast.86), channel_id=2, replica_groups=mesh['day'=8,'pt'=4] {'pt'}, use_global_device_ids=true, to_apply=%region_24.25.clone | all-reduce | flops 2048 | bytes 16384
  (317 shorter events, 273.7 us)
Async XLA Ops:
  0.6 27.7 %copy-start.6 = (u32[32]{0:T(128)S(1)}, u32[32]{0:T(128)}, u32[]{:S(2)}) copy-start(u32[32]{0:T(128)} %constant.212) | copy-start | bytes 388
  0.6 26.3 %copy-start.3 = (bf16[1,64,512]{2,1,0:T(8,128)(2,1)S(1)}, bf16[1,64,512]{2,1,0:T(8,128)(2,1)}, u32[]{:S(2)}) copy-start(bf16[1,64,512]{2,1,0:T(8,128)(2,1)} %param.20) | copy-start | bytes 196612
  0.7 29.0 %copy-start.4 = (bf16[1,64,2048]{2,1,0:T(8,128)(2,1)S(1)}, bf16[1,64,2048]{2,1,0:T(8,128)(2,1)}, u32[]{:S(2)}) copy-start(bf16[1,64,2048]{2,1,0:T(8,128)(2,1)} %param.21) | copy-start | bytes 786436
  8.3 21.4 %collective-permute-start.3 = (bf16[1,64,2048]{2,1,0:T(8,128)(2,1)S(1)}, bf16[1,64,2048]{2,1,0:T(8,128)(2,1)S(1)}, u32[]{:S(2)}, u32[]{:S(2)}) collective-permute-start(bf16[1,64,2048]{2,1,0:T(8,128)(2,1)S(1)} %all_gather.28), channel_id=1, source_target_pairs={{4,0},{8,4},{12,8},{16,12},{20,16},{24,20},{28,24},{5,1},{9,5},{13... | collective-permute-start | bytes 786440 | tf_op jit(solution)/shard_map/ppermute | solution.py:17
  9.5 20.2 %collective-permute-start.2 = (bf16[1,64,2048]{2,1,0:T(8,128)(2,1)S(1)}, bf16[1,64,2048]{2,1,0:T(8,128)(2,1)S(1)}, u32[]{:S(2)}, u32[]{:S(2)}) collective-permute-start(bf16[1,64,2048]{2,1,0:T(8,128)(2,1)S(1)} %all_gather.28), channel_id=1, source_target_pairs={{0,4},{4,8},{8,12},{12,16},{16,20},{20,24},{24,28},{1,5},{5,9},{9,... | collective-permute-start | bytes 786440 | tf_op jit(solution)/shard_map/ppermute | solution.py:15
  29.9 338.6 %copy-start.2 = (f32[1,64,512]{2,1,0:T(8,128)S(1)}, f32[1,64,512]{2,1,0:T(8,128)}, u32[]{:S(2)}) copy-start(f32[1,64,512]{2,1,0:T(8,128)} %param.22) | copy-start | bytes 393220
  30.0 338.6 %copy-start.5 = (f32[1,512]{1,0:T(1,128)S(1)}, f32[1,512]{1,0:T(1,128)}, u32[]{:S(2)}) copy-start(f32[1,512]{1,0:T(1,128)} %param.23) | copy-start | bytes 6148
  43.8 6.2 %collective-permute-start = (bf16[16,2048]{1,0:T(8,128)(2,1)S(1)}, bf16[16,2048]{1,0:T(8,128)(2,1)S(1)}, u32[]{:S(2)}, u32[]{:S(2)}) collective-permute-start(bf16[16,2048]{1,0:T(8,128)(2,1)S(1)} %get-tuple-element.1314), channel_id=1, source_target_pairs={{0,4},{4,8},{8,12},{12,16},{16,20},{20,24},{24,28},{1,5},{5,9},{9,... | collective-permute-start | bytes 196616 | tf_op jit(solution)/shard_map/while/body/eval_jaxpr/ppermute | solution.py:27
  48.1 6.2 %collective-permute-start.1 = (bf16[16,2048]{1,0:T(8,128)(2,1)S(1)}, bf16[16,2048]{1,0:T(8,128)(2,1)S(1)}, u32[]{:S(2)}, u32[]{:S(2)}) collective-permute-start(bf16[16,2048]{1,0:T(8,128)(2,1)S(1)} %get-tuple-element.1315), channel_id=1, source_target_pairs={{4,0},{8,4},{12,8},{16,12},{20,16},{24,20},{28,24},{5,1},{9,5},{13... | collective-permute-start | bytes 196616 | tf_op jit(solution)/shard_map/while/body/eval_jaxpr/ppermute | solution.py:27
  68.0 11.8 %collective-permute-start = (bf16[16,2048]{1,0:T(8,128)(2,1)S(1)}, bf16[16,2048]{1,0:T(8,128)(2,1)S(1)}, u32[]{:S(2)}, u32[]{:S(2)}) collective-permute-start(bf16[16,2048]{1,0:T(8,128)(2,1)S(1)} %get-tuple-element.1314), channel_id=1, source_target_pairs={{0,4},{4,8},{8,12},{12,16},{16,20},{20,24},{24,28},{1,5},{5,9},{9,... | collective-permute-start | bytes 196616 | tf_op jit(solution)/shard_map/while/body/eval_jaxpr/ppermute | solution.py:27
  77.9 6.2 %collective-permute-start.1 = (bf16[16,2048]{1,0:T(8,128)(2,1)S(1)}, bf16[16,2048]{1,0:T(8,128)(2,1)S(1)}, u32[]{:S(2)}, u32[]{:S(2)}) collective-permute-start(bf16[16,2048]{1,0:T(8,128)(2,1)S(1)} %get-tuple-element.1315), channel_id=1, source_target_pairs={{4,0},{8,4},{12,8},{16,12},{20,16},{24,20},{28,24},{5,1},{9,5},{13... | collective-permute-start | bytes 196616 | tf_op jit(solution)/shard_map/while/body/eval_jaxpr/ppermute | solution.py:27
  97.8 11.2 %collective-permute-start = (bf16[16,2048]{1,0:T(8,128)(2,1)S(1)}, bf16[16,2048]{1,0:T(8,128)(2,1)S(1)}, u32[]{:S(2)}, u32[]{:S(2)}) collective-permute-start(bf16[16,2048]{1,0:T(8,128)(2,1)S(1)} %get-tuple-element.1314), channel_id=1, source_target_pairs={{0,4},{4,8},{8,12},{12,16},{16,20},{20,24},{24,28},{1,5},{5,9},{9,... | collective-permute-start | bytes 196616 | tf_op jit(solution)/shard_map/while/body/eval_jaxpr/ppermute | solution.py:27
  107.1 6.2 %collective-permute-start.1 = (bf16[16,2048]{1,0:T(8,128)(2,1)S(1)}, bf16[16,2048]{1,0:T(8,128)(2,1)S(1)}, u32[]{:S(2)}, u32[]{:S(2)}) collective-permute-start(bf16[16,2048]{1,0:T(8,128)(2,1)S(1)} %get-tuple-element.1315), channel_id=1, source_target_pairs={{4,0},{8,4},{12,8},{16,12},{20,16},{24,20},{28,24},{5,1},{9,5},{13... | collective-permute-start | bytes 196616 | tf_op jit(solution)/shard_map/while/body/eval_jaxpr/ppermute | solution.py:27
  127.0 11.2 %collective-permute-start = (bf16[16,2048]{1,0:T(8,128)(2,1)S(1)}, bf16[16,2048]{1,0:T(8,128)(2,1)S(1)}, u32[]{:S(2)}, u32[]{:S(2)}) collective-permute-start(bf16[16,2048]{1,0:T(8,128)(2,1)S(1)} %get-tuple-element.1314), channel_id=1, source_target_pairs={{0,4},{4,8},{8,12},{12,16},{16,20},{20,24},{24,28},{1,5},{5,9},{9,... | collective-permute-start | bytes 196616 | tf_op jit(solution)/shard_map/while/body/eval_jaxpr/ppermute | solution.py:27
  136.4 6.2 %collective-permute-start.1 = (bf16[16,2048]{1,0:T(8,128)(2,1)S(1)}, bf16[16,2048]{1,0:T(8,128)(2,1)S(1)}, u32[]{:S(2)}, u32[]{:S(2)}) collective-permute-start(bf16[16,2048]{1,0:T(8,128)(2,1)S(1)} %get-tuple-element.1315), channel_id=1, source_target_pairs={{4,0},{8,4},{12,8},{16,12},{20,16},{24,20},{28,24},{5,1},{9,5},{13... | collective-permute-start | bytes 196616 | tf_op jit(solution)/shard_map/while/body/eval_jaxpr/ppermute | solution.py:27
  156.3 11.2 %collective-permute-start = (bf16[16,2048]{1,0:T(8,128)(2,1)S(1)}, bf16[16,2048]{1,0:T(8,128)(2,1)S(1)}, u32[]{:S(2)}, u32[]{:S(2)}) collective-permute-start(bf16[16,2048]{1,0:T(8,128)(2,1)S(1)} %get-tuple-element.1314), channel_id=1, source_target_pairs={{0,4},{4,8},{8,12},{12,16},{16,20},{20,24},{24,28},{1,5},{5,9},{9,... | collective-permute-start | bytes 196616 | tf_op jit(solution)/shard_map/while/body/eval_jaxpr/ppermute | solution.py:27
  165.6 6.2 %collective-permute-start.1 = (bf16[16,2048]{1,0:T(8,128)(2,1)S(1)}, bf16[16,2048]{1,0:T(8,128)(2,1)S(1)}, u32[]{:S(2)}, u32[]{:S(2)}) collective-permute-start(bf16[16,2048]{1,0:T(8,128)(2,1)S(1)} %get-tuple-element.1315), channel_id=1, source_target_pairs={{4,0},{8,4},{12,8},{16,12},{20,16},{24,20},{28,24},{5,1},{9,5},{13... | collective-permute-start | bytes 196616 | tf_op jit(solution)/shard_map/while/body/eval_jaxpr/ppermute | solution.py:27
  185.5 12.9 %collective-permute-start = (bf16[16,2048]{1,0:T(8,128)(2,1)S(1)}, bf16[16,2048]{1,0:T(8,128)(2,1)S(1)}, u32[]{:S(2)}, u32[]{:S(2)}) collective-permute-start(bf16[16,2048]{1,0:T(8,128)(2,1)S(1)} %get-tuple-element.1314), channel_id=1, source_target_pairs={{0,4},{4,8},{8,12},{12,16},{16,20},{20,24},{24,28},{1,5},{5,9},{9,... | collective-permute-start | bytes 196616 | tf_op jit(solution)/shard_map/while/body/eval_jaxpr/ppermute | solution.py:27
  196.5 19.0 %collective-permute-start.1 = (bf16[16,2048]{1,0:T(8,128)(2,1)S(1)}, bf16[16,2048]{1,0:T(8,128)(2,1)S(1)}, u32[]{:S(2)}, u32[]{:S(2)}) collective-permute-start(bf16[16,2048]{1,0:T(8,128)(2,1)S(1)} %get-tuple-element.1315), channel_id=1, source_target_pairs={{4,0},{8,4},{12,8},{16,12},{20,16},{24,20},{28,24},{5,1},{9,5},{13... | collective-permute-start | bytes 196616 | tf_op jit(solution)/shard_map/while/body/eval_jaxpr/ppermute | solution.py:27
  229.3 13.1 %collective-permute-start = (bf16[16,2048]{1,0:T(8,128)(2,1)S(1)}, bf16[16,2048]{1,0:T(8,128)(2,1)S(1)}, u32[]{:S(2)}, u32[]{:S(2)}) collective-permute-start(bf16[16,2048]{1,0:T(8,128)(2,1)S(1)} %get-tuple-element.1314), channel_id=1, source_target_pairs={{0,4},{4,8},{8,12},{12,16},{16,20},{20,24},{24,28},{1,5},{5,9},{9,... | collective-permute-start | bytes 196616 | tf_op jit(solution)/shard_map/while/body/eval_jaxpr/ppermute | solution.py:27
  240.5 6.2 %collective-permute-start.1 = (bf16[16,2048]{1,0:T(8,128)(2,1)S(1)}, bf16[16,2048]{1,0:T(8,128)(2,1)S(1)}, u32[]{:S(2)}, u32[]{:S(2)}) collective-permute-start(bf16[16,2048]{1,0:T(8,128)(2,1)S(1)} %get-tuple-element.1315), channel_id=1, source_target_pairs={{4,0},{8,4},{12,8},{16,12},{20,16},{24,20},{28,24},{5,1},{9,5},{13... | collective-permute-start | bytes 196616 | tf_op jit(solution)/shard_map/while/body/eval_jaxpr/ppermute | solution.py:27
  266.8 9.4 %collective-permute-start = (bf16[16,2048]{1,0:T(8,128)(2,1)S(1)}, bf16[16,2048]{1,0:T(8,128)(2,1)S(1)}, u32[]{:S(2)}, u32[]{:S(2)}) collective-permute-start(bf16[16,2048]{1,0:T(8,128)(2,1)S(1)} %get-tuple-element.1314), channel_id=1, source_target_pairs={{0,4},{4,8},{8,12},{12,16},{16,20},{20,24},{24,28},{1,5},{5,9},{9,... | collective-permute-start | bytes 196616 | tf_op jit(solution)/shard_map/while/body/eval_jaxpr/ppermute | solution.py:27
  274.3 6.2 %collective-permute-start.1 = (bf16[16,2048]{1,0:T(8,128)(2,1)S(1)}, bf16[16,2048]{1,0:T(8,128)(2,1)S(1)}, u32[]{:S(2)}, u32[]{:S(2)}) collective-permute-start(bf16[16,2048]{1,0:T(8,128)(2,1)S(1)} %get-tuple-element.1315), channel_id=1, source_target_pairs={{4,0},{8,4},{12,8},{16,12},{20,16},{24,20},{28,24},{5,1},{9,5},{13... | collective-permute-start | bytes 196616 | tf_op jit(solution)/shard_map/while/body/eval_jaxpr/ppermute | solution.py:27
  300.6 6.6 %collective-permute-start = (bf16[16,2048]{1,0:T(8,128)(2,1)S(1)}, bf16[16,2048]{1,0:T(8,128)(2,1)S(1)}, u32[]{:S(2)}, u32[]{:S(2)}) collective-permute-start(bf16[16,2048]{1,0:T(8,128)(2,1)S(1)} %get-tuple-element.1314), channel_id=1, source_target_pairs={{0,4},{4,8},{8,12},{12,16},{16,20},{20,24},{24,28},{1,5},{5,9},{9,... | collective-permute-start | bytes 196616 | tf_op jit(solution)/shard_map/while/body/eval_jaxpr/ppermute | solution.py:27
  305.4 6.2 %collective-permute-start.1 = (bf16[16,2048]{1,0:T(8,128)(2,1)S(1)}, bf16[16,2048]{1,0:T(8,128)(2,1)S(1)}, u32[]{:S(2)}, u32[]{:S(2)}) collective-permute-start(bf16[16,2048]{1,0:T(8,128)(2,1)S(1)} %get-tuple-element.1315), channel_id=1, source_target_pairs={{4,0},{8,4},{12,8},{16,12},{20,16},{24,20},{28,24},{5,1},{9,5},{13... | collective-permute-start | bytes 196616 | tf_op jit(solution)/shard_map/while/body/eval_jaxpr/ppermute | solution.py:27
  331.7 4.8 %collective-permute-start = (bf16[16,2048]{1,0:T(8,128)(2,1)S(1)}, bf16[16,2048]{1,0:T(8,128)(2,1)S(1)}, u32[]{:S(2)}, u32[]{:S(2)}) collective-permute-start(bf16[16,2048]{1,0:T(8,128)(2,1)S(1)} %get-tuple-element.1314), channel_id=1, source_target_pairs={{0,4},{4,8},{8,12},{12,16},{16,20},{20,24},{24,28},{1,5},{5,9},{9,... | collective-permute-start | bytes 196616 | tf_op jit(solution)/shard_map/while/body/eval_jaxpr/ppermute | solution.py:27
  334.6 6.2 %collective-permute-start.1 = (bf16[16,2048]{1,0:T(8,128)(2,1)S(1)}, bf16[16,2048]{1,0:T(8,128)(2,1)S(1)}, u32[]{:S(2)}, u32[]{:S(2)}) collective-permute-start(bf16[16,2048]{1,0:T(8,128)(2,1)S(1)} %get-tuple-element.1315), channel_id=1, source_target_pairs={{4,0},{8,4},{12,8},{16,12},{20,16},{24,20},{28,24},{5,1},{9,5},{13... | collective-permute-start | bytes 196616 | tf_op jit(solution)/shard_map/while/body/eval_jaxpr/ppermute | solution.py:27
  361.0 3.4 collective-permute-start
  362.3 6.2 %collective-permute-start.1 = (bf16[16,2048]{1,0:T(8,128)(2,1)S(1)}, bf16[16,2048]{1,0:T(8,128)(2,1)S(1)}, u32[]{:S(2)}, u32[]{:S(2)}) collective-permute-start(bf16[16,2048]{1,0:T(8,128)(2,1)S(1)} %get-tuple-element.1315), channel_id=1, source_target_pairs={{4,0},{8,4},{12,8},{16,12},{20,16},{24,20},{28,24},{5,1},{9,5},{13... | collective-permute-start | bytes 196616 | tf_op jit(solution)/shard_map/while/body/eval_jaxpr/ppermute | solution.py:27
  368.5 5.3 %copy-start = (f32[64,512]{1,0:T(8,128)}, f32[64,512]{1,0:T(8,128)S(1)}, u32[]{:S(2)}) copy-start(f32[64,512]{1,0:T(8,128)S(1)} %get-tuple-element.741) | copy-start | bytes 393220
  368.5 5.3 %copy-start.1 = (f32[64,512]{1,0:T(8,128)}, f32[64,512]{1,0:T(8,128)S(1)}, u32[]{:S(2)}) copy-start(f32[64,512]{1,0:T(8,128)S(1)} %get-tuple-element.742) | copy-start | bytes 393220
where the time goes:
time: 441 us; the launch traced here: 438 us
  blocking collectives  151 us (34%)
  starting transfers between devices  101 us (23%)
  waiting for transfers between devices  65.4 us (15%)
  matrix products  58.2 us (13%)
  local copies, waits for them, and re-layouts  25.9 us (6%)
  other arithmetic  21.6 us (5%)
  loops' own time  11.7 us (3%)
    ppermute x22, starting transfers between devices, shifted(): return lax.ppermute(block, axis, route)  95 us
    ppermute x22, waiting for transfers between devices, shifted(): return lax.ppermute(block, axis, route)  65.4 us
    all_gather x11, blocking collectives, one_step(): lax.all_gather(backward_piece, 'pt', axis=1, tiled=True)  59.5 us
    all_gather x11, blocking collectives, one_step(): lax.all_gather(forward_piece, 'pt', axis=1, tiled=True)  59.4 us
    dot_general x16, matrix products, add_rows(): jnp.dot(sent_part, kernel_rows(source_pts, source_norm, block_index), pre...  27 us
    dot_general x8, matrix products, ratio_part(): jnp.dot(fit_rows(block_index), inverse, precision=lax.Precision.HIGHEST)  13.8 us
    another operation x18, local copies, waits for them, and re-layouts  11.1 us
    dynamic_slice x16, local copies, waits for them, and re-layouts, shards(): lax.map(density_part, jnp.arange(fit_blocks))  9.38 us
  transfers between devices with their start and end apart: 24, of which 22 were waited for; matrix products, arithmetic and copies ran while one was open for 0% of the time, Pallas kernels for 0%

commit v1 on v0

v1 whole, which is shorter than its diff:
```python
import jax
import jax.numpy as jnp
from jax import lax
from jax.sharding import PartitionSpec as P


def shifted(block, axis, distance):
    devices = range(lax.axis_size(axis))
    route = [(i - distance, i) for i in devices if i - distance in devices]
    return lax.ppermute(block, axis, route)


def norm_of(coords):
    wide = coords.astype(jnp.float32)
    return jnp.sum(wide * wide, axis=0)


def squared_dist(left_pts, left_norm, right_pts, right_norm):
    inner = lax.dot_general(
        left_pts, right_pts, (((0,), (0,)), ((), ())), preferred_element_type=jnp.float32
    )
    return left_norm[:, None] + right_norm[None, :] - 2.0 * inner


def shards(points, cells, clone_weight, potential, support_count, cell_count):
    pt_rank = lax.axis_index("pt")
    day_index = lax.axis_index("day")
    day_count = lax.axis_size("day")
    own_pts = points[0]
    per_device = own_pts.shape[1]
    day_pts = lax.all_gather(own_pts, "pt", axis=1, tiled=True)
    before_pts = shifted(day_pts, "day", 1)
    after_pts = shifted(day_pts, "day", -1)
    support_total = day_pts.shape[1]
    block_cw = lax.all_to_all(clone_weight[0], "pt", 0, 1, tiled=True)
    full_pot = lax.all_gather(potential[0], "pt", axis=0, tiled=True)
    block_weight = block_cw * full_pot[None, :]
    block_rows = block_cw.shape[0]
    live_total = support_count[0].astype(jnp.float32)
    live_all = (jnp.arange(support_total, dtype=jnp.int32) < support_count[0]).astype(jnp.float32)
    live_own = lax.dynamic_slice_in_dim(live_all, pt_rank * per_device, per_device)
    day_norm = norm_of(day_pts)
    forward_kernel = jnp.exp(
        -squared_dist(before_pts, norm_of(before_pts), day_pts, day_norm)
    ).astype(jnp.bfloat16)
    backward_kernel = jnp.exp(
        -squared_dist(after_pts, norm_of(after_pts), day_pts, day_norm)
    ).astype(jnp.bfloat16)

    def settle(values):
        masked = values * live_all[None, :]
        return masked * live_total / jnp.sum(masked, axis=1, keepdims=True)

    seed_rows = jnp.broadcast_to(live_all[None, :], (block_rows, support_total))
    forward_rows = seed_rows
    backward_rows = seed_rows
    for step in range(day_count - 1):
        forward_in = shifted((forward_rows * block_weight).astype(jnp.bfloat16), "day", 1)
        backward_in = shifted((backward_rows * block_weight).astype(jnp.bfloat16), "day", -1)
        forward_new = settle(
            jnp.dot(forward_in, forward_kernel, preferred_element_type=jnp.float32)
        )
        backward_new = settle(
            jnp.dot(backward_in, backward_kernel, preferred_element_type=jnp.float32)
        )
        forward_rows = jnp.where(day_index == step + 1, forward_new, forward_rows)
        backward_rows = jnp.where(day_index == day_count - 2 - step, backward_new, backward_rows)

    forward_out = lax.all_to_all(forward_rows, "pt", 1, 0, tiled=True)
    backward_out = lax.all_to_all(backward_rows, "pt", 1, 0, tiled=True)
    mass_part = jnp.sum(forward_rows * block_cw * backward_rows, axis=0)
    full_mass = live_all * full_pot * lax.psum(mass_part, "pt")
    mass_total = jnp.sum(full_mass)

    cell_total = cell_count[0]
    cell_total_f = cell_total.astype(jnp.float32)
    own_cells = cells[0]
    own_slots = own_cells.shape[1]
    cell_norm = norm_of(own_cells)
    fit_kernel = jnp.exp(-squared_dist(day_pts, day_norm, own_cells, cell_norm))
    density = jnp.sum(full_mass[:, None] * fit_kernel, axis=0) / mass_total
    cell_live = (pt_rank * own_slots + jnp.arange(own_slots, dtype=jnp.int32) < cell_total).astype(
        jnp.float32
    )
    inverse = cell_live / density
    ratio_rows = jnp.sum(fit_kernel * inverse[None, :], axis=1)
    summed = lax.psum_scatter(ratio_rows, "pt", scatter_dimension=0, tiled=True)
    fit_rows_out = live_own / cell_total_f * summed
    return (forward_out[None], backward_out[None], fit_rows_out[None])


def solution(mesh):
    in_specs = (
        P("day", None, "pt"),
        P("day", None, "pt"),
        P("day", None, "pt"),
        P("day", "pt"),
        P("day"),
        P("day"),
    )
    out_specs = (P("day", None, "pt"), P("day", None, "pt"), P("day", "pt"))
    return jax.shard_map(shards, mesh=mesh, in_specs=in_specs, out_specs=out_specs, check_vma=False)
```

time: 441 us -> 179 us (0.41)
  blocking collectives: 151 us -> 26.1 us
  starting transfers between devices: 101 us -> 58.1 us
  waiting for transfers between devices: 65.4 us -> 27.5 us
  local copies, waits for them, and re-layouts: 25.9 us -> 3.84 us
  other arithmetic: 21.6 us -> 8.42 us
  loops' own time: 11.7 us -> 0 us
  matrix products: 58.2 us -> 50.3 us
    all_gather x26 -> x2, blocking collectives: 144 us -> 12.8 us  [the longest x1 7.46 us: shards(): day_pts = lax.all_gather(own_pts, 'pt', axis=1, tiled=True)]
    ppermute x22 -> x16, starting transfers between devices: 95 us -> 47.9 us  [shifted(): return lax.ppermute(block, axis, route)]
    ppermute x22 -> x16, waiting for transfers between devices: 65.4 us -> 23.6 us  [shifted(): return lax.ppermute(block, axis, route)]
    dynamic_slice x56 -> x0, local copies, waits for them, and re-layouts: 12.5 us -> none  [the longest x16 9.38 us: shards(): lax.map(density_part, jnp.arange(fit_blocks))]
    another operation x29 -> x0, loops' own time: 11.7 us -> none  [the longest x1 5.51 us: shards(): lax.map(ratio_part, jnp.arange(fit_blocks)).reshape(support_total)]
    another operation x18 -> x0, local copies, waits for them, and re-layouts: 11.1 us -> none
    dot_general x32 -> x14, matrix products: 49.5 us -> 38.9 us  [the longest x7 19.4 us: shards(): jnp.dot(backward_in, backward_kernel, preferred_element_type=jnp.float32)]
    all_to_all x0 -> x3, starting transfers between devices: none -> 10.2 us  [the longest x1 3.55 us: shards(): forward_out = lax.all_to_all(forward_rows, 'pt', 1, 0, tiled=True)]
  transfers between devices with their start and end apart: 24 -> 19, of which waited for: 22 -> 8; matrix products, arithmetic and copies ran while one was open for 0% -> 22% of each run, Pallas kernels for 0% -> 0%
where the time goes in v1:
time: 179 us; the launch traced here: 178 us
  starting transfers between devices  58.1 us (32%)
  matrix products  50.3 us (28%)
  waiting for transfers between devices  27.5 us (15%)
  blocking collectives  26.1 us (15%)
  other arithmetic  8.42 us (5%)
  local copies, waits for them, and re-layouts  3.84 us (2%)
  between operations  3.2 us (2%)
    ppermute x16, starting transfers between devices, shifted(): return lax.ppermute(block, axis, route)  47.9 us
    ppermute x16, waiting for transfers between devices, shifted(): return lax.ppermute(block, axis, route)  23.6 us
    dot_general x7, matrix products, shards(): jnp.dot(backward_in, backward_kernel, preferred_element_type=jnp.float32)  19.4 us
    dot_general x7, matrix products, shards(): jnp.dot(forward_in, forward_kernel, preferred_element_type=jnp.float32)  19.4 us
    dot_general x3, matrix products, squared_dist(): lax.dot_general(left_pts, right_pts, (((0,), (0,)), ((), ())), preferred_...  11.5 us
    unnamed x1, blocking collectives  7.54 us
    all_gather x1, blocking collectives, shards(): day_pts = lax.all_gather(own_pts, 'pt', axis=1, tiled=True)  7.46 us
    psum x1, blocking collectives, shards(): full_mass = live_all * full_pot * lax.psum(mass_part, 'pt')  5.77 us
  transfers between devices with their start and end apart: 19, of which 8 were waited for; matrix products, arithmetic and copies ran while one was open for 22% of the time, Pallas kernels for 0%

profile of v1, /device:TPU:0, one launch (start us, length us, event | category | flops | bytes accessed | tf_op | source)
XLA Modules:
  0.0 177.5 jit_solution(11294522585497066380)
XLA Ops:
  0.6 7.5 %all-gather.1 = bf16[1,64,2048]{2,1,0:T(8,128)(2,1)S(1)} all-gather(bf16[1,64,512]{2,1,0:T(8,128)(2,1)} %param.6), channel_id=3, replica_groups=mesh['day'=8,'pt'=4] {'pt'}, dimensions={2}, use_global_device_ids=true | all-gather | bytes 327680 | tf_op jit(solution)/shard_map/all_gather | solution.py:31
  8.1 3.4 %collective-permute-start.1 = (bf16[64,2048]{1,0:T(8,128)(2,1)S(1)}, bf16[64,2048]{1,0:T(8,128)(2,1)S(1)}, u32[]{:S(2)}, u32[]{:S(2)}) collective-permute-start(bf16[64,2048]{1,0:T(8,128)(2,1)S(1)} %bitcast.106), channel_id=1, source_target_pairs={{0,4},{4,8},{8,12},{12,16},{16,20},{20,24},{24,28},{1,5},{5,9},{9,... | collective-permute-start | bytes 786440 | tf_op jit(solution)/shard_map/ppermute | solution.py:10
  12.8 3.3 %all-to-all-start = ((f32[4,16,512]{2,1,0:T(8,128)}), f32[4,16,512]{2,1,0:T(8,128)S(1)}, u32[]{:S(2)}, u32[]{:S(2)}) async-start(f32[4,16,512]{2,1,0:T(8,128)} %bitcast.113), calls=%async_computation | async-start | bytes 262144 | tf_op jit(solution)/shard_map/all_to_all | solution.py:35
  16.9 5.4 %all-gather = f32[1,2048]{1,0:T(1,128)S(1)} all-gather(f32[1,512]{1,0:T(1,128)} %param.9), channel_id=2, replica_groups=mesh['day'=8,'pt'=4] {'pt'}, dimensions={1}, use_global_device_ids=true | all-gather | bytes 10240 | tf_op jit(solution)/shard_map/all_gather | solution.py:36
  22.3 4.5 %collective-permute-start = (bf16[16,2048]{1,0:T(8,128)(2,1)S(1)}, bf16[16,2048]{1,0:T(8,128)(2,1)S(1)}, u32[]{:S(2)}, u32[]{:S(2)}) collective-permute-start(bf16[16,2048]{1,0:T(8,128)(2,1)S(1)} %multiply_convert_fusion.12), channel_id=1, source_target_pairs={{0,4},{4,8},{8,12},{12,16},{16,20},{20,24},{24,28},{1,5},{5,9},{9,... | collective-permute-start | bytes 196616 | tf_op jit(solution)/shard_map/ppermute | solution.py:10
  28.3 3.6 %exponential_convert_fusion.1 = bf16[2048,2048]{1,0:T(8,128)(2,1)S(1)} fusion(bf16[64,2048]{1,0:T(8,128)(2,1)S(1)} %collective-permute-done.1, f32[2048]{0:T(1024)S(1)} %multiply_reduce_fusion.4, f32[2048]{0:T(1024)S(1)} %multiply_reduce_fusion.5, bf16[1,64,2048]{2,1,0:T(8,128)(2,1)S(1)} %all-gather.1), kind=kOutput, calls=%fused_computation.4 | convolution fusion | flops 557842432 | bytes 8929280 | tf_op jit(solution)/shard_map/dot_general | solution.py:19
  33.3 5.0 %collective-permute-start.2 = (bf16[16,2048]{1,0:T(8,128)(2,1)S(1)}, bf16[16,2048]{1,0:T(8,128)(2,1)S(1)}, u32[]{:S(2)}, u32[]{:S(2)}) collective-permute-start(bf16[16,2048]{1,0:T(8,128)(2,1)S(1)} %multiply_convert_fusion.11), channel_id=1, source_target_pairs={{0,4},{4,8},{8,12},{12,16},{16,20},{20,24},{24,28},{1,5},{5,9},{9,... | collective-permute-start | bytes 196616 | tf_op jit(solution)/shard_map/ppermute | solution.py:10
  38.4 3.6 %exponential_convert_fusion = bf16[2048,2048]{1,0:T(8,128)(2,1)S(1)} fusion(bf16[64,2048]{1,0:T(8,128)(2,1)S(1)} %collective-permute-done.9, f32[2048]{0:T(1024)S(1)} %multiply_reduce_fusion.3, f32[2048]{0:T(1024)S(1)} %multiply_reduce_fusion.4, bf16[1,64,2048]{2,1,0:T(8,128)(2,1)S(1)} %all-gather.1), kind=kOutput, calls=%fused_computation.3 | convolution fusion | flops 557842432 | bytes 8929280 | tf_op jit(solution)/shard_map/dot_general | solution.py:19
  45.3 4.8 %collective-permute-start.3 = (bf16[16,2048]{1,0:T(8,128)(2,1)S(1)}, bf16[16,2048]{1,0:T(8,128)(2,1)S(1)}, u32[]{:S(2)}, u32[]{:S(2)}) collective-permute-start(bf16[16,2048]{1,0:T(8,128)(2,1)S(1)} %get-tuple-element.18), channel_id=1, source_target_pairs={{0,4},{4,8},{8,12},{12,16},{16,20},{20,24},{24,28},{1,5},{5,9},{9,... | collective-permute-start | bytes 196616 | tf_op jit(solution)/shard_map/ppermute | solution.py:10
  50.1 1.9 %collective-permute-done.3 = bf16[16,2048]{1,0:T(8,128)(2,1)S(1)} collective-permute-done((bf16[16,2048]{1,0:T(8,128)(2,1)S(1)}, bf16[16,2048]{1,0:T(8,128)(2,1)S(1)}, u32[]{:S(2)}, u32[]{:S(2)}) %collective-permute-start.3) | collective-permute-done | bytes 65568 | tf_op jit(solution)/shard_map/ppermute | solution.py:10
  52.0 4.7 %fusion.10 = (f32[16]{0:T(128)S(1)}, f32[16,2048]{1,0:T(8,128)S(1)}) fusion(f32[2048]{0:T(1024)S(1)} %fusion.2, bf16[16,2048]{1,0:T(8,128)(2,1)S(1)} %collective-permute-done.3, bf16[2048,2048]{1,0:T(8,128)(2,1)} %copy-done), kind=kOutput, calls=%fused_computation.69 | convolution fusion | flops 134283248 | bytes 8593472 | tf_op jit(solution)/shard_map/dot_general | solution.py:61
  56.8 4.3 %collective-permute-start.4 = (bf16[16,2048]{1,0:T(8,128)(2,1)S(1)}, bf16[16,2048]{1,0:T(8,128)(2,1)S(1)}, u32[]{:S(2)}, u32[]{:S(2)}) collective-permute-start(bf16[16,2048]{1,0:T(8,128)(2,1)S(1)} %multiply_convert_fusion.9), channel_id=1, source_target_pairs={{0,4},{4,8},{8,12},{12,16},{16,20},{20,24},{24,28},{1,5},{5,9},{9,... | collective-permute-start | bytes 196616 | tf_op jit(solution)/shard_map/ppermute | solution.py:10
  61.1 1.9 %collective-permute-done.4 = bf16[16,2048]{1,0:T(8,128)(2,1)S(1)} collective-permute-done((bf16[16,2048]{1,0:T(8,128)(2,1)S(1)}, bf16[16,2048]{1,0:T(8,128)(2,1)S(1)}, u32[]{:S(2)}, u32[]{:S(2)}) %collective-permute-start.4) | collective-permute-done | bytes 65568 | tf_op jit(solution)/shard_map/ppermute | solution.py:10
  63.0 4.7 %fusion.11 = (f32[16]{0:T(128)S(1)}, f32[16,2048]{1,0:T(8,128)S(1)}) fusion(f32[2048]{0:T(1024)S(1)} %fusion.2, bf16[16,2048]{1,0:T(8,128)(2,1)S(1)} %collective-permute-done.4, bf16[2048,2048]{1,0:T(8,128)(2,1)} %copy-done), kind=kOutput, calls=%fused_computation.70 | convolution fusion | flops 134283248 | bytes 8593472 | tf_op jit(solution)/shard_map/dot_general | solution.py:61
  67.8 4.3 %collective-permute-start.5 = (bf16[16,2048]{1,0:T(8,128)(2,1)S(1)}, bf16[16,2048]{1,0:T(8,128)(2,1)S(1)}, u32[]{:S(2)}, u32[]{:S(2)}) collective-permute-start(bf16[16,2048]{1,0:T(8,128)(2,1)S(1)} %get-tuple-element.16), channel_id=1, source_target_pairs={{0,4},{4,8},{8,12},{12,16},{16,20},{20,24},{24,28},{1,5},{5,9},{9,... | collective-permute-start | bytes 196616 | tf_op jit(solution)/shard_map/ppermute | solution.py:10
  73.9 4.8 %fusion.12 = (f32[16]{0:T(128)S(1)}, f32[16,2048]{1,0:T(8,128)S(1)}) fusion(f32[2048]{0:T(1024)S(1)} %fusion.2, bf16[16,2048]{1,0:T(8,128)(2,1)S(1)} %collective-permute-done.5, bf16[2048,2048]{1,0:T(8,128)(2,1)} %copy-done), kind=kOutput, calls=%fused_computation.71 | convolution fusion | flops 134283248 | bytes 8593472 | tf_op jit(solution)/shard_map/dot_general | solution.py:61
  78.9 4.7 %collective-permute-start.6 = (bf16[16,2048]{1,0:T(8,128)(2,1)S(1)}, bf16[16,2048]{1,0:T(8,128)(2,1)S(1)}, u32[]{:S(2)}, u32[]{:S(2)}) collective-permute-start(bf16[16,2048]{1,0:T(8,128)(2,1)S(1)} %multiply_convert_fusion.7), channel_id=1, source_target_pairs={{0,4},{4,8},{8,12},{12,16},{16,20},{20,24},{24,28},{1,5},{5,9},{9,... | collective-permute-start | bytes 196616 | tf_op jit(solution)/shard_map/ppermute | solution.py:10
  83.6 4.7 %fusion.14 = (f32[16]{0:T(128)S(1)}, f32[16,2048]{1,0:T(8,128)S(1)}) fusion(f32[2048]{0:T(1024)S(1)} %fusion.2, bf16[16,2048]{1,0:T(8,128)(2,1)S(1)} %collective-permute-done.10, bf16[2048,2048]{1,0:T(8,128)(2,1)} %copy-done.1), kind=kOutput, calls=%fused_computation.73 | convolution fusion | flops 134283248 | bytes 8593472 | tf_op jit(solution)/shard_map/dot_general | solution.py:64
  91.1 5.7 %collective-permute-done.11 = bf16[16,2048]{1,0:T(8,128)(2,1)S(1)} collective-permute-done((bf16[16,2048]{1,0:T(8,128)(2,1)S(1)}, bf16[16,2048]{1,0:T(8,128)(2,1)S(1)}, u32[]{:S(2)}, u32[]{:S(2)}) %collective-permute-start.11) | collective-permute-done | bytes 65568 | tf_op jit(solution)/shard_map/ppermute | solution.py:10
  99.7 5.8 %collective-permute-done.12 = bf16[16,2048]{1,0:T(8,128)(2,1)S(1)} collective-permute-done((bf16[16,2048]{1,0:T(8,128)(2,1)S(1)}, bf16[16,2048]{1,0:T(8,128)(2,1)S(1)}, u32[]{:S(2)}, u32[]{:S(2)}) %collective-permute-start.12) | collective-permute-done | bytes 65568 | tf_op jit(solution)/shard_map/ppermute | solution.py:10
  110.1 3.8 %collective-permute-done.13 = bf16[16,2048]{1,0:T(8,128)(2,1)S(1)} collective-permute-done((bf16[16,2048]{1,0:T(8,128)(2,1)S(1)}, bf16[16,2048]{1,0:T(8,128)(2,1)S(1)}, u32[]{:S(2)}, u32[]{:S(2)}) %collective-permute-start.13) | collective-permute-done | bytes 65568 | tf_op jit(solution)/shard_map/ppermute | solution.py:10
  113.9 4.8 %fusion.17 = (f32[16]{0:T(128)S(1)}, f32[16,2048]{1,0:T(8,128)S(1)}) fusion(f32[2048]{0:T(1024)S(1)} %fusion.2, bf16[16,2048]{1,0:T(8,128)(2,1)S(1)} %collective-permute-done.13, bf16[2048,2048]{1,0:T(8,128)(2,1)} %copy-done.1), kind=kOutput, calls=%fused_computation.76 | convolution fusion | flops 134283248 | bytes 8593472 | tf_op jit(solution)/shard_map/dot_general | solution.py:64
  120.5 5.7 %collective-permute-start.7 = (bf16[16,2048]{1,0:T(8,128)(2,1)S(1)}, bf16[16,2048]{1,0:T(8,128)(2,1)S(1)}, u32[]{:S(2)}, u32[]{:S(2)}) collective-permute-start(bf16[16,2048]{1,0:T(8,128)(2,1)S(1)} %get-tuple-element.14), channel_id=1, source_target_pairs={{0,4},{4,8},{8,12},{12,16},{16,20},{20,24},{24,28},{1,5},{5,9},{9,... | collective-permute-start | bytes 196616 | tf_op jit(solution)/shard_map/ppermute | solution.py:10
  126.3 4.7 %fusion.18 = (f32[16]{0:T(128)S(1)}, f32[16,2048]{1,0:T(8,128)S(1)}) fusion(f32[2048]{0:T(1024)S(1)} %fusion.2, bf16[16,2048]{1,0:T(8,128)(2,1)S(1)} %collective-permute-done.14, bf16[2048,2048]{1,0:T(8,128)(2,1)} %copy-done.1), kind=kOutput, calls=%fused_computation.77 | convolution fusion | flops 134283248 | bytes 8593472 | tf_op jit(solution)/shard_map/dot_general | solution.py:64
  133.7 4.4 %collective-permute-done.15 = bf16[16,2048]{1,0:T(8,128)(2,1)S(1)} collective-permute-done((bf16[16,2048]{1,0:T(8,128)(2,1)S(1)}, bf16[16,2048]{1,0:T(8,128)(2,1)S(1)}, u32[]{:S(2)}, u32[]{:S(2)}) %collective-permute-start.15) | collective-permute-done | bytes 65568 | tf_op jit(solution)/shard_map/ppermute | solution.py:10
  139.6 5.8 %psum.7 = f32[2048]{0:T(1024)S(1)} all-reduce(f32[2048]{0:T(1024)S(1)} %get-tuple-element.5), channel_id=1, replica_groups=mesh['day'=8,'pt'=4] {'pt'}, use_global_device_ids=true, to_apply=%region_19.20 | all-reduce | flops 2048 | bytes 16384 | tf_op jit(solution)/shard_map/psum | solution.py:72
  146.0 3.5 %all-to-all-start.1 = ((f32[16,4,512]{2,0,1:T(8,128)}), f32[16,4,512]{2,0,1:T(8,128)S(1)}, u32[]{:S(2)}, u32[]{:S(2)}) async-start(f32[16,4,512]{2,0,1:T(8,128)} %bitcast.68), calls=%async_computation.1 | async-start | bytes 262144 | tf_op jit(solution)/shard_map/all_to_all | solution.py:69
  150.2 4.3 %multiply_reduce_fusion.1 = (f32[2048]{0:T(1024)S(1)}, f32[2048,2048]{1,0:T(8,128)S(1)}) fusion(f32[2048]{0:T(1024)S(1)} %get-tuple-element.4, f32[2048]{0:T(1024)S(1)} %multiply_reduce_fusion.2, f32[2048]{0:T(1024)S(1)} %multiply_reduce_fusion.4, bf16[1,64,2048]{2,1,0:T(8,128)(2,1)S(1)} %copy-done.2, bf16[1,64,2048]{2,1,0:T(8,128)(2,1)S(1)} %all-gather.1), kind=kOutput, calls=%fused_computation.1 | convolution fusion | flops 562034688 | bytes 17334272 | tf_op jit(solution)/shard_map/dot_general | solution.py:19
  155.1 5.0 %multiply_reduce_fusion = f32[2048]{0:T(1024)S(1)} fusion(f32[2048,2048]{1,0:T(8,128)S(1)} %get-tuple-element.52, f32[2048]{0:T(1024)S(1)} %select_divide_fusion, f32[2048]{0:T(1024)S(1)} %multiply_reduce_fusion.2, f32[2048]{0:T(1024)S(1)} %multiply_reduce_fusion.4), kind=kLoop, calls=%fused_computation | loop fusion | flops 25163776 | bytes 16809984 | tf_op jit(solution)/shard_map/reduce_sum | solution.py:86
  160.8 7.5 %all-reduce = f32[2048]{0:T(1024)S(1)} all-reduce(f32[2048]{0:T(1024)S(1)} %multiply_reduce_fusion), channel_id=4, replica_groups=mesh['day'=8,'pt'=4] {'pt'}, use_global_device_ids=true, to_apply=%region_23.24.clone | all-reduce | flops 2048 | bytes 16384
  168.3 3.3 %all-to-all-start.2 = ((f32[16,4,512]{2,0,1:T(8,128)}), f32[16,4,512]{2,0,1:T(8,128)S(1)}, u32[]{:S(2)}, u32[]{:S(2)}) async-start(f32[16,4,512]{2,0,1:T(8,128)} %bitcast.67), calls=%async_computation.2 | async-start | bytes 262144 | tf_op jit(solution)/shard_map/all_to_all | solution.py:70
  172.3 3.9 %all-to-all-done.2 = f32[16,4,512]{2,0,1:T(8,128)S(1)} async-done(((f32[16,4,512]{2,0,1:T(8,128)}), f32[16,4,512]{2,0,1:T(8,128)S(1)}, u32[]{:S(2)}, u32[]{:S(2)}) %all-to-all-start.2) | async-done | bytes 131104 | tf_op jit(solution)/shard_map/all_to_all | solution.py:70
  (82 shorter events, 29.1 us)
Async XLA Ops:
  8.1 20.1 %collective-permute-start.1 = (bf16[64,2048]{1,0:T(8,128)(2,1)S(1)}, bf16[64,2048]{1,0:T(8,128)(2,1)S(1)}, u32[]{:S(2)}, u32[]{:S(2)}) collective-permute-start(bf16[64,2048]{1,0:T(8,128)(2,1)S(1)} %bitcast.106), channel_id=1, source_target_pairs={{0,4},{4,8},{8,12},{12,16},{16,20},{20,24},{24,28},{1,5},{5,9},{9,... | collective-permute-start | bytes 786440 | tf_op jit(solution)/shard_map/ppermute | solution.py:10
  11.5 26.8 %collective-permute-start.9 = (bf16[64,2048]{1,0:T(8,128)(2,1)S(1)}, bf16[64,2048]{1,0:T(8,128)(2,1)S(1)}, u32[]{:S(2)}, u32[]{:S(2)}) collective-permute-start(bf16[64,2048]{1,0:T(8,128)(2,1)S(1)} %bitcast.107), channel_id=1, source_target_pairs={{4,0},{8,4},{12,8},{16,12},{20,16},{24,20},{28,24},{5,1},{9,5},{13... | collective-permute-start | bytes 786440 | tf_op jit(solution)/shard_map/ppermute | solution.py:10
  12.8 9.5 %all-to-all-start = ((f32[4,16,512]{2,1,0:T(8,128)}), f32[4,16,512]{2,1,0:T(8,128)S(1)}, u32[]{:S(2)}, u32[]{:S(2)}) async-start(f32[4,16,512]{2,1,0:T(8,128)} %bitcast.113), calls=%async_computation | async-start | bytes 262144 | tf_op jit(solution)/shard_map/all_to_all | solution.py:35
  22.3 9.6 %collective-permute-start = (bf16[16,2048]{1,0:T(8,128)(2,1)S(1)}, bf16[16,2048]{1,0:T(8,128)(2,1)S(1)}, u32[]{:S(2)}, u32[]{:S(2)}) collective-permute-start(bf16[16,2048]{1,0:T(8,128)(2,1)S(1)} %multiply_convert_fusion.12), channel_id=1, source_target_pairs={{0,4},{4,8},{8,12},{12,16},{16,20},{20,24},{24,28},{1,5},{5,9},{9,... | collective-permute-start | bytes 196616 | tf_op jit(solution)/shard_map/ppermute | solution.py:10
  26.9 15.1 %collective-permute-start.8 = (bf16[16,2048]{1,0:T(8,128)(2,1)S(1)}, bf16[16,2048]{1,0:T(8,128)(2,1)S(1)}, u32[]{:S(2)}, u32[]{:S(2)}) collective-permute-start(bf16[16,2048]{1,0:T(8,128)(2,1)S(1)} %multiply_convert_fusion.12), channel_id=1, source_target_pairs={{4,0},{8,4},{12,8},{16,12},{20,16},{24,20},{28,24},{5,1},{9,5},{13... | collective-permute-start | bytes 196616 | tf_op jit(solution)/shard_map/ppermute | solution.py:10
  31.9 11.4 %copy-start = (bf16[2048,2048]{1,0:T(8,128)(2,1)}, bf16[2048,2048]{1,0:T(8,128)(2,1)S(1)}, u32[]{:S(2)}) copy-start(bf16[2048,2048]{1,0:T(8,128)(2,1)S(1)} %exponential_convert_fusion.1) | copy-start | bytes 25165828
  33.3 10.0 %collective-permute-start.2 = (bf16[16,2048]{1,0:T(8,128)(2,1)S(1)}, bf16[16,2048]{1,0:T(8,128)(2,1)S(1)}, u32[]{:S(2)}, u32[]{:S(2)}) collective-permute-start(bf16[16,2048]{1,0:T(8,128)(2,1)S(1)} %multiply_convert_fusion.11), channel_id=1, source_target_pairs={{0,4},{4,8},{8,12},{12,16},{16,20},{20,24},{24,28},{1,5},{5,9},{9,... | collective-permute-start | bytes 196616 | tf_op jit(solution)/shard_map/ppermute | solution.py:10
  41.9 3.2 %copy-start.1 = (bf16[2048,2048]{1,0:T(8,128)(2,1)}, bf16[2048,2048]{1,0:T(8,128)(2,1)S(1)}, u32[]{:S(2)}) copy-start(bf16[2048,2048]{1,0:T(8,128)(2,1)S(1)} %exponential_convert_fusion) | copy-start | bytes 25165828
  45.3 6.7 %collective-permute-start.3 = (bf16[16,2048]{1,0:T(8,128)(2,1)S(1)}, bf16[16,2048]{1,0:T(8,128)(2,1)S(1)}, u32[]{:S(2)}, u32[]{:S(2)}) collective-permute-start(bf16[16,2048]{1,0:T(8,128)(2,1)S(1)} %get-tuple-element.18), channel_id=1, source_target_pairs={{0,4},{4,8},{8,12},{12,16},{16,20},{20,24},{24,28},{1,5},{5,9},{9,... | collective-permute-start | bytes 196616 | tf_op jit(solution)/shard_map/ppermute | solution.py:10
  56.8 6.2 %collective-permute-start.4 = (bf16[16,2048]{1,0:T(8,128)(2,1)S(1)}, bf16[16,2048]{1,0:T(8,128)(2,1)S(1)}, u32[]{:S(2)}, u32[]{:S(2)}) collective-permute-start(bf16[16,2048]{1,0:T(8,128)(2,1)S(1)} %multiply_convert_fusion.9), channel_id=1, source_target_pairs={{0,4},{4,8},{8,12},{12,16},{16,20},{20,24},{24,28},{1,5},{5,9},{9,... | collective-permute-start | bytes 196616 | tf_op jit(solution)/shard_map/ppermute | solution.py:10
  67.8 6.2 %collective-permute-start.5 = (bf16[16,2048]{1,0:T(8,128)(2,1)S(1)}, bf16[16,2048]{1,0:T(8,128)(2,1)S(1)}, u32[]{:S(2)}, u32[]{:S(2)}) collective-permute-start(bf16[16,2048]{1,0:T(8,128)(2,1)S(1)} %get-tuple-element.16), channel_id=1, source_target_pairs={{0,4},{4,8},{8,12},{12,16},{16,20},{20,24},{24,28},{1,5},{5,9},{9,... | collective-permute-start | bytes 196616 | tf_op jit(solution)/shard_map/ppermute | solution.py:10
  72.1 16.3 %slice-start = ((s8[8388608]{0:T(1024)(128)(4,1)}), s8[4194304]{0:T(1024)(128)(4,1)S(1)}, s32[]{:S(2)}) async-start(s8[8388608]{0:T(1024)(128)(4,1)} %bitcast.74), calls=%async_computation.3 | async-start | bytes 8388608
  72.1 11.5 %collective-permute-start.10 = (bf16[16,2048]{1,0:T(8,128)(2,1)S(1)}, bf16[16,2048]{1,0:T(8,128)(2,1)S(1)}, u32[]{:S(2)}, u32[]{:S(2)}) collective-permute-start(bf16[16,2048]{1,0:T(8,128)(2,1)S(1)} %get-tuple-element.20), channel_id=1, source_target_pairs={{4,0},{8,4},{12,8},{16,12},{20,16},{24,20},{28,24},{5,1},{9,5},{13... | collective-permute-start | bytes 196616 | tf_op jit(solution)/shard_map/ppermute | solution.py:10
  73.9 22.9 %slice-start.4 = ((s8[8388608]{0:T(1024)(128)(4,1)}), s8[4194304]{0:T(1024)(128)(4,1)S(1)}, s32[]{:S(2)}) async-start(s8[8388608]{0:T(1024)(128)(4,1)} %bitcast.78), calls=%async_computation.7 | async-start | bytes 8388608
  78.8 9.6 %slice-start.1 = ((s8[8388608]{0:T(1024)(128)(4,1)}), s8[4194304]{0:T(1024)(128)(4,1)S(1)}, s32[]{:S(2)}) async-start(s8[8388608]{0:T(1024)(128)(4,1)} %bitcast.74), calls=%async_computation.4 | async-start | bytes 8388608
  78.9 17.9 %slice-start.5 = ((s8[8388608]{0:T(1024)(128)(4,1)}), s8[4194304]{0:T(1024)(128)(4,1)S(1)}, s32[]{:S(2)}) async-start(s8[8388608]{0:T(1024)(128)(4,1)} %bitcast.78), calls=%async_computation.8 | async-start | bytes 8388608
  78.9 9.4 %collective-permute-start.6 = (bf16[16,2048]{1,0:T(8,128)(2,1)S(1)}, bf16[16,2048]{1,0:T(8,128)(2,1)S(1)}, u32[]{:S(2)}, u32[]{:S(2)}) collective-permute-start(bf16[16,2048]{1,0:T(8,128)(2,1)S(1)} %multiply_convert_fusion.7), channel_id=1, source_target_pairs={{0,4},{4,8},{8,12},{12,16},{16,20},{20,24},{24,28},{1,5},{5,9},{9,... | collective-permute-start | bytes 196616 | tf_op jit(solution)/shard_map/ppermute | solution.py:10
  89.8 19.0 %copy-start.3 = (u32[32]{0:T(128)S(1)}, u32[32]{0:T(128)}, u32[]{:S(2)}) copy-start(u32[32]{0:T(128)} %constant.43) | copy-start | bytes 388
  89.8 7.0 %collective-permute-start.11 = (bf16[16,2048]{1,0:T(8,128)(2,1)S(1)}, bf16[16,2048]{1,0:T(8,128)(2,1)S(1)}, u32[]{:S(2)}, u32[]{:S(2)}) collective-permute-start(bf16[16,2048]{1,0:T(8,128)(2,1)S(1)} %get-tuple-element.21), channel_id=1, source_target_pairs={{4,0},{8,4},{12,8},{16,12},{20,16},{24,20},{28,24},{5,1},{9,5},{13... | collective-permute-start | bytes 196616 | tf_op jit(solution)/shard_map/ppermute | solution.py:10
  98.2 22.2 %copy-start.2 = (bf16[1,64,2048]{2,1,0:T(8,128)(2,1)S(1)}, bf16[1,64,2048]{2,1,0:T(8,128)(2,1)}, u32[]{:S(2)}) copy-start(bf16[1,64,2048]{2,1,0:T(8,128)(2,1)} %param.7) | copy-start | bytes 786436
  98.2 7.2 %collective-permute-start.12 = (bf16[16,2048]{1,0:T(8,128)(2,1)S(1)}, bf16[16,2048]{1,0:T(8,128)(2,1)S(1)}, u32[]{:S(2)}, u32[]{:S(2)}) collective-permute-start(bf16[16,2048]{1,0:T(8,128)(2,1)S(1)} %multiply_convert_fusion.3), channel_id=1, source_target_pairs={{4,0},{8,4},{12,8},{16,12},{20,16},{24,20},{28,24},{5,1},{9,5},{13... | collective-permute-start | bytes 196616 | tf_op jit(solution)/shard_map/ppermute | solution.py:10
  106.8 7.1 %collective-permute-start.13 = (bf16[16,2048]{1,0:T(8,128)(2,1)S(1)}, bf16[16,2048]{1,0:T(8,128)(2,1)S(1)}, u32[]{:S(2)}, u32[]{:S(2)}) collective-permute-start(bf16[16,2048]{1,0:T(8,128)(2,1)S(1)} %get-tuple-element.10), channel_id=1, source_target_pairs={{4,0},{8,4},{12,8},{16,12},{20,16},{24,20},{28,24},{5,1},{9,5},{13... | collective-permute-start | bytes 196616 | tf_op jit(solution)/shard_map/ppermute | solution.py:10
  110.1 22.3 %slice-start.2 = ((s8[8388608]{0:T(1024)(128)(4,1)}), s8[4194304]{0:T(1024)(128)(4,1)S(1)}, s32[]{:S(2)}) async-start(s8[8388608]{0:T(1024)(128)(4,1)} %bitcast.76), calls=%async_computation.5 | async-start | bytes 8388608
  113.9 24.2 %slice-start.6 = ((s8[8388608]{0:T(1024)(128)(4,1)}), s8[4194304]{0:T(1024)(128)(4,1)S(1)}, s32[]{:S(2)}) async-start(s8[8388608]{0:T(1024)(128)(4,1)} %bitcast.80), calls=%async_computation.9 | async-start | bytes 8388608
  118.9 13.5 %slice-start.3 = ((s8[8388608]{0:T(1024)(128)(4,1)}), s8[4194304]{0:T(1024)(128)(4,1)S(1)}, s32[]{:S(2)}) async-start(s8[8388608]{0:T(1024)(128)(4,1)} %bitcast.76), calls=%async_computation.6 | async-start | bytes 8388608
  118.9 7.4 %collective-permute-start.14 = (bf16[16,2048]{1,0:T(8,128)(2,1)S(1)}, bf16[16,2048]{1,0:T(8,128)(2,1)S(1)}, u32[]{:S(2)}, u32[]{:S(2)}) collective-permute-start(bf16[16,2048]{1,0:T(8,128)(2,1)S(1)} %multiply_convert_fusion.1), channel_id=1, source_target_pairs={{4,0},{8,4},{12,8},{16,12},{20,16},{24,20},{28,24},{5,1},{9,5},{13... | collective-permute-start | bytes 196616 | tf_op jit(solution)/shard_map/ppermute | solution.py:10
  120.5 17.6 %slice-start.7 = ((s8[8388608]{0:T(1024)(128)(4,1)}), s8[4194304]{0:T(1024)(128)(4,1)S(1)}, s32[]{:S(2)}) async-start(s8[8388608]{0:T(1024)(128)(4,1)} %bitcast.80), calls=%async_computation.10 | async-start | bytes 8388608
  120.5 11.8 %collective-permute-start.7 = (bf16[16,2048]{1,0:T(8,128)(2,1)S(1)}, bf16[16,2048]{1,0:T(8,128)(2,1)S(1)}, u32[]{:S(2)}, u32[]{:S(2)}) collective-permute-start(bf16[16,2048]{1,0:T(8,128)(2,1)S(1)} %get-tuple-element.14), channel_id=1, source_target_pairs={{0,4},{4,8},{8,12},{12,16},{16,20},{20,24},{24,28},{1,5},{5,9},{9,... | collective-permute-start | bytes 196616 | tf_op jit(solution)/shard_map/ppermute | solution.py:10
  131.1 7.1 %collective-permute-start.15 = (bf16[16,2048]{1,0:T(8,128)(2,1)S(1)}, bf16[16,2048]{1,0:T(8,128)(2,1)S(1)}, u32[]{:S(2)}, u32[]{:S(2)}) collective-permute-start(bf16[16,2048]{1,0:T(8,128)(2,1)S(1)} %get-tuple-element.8), channel_id=1, source_target_pairs={{4,0},{8,4},{12,8},{16,12},{20,16},{24,20},{28,24},{5,1},{9,5},{13... | collective-permute-start | bytes 196616 | tf_op jit(solution)/shard_map/ppermute | solution.py:10
  146.0 22.3 %all-to-all-start.1 = ((f32[16,4,512]{2,0,1:T(8,128)}), f32[16,4,512]{2,0,1:T(8,128)S(1)}, u32[]{:S(2)}, u32[]{:S(2)}) async-start(f32[16,4,512]{2,0,1:T(8,128)} %bitcast.68), calls=%async_computation.1 | async-start | bytes 262144 | tf_op jit(solution)/shard_map/all_to_all | solution.py:69
  168.3 7.9 %all-to-all-start.2 = ((f32[16,4,512]{2,0,1:T(8,128)}), f32[16,4,512]{2,0,1:T(8,128)S(1)}, u32[]{:S(2)}, u32[]{:S(2)}) async-start(f32[16,4,512]{2,0,1:T(8,128)} %bitcast.67), calls=%async_computation.2 | async-start | bytes 262144 | tf_op jit(solution)/shard_map/all_to_all | solution.py:70

commit v2 on v1

--- a/solution.py
+++ b/solution.py
@@ -40,31 +40,36 @@
     live_all = (jnp.arange(support_total, dtype=jnp.int32) < support_count[0]).astype(jnp.float32)
     live_own = lax.dynamic_slice_in_dim(live_all, pt_rank * per_device, per_device)
     day_norm = norm_of(day_pts)
-    forward_kernel = jnp.exp(
-        -squared_dist(before_pts, norm_of(before_pts), day_pts, day_norm)
-    ).astype(jnp.bfloat16)
-    backward_kernel = jnp.exp(
-        -squared_dist(after_pts, norm_of(after_pts), day_pts, day_norm)
+    source_pts = jnp.stack([before_pts, after_pts])
+    source_norm = jnp.stack([norm_of(before_pts), norm_of(after_pts)])
+    inner = lax.dot_general(
+        source_pts, day_pts, (((1,), (0,)), ((), ())), preferred_element_type=jnp.float32
+    )
+    chain_kernel = jnp.exp(
+        -(source_norm[:, :, None] + day_norm[None, None, :] - 2.0 * inner)
     ).astype(jnp.bfloat16)
 
     def settle(values):
-        masked = values * live_all[None, :]
-        return masked * live_total / jnp.sum(masked, axis=1, keepdims=True)
+        masked = values * live_all[None, None, :]
+        return masked * live_total / jnp.sum(masked, axis=2, keepdims=True)
 
-    seed_rows = jnp.broadcast_to(live_all[None, :], (block_rows, support_total))
-    forward_rows = seed_rows
-    backward_rows = seed_rows
+    seed_rows = jnp.broadcast_to(live_all[None, None, :], (2, block_rows, support_total))
+    rows = seed_rows
     for step in range(day_count - 1):
-        forward_in = shifted((forward_rows * block_weight).astype(jnp.bfloat16), "day", 1)
-        backward_in = shifted((backward_rows * block_weight).astype(jnp.bfloat16), "day", -1)
-        forward_new = settle(
-            jnp.dot(forward_in, forward_kernel, preferred_element_type=jnp.float32)
+        sent = (rows * block_weight[None]).astype(jnp.bfloat16)
+        arrived = jnp.stack([shifted(sent[0], "day", 1), shifted(sent[1], "day", -1)])
+        fresh = settle(
+            lax.dot_general(
+                arrived,
+                chain_kernel,
+                (((2,), (1,)), ((0,), (0,))),
+                preferred_element_type=jnp.float32,
+            )
         )
-        backward_new = settle(
-            jnp.dot(backward_in, backward_kernel, preferred_element_type=jnp.float32)
-        )
-        forward_rows = jnp.where(day_index == step + 1, forward_new, forward_rows)
-        backward_rows = jnp.where(day_index == day_count - 2 - step, backward_new, backward_rows)
+        keep = jnp.stack([day_index == step + 1, day_index == day_count - 2 - step])
+        rows = jnp.where(keep[:, None, None], fresh, rows)
+    forward_rows = rows[0]
+    backward_rows = rows[1]
 
     forward_out = lax.all_to_all(forward_rows, "pt", 1, 0, tiled=True)
     backward_out = lax.all_to_all(backward_rows, "pt", 1, 0, tiled=True)

time: 179 us -> 159 us (0.89)
  matrix products: 50.3 us -> 27.6 us
  waiting for transfers between devices: 27.5 us -> 33.3 us
  starting transfers between devices: 58.1 us -> 54 us
    dot_general x14 -> x8, matrix products: 38.9 us -> 23.2 us  [the longest x7 16 us: shards(): lax.dot_general(arrived, chain_kernel, (((2,), (1,)), ((0,), (0,))), pref...]
    dot_general x3 -> x1, matrix products: 11.5 us -> 4.47 us  [squared_dist(): lax.dot_general(left_pts, right_pts, (((0,), (0,)), ((), ())), preferred_...]
    ppermute x16, waiting for transfers between devices: 23.6 us -> 29.4 us  [shifted(): return lax.ppermute(block, axis, route)]
    ppermute x16, starting transfers between devices: 47.9 us -> 43.8 us  [shifted(): return lax.ppermute(block, axis, route)]
  transfers between devices with their start and end apart: 19 -> 19, of which waited for: 8 -> 13; matrix products, arithmetic and copies ran while one was open for 22% -> 14% of each run, Pallas kernels for 0% -> 0%
where the time goes in v2:
time: 159 us; the launch traced here: 158 us
  starting transfers between devices  54 us (34%)
  waiting for transfers between devices  33.3 us (21%)
  matrix products  27.6 us (17%)
  blocking collectives  26.1 us (16%)
  other arithmetic  9.73 us (6%)
  local copies, waits for them, and re-layouts  4.32 us (3%)
  between operations  3.07 us (2%)
    ppermute x16, starting transfers between devices, shifted(): return lax.ppermute(block, axis, route)  43.8 us
    ppermute x16, waiting for transfers between devices, shifted(): return lax.ppermute(block, axis, route)  29.4 us
    dot_general x7, matrix products, shards(): lax.dot_general(arrived, chain_kernel, (((2,), (1,)), ((0,), (0,))), pref...  16 us
    unnamed x1, blocking collectives  7.47 us
    all_gather x1, blocking collectives, shards(): day_pts = lax.all_gather(own_pts, 'pt', axis=1, tiled=True)  7.46 us
    dot_general x1, matrix products, shards(): lax.dot_general(source_pts, day_pts, (((1,), (0,)), ((), ())), preferred_...  7.13 us
    psum x1, blocking collectives, shards(): full_mass = live_all * full_pot * lax.psum(mass_part, 'pt')  5.77 us
    all_gather x1, blocking collectives, shards(): full_pot = lax.all_gather(potential[0], 'pt', axis=0, tiled=True)  5.38 us
  transfers between devices with their start and end apart: 19, of which 13 were waited for; matrix products, arithmetic and copies ran while one was open for 14% of the time, Pallas kernels for 0%

profile of v2, /device:TPU:0, one launch (start us, length us, event | category | flops | bytes accessed | tf_op | source)
XLA Modules:
  0.0 158.2 jit_solution(5743984149731426951)
XLA Ops:
  0.6 7.5 %all-gather.1 = bf16[1,64,2048]{2,1,0:T(8,128)(2,1)S(1)} all-gather(bf16[1,64,512]{2,1,0:T(8,128)(2,1)} %param.6), channel_id=3, replica_groups=mesh['day'=8,'pt'=4] {'pt'}, dimensions={2}, use_global_device_ids=true | all-gather | bytes 327680 | tf_op jit(solution)/shard_map/all_gather | solution.py:31
  8.1 3.4 %collective-permute-start.2 = (bf16[64,2048]{1,0:T(8,128)(2,1)S(1)}, bf16[64,2048]{1,0:T(8,128)(2,1)S(1)}, u32[]{:S(2)}, u32[]{:S(2)}) collective-permute-start(bf16[64,2048]{1,0:T(8,128)(2,1)S(1)} %bitcast.112), channel_id=1, source_target_pairs={{0,4},{4,8},{8,12},{12,16},{16,20},{20,24},{24,28},{1,5},{5,9},{9,... | collective-permute-start | bytes 786440 | tf_op jit(solution)/shard_map/ppermute | solution.py:10
  12.8 3.3 %all-to-all-start = ((f32[4,16,512]{2,1,0:T(8,128)}), f32[4,16,512]{2,1,0:T(8,128)S(1)}, u32[]{:S(2)}, u32[]{:S(2)}) async-start(f32[4,16,512]{2,1,0:T(8,128)} %bitcast.119), calls=%async_computation | async-start | bytes 262144 | tf_op jit(solution)/shard_map/all_to_all | solution.py:35
  16.9 5.4 %all-gather = f32[1,2048]{1,0:T(1,128)S(1)} all-gather(f32[1,512]{1,0:T(1,128)} %param.9), channel_id=2, replica_groups=mesh['day'=8,'pt'=4] {'pt'}, dimensions={1}, use_global_device_ids=true | all-gather | bytes 10240 | tf_op jit(solution)/shard_map/all_gather | solution.py:36
  26.1 4.5 %collective-permute-start = (bf16[16,2048]{1,0:T(8,128)(2,1)S(1)}, bf16[16,2048]{1,0:T(8,128)(2,1)S(1)}, u32[]{:S(2)}, u32[]{:S(2)}) collective-permute-start(bf16[16,2048]{1,0:T(8,128)(2,1)S(1)} %get-tuple-element.19), channel_id=1, source_target_pairs={{0,4},{4,8},{8,12},{12,16},{16,20},{20,24},{24,28},{1,5},{5,9},{9,... | collective-permute-start | bytes 196616 | tf_op jit(solution)/shard_map/ppermute | solution.py:10
  32.2 7.1 %exponential_convert_fusion = bf16[2,2048,2048]{2,1,0:T(8,128)(2,1)S(1)} fusion(f32[2048]{0:T(1024)S(1)} %multiply_reduce_fusion.3, f32[2,2048]{1,0:T(2,128)S(1)} %pad_maximum_fusion, bf16[1,64,2048]{2,1,0:T(8,128)(2,1)S(1)} %bitcast.118, bf16[1,64,2048]{2,1,0:T(8,128)(2,1)S(1)} %bitcast.117, bf16[1,64,2048]{2,1,0:T(8,128)(2,1)S(1)} %all-gather.1), kind=kOutput, calls=%fused_computation.6 | convolution fusion | flops 1115947008 | bytes 17588224 | tf_op jit(solution)/shard_map/dot_general | solution.py:45
  39.4 2.3 %convolution_multiply_fusion.6 = f32[2,16,2048]{2,1,0:T(8,128)S(1)} fusion(bf16[2,2048,2048]{2,1,0:T(8,128)(2,1)S(1)} %exponential_convert_fusion, bf16[1,16,2048]{2,1,0:T(8,128)(2,1)S(1)} %bitcast.123, bf16[1,16,2048]{2,1,0:T(8,128)(2,1)S(1)} %bitcast.122, f32[2048]{0:T(1024)S(1)} %fusion.34), kind=kOutput, calls=%fused_computation.16 | convolution fusion | flops 268566528 | bytes 17178624 | tf_op jit(solution)/shard_map/dot_general | solution.py:62
  41.8 5.0 %collective-permute-start.4 = (bf16[16,2048]{1,0:T(8,128)(2,1)S(1)}, bf16[16,2048]{1,0:T(8,128)(2,1)S(1)}, u32[]{:S(2)}, u32[]{:S(2)}) collective-permute-start(bf16[16,2048]{1,0:T(8,128)(2,1)S(1)} %get-tuple-element.17), channel_id=1, source_target_pairs={{0,4},{4,8},{8,12},{12,16},{16,20},{20,24},{24,28},{1,5},{5,9},{9,... | collective-permute-start | bytes 196616 | tf_op jit(solution)/shard_map/ppermute | solution.py:10
  48.7 5.2 %collective-permute-done.5 = bf16[16,2048]{1,0:T(8,128)(2,1)S(1)} collective-permute-done((bf16[16,2048]{1,0:T(8,128)(2,1)S(1)}, bf16[16,2048]{1,0:T(8,128)(2,1)S(1)}, u32[]{:S(2)}, u32[]{:S(2)}) %collective-permute-start.5) | collective-permute-done | bytes 65568 | tf_op jit(solution)/shard_map/ppermute | solution.py:10
  53.8 2.3 %convolution_multiply_fusion.5 = f32[2,16,2048]{2,1,0:T(8,128)S(1)} fusion(bf16[2,2048,2048]{2,1,0:T(8,128)(2,1)S(1)} %exponential_convert_fusion, bf16[1,16,2048]{2,1,0:T(8,128)(2,1)S(1)} %bitcast.134, bf16[1,16,2048]{2,1,0:T(8,128)(2,1)S(1)} %bitcast.129, f32[2048]{0:T(1024)S(1)} %fusion.34), kind=kOutput, calls=%fused_computation.15 | convolution fusion | flops 268566528 | bytes 17178624 | tf_op jit(solution)/shard_map/dot_general | solution.py:62
  56.3 4.8 %collective-permute-start.6 = (bf16[16,2048]{1,0:T(8,128)(2,1)S(1)}, bf16[16,2048]{1,0:T(8,128)(2,1)S(1)}, u32[]{:S(2)}, u32[]{:S(2)}) collective-permute-start(bf16[16,2048]{1,0:T(8,128)(2,1)S(1)} %get-tuple-element.15), channel_id=1, source_target_pairs={{0,4},{4,8},{8,12},{12,16},{16,20},{20,24},{24,28},{1,5},{5,9},{9,... | collective-permute-start | bytes 196616 | tf_op jit(solution)/shard_map/ppermute | solution.py:10
  63.6 3.7 %collective-permute-done.7 = bf16[16,2048]{1,0:T(8,128)(2,1)S(1)} collective-permute-done((bf16[16,2048]{1,0:T(8,128)(2,1)S(1)}, bf16[16,2048]{1,0:T(8,128)(2,1)S(1)}, u32[]{:S(2)}, u32[]{:S(2)}) %collective-permute-start.7) | collective-permute-done | bytes 65568 | tf_op jit(solution)/shard_map/ppermute | solution.py:10
  67.3 2.3 %convolution_multiply_fusion.4 = f32[2,16,2048]{2,1,0:T(8,128)S(1)} fusion(bf16[2,2048,2048]{2,1,0:T(8,128)(2,1)S(1)} %exponential_convert_fusion, bf16[1,16,2048]{2,1,0:T(8,128)(2,1)S(1)} %bitcast.135, bf16[1,16,2048]{2,1,0:T(8,128)(2,1)S(1)} %bitcast.130, f32[2048]{0:T(1024)S(1)} %fusion.34), kind=kOutput, calls=%fused_computation.14 | convolution fusion | flops 268566528 | bytes 17178624 | tf_op jit(solution)/shard_map/dot_general | solution.py:62
  69.7 2.9 %collective-permute-start.8 = (bf16[16,2048]{1,0:T(8,128)(2,1)S(1)}, bf16[16,2048]{1,0:T(8,128)(2,1)S(1)}, u32[]{:S(2)}, u32[]{:S(2)}) collective-permute-start(bf16[16,2048]{1,0:T(8,128)(2,1)S(1)} %get-tuple-element.13), channel_id=1, source_target_pairs={{0,4},{4,8},{8,12},{12,16},{16,20},{20,24},{24,28},{1,5},{5,9},{9,... | collective-permute-start | bytes 196616 | tf_op jit(solution)/shard_map/ppermute | solution.py:10
  74.5 4.3 %collective-permute-done.9 = bf16[16,2048]{1,0:T(8,128)(2,1)S(1)} collective-permute-done((bf16[16,2048]{1,0:T(8,128)(2,1)S(1)}, bf16[16,2048]{1,0:T(8,128)(2,1)S(1)}, u32[]{:S(2)}, u32[]{:S(2)}) %collective-permute-start.9) | collective-permute-done | bytes 65568 | tf_op jit(solution)/shard_map/ppermute | solution.py:10
  78.8 2.3 %convolution_multiply_fusion.3 = f32[2,16,2048]{2,1,0:T(8,128)S(1)} fusion(bf16[2,2048,2048]{2,1,0:T(8,128)(2,1)S(1)} %exponential_convert_fusion, bf16[1,16,2048]{2,1,0:T(8,128)(2,1)S(1)} %bitcast.131, bf16[1,16,2048]{2,1,0:T(8,128)(2,1)S(1)} %bitcast.125, f32[2048]{0:T(1024)S(1)} %fusion.34), kind=kOutput, calls=%fused_computation.13 | convolution fusion | flops 268566528 | bytes 17178624 | tf_op jit(solution)/shard_map/dot_general | solution.py:62
  81.3 4.8 %collective-permute-start.10 = (bf16[16,2048]{1,0:T(8,128)(2,1)S(1)}, bf16[16,2048]{1,0:T(8,128)(2,1)S(1)}, u32[]{:S(2)}, u32[]{:S(2)}) collective-permute-start(bf16[16,2048]{1,0:T(8,128)(2,1)S(1)} %get-tuple-element.11), channel_id=1, source_target_pairs={{0,4},{4,8},{8,12},{12,16},{16,20},{20,24},{24,28},{1,5},{5,9},{9,... | collective-permute-start | bytes 196616 | tf_op jit(solution)/shard_map/ppermute | solution.py:10
  88.0 4.3 %collective-permute-done.11 = bf16[16,2048]{1,0:T(8,128)(2,1)S(1)} collective-permute-done((bf16[16,2048]{1,0:T(8,128)(2,1)S(1)}, bf16[16,2048]{1,0:T(8,128)(2,1)S(1)}, u32[]{:S(2)}, u32[]{:S(2)}) %collective-permute-start.11) | collective-permute-done | bytes 65568 | tf_op jit(solution)/shard_map/ppermute | solution.py:10
  92.3 2.3 %convolution_multiply_fusion.2 = f32[2,16,2048]{2,1,0:T(8,128)S(1)} fusion(bf16[2,2048,2048]{2,1,0:T(8,128)(2,1)S(1)} %exponential_convert_fusion, bf16[1,16,2048]{2,1,0:T(8,128)(2,1)S(1)} %bitcast.132, bf16[1,16,2048]{2,1,0:T(8,128)(2,1)S(1)} %bitcast.126, f32[2048]{0:T(1024)S(1)} %fusion.34), kind=kOutput, calls=%fused_computation.12 | convolution fusion | flops 268566528 | bytes 17178624 | tf_op jit(solution)/shard_map/dot_general | solution.py:62
  94.7 2.9 %collective-permute-start.12 = (bf16[16,2048]{1,0:T(8,128)(2,1)S(1)}, bf16[16,2048]{1,0:T(8,128)(2,1)S(1)}, u32[]{:S(2)}, u32[]{:S(2)}) collective-permute-start(bf16[16,2048]{1,0:T(8,128)(2,1)S(1)} %get-tuple-element.9), channel_id=1, source_target_pairs={{0,4},{4,8},{8,12},{12,16},{16,20},{20,24},{24,28},{1,5},{5,9},{9,... | collective-permute-start | bytes 196616 | tf_op jit(solution)/shard_map/ppermute | solution.py:10
  99.5 4.3 %collective-permute-done.13 = bf16[16,2048]{1,0:T(8,128)(2,1)S(1)} collective-permute-done((bf16[16,2048]{1,0:T(8,128)(2,1)S(1)}, bf16[16,2048]{1,0:T(8,128)(2,1)S(1)}, u32[]{:S(2)}, u32[]{:S(2)}) %collective-permute-start.13) | collective-permute-done | bytes 65568 | tf_op jit(solution)/shard_map/ppermute | solution.py:10
  103.8 2.3 %convolution_multiply_fusion.1 = f32[2,16,2048]{2,1,0:T(8,128)S(1)} fusion(bf16[2,2048,2048]{2,1,0:T(8,128)(2,1)S(1)} %exponential_convert_fusion, bf16[1,16,2048]{2,1,0:T(8,128)(2,1)S(1)} %bitcast.133, bf16[1,16,2048]{2,1,0:T(8,128)(2,1)S(1)} %bitcast.127, f32[2048]{0:T(1024)S(1)} %fusion.34), kind=kOutput, calls=%fused_computation.11 | convolution fusion | flops 268566528 | bytes 17178624 | tf_op jit(solution)/shard_map/dot_general | solution.py:62
  106.3 4.9 %collective-permute-start.14 = (bf16[16,2048]{1,0:T(8,128)(2,1)S(1)}, bf16[16,2048]{1,0:T(8,128)(2,1)S(1)}, u32[]{:S(2)}, u32[]{:S(2)}) collective-permute-start(bf16[16,2048]{1,0:T(8,128)(2,1)S(1)} %get-tuple-element.7), channel_id=1, source_target_pairs={{0,4},{4,8},{8,12},{12,16},{16,20},{20,24},{24,28},{1,5},{5,9},{9,... | collective-permute-start | bytes 196616 | tf_op jit(solution)/shard_map/ppermute | solution.py:10
  113.0 4.3 %collective-permute-done.15 = bf16[16,2048]{1,0:T(8,128)(2,1)S(1)} collective-permute-done((bf16[16,2048]{1,0:T(8,128)(2,1)S(1)}, bf16[16,2048]{1,0:T(8,128)(2,1)S(1)}, u32[]{:S(2)}, u32[]{:S(2)}) %collective-permute-start.15) | collective-permute-done | bytes 65568 | tf_op jit(solution)/shard_map/ppermute | solution.py:10
  117.3 2.4 %fusion.46 = (f32[2,16]{1,0:T(2,128)S(1)}, f32[2,16,2048]{2,1,0:T(8,128)S(1)}) fusion(f32[2048]{0:T(1024)S(1)} %fusion.34, bf16[2,2048,2048]{2,1,0:T(8,128)(2,1)S(1)} %exponential_convert_fusion, bf16[1,16,2048]{2,1,0:T(8,128)(2,1)S(1)} %bitcast.128, bf16[1,16,2048]{2,1,0:T(8,128)(2,1)S(1)} %bitcast.124), kind=kOutput, calls=%fused_computation.105 | convolution fusion | flops 268632032 | bytes 17178752 | tf_op jit(solution)/shard_map/dot_general | solution.py:62
  119.8 5.8 %psum.7 = f32[2048]{0:T(1024)S(1)} all-reduce(f32[2048]{0:T(1024)S(1)} %fusion.33), channel_id=1, replica_groups=mesh['day'=8,'pt'=4] {'pt'}, use_global_device_ids=true, to_apply=%region_12.13 | all-reduce | flops 2048 | bytes 16384 | tf_op jit(solution)/shard_map/psum | solution.py:77
  126.4 3.5 %all-to-all-start.1 = ((f32[16,4,512]{2,0,1:T(8,128)}), f32[16,4,512]{2,0,1:T(8,128)S(1)}, u32[]{:S(2)}, u32[]{:S(2)}) async-start(f32[16,4,512]{2,0,1:T(8,128)} %copy.13), calls=%async_computation.1 | async-start | bytes 262144 | tf_op jit(solution)/shard_map/all_to_all | solution.py:74
  130.6 4.5 %multiply_reduce_fusion.1 = (f32[2048]{0:T(1024)S(1)}, f32[2048,2048]{1,0:T(8,128)S(1)}) fusion(f32[2048]{0:T(1024)S(1)} %get-tuple-element.4, f32[2048]{0:T(1024)S(1)} %multiply_reduce_fusion.2, f32[2048]{0:T(1024)S(1)} %multiply_reduce_fusion.3, bf16[1,64,2048]{2,1,0:T(8,128)(2,1)S(1)} %copy-done, bf16[1,64,2048]{2,1,0:T(8,128)(2,1)S(1)} %all-gather.1), kind=kOutput, calls=%fused_computation.8 | convolution fusion | flops 562034688 | bytes 17334272 | tf_op jit(solution)/shard_map/dot_general | solution.py:19
  135.7 5.0 %multiply_reduce_fusion = f32[2048]{0:T(1024)S(1)} fusion(f32[2048,2048]{1,0:T(8,128)S(1)} %get-tuple-element.36, f32[2048]{0:T(1024)S(1)} %select_divide_fusion, f32[2048]{0:T(1024)S(1)} %multiply_reduce_fusion.2, f32[2048]{0:T(1024)S(1)} %multiply_reduce_fusion.3), kind=kLoop, calls=%fused_computation.7 | loop fusion | flops 25163776 | bytes 16809984 | tf_op jit(solution)/shard_map/reduce_sum | solution.py:91
  141.5 7.5 %all-reduce = f32[2048]{0:T(1024)S(1)} all-reduce(f32[2048]{0:T(1024)S(1)} %multiply_reduce_fusion), channel_id=4, replica_groups=mesh['day'=8,'pt'=4] {'pt'}, use_global_device_ids=true, to_apply=%region_16.17.clone | all-reduce | flops 2048 | bytes 16384
  149.0 3.3 %all-to-all-start.2 = ((f32[16,4,512]{2,0,1:T(8,128)}), f32[16,4,512]{2,0,1:T(8,128)S(1)}, u32[]{:S(2)}, u32[]{:S(2)}) async-start(f32[16,4,512]{2,0,1:T(8,128)} %copy.14), calls=%async_computation.2 | async-start | bytes 262144 | tf_op jit(solution)/shard_map/all_to_all | solution.py:75
  153.0 3.9 %all-to-all-done.2 = f32[16,4,512]{2,0,1:T(8,128)S(1)} async-done(((f32[16,4,512]{2,0,1:T(8,128)}), f32[16,4,512]{2,0,1:T(8,128)S(1)}, u32[]{:S(2)}, u32[]{:S(2)}) %all-to-all-start.2) | async-done | bytes 131104 | tf_op jit(solution)/shard_map/all_to_all | solution.py:75
  (64 shorter events, 23.1 us)
Async XLA Ops:
  8.1 23.9 %collective-permute-start.2 = (bf16[64,2048]{1,0:T(8,128)(2,1)S(1)}, bf16[64,2048]{1,0:T(8,128)(2,1)S(1)}, u32[]{:S(2)}, u32[]{:S(2)}) collective-permute-start(bf16[64,2048]{1,0:T(8,128)(2,1)S(1)} %bitcast.112), channel_id=1, source_target_pairs={{0,4},{4,8},{8,12},{12,16},{16,20},{20,24},{24,28},{1,5},{5,9},{9,... | collective-permute-start | bytes 786440 | tf_op jit(solution)/shard_map/ppermute | solution.py:10
  11.5 20.6 %collective-permute-start.3 = (bf16[64,2048]{1,0:T(8,128)(2,1)S(1)}, bf16[64,2048]{1,0:T(8,128)(2,1)S(1)}, u32[]{:S(2)}, u32[]{:S(2)}) collective-permute-start(bf16[64,2048]{1,0:T(8,128)(2,1)S(1)} %bitcast.113), channel_id=1, source_target_pairs={{4,0},{8,4},{12,8},{16,12},{20,16},{24,20},{28,24},{5,1},{9,5},{13... | collective-permute-start | bytes 786440 | tf_op jit(solution)/shard_map/ppermute | solution.py:10
  12.8 13.3 %all-to-all-start = ((f32[4,16,512]{2,1,0:T(8,128)}), f32[4,16,512]{2,1,0:T(8,128)S(1)}, u32[]{:S(2)}, u32[]{:S(2)}) async-start(f32[4,16,512]{2,1,0:T(8,128)} %bitcast.119), calls=%async_computation | async-start | bytes 262144 | tf_op jit(solution)/shard_map/all_to_all | solution.py:35
  26.1 13.2 %collective-permute-start = (bf16[16,2048]{1,0:T(8,128)(2,1)S(1)}, bf16[16,2048]{1,0:T(8,128)(2,1)S(1)}, u32[]{:S(2)}, u32[]{:S(2)}) collective-permute-start(bf16[16,2048]{1,0:T(8,128)(2,1)S(1)} %get-tuple-element.19), channel_id=1, source_target_pairs={{0,4},{4,8},{8,12},{12,16},{16,20},{20,24},{24,28},{1,5},{5,9},{9,... | collective-permute-start | bytes 196616 | tf_op jit(solution)/shard_map/ppermute | solution.py:10
  30.7 8.7 %collective-permute-start.1 = (bf16[16,2048]{1,0:T(8,128)(2,1)S(1)}, bf16[16,2048]{1,0:T(8,128)(2,1)S(1)}, u32[]{:S(2)}, u32[]{:S(2)}) collective-permute-start(bf16[16,2048]{1,0:T(8,128)(2,1)S(1)} %get-tuple-element.20), channel_id=1, source_target_pairs={{4,0},{8,4},{12,8},{16,12},{20,16},{24,20},{28,24},{5,1},{9,5},{13... | collective-permute-start | bytes 196616 | tf_op jit(solution)/shard_map/ppermute | solution.py:10
  41.8 6.9 %collective-permute-start.4 = (bf16[16,2048]{1,0:T(8,128)(2,1)S(1)}, bf16[16,2048]{1,0:T(8,128)(2,1)S(1)}, u32[]{:S(2)}, u32[]{:S(2)}) collective-permute-start(bf16[16,2048]{1,0:T(8,128)(2,1)S(1)} %get-tuple-element.17), channel_id=1, source_target_pairs={{0,4},{4,8},{8,12},{12,16},{16,20},{20,24},{24,28},{1,5},{5,9},{9,... | collective-permute-start | bytes 196616 | tf_op jit(solution)/shard_map/ppermute | solution.py:10
  46.8 7.1 %collective-permute-start.5 = (bf16[16,2048]{1,0:T(8,128)(2,1)S(1)}, bf16[16,2048]{1,0:T(8,128)(2,1)S(1)}, u32[]{:S(2)}, u32[]{:S(2)}) collective-permute-start(bf16[16,2048]{1,0:T(8,128)(2,1)S(1)} %get-tuple-element.18), channel_id=1, source_target_pairs={{4,0},{8,4},{12,8},{16,12},{20,16},{24,20},{28,24},{5,1},{9,5},{13... | collective-permute-start | bytes 196616 | tf_op jit(solution)/shard_map/ppermute | solution.py:10
  56.3 7.3 %collective-permute-start.6 = (bf16[16,2048]{1,0:T(8,128)(2,1)S(1)}, bf16[16,2048]{1,0:T(8,128)(2,1)S(1)}, u32[]{:S(2)}, u32[]{:S(2)}) collective-permute-start(bf16[16,2048]{1,0:T(8,128)(2,1)S(1)} %get-tuple-element.15), channel_id=1, source_target_pairs={{0,4},{4,8},{8,12},{12,16},{16,20},{20,24},{24,28},{1,5},{5,9},{9,... | collective-permute-start | bytes 196616 | tf_op jit(solution)/shard_map/ppermute | solution.py:10
  61.1 6.2 %collective-permute-start.7 = (bf16[16,2048]{1,0:T(8,128)(2,1)S(1)}, bf16[16,2048]{1,0:T(8,128)(2,1)S(1)}, u32[]{:S(2)}, u32[]{:S(2)}) collective-permute-start(bf16[16,2048]{1,0:T(8,128)(2,1)S(1)} %get-tuple-element.16), channel_id=1, source_target_pairs={{4,0},{8,4},{12,8},{16,12},{20,16},{24,20},{28,24},{5,1},{9,5},{13... | collective-permute-start | bytes 196616 | tf_op jit(solution)/shard_map/ppermute | solution.py:10
  69.7 4.8 %collective-permute-start.8 = (bf16[16,2048]{1,0:T(8,128)(2,1)S(1)}, bf16[16,2048]{1,0:T(8,128)(2,1)S(1)}, u32[]{:S(2)}, u32[]{:S(2)}) collective-permute-start(bf16[16,2048]{1,0:T(8,128)(2,1)S(1)} %get-tuple-element.13), channel_id=1, source_target_pairs={{0,4},{4,8},{8,12},{12,16},{16,20},{20,24},{24,28},{1,5},{5,9},{9,... | collective-permute-start | bytes 196616 | tf_op jit(solution)/shard_map/ppermute | solution.py:10
  72.7 6.2 %collective-permute-start.9 = (bf16[16,2048]{1,0:T(8,128)(2,1)S(1)}, bf16[16,2048]{1,0:T(8,128)(2,1)S(1)}, u32[]{:S(2)}, u32[]{:S(2)}) collective-permute-start(bf16[16,2048]{1,0:T(8,128)(2,1)S(1)} %get-tuple-element.14), channel_id=1, source_target_pairs={{4,0},{8,4},{12,8},{16,12},{20,16},{24,20},{28,24},{5,1},{9,5},{13... | collective-permute-start | bytes 196616 | tf_op jit(solution)/shard_map/ppermute | solution.py:10
  81.3 6.7 %collective-permute-start.10 = (bf16[16,2048]{1,0:T(8,128)(2,1)S(1)}, bf16[16,2048]{1,0:T(8,128)(2,1)S(1)}, u32[]{:S(2)}, u32[]{:S(2)}) collective-permute-start(bf16[16,2048]{1,0:T(8,128)(2,1)S(1)} %get-tuple-element.11), channel_id=1, source_target_pairs={{0,4},{4,8},{8,12},{12,16},{16,20},{20,24},{24,28},{1,5},{5,9},{9,... | collective-permute-start | bytes 196616 | tf_op jit(solution)/shard_map/ppermute | solution.py:10
  86.1 6.2 %collective-permute-start.11 = (bf16[16,2048]{1,0:T(8,128)(2,1)S(1)}, bf16[16,2048]{1,0:T(8,128)(2,1)S(1)}, u32[]{:S(2)}, u32[]{:S(2)}) collective-permute-start(bf16[16,2048]{1,0:T(8,128)(2,1)S(1)} %get-tuple-element.12), channel_id=1, source_target_pairs={{4,0},{8,4},{12,8},{16,12},{20,16},{24,20},{28,24},{5,1},{9,5},{13... | collective-permute-start | bytes 196616 | tf_op jit(solution)/shard_map/ppermute | solution.py:10
  94.7 4.8 %collective-permute-start.12 = (bf16[16,2048]{1,0:T(8,128)(2,1)S(1)}, bf16[16,2048]{1,0:T(8,128)(2,1)S(1)}, u32[]{:S(2)}, u32[]{:S(2)}) collective-permute-start(bf16[16,2048]{1,0:T(8,128)(2,1)S(1)} %get-tuple-element.9), channel_id=1, source_target_pairs={{0,4},{4,8},{8,12},{12,16},{16,20},{20,24},{24,28},{1,5},{5,9},{9,... | collective-permute-start | bytes 196616 | tf_op jit(solution)/shard_map/ppermute | solution.py:10
  97.6 6.2 %collective-permute-start.13 = (bf16[16,2048]{1,0:T(8,128)(2,1)S(1)}, bf16[16,2048]{1,0:T(8,128)(2,1)S(1)}, u32[]{:S(2)}, u32[]{:S(2)}) collective-permute-start(bf16[16,2048]{1,0:T(8,128)(2,1)S(1)} %get-tuple-element.10), channel_id=1, source_target_pairs={{4,0},{8,4},{12,8},{16,12},{20,16},{24,20},{28,24},{5,1},{9,5},{13... | collective-permute-start | bytes 196616 | tf_op jit(solution)/shard_map/ppermute | solution.py:10
  106.1 24.5 %copy-start = (bf16[1,64,2048]{2,1,0:T(8,128)(2,1)S(1)}, bf16[1,64,2048]{2,1,0:T(8,128)(2,1)}, u32[]{:S(2)}) copy-start(bf16[1,64,2048]{2,1,0:T(8,128)(2,1)} %param.7) | copy-start | bytes 786436
  106.3 6.7 %collective-permute-start.14 = (bf16[16,2048]{1,0:T(8,128)(2,1)S(1)}, bf16[16,2048]{1,0:T(8,128)(2,1)S(1)}, u32[]{:S(2)}, u32[]{:S(2)}) collective-permute-start(bf16[16,2048]{1,0:T(8,128)(2,1)S(1)} %get-tuple-element.7), channel_id=1, source_target_pairs={{0,4},{4,8},{8,12},{12,16},{16,20},{20,24},{24,28},{1,5},{5,9},{9,... | collective-permute-start | bytes 196616 | tf_op jit(solution)/shard_map/ppermute | solution.py:10
  111.1 6.2 %collective-permute-start.15 = (bf16[16,2048]{1,0:T(8,128)(2,1)S(1)}, bf16[16,2048]{1,0:T(8,128)(2,1)S(1)}, u32[]{:S(2)}, u32[]{:S(2)}) collective-permute-start(bf16[16,2048]{1,0:T(8,128)(2,1)S(1)} %get-tuple-element.8), channel_id=1, source_target_pairs={{4,0},{8,4},{12,8},{16,12},{20,16},{24,20},{28,24},{5,1},{9,5},{13... | collective-permute-start | bytes 196616 | tf_op jit(solution)/shard_map/ppermute | solution.py:10
  126.4 22.6 %all-to-all-start.1 = ((f32[16,4,512]{2,0,1:T(8,128)}), f32[16,4,512]{2,0,1:T(8,128)S(1)}, u32[]{:S(2)}, u32[]{:S(2)}) async-start(f32[16,4,512]{2,0,1:T(8,128)} %copy.13), calls=%async_computation.1 | async-start | bytes 262144 | tf_op jit(solution)/shard_map/all_to_all | solution.py:74
  149.0 7.9 %all-to-all-start.2 = ((f32[16,4,512]{2,0,1:T(8,128)}), f32[16,4,512]{2,0,1:T(8,128)S(1)}, u32[]{:S(2)}, u32[]{:S(2)}) async-start(f32[16,4,512]{2,0,1:T(8,128)} %copy.14), calls=%async_computation.2 | async-start | bytes 262144 | tf_op jit(solution)/shard_map/all_to_all | solution.py:75

commit v3 on v2

--- a/solution.py
+++ b/solution.py
@@ -32,10 +32,9 @@
     before_pts = shifted(day_pts, "day", 1)
     after_pts = shifted(day_pts, "day", -1)
     support_total = day_pts.shape[1]
-    block_cw = lax.all_to_all(clone_weight[0], "pt", 0, 1, tiled=True)
-    full_pot = lax.all_gather(potential[0], "pt", axis=0, tiled=True)
-    block_weight = block_cw * full_pot[None, :]
-    block_rows = block_cw.shape[0]
+    own_weight = clone_weight[0] * potential[0][None, :]
+    block_weight = lax.all_to_all(own_weight, "pt", 0, 1, tiled=True)
+    block_rows = block_weight.shape[0]
     live_total = support_count[0].astype(jnp.float32)
     live_all = (jnp.arange(support_total, dtype=jnp.int32) < support_count[0]).astype(jnp.float32)
     live_own = lax.dynamic_slice_in_dim(live_all, pt_rank * per_device, per_device)
@@ -56,8 +55,16 @@
     seed_rows = jnp.broadcast_to(live_all[None, None, :], (2, block_rows, support_total))
     rows = seed_rows
     for step in range(day_count - 1):
+        forward_from = step
+        backward_from = day_count - 1 - step
         sent = (rows * block_weight[None]).astype(jnp.bfloat16)
-        arrived = jnp.stack([shifted(sent[0], "day", 1), shifted(sent[1], "day", -1)])
+        if forward_from != backward_from:
+            outgoing = jnp.where(day_index == forward_from, sent[0], sent[1])
+            route = [(forward_from, forward_from + 1), (backward_from, backward_from - 1)]
+            incoming = lax.ppermute(outgoing, "day", route)
+            arrived = jnp.stack([incoming, incoming])
+        else:
+            arrived = jnp.stack([shifted(sent[0], "day", 1), shifted(sent[1], "day", -1)])
         fresh = settle(
             lax.dot_general(
                 arrived,
@@ -73,8 +80,8 @@
 
     forward_out = lax.all_to_all(forward_rows, "pt", 1, 0, tiled=True)
     backward_out = lax.all_to_all(backward_rows, "pt", 1, 0, tiled=True)
-    mass_part = jnp.sum(forward_rows * block_cw * backward_rows, axis=0)
-    full_mass = live_all * full_pot * lax.psum(mass_part, "pt")
+    mass_part = jnp.sum(forward_rows * block_weight * backward_rows, axis=0)
+    full_mass = live_all * lax.psum(mass_part, "pt")
     mass_total = jnp.sum(full_mass)
 
     cell_total = cell_count[0]

time: 159 us -> 122 us (0.77)
  starting transfers between devices: 54 us -> 24.3 us
  blocking collectives: 26.1 us -> 20.5 us
  waiting for transfers between devices: 33.3 us -> 30.2 us
    ppermute x16 -> x2, starting transfers between devices: 43.8 us -> 4.7 us  [shifted(): return lax.ppermute(block, axis, route)]
    ppermute x16 -> x2, waiting for transfers between devices: 29.4 us -> 0.01 us  [shifted(): return lax.ppermute(block, axis, route)]
    ppermute x0 -> x7, waiting for transfers between devices: none -> 26.1 us  [shards(): incoming = lax.ppermute(outgoing, 'day', route)]
    ppermute x0 -> x7, starting transfers between devices: none -> 9.35 us  [shards(): incoming = lax.ppermute(outgoing, 'day', route)]
    all_gather x1 -> x0, blocking collectives: 5.38 us -> none  [shards(): full_pot = lax.all_gather(potential[0], 'pt', axis=0, tiled=True)]
  transfers between devices with their start and end apart: 19 -> 12, of which waited for: 13 -> 3; matrix products, arithmetic and copies ran while one was open for 14% -> 20% of each run, Pallas kernels for 0% -> 0%
where the time goes in v3:
time: 122 us; the launch traced here: 121 us
  waiting for transfers between devices  30.2 us (25%)
  matrix products  27.5 us (23%)
  starting transfers between devices  24.3 us (20%)
  blocking collectives  20.5 us (17%)
  other arithmetic  11.3 us (9%)
  local copies, waits for them, and re-layouts  4.16 us (3%)
  between operations  2.89 us (2%)
    ppermute x7, waiting for transfers between devices, shards(): incoming = lax.ppermute(outgoing, 'day', route)  26.1 us
    dot_general x7, matrix products, shards(): lax.dot_general(arrived, chain_kernel, (((2,), (1,)), ((0,), (0,))), pref...  16 us
    ppermute x7, starting transfers between devices, shards(): incoming = lax.ppermute(outgoing, 'day', route)  9.35 us
    all_gather x1, blocking collectives, shards(): day_pts = lax.all_gather(own_pts, 'pt', axis=1, tiled=True)  7.46 us
    unnamed x1, blocking collectives  7.28 us
    dot_general x1, matrix products, shards(): lax.dot_general(source_pts, day_pts, (((1,), (0,)), ((), ())), preferred_...  7.19 us
    psum x1, blocking collectives, shards(): full_mass = live_all * lax.psum(mass_part, 'pt')  5.77 us
    reduce_sum x1, other arithmetic, shards(): ratio_rows = jnp.sum(fit_kernel * inverse[None, :], axis=1)  4.9 us
  transfers between devices with their start and end apart: 12, of which 3 were waited for; matrix products, arithmetic and copies ran while one was open for 20% of the time, Pallas kernels for 0%

profile of v3, /device:TPU:0, one launch (start us, length us, event | category | flops | bytes accessed | tf_op | source)
XLA Modules:
  0.0 120.9 jit_solution(5682585419470632230)
XLA Ops:
  0.6 7.5 %all-gather = bf16[1,64,2048]{2,1,0:T(8,128)(2,1)S(1)} all-gather(bf16[1,64,512]{2,1,0:T(8,128)(2,1)} %param.6), channel_id=2, replica_groups=mesh['day'=8,'pt'=4] {'pt'}, dimensions={2}, use_global_device_ids=true | all-gather | bytes 327680 | tf_op jit(solution)/shard_map/all_gather | solution.py:31
  8.1 3.4 %collective-permute-start.1 = (bf16[64,2048]{1,0:T(8,128)(2,1)S(1)}, bf16[64,2048]{1,0:T(8,128)(2,1)S(1)}, u32[]{:S(2)}, u32[]{:S(2)}) collective-permute-start(bf16[64,2048]{1,0:T(8,128)(2,1)S(1)} %bitcast.97), channel_id=1, source_target_pairs={{0,4},{4,8},{8,12},{12,16},{16,20},{20,24},{24,28},{1,5},{5,9},{9,... | collective-permute-start | bytes 786440 | tf_op jit(solution)/shard_map/ppermute | solution.py:10
  11.5 1.3 %collective-permute-start.2 = (bf16[64,2048]{1,0:T(8,128)(2,1)S(1)}, bf16[64,2048]{1,0:T(8,128)(2,1)S(1)}, u32[]{:S(2)}, u32[]{:S(2)}) collective-permute-start(bf16[64,2048]{1,0:T(8,128)(2,1)S(1)} %bitcast.98), channel_id=1, source_target_pairs={{4,0},{8,4},{12,8},{16,12},{20,16},{24,20},{28,24},{5,1},{9,5},{13... | collective-permute-start | bytes 786440 | tf_op jit(solution)/shard_map/ppermute | solution.py:10
  12.8 1.6 %broadcast_multiply_fusion = f32[4,16,512]{2,1,0:T(8,128)} fusion(f32[4,16,512]{2,1,0:T(8,128)} %bitcast.104, f32[512]{0:T(512)} %bitcast.114), kind=kLoop, calls=%fused_computation.79 | loop fusion | flops 32768 | bytes 264192 | tf_op jit(solution)/shard_map/mul | solution.py:35
  14.4 3.3 %all-to-all-start = ((f32[4,16,512]{2,1,0:T(8,128)}), f32[4,16,512]{2,1,0:T(8,128)S(1)}, u32[]{:S(2)}, u32[]{:S(2)}) async-start(f32[4,16,512]{2,1,0:T(8,128)} %broadcast_multiply_fusion), calls=%async_computation | async-start | bytes 262144 | tf_op jit(solution)/shard_map/all_to_all | solution.py:36
  18.5 1.0 multiply_reduce_fusion.2
  20.2 1.2 %dynamic-slice = u32[1]{0:T(128)} dynamic-slice(u32[32]{0:T(128)} %constant.44, u32[]{:T(128)S(6)} %add.53), dynamic_slice_sizes={1} | dynamic-slice | bytes 12
  22.3 4.5 %collective-permute-start = (bf16[16,2048]{1,0:T(8,128)(2,1)S(1)}, bf16[16,2048]{1,0:T(8,128)(2,1)S(1)}, u32[]{:S(2)}, u32[]{:S(2)}) collective-permute-start(bf16[16,2048]{1,0:T(8,128)(2,1)S(1)} %fusion.40), channel_id=1, source_target_pairs={{0,4},{28,24},{1,5},{29,25},{2,6},{30,26},{3,7},{31,27}} | collective-permute-start | bytes 196616 | tf_op jit(solution)/shard_map/ppermute | solution.py:64
  27.1 7.2 %exponential_convert_fusion = bf16[2,2048,2048]{2,1,0:T(8,128)(2,1)S(1)} fusion(f32[2048]{0:T(1024)S(1)} %multiply_reduce_fusion.3, f32[2,2048]{1,0:T(2,128)S(1)} %pad_maximum_fusion, bf16[1,64,2048]{2,1,0:T(8,128)(2,1)S(1)} %bitcast.103, bf16[1,64,2048]{2,1,0:T(8,128)(2,1)S(1)} %bitcast.102, bf16[1,64,2048]{2,1,0:T(8,128)(2,1)S(1)} %all-gather), kind=kOutput, calls=%fused_computation.6 | convolution fusion | flops 1115947008 | bytes 17588224 | tf_op jit(solution)/shard_map/dot_general | solution.py:44
  34.3 2.3 %convolution_multiply_fusion.6 = f32[2,16,2048]{2,1,0:T(8,128)S(1)} fusion(bf16[2,2048,2048]{2,1,0:T(8,128)(2,1)S(1)} %exponential_convert_fusion, bf16[1,16,2048]{2,1,0:T(8,128)(2,1)S(1)} %bitcast.105, f32[2048]{0:T(1024)S(1)} %fusion.42), kind=kOutput, calls=%fused_computation.16 | convolution fusion | flops 268566528 | bytes 17113088 | tf_op jit(solution)/shard_map/dot_general | solution.py:69
  36.7 0.7 collective-permute-start.3
  37.5 2.3 %convolution_multiply_fusion.5 = f32[2,16,2048]{2,1,0:T(8,128)S(1)} fusion(bf16[2,2048,2048]{2,1,0:T(8,128)(2,1)S(1)} %exponential_convert_fusion, bf16[1,16,2048]{2,1,0:T(8,128)(2,1)S(1)} %bitcast.109, f32[2048]{0:T(1024)S(1)} %fusion.42), kind=kOutput, calls=%fused_computation.15 | convolution fusion | flops 268566528 | bytes 17113088 | tf_op jit(solution)/shard_map/dot_general | solution.py:69
  40.0 0.7 collective-permute-start.4
  40.7 2.3 %convolution_multiply_fusion.4 = f32[2,16,2048]{2,1,0:T(8,128)S(1)} fusion(bf16[2,2048,2048]{2,1,0:T(8,128)(2,1)S(1)} %exponential_convert_fusion, bf16[1,16,2048]{2,1,0:T(8,128)(2,1)S(1)} %bitcast.110, f32[2048]{0:T(1024)S(1)} %fusion.42), kind=kOutput, calls=%fused_computation.14 | convolution fusion | flops 268566528 | bytes 17113088 | tf_op jit(solution)/shard_map/dot_general | solution.py:69
  43.2 0.8 collective-permute-start.5
  44.1 2.3 %convolution_multiply_fusion.3 = f32[2,16,2048]{2,1,0:T(8,128)S(1)} fusion(bf16[2,2048,2048]{2,1,0:T(8,128)(2,1)S(1)} %exponential_convert_fusion, bf16[1,16,2048]{2,1,0:T(8,128)(2,1)S(1)} %bitcast.106, f32[2048]{0:T(1024)S(1)} %fusion.42), kind=kOutput, calls=%fused_computation.13 | convolution fusion | flops 268566528 | bytes 17113088 | tf_op jit(solution)/shard_map/dot_general | solution.py:69
  46.5 0.7 collective-permute-start.6
  47.3 2.3 %convolution_multiply_fusion.2 = f32[2,16,2048]{2,1,0:T(8,128)S(1)} fusion(bf16[2,2048,2048]{2,1,0:T(8,128)(2,1)S(1)} %exponential_convert_fusion, bf16[1,16,2048]{2,1,0:T(8,128)(2,1)S(1)} %bitcast.107, f32[2048]{0:T(1024)S(1)} %fusion.42), kind=kOutput, calls=%fused_computation.12 | convolution fusion | flops 268566528 | bytes 17113088 | tf_op jit(solution)/shard_map/dot_general | solution.py:69
  49.7 0.7 collective-permute-start.7
  50.5 2.3 %convolution_multiply_fusion.1 = f32[2,16,2048]{2,1,0:T(8,128)S(1)} fusion(bf16[2,2048,2048]{2,1,0:T(8,128)(2,1)S(1)} %exponential_convert_fusion, bf16[1,16,2048]{2,1,0:T(8,128)(2,1)S(1)} %bitcast.108, f32[2048]{0:T(1024)S(1)} %fusion.42), kind=kOutput, calls=%fused_computation.11 | convolution fusion | flops 268566528 | bytes 17113088 | tf_op jit(solution)/shard_map/dot_general | solution.py:69
  52.9 1.3 %collective-permute-start.8 = (bf16[16,2048]{1,0:T(8,128)(2,1)S(1)}, bf16[16,2048]{1,0:T(8,128)(2,1)S(1)}, u32[]{:S(2)}, u32[]{:S(2)}) collective-permute-start(bf16[16,2048]{1,0:T(8,128)(2,1)S(1)} %fusion.34), channel_id=1, source_target_pairs={{24,28},{4,0},{25,29},{5,1},{26,30},{6,2},{27,31},{7,3}} | collective-permute-start | bytes 196616 | tf_op jit(solution)/shard_map/ppermute | solution.py:64
  54.3 26.1 %collective-permute-done.8 = bf16[16,2048]{1,0:T(8,128)(2,1)S(1)} collective-permute-done((bf16[16,2048]{1,0:T(8,128)(2,1)S(1)}, bf16[16,2048]{1,0:T(8,128)(2,1)S(1)}, u32[]{:S(2)}, u32[]{:S(2)}) %collective-permute-start.8) | collective-permute-done | bytes 65568 | tf_op jit(solution)/shard_map/ppermute | solution.py:64
  80.4 2.4 %fusion.55 = (f32[2,16]{1,0:T(2,128)S(1)}, f32[2,16,2048]{2,1,0:T(8,128)S(1)}) fusion(f32[2048]{0:T(1024)S(1)} %fusion.42, bf16[2,2048,2048]{2,1,0:T(8,128)(2,1)S(1)} %exponential_convert_fusion, bf16[1,16,2048]{2,1,0:T(8,128)(2,1)S(1)} %bitcast.111), kind=kOutput, calls=%fused_computation.105 | convolution fusion | flops 268632032 | bytes 17113216 | tf_op jit(solution)/shard_map/dot_general | solution.py:69
  83.0 5.8 %psum.7 = f32[2048]{0:T(1024)S(1)} all-reduce(f32[2048]{0:T(1024)S(1)} %fusion.33), channel_id=1, replica_groups=mesh['day'=8,'pt'=4] {'pt'}, use_global_device_ids=true, to_apply=%region_12.13 | all-reduce | flops 2048 | bytes 16384 | tf_op jit(solution)/shard_map/psum | solution.py:84
  88.8 0.7 copy.13
  89.5 3.5 %all-to-all-start.1 = ((f32[16,4,512]{2,0,1:T(8,128)}), f32[16,4,512]{2,0,1:T(8,128)S(1)}, u32[]{:S(2)}, u32[]{:S(2)}) async-start(f32[16,4,512]{2,0,1:T(8,128)} %copy.13), calls=%async_computation.1 | async-start | bytes 262144 | tf_op jit(solution)/shard_map/all_to_all | solution.py:81
  93.7 4.3 %multiply_reduce_fusion.1 = (f32[2048]{0:T(1024)S(1)}, f32[2048,2048]{1,0:T(8,128)S(1)}) fusion(f32[2048]{0:T(1024)S(1)} %get-tuple-element.4, f32[2048]{0:T(1024)S(1)} %multiply_reduce_fusion.2, f32[2048]{0:T(1024)S(1)} %multiply_reduce_fusion.3, bf16[1,64,2048]{2,1,0:T(8,128)(2,1)S(1)} %copy-done, bf16[1,64,2048]{2,1,0:T(8,128)(2,1)S(1)} %all-gather), kind=kOutput, calls=%fused_computation.8 | convolution fusion | flops 562034688 | bytes 17334272 | tf_op jit(solution)/shard_map/dot_general | solution.py:19
  98.7 4.9 %multiply_reduce_fusion = f32[2048]{0:T(1024)S(1)} fusion(f32[2048,2048]{1,0:T(8,128)S(1)} %get-tuple-element.22, f32[2048]{0:T(1024)S(1)} %select_divide_fusion, f32[2048]{0:T(1024)S(1)} %multiply_reduce_fusion.2, f32[2048]{0:T(1024)S(1)} %multiply_reduce_fusion.3), kind=kLoop, calls=%fused_computation.7 | loop fusion | flops 25163776 | bytes 16809984 | tf_op jit(solution)/shard_map/reduce_sum | solution.py:98
  103.7 0.7 copy.14
  104.4 7.3 %all-reduce = f32[2048]{0:T(1024)S(1)} all-reduce(f32[2048]{0:T(1024)S(1)} %multiply_reduce_fusion), channel_id=3, replica_groups=mesh['day'=8,'pt'=4] {'pt'}, use_global_device_ids=true, to_apply=%region_16.17.clone | all-reduce | flops 2048 | bytes 16384
  111.7 3.3 %all-to-all-start.2 = ((f32[16,4,512]{2,0,1:T(8,128)}), f32[16,4,512]{2,0,1:T(8,128)S(1)}, u32[]{:S(2)}, u32[]{:S(2)}) async-start(f32[16,4,512]{2,0,1:T(8,128)} %copy.14), calls=%async_computation.2 | async-start | bytes 262144 | tf_op jit(solution)/shard_map/all_to_all | solution.py:82
  115.7 3.9 %all-to-all-done.2 = f32[16,4,512]{2,0,1:T(8,128)S(1)} async-done(((f32[16,4,512]{2,0,1:T(8,128)}), f32[16,4,512]{2,0,1:T(8,128)S(1)}, u32[]{:S(2)}, u32[]{:S(2)}) %all-to-all-start.2) | async-done | bytes 131104 | tf_op jit(solution)/shard_map/all_to_all | solution.py:82
  (49 shorter events, 5.6 us)
Async XLA Ops:
  8.1 18.8 %collective-permute-start.1 = (bf16[64,2048]{1,0:T(8,128)(2,1)S(1)}, bf16[64,2048]{1,0:T(8,128)(2,1)S(1)}, u32[]{:S(2)}, u32[]{:S(2)}) collective-permute-start(bf16[64,2048]{1,0:T(8,128)(2,1)S(1)} %bitcast.97), channel_id=1, source_target_pairs={{0,4},{4,8},{8,12},{12,16},{16,20},{20,24},{24,28},{1,5},{5,9},{9,... | collective-permute-start | bytes 786440 | tf_op jit(solution)/shard_map/ppermute | solution.py:10
  11.5 15.5 %collective-permute-start.2 = (bf16[64,2048]{1,0:T(8,128)(2,1)S(1)}, bf16[64,2048]{1,0:T(8,128)(2,1)S(1)}, u32[]{:S(2)}, u32[]{:S(2)}) collective-permute-start(bf16[64,2048]{1,0:T(8,128)(2,1)S(1)} %bitcast.98), channel_id=1, source_target_pairs={{4,0},{8,4},{12,8},{16,12},{20,16},{24,20},{28,24},{5,1},{9,5},{13... | collective-permute-start | bytes 786440 | tf_op jit(solution)/shard_map/ppermute | solution.py:10
  14.4 7.9 %all-to-all-start = ((f32[4,16,512]{2,1,0:T(8,128)}), f32[4,16,512]{2,1,0:T(8,128)S(1)}, u32[]{:S(2)}, u32[]{:S(2)}) async-start(f32[4,16,512]{2,1,0:T(8,128)} %broadcast_multiply_fusion), calls=%async_computation | async-start | bytes 262144 | tf_op jit(solution)/shard_map/all_to_all | solution.py:36
  22.3 12.0 %collective-permute-start = (bf16[16,2048]{1,0:T(8,128)(2,1)S(1)}, bf16[16,2048]{1,0:T(8,128)(2,1)S(1)}, u32[]{:S(2)}, u32[]{:S(2)}) collective-permute-start(bf16[16,2048]{1,0:T(8,128)(2,1)S(1)} %fusion.40), channel_id=1, source_target_pairs={{0,4},{28,24},{1,5},{29,25},{2,6},{30,26},{3,7},{31,27}} | collective-permute-start | bytes 196616 | tf_op jit(solution)/shard_map/ppermute | solution.py:64
  36.7 0.8 collective-permute-start.3
  40.0 0.8 collective-permute-start.4
  43.2 0.9 collective-permute-start.5
  46.5 0.8 collective-permute-start.6
  49.7 0.8 collective-permute-start.7
  52.8 40.9 %copy-start = (bf16[1,64,2048]{2,1,0:T(8,128)(2,1)S(1)}, bf16[1,64,2048]{2,1,0:T(8,128)(2,1)}, u32[]{:S(2)}) copy-start(bf16[1,64,2048]{2,1,0:T(8,128)(2,1)} %param.7) | copy-start | bytes 786436
  52.9 27.5 %collective-permute-start.8 = (bf16[16,2048]{1,0:T(8,128)(2,1)S(1)}, bf16[16,2048]{1,0:T(8,128)(2,1)S(1)}, u32[]{:S(2)}, u32[]{:S(2)}) collective-permute-start(bf16[16,2048]{1,0:T(8,128)(2,1)S(1)} %fusion.34), channel_id=1, source_target_pairs={{24,28},{4,0},{25,29},{5,1},{26,30},{6,2},{27,31},{7,3}} | collective-permute-start | bytes 196616 | tf_op jit(solution)/shard_map/ppermute | solution.py:64
  89.5 22.1 %all-to-all-start.1 = ((f32[16,4,512]{2,0,1:T(8,128)}), f32[16,4,512]{2,0,1:T(8,128)S(1)}, u32[]{:S(2)}, u32[]{:S(2)}) async-start(f32[16,4,512]{2,0,1:T(8,128)} %copy.13), calls=%async_computation.1 | async-start | bytes 262144 | tf_op jit(solution)/shard_map/all_to_all | solution.py:81
  111.7 7.9 %all-to-all-start.2 = ((f32[16,4,512]{2,0,1:T(8,128)}), f32[16,4,512]{2,0,1:T(8,128)S(1)}, u32[]{:S(2)}, u32[]{:S(2)}) async-start(f32[16,4,512]{2,0,1:T(8,128)} %copy.14), calls=%async_computation.2 | async-start | bytes 262144 | tf_op jit(solution)/shard_map/all_to_all | solution.py:82

commit v4 on v3

--- a/solution.py
+++ b/solution.py
@@ -29,8 +29,6 @@
     own_pts = points[0]
     per_device = own_pts.shape[1]
     day_pts = lax.all_gather(own_pts, "pt", axis=1, tiled=True)
-    before_pts = shifted(day_pts, "day", 1)
-    after_pts = shifted(day_pts, "day", -1)
     support_total = day_pts.shape[1]
     own_weight = clone_weight[0] * potential[0][None, :]
     block_weight = lax.all_to_all(own_weight, "pt", 0, 1, tiled=True)
@@ -39,47 +37,50 @@
     live_all = (jnp.arange(support_total, dtype=jnp.int32) < support_count[0]).astype(jnp.float32)
     live_own = lax.dynamic_slice_in_dim(live_all, pt_rank * per_device, per_device)
     day_norm = norm_of(day_pts)
-    source_pts = jnp.stack([before_pts, after_pts])
-    source_norm = jnp.stack([norm_of(before_pts), norm_of(after_pts)])
-    inner = lax.dot_general(
-        source_pts, day_pts, (((1,), (0,)), ((), ())), preferred_element_type=jnp.float32
-    )
-    chain_kernel = jnp.exp(
-        -(source_norm[:, :, None] + day_norm[None, None, :] - 2.0 * inner)
-    ).astype(jnp.bfloat16)
+
+    def chain_kernel(source_pts):
+        dist = squared_dist(source_pts, norm_of(source_pts), day_pts, day_norm)
+        return jnp.exp(-dist).astype(jnp.bfloat16)
+
+    half = day_count // 2
+    switch_step = half - 1
+    first_forward = day_index < half
+    first_route = [(d - 1, d) for d in range(1, half)]
+    first_route += [(d + 1, d) for d in range(half, day_count - 1)]
+    first_kernel = chain_kernel(lax.ppermute(day_pts, "day", first_route))
 
     def settle(values):
-        masked = values * live_all[None, None, :]
-        return masked * live_total / jnp.sum(masked, axis=2, keepdims=True)
+        masked = values * live_all[None, :]
+        return masked * live_total / jnp.sum(masked, axis=1, keepdims=True)
 
-    seed_rows = jnp.broadcast_to(live_all[None, None, :], (2, block_rows, support_total))
-    rows = seed_rows
+    rows = jnp.broadcast_to(live_all[None, None, :], (2, block_rows, support_total))
+    later_kernel = None
     for step in range(day_count - 1):
+        if step == min(1, switch_step):
+            later_pts, rows = lax.optimization_barrier((day_pts, rows))
+            later_source = jnp.where(
+                first_forward,
+                lax.ppermute(later_pts, "day", [(d + 1, d) for d in range(half)]),
+                lax.ppermute(later_pts, "day", [(d - 1, d) for d in range(half, day_count)]),
+            )
+        if step == switch_step:
+            later_source, rows = lax.optimization_barrier((later_source, rows))
+            later_kernel = chain_kernel(later_source)
+        kernel = first_kernel if step < switch_step else later_kernel
         forward_from = step
         backward_from = day_count - 1 - step
         sent = (rows * block_weight[None]).astype(jnp.bfloat16)
-        if forward_from != backward_from:
-            outgoing = jnp.where(day_index == forward_from, sent[0], sent[1])
-            route = [(forward_from, forward_from + 1), (backward_from, backward_from - 1)]
-            incoming = lax.ppermute(outgoing, "day", route)
-            arrived = jnp.stack([incoming, incoming])
-        else:
-            arrived = jnp.stack([shifted(sent[0], "day", 1), shifted(sent[1], "day", -1)])
-        fresh = settle(
-            lax.dot_general(
-                arrived,
-                chain_kernel,
-                (((2,), (1,)), ((0,), (0,))),
-                preferred_element_type=jnp.float32,
-            )
-        )
+        outgoing = jnp.where(day_index == forward_from, sent[0], sent[1])
+        route = [(forward_from, forward_from + 1), (backward_from, backward_from - 1)]
+        incoming = lax.ppermute(outgoing, "day", route)
+        fresh = settle(jnp.dot(incoming, kernel, preferred_element_type=jnp.float32))
         keep = jnp.stack([day_index == step + 1, day_index == day_count - 2 - step])
-        rows = jnp.where(keep[:, None, None], fresh, rows)
+        rows = jnp.where(keep[:, None, None], fresh[None], rows)
     forward_rows = rows[0]
     backward_rows = rows[1]
-
-    forward_out = lax.all_to_all(forward_rows, "pt", 1, 0, tiled=True)
-    backward_out = lax.all_to_all(backward_rows, "pt", 1, 0, tiled=True)
+    both_out = lax.all_to_all(rows, "pt", 2, 1, tiled=True)
+    forward_out = both_out[0]
+    backward_out = both_out[1]
     mass_part = jnp.sum(forward_rows * block_weight * backward_rows, axis=0)
     full_mass = live_all * lax.psum(mass_part, "pt")
     mass_total = jnp.sum(full_mass)

time: 122 us -> 119 us (0.975)
  local copies, waits for them, and re-layouts: 4.16 us -> 11.6 us
  matrix products: 27.5 us -> 20.7 us
  starting transfers between devices: 24.3 us -> 21.8 us
  waiting for transfers between devices: 30.2 us -> 27.7 us
  other arithmetic: 11.3 us -> 13.2 us
    dot_general x8 -> x7, matrix products: 23.2 us -> 9.16 us  [shards(): jnp.dot(incoming, kernel, preferred_element_type=jnp.float32)]
    ppermute x2 -> x3, waiting for transfers between devices: 0.01 us -> 9.41 us  [the longest x1 9.41 us: shards(): lax.ppermute(later_pts, 'day', [(d + 1, d) for d in range(half)])]
    ppermute x7, waiting for transfers between devices: 26.1 us -> 18.3 us  [shards(): incoming = lax.ppermute(outgoing, 'day', route)]
    dot_general x1 -> x3, matrix products: 4.31 us -> 11.5 us  [squared_dist(): lax.dot_general(left_pts, right_pts, (((0,), (0,)), ((), ())), preferred_...]
    unnamed x5, local copies, waits for them, and re-layouts: 2.55 us -> 7.72 us
    all_to_all x2 -> x1, waiting for transfers between devices: 3.91 us -> 0.01 us  [shards(): both_out = lax.all_to_all(rows, 'pt', 2, 1, tiled=True)]
    all_to_all x2 -> x1, starting transfers between devices: 6.88 us -> 3.4 us  [shards(): both_out = lax.all_to_all(rows, 'pt', 2, 1, tiled=True)]
    slice x1 -> x3, local copies, waits for them, and re-layouts: 0.02 us -> 1.42 us  [the longest x2 0.72 us: shards(): backward_out = both_out[1]]
  transfers between devices with their start and end apart: 12 -> 12, of which waited for: 3 -> 2; matrix products, arithmetic and copies ran while one was open for 20% -> 19% of each run, Pallas kernels for 0% -> 0%
where the time goes in v4:
time: 119 us; the launch traced here: 118 us
  waiting for transfers between devices  27.7 us (23%)
  starting transfers between devices  21.8 us (18%)
  matrix products  20.7 us (17%)
  blocking collectives  20.3 us (17%)
  other arithmetic  13.2 us (11%)
  local copies, waits for them, and re-layouts  11.6 us (10%)
  between operations  3.1 us (3%)
    ppermute x7, waiting for transfers between devices, shards(): incoming = lax.ppermute(outgoing, 'day', route)  18.3 us
    dot_general x3, matrix products, squared_dist(): lax.dot_general(left_pts, right_pts, (((0,), (0,)), ((), ())), preferred_...  11.5 us
    ppermute x1, waiting for transfers between devices, shards(): lax.ppermute(later_pts, 'day', [(d + 1, d) for d in range(half)])  9.41 us
    dot_general x7, matrix products, shards(): jnp.dot(incoming, kernel, preferred_element_type=jnp.float32)  9.16 us
    ppermute x7, starting transfers between devices, shards(): incoming = lax.ppermute(outgoing, 'day', route)  8.24 us
    unnamed x5, local copies, waits for them, and re-layouts  7.72 us
    unnamed x1, blocking collectives  7.69 us
    all_gather x1, blocking collectives, shards(): day_pts = lax.all_gather(own_pts, 'pt', axis=1, tiled=True)  6.85 us
  transfers between devices with their start and end apart: 12, of which 2 were waited for; matrix products, arithmetic and copies ran while one was open for 19% of the time, Pallas kernels for 0%

profile of v4, /device:TPU:0, one launch (start us, length us, event | category | flops | bytes accessed | tf_op | source)
XLA Modules:
  0.0 118.3 jit_solution(9733550079531027342)
XLA Ops:
  0.6 1.6 %broadcast_multiply_fusion = f32[4,16,512]{2,1,0:T(8,128)} fusion(f32[4,16,512]{2,1,0:T(8,128)} %bitcast.101, f32[512]{0:T(512)} %bitcast.104), kind=kLoop, calls=%fused_computation.56 | loop fusion | flops 32768 | bytes 264192 | tf_op jit(solution)/shard_map/mul | solution.py:33
  2.2 4.3 %all-to-all-start = ((f32[4,16,512]{2,1,0:T(8,128)}), f32[4,16,512]{2,1,0:T(8,128)S(1)}, u32[]{:S(2)}, u32[]{:S(2)}) async-start(f32[4,16,512]{2,1,0:T(8,128)} %broadcast_multiply_fusion), calls=%async_computation | async-start | bytes 262144 | tf_op jit(solution)/shard_map/all_to_all | solution.py:34
  6.5 6.8 %all-gather = bf16[1,64,2048]{2,1,0:T(8,128)(2,1)S(1)} all-gather(bf16[1,64,512]{2,1,0:T(8,128)(2,1)} %param.6), channel_id=2, replica_groups=mesh['day'=8,'pt'=4] {'pt'}, dimensions={2}, use_global_device_ids=true | all-gather | bytes 327680 | tf_op jit(solution)/shard_map/all_gather | solution.py:31
  13.3 3.9 %collective-permute-start.1 = (bf16[64,2048]{1,0:T(8,128)(2,1)S(1)}, bf16[64,2048]{1,0:T(8,128)(2,1)S(1)}, u32[]{:S(2)}, u32[]{:S(2)}) collective-permute-start(bf16[64,2048]{1,0:T(8,128)(2,1)S(1)} %bitcast.97), channel_id=1, source_target_pairs={{0,4},{4,8},{8,12},{20,16},{24,20},{28,24},{1,5},{5,9},{9,13},{21,... | collective-permute-start | bytes 786440 | tf_op jit(solution)/shard_map/ppermute | solution.py:50
  18.0 1.0 multiply_reduce_fusion.2
  19.7 1.3 %dynamic-slice = u32[1]{0:T(128)} dynamic-slice(u32[32]{0:T(128)} %constant.43, u32[]{:T(128)S(6)} %add.66), dynamic_slice_sizes={1} | dynamic-slice | bytes 12
  21.9 3.4 %collective-permute-start = (bf16[16,2048]{1,0:T(8,128)(2,1)S(1)}, bf16[16,2048]{1,0:T(8,128)(2,1)S(1)}, u32[]{:S(2)}, u32[]{:S(2)}) collective-permute-start(bf16[16,2048]{1,0:T(8,128)(2,1)S(1)} %fusion.11), channel_id=1, source_target_pairs={{0,4},{28,24},{1,5},{29,25},{2,6},{30,26},{3,7},{31,27}} | collective-permute-start | bytes 196616 | tf_op jit(solution)/shard_map/ppermute | solution.py:75
  25.4 3.6 %exponential_convert_fusion.1 = bf16[2048,2048]{1,0:T(8,128)(2,1)S(1)} fusion(bf16[64,2048]{1,0:T(8,128)(2,1)S(1)} %collective-permute-done.1, f32[2048]{0:T(1024)S(1)} %multiply_reduce_fusion.4, f32[2048]{0:T(1024)S(1)} %multiply_reduce_fusion.5, bf16[1,64,2048]{2,1,0:T(8,128)(2,1)S(1)} %all-gather), kind=kOutput, calls=%fused_computation.4 | convolution fusion | flops 557842432 | bytes 8929280 | tf_op jit(solution)/shard_map/dot_general | solution.py:19
  29.0 1.3 %fusion.20 = (f32[16]{0:T(128)S(1)}, f32[16,2048]{1,0:T(8,128)S(1)}) fusion(f32[2048]{0:T(1024)S(1)} %fusion.13, bf16[16,2048]{1,0:T(8,128)(2,1)S(1)} %collective-permute-done, bf16[2048,2048]{1,0:T(8,128)(2,1)S(1)} %exponential_convert_fusion.1), kind=kOutput, calls=%fused_computation.75 | convolution fusion | flops 134283248 | bytes 8593472 | tf_op jit(solution)/shard_map/dot_general | solution.py:76
  31.3 1.3 %fusion.21 = (f32[16]{0:T(128)S(1)}, f32[16,2048]{1,0:T(8,128)S(1)}) fusion(f32[2048]{0:T(1024)S(1)} %fusion.13, bf16[16,2048]{1,0:T(8,128)(2,1)S(1)} %collective-permute-done.4, bf16[2048,2048]{1,0:T(8,128)(2,1)S(1)} %exponential_convert_fusion.1), kind=kOutput, calls=%fused_computation.76 | convolution fusion | flops 134283248 | bytes 8593472 | tf_op jit(solution)/shard_map/dot_general | solution.py:76
  33.6 1.3 %collective-permute-start.2 = (bf16[64,2048]{1,0:T(8,128)(2,1)S(1)}, bf16[64,2048]{1,0:T(8,128)(2,1)S(1)}, u32[]{:S(2)}, u32[]{:S(2)}) collective-permute-start(bf16[64,2048]{1,0:T(8,128)(2,1)S(1)} %bitcast.98), channel_id=1, source_target_pairs={{4,0},{8,4},{12,8},{16,12},{5,1},{9,5},{13,9},{17,13},{6,2},{10,6}... | collective-permute-start | bytes 786440 | tf_op jit(solution)/shard_map/ppermute | solution.py:63
  35.6 1.3 %fusion.22 = (f32[16]{0:T(128)S(1)}, f32[16,2048]{1,0:T(8,128)S(1)}) fusion(f32[2048]{0:T(1024)S(1)} %fusion.13, bf16[16,2048]{1,0:T(8,128)(2,1)S(1)} %collective-permute-done.5, bf16[2048,2048]{1,0:T(8,128)(2,1)S(1)} %exponential_convert_fusion.1), kind=kOutput, calls=%fused_computation.77 | convolution fusion | flops 134283248 | bytes 8593472 | tf_op jit(solution)/shard_map/dot_general | solution.py:76
  37.1 9.4 %collective-permute-done.2 = bf16[64,2048]{1,0:T(8,128)(2,1)S(1)} collective-permute-done((bf16[64,2048]{1,0:T(8,128)(2,1)S(1)}, bf16[64,2048]{1,0:T(8,128)(2,1)S(1)}, u32[]{:S(2)}, u32[]{:S(2)}) %collective-permute-start.2) | collective-permute-done | bytes 262176 | tf_op jit(solution)/shard_map/ppermute | solution.py:63
  47.4 3.6 %exponential_convert_fusion = bf16[2048,2048]{1,0:T(8,128)(2,1)S(1)} fusion(bf16[64,2048]{1,0:T(8,128)(2,1)S(1)} %broadcast_select_fusion, f32[2048]{0:T(1024)S(1)} %multiply_reduce_fusion.3, f32[2048]{0:T(1024)S(1)} %multiply_reduce_fusion.4, bf16[1,64,2048]{2,1,0:T(8,128)(2,1)S(1)} %all-gather), kind=kOutput, calls=%fused_computation.3 | convolution fusion | flops 557842432 | bytes 8929280 | tf_op jit(solution)/shard_map/dot_general | solution.py:19
  51.0 1.3 %fusion.23 = (f32[16]{0:T(128)S(1)}, f32[16,2048]{1,0:T(8,128)S(1)}) fusion(f32[2048]{0:T(1024)S(1)} %fusion.13, bf16[16,2048]{1,0:T(8,128)(2,1)S(1)} %collective-permute-done.6, bf16[2048,2048]{1,0:T(8,128)(2,1)S(1)} %exponential_convert_fusion), kind=kOutput, calls=%fused_computation.78 | convolution fusion | flops 134283248 | bytes 8593472 | tf_op jit(solution)/shard_map/dot_general | solution.py:76
  53.3 1.3 %fusion.24 = (f32[16]{0:T(128)S(1)}, f32[16,2048]{1,0:T(8,128)S(1)}) fusion(f32[2048]{0:T(1024)S(1)} %fusion.13, bf16[16,2048]{1,0:T(8,128)(2,1)S(1)} %collective-permute-done.7, bf16[2048,2048]{1,0:T(8,128)(2,1)S(1)} %exponential_convert_fusion), kind=kOutput, calls=%fused_computation.79 | convolution fusion | flops 134283248 | bytes 8593472 | tf_op jit(solution)/shard_map/dot_general | solution.py:76
  54.8 0.8 collective-permute-start.8
  55.8 1.3 %fusion.25 = (f32[16]{0:T(128)S(1)}, f32[16,2048]{1,0:T(8,128)S(1)}) fusion(f32[2048]{0:T(1024)S(1)} %fusion.13, bf16[16,2048]{1,0:T(8,128)(2,1)S(1)} %collective-permute-done.8, bf16[2048,2048]{1,0:T(8,128)(2,1)S(1)} %exponential_convert_fusion), kind=kOutput, calls=%fused_computation.80 | convolution fusion | flops 134283248 | bytes 8593472 | tf_op jit(solution)/shard_map/dot_general | solution.py:76
  57.3 1.3 %collective-permute-start.9 = (bf16[16,2048]{1,0:T(8,128)(2,1)S(1)}, bf16[16,2048]{1,0:T(8,128)(2,1)S(1)}, u32[]{:S(2)}, u32[]{:S(2)}) collective-permute-start(bf16[16,2048]{1,0:T(8,128)(2,1)S(1)} %fusion.5), channel_id=1, source_target_pairs={{24,28},{4,0},{25,29},{5,1},{26,30},{6,2},{27,31},{7,3}} | collective-permute-start | bytes 196616 | tf_op jit(solution)/shard_map/ppermute | solution.py:75
  58.7 18.3 %collective-permute-done.9 = bf16[16,2048]{1,0:T(8,128)(2,1)S(1)} collective-permute-done((bf16[16,2048]{1,0:T(8,128)(2,1)S(1)}, bf16[16,2048]{1,0:T(8,128)(2,1)S(1)}, u32[]{:S(2)}, u32[]{:S(2)}) %collective-permute-start.9) | collective-permute-done | bytes 65568 | tf_op jit(solution)/shard_map/ppermute | solution.py:75
  77.0 1.3 %fusion.26 = (f32[16]{0:T(128)S(1)}, f32[16,2048]{1,0:T(8,128)S(1)}) fusion(f32[2048]{0:T(1024)S(1)} %fusion.13, bf16[16,2048]{1,0:T(8,128)(2,1)S(1)} %collective-permute-done.9, bf16[2048,2048]{1,0:T(8,128)(2,1)S(1)} %exponential_convert_fusion), kind=kOutput, calls=%fused_computation.81 | convolution fusion | flops 134283248 | bytes 8593472 | tf_op jit(solution)/shard_map/dot_general | solution.py:76
  78.6 1.0 copy.14
  79.6 5.8 %psum.7 = f32[2048]{0:T(1024)S(1)} all-reduce(f32[2048]{0:T(1024)S(1)} %fusion.3), channel_id=1, replica_groups=mesh['day'=8,'pt'=4] {'pt'}, use_global_device_ids=true, to_apply=%region_12.13 | all-reduce | flops 2048 | bytes 16384 | tf_op jit(solution)/shard_map/psum | solution.py:85
  85.4 3.6 %reshape.81 = f32[4,1,16384]{2,1,0:T(1,128)} reshape(f32[2048,2,16]{2,1,0:T(2,128)S(1)} %bitcast.94) | data formatting | bytes 524288
  89.0 3.4 %all-to-all-start.1 = ((f32[4,1,16384]{2,1,0:T(1,128)}), f32[4,1,16384]{2,1,0:T(1,128)S(1)}, u32[]{:S(2)}, u32[]{:S(2)}) async-start(f32[4,1,16384]{2,1,0:T(1,128)} %reshape.81), calls=%async_computation.1 | async-start | bytes 524288 | tf_op jit(solution)/shard_map/all_to_all | solution.py:81
  93.0 4.3 %multiply_reduce_fusion.1 = (f32[2048]{0:T(1024)S(1)}, f32[2048,2048]{1,0:T(8,128)S(1)}) fusion(f32[2048]{0:T(1024)S(1)} %get-tuple-element.12, f32[2048]{0:T(1024)S(1)} %multiply_reduce_fusion.2, f32[2048]{0:T(1024)S(1)} %multiply_reduce_fusion.4, bf16[1,64,2048]{2,1,0:T(8,128)(2,1)S(1)} %copy-done, bf16[1,64,2048]{2,1,0:T(8,128)(2,1)S(1)} %all-gather), kind=kOutput, calls=%fused_computation.1 | convolution fusion | flops 562034688 | bytes 17334272 | tf_op jit(solution)/shard_map/dot_general | solution.py:19
  98.0 5.0 %multiply_reduce_fusion = f32[2048]{0:T(1024)S(1)} fusion(f32[2048,2048]{1,0:T(8,128)S(1)} %get-tuple-element.30, f32[2048]{0:T(1024)S(1)} %select_divide_fusion, f32[2048]{0:T(1024)S(1)} %multiply_reduce_fusion.2, f32[2048]{0:T(1024)S(1)} %multiply_reduce_fusion.4), kind=kLoop, calls=%fused_computation | loop fusion | flops 25163776 | bytes 16809984 | tf_op jit(solution)/shard_map/reduce_sum | solution.py:99
  102.9 7.7 %all-reduce = f32[2048]{0:T(1024)S(1)} all-reduce(f32[2048]{0:T(1024)S(1)} %multiply_reduce_fusion), channel_id=3, replica_groups=mesh['day'=8,'pt'=4] {'pt'}, use_global_device_ids=true, to_apply=%region_16.17.clone | all-reduce | flops 2048 | bytes 16384
  111.8 1.4 %reduce = f32[4,16384]{1,0:T(4,128)S(1)} reduce(f32[4,1,16384]{2,1,0:T(1,128)S(1)} %all-to-all-done.1, f32[]{:T(128)} %broadcast.84), dimensions={1}, to_apply=%all_to_all.23.reduce_sub_computation | reduce | bytes 524292 | tf_op jit(solution)/shard_map/all_to_all | solution.py:81
  113.2 2.8 %reshape.82 = f32[2048,2,16]{2,1,0:T(2,128)S(1)} reshape(f32[4,16384]{1,0:T(4,128)S(1)} %reduce) | data formatting | bytes 524288
  116.0 0.9 copy.18
  116.9 0.7 copy.16
  (60 shorter events, 8.8 us)
Async XLA Ops:
  2.2 19.6 %all-to-all-start = ((f32[4,16,512]{2,1,0:T(8,128)}), f32[4,16,512]{2,1,0:T(8,128)S(1)}, u32[]{:S(2)}, u32[]{:S(2)}) async-start(f32[4,16,512]{2,1,0:T(8,128)} %broadcast_multiply_fusion), calls=%async_computation | async-start | bytes 262144 | tf_op jit(solution)/shard_map/all_to_all | solution.py:34
  13.3 12.0 %collective-permute-start.1 = (bf16[64,2048]{1,0:T(8,128)(2,1)S(1)}, bf16[64,2048]{1,0:T(8,128)(2,1)S(1)}, u32[]{:S(2)}, u32[]{:S(2)}) collective-permute-start(bf16[64,2048]{1,0:T(8,128)(2,1)S(1)} %bitcast.97), channel_id=1, source_target_pairs={{0,4},{4,8},{8,12},{20,16},{24,20},{28,24},{1,5},{5,9},{9,13},{21,... | collective-permute-start | bytes 786440 | tf_op jit(solution)/shard_map/ppermute | solution.py:50
  21.9 7.2 %collective-permute-start = (bf16[16,2048]{1,0:T(8,128)(2,1)S(1)}, bf16[16,2048]{1,0:T(8,128)(2,1)S(1)}, u32[]{:S(2)}, u32[]{:S(2)}) collective-permute-start(bf16[16,2048]{1,0:T(8,128)(2,1)S(1)} %fusion.11), channel_id=1, source_target_pairs={{0,4},{28,24},{1,5},{29,25},{2,6},{30,26},{3,7},{31,27}} | collective-permute-start | bytes 196616 | tf_op jit(solution)/shard_map/ppermute | solution.py:75
  30.6 0.8 collective-permute-start.4
  32.9 2.7 %collective-permute-start.5 = (bf16[16,2048]{1,0:T(8,128)(2,1)S(1)}, bf16[16,2048]{1,0:T(8,128)(2,1)S(1)}, u32[]{:S(2)}, u32[]{:S(2)}) collective-permute-start(bf16[16,2048]{1,0:T(8,128)(2,1)S(1)} %fusion.9), channel_id=1, source_target_pairs={{8,12},{20,16},{9,13},{21,17},{10,14},{22,18},{11,15},{23,19}} | collective-permute-start | bytes 196616 | tf_op jit(solution)/shard_map/ppermute | solution.py:75
  33.6 12.9 %collective-permute-start.2 = (bf16[64,2048]{1,0:T(8,128)(2,1)S(1)}, bf16[64,2048]{1,0:T(8,128)(2,1)S(1)}, u32[]{:S(2)}, u32[]{:S(2)}) collective-permute-start(bf16[64,2048]{1,0:T(8,128)(2,1)S(1)} %bitcast.98), channel_id=1, source_target_pairs={{4,0},{8,4},{12,8},{16,12},{5,1},{9,5},{13,9},{17,13},{6,2},{10,6}... | collective-permute-start | bytes 786440 | tf_op jit(solution)/shard_map/ppermute | solution.py:63
  34.9 11.6 %collective-permute-start.3 = (bf16[64,2048]{1,0:T(8,128)(2,1)S(1)}, bf16[64,2048]{1,0:T(8,128)(2,1)S(1)}, u32[]{:S(2)}, u32[]{:S(2)}) collective-permute-start(bf16[64,2048]{1,0:T(8,128)(2,1)S(1)} %bitcast.99), channel_id=1, source_target_pairs={{12,16},{16,20},{20,24},{24,28},{13,17},{17,21},{21,25},{25,29},{1... | collective-permute-start | bytes 786440 | tf_op jit(solution)/shard_map/ppermute | solution.py:64
  46.7 4.3 %collective-permute-start.6 = (bf16[16,2048]{1,0:T(8,128)(2,1)S(1)}, bf16[16,2048]{1,0:T(8,128)(2,1)S(1)}, u32[]{:S(2)}, u32[]{:S(2)}) collective-permute-start(bf16[16,2048]{1,0:T(8,128)(2,1)S(1)} %fusion.8), channel_id=1, source_target_pairs={{12,16},{16,12},{13,17},{17,13},{14,18},{18,14},{15,19},{19,15}} | collective-permute-start | bytes 196616 | tf_op jit(solution)/shard_map/ppermute | solution.py:75
  52.5 0.8 collective-permute-start.7
  53.3 39.7 %copy-start = (bf16[1,64,2048]{2,1,0:T(8,128)(2,1)S(1)}, bf16[1,64,2048]{2,1,0:T(8,128)(2,1)}, u32[]{:S(2)}) copy-start(bf16[1,64,2048]{2,1,0:T(8,128)(2,1)} %param.7) | copy-start | bytes 786436
  54.8 0.9 collective-permute-start.8
  57.3 19.6 %collective-permute-start.9 = (bf16[16,2048]{1,0:T(8,128)(2,1)S(1)}, bf16[16,2048]{1,0:T(8,128)(2,1)S(1)}, u32[]{:S(2)}, u32[]{:S(2)}) collective-permute-start(bf16[16,2048]{1,0:T(8,128)(2,1)S(1)} %fusion.5), channel_id=1, source_target_pairs={{24,28},{4,0},{25,29},{5,1},{26,30},{6,2},{27,31},{7,3}} | collective-permute-start | bytes 196616 | tf_op jit(solution)/shard_map/ppermute | solution.py:75
  89.0 22.3 %all-to-all-start.1 = ((f32[4,1,16384]{2,1,0:T(1,128)}), f32[4,1,16384]{2,1,0:T(1,128)S(1)}, u32[]{:S(2)}, u32[]{:S(2)}) async-start(f32[4,1,16384]{2,1,0:T(1,128)} %reshape.81), calls=%async_computation.1 | async-start | bytes 524288 | tf_op jit(solution)/shard_map/all_to_all | solution.py:81

commit v5 on v4

--- a/solution.py
+++ b/solution.py
@@ -31,8 +31,9 @@
     day_pts = lax.all_gather(own_pts, "pt", axis=1, tiled=True)
     support_total = day_pts.shape[1]
     own_weight = clone_weight[0] * potential[0][None, :]
-    block_weight = lax.all_to_all(own_weight, "pt", 0, 1, tiled=True)
-    block_rows = block_weight.shape[0]
+    full_weight = lax.all_gather(own_weight, "pt", axis=1, tiled=True)
+    block_rows = full_weight.shape[0] // lax.axis_size("pt")
+    block_weight = lax.dynamic_slice_in_dim(full_weight, pt_rank * block_rows, block_rows, 0)
     live_total = support_count[0].astype(jnp.float32)
     live_all = (jnp.arange(support_total, dtype=jnp.int32) < support_count[0]).astype(jnp.float32)
     live_own = lax.dynamic_slice_in_dim(live_all, pt_rank * per_device, per_device)
@@ -76,13 +77,11 @@
         fresh = settle(jnp.dot(incoming, kernel, preferred_element_type=jnp.float32))
         keep = jnp.stack([day_index == step + 1, day_index == day_count - 2 - step])
         rows = jnp.where(keep[:, None, None], fresh[None], rows)
-    forward_rows = rows[0]
-    backward_rows = rows[1]
-    both_out = lax.all_to_all(rows, "pt", 2, 1, tiled=True)
-    forward_out = both_out[0]
-    backward_out = both_out[1]
-    mass_part = jnp.sum(forward_rows * block_weight * backward_rows, axis=0)
-    full_mass = live_all * lax.psum(mass_part, "pt")
+    every_rows = lax.all_gather(rows, "pt", axis=1, tiled=True)
+    full_mass = live_all * jnp.sum(every_rows[0] * full_weight * every_rows[1], axis=0)
+    own_rows = lax.dynamic_slice_in_dim(every_rows, pt_rank * per_device, per_device, 2)
+    forward_out = own_rows[0]
+    backward_out = own_rows[1]
     mass_total = jnp.sum(full_mass)
 
     cell_total = cell_count[0]

time: 119 us -> 133 us (1.12)
  waiting for transfers between devices: 27.7 us -> 48.5 us
  between operations: 3.1 us -> 16.4 us
  starting transfers between devices: 21.8 us -> 11.6 us
  local copies, waits for them, and re-layouts: 11.6 us -> 2.29 us
    all_gather x0 -> x1, waiting for transfers between devices: none -> 13.5 us  [shards(): every_rows = lax.all_gather(rows, 'pt', axis=1, tiled=True)]
    all_gather x0 -> x1, blocking collectives: none -> 8.68 us  [shards(): full_weight = lax.all_gather(own_weight, 'pt', axis=1, tiled=True)]
    all_to_all x2 -> x0, starting transfers between devices: 7.67 us -> none  [the longest x1 4.26 us: shards(): block_weight = lax.all_to_all(own_weight, 'pt', 0, 1, tiled=True)]
    unnamed x5, local copies, waits for them, and re-layouts: 7.72 us -> 0.6 us
    ppermute x1, waiting for transfers between devices: 0.01 us -> 6.01 us  [shards(): first_kernel = chain_kernel(lax.ppermute(day_pts, 'day', first_route))]
    psum x1 -> x0, blocking collectives: 5.77 us -> none  [shards(): full_mass = live_all * lax.psum(mass_part, 'pt')]
    ppermute x1, starting transfers between devices: 3.91 us -> 1.37 us  [shards(): first_kernel = chain_kernel(lax.ppermute(day_pts, 'day', first_route))]
    unnamed x1, blocking collectives: 7.69 us -> 6.02 us
  transfers between devices with their start and end apart: 12 -> 11, of which waited for: 2 -> 4; matrix products, arithmetic and copies ran while one was open for 19% -> 8% of each run, Pallas kernels for 0% -> 0%
where the time goes in v5:
time: 133 us; the launch traced here: 132 us
  waiting for transfers between devices  48.5 us (36%)
  blocking collectives  20.7 us (16%)
  matrix products  20.6 us (15%)
  between operations  16.4 us (12%)
  other arithmetic  12.2 us (9%)
  starting transfers between devices  11.6 us (9%)
  local copies, waits for them, and re-layouts  2.29 us (2%)
    ppermute x7, waiting for transfers between devices, shards(): incoming = lax.ppermute(outgoing, 'day', route)  18.3 us
    all_gather x1, waiting for transfers between devices, shards(): every_rows = lax.all_gather(rows, 'pt', axis=1, tiled=True)  13.5 us
    dot_general x3, matrix products, squared_dist(): lax.dot_general(left_pts, right_pts, (((0,), (0,)), ((), ())), preferred_...  11.5 us
    ppermute x1, waiting for transfers between devices, shards(): lax.ppermute(later_pts, 'day', [(d + 1, d) for d in range(half)])  10.6 us
    dot_general x7, matrix products, shards(): jnp.dot(incoming, kernel, preferred_element_type=jnp.float32)  9.16 us
    all_gather x1, blocking collectives, shards(): full_weight = lax.all_gather(own_weight, 'pt', axis=1, tiled=True)  8.68 us
    ppermute x7, starting transfers between devices, shards(): incoming = lax.ppermute(outgoing, 'day', route)  8.19 us
    unnamed x1, blocking collectives  6.02 us
  transfers between devices with their start and end apart: 11, of which 4 were waited for; matrix products, arithmetic and copies ran while one was open for 8% of the time, Pallas kernels for 0%

profile of v5, /device:TPU:0, one launch (start us, length us, event | category | flops | bytes accessed | tf_op | source)
XLA Modules:
  0.0 132.2 jit_solution(3300377594844370672)
XLA Ops:
  7.9 0.9 bitcast_multiply_fusion
  8.8 8.7 %all_gather.10 = f32[64,2048]{1,0:T(8,128)S(1)} all-gather(f32[64,512]{1,0:T(8,128)S(1)} %bitcast_multiply_fusion), channel_id=1, replica_groups=mesh['day'=8,'pt'=4] {'pt'}, dimensions={1}, use_global_device_ids=true | all-gather | bytes 655360 | tf_op jit(solution)/shard_map/all_gather | solution.py:34
  17.5 3.4 %collective-permute-start = (bf16[16,2048]{1,0:T(8,128)(2,1)S(1)}, bf16[16,2048]{1,0:T(8,128)(2,1)S(1)}, u32[]{:S(2)}, u32[]{:S(2)}) collective-permute-start(bf16[16,2048]{1,0:T(8,128)(2,1)S(1)} %fusion.11), channel_id=1, source_target_pairs={{0,4},{28,24},{1,5},{29,25},{2,6},{30,26},{3,7},{31,27}} | collective-permute-start | bytes 196616 | tf_op jit(solution)/shard_map/ppermute | solution.py:76
  20.9 6.0 %all-gather = bf16[1,64,2048]{2,1,0:T(8,128)(2,1)S(1)} all-gather(bf16[1,64,512]{2,1,0:T(8,128)(2,1)} %param.6), channel_id=2, replica_groups=mesh['day'=8,'pt'=4] {'pt'}, dimensions={2}, use_global_device_ids=true | all-gather | bytes 327680 | tf_op jit(solution)/shard_map/all_gather | solution.py:31
  26.9 1.4 %collective-permute-start.1 = (bf16[64,2048]{1,0:T(8,128)(2,1)S(1)}, bf16[64,2048]{1,0:T(8,128)(2,1)S(1)}, u32[]{:S(2)}, u32[]{:S(2)}) collective-permute-start(bf16[64,2048]{1,0:T(8,128)(2,1)S(1)} %bitcast.78), channel_id=1, source_target_pairs={{0,4},{4,8},{8,12},{20,16},{24,20},{28,24},{1,5},{5,9},{9,13},{21,... | collective-permute-start | bytes 786440 | tf_op jit(solution)/shard_map/ppermute | solution.py:51
  28.5 6.0 %collective-permute-done.1 = bf16[64,2048]{1,0:T(8,128)(2,1)S(1)} collective-permute-done((bf16[64,2048]{1,0:T(8,128)(2,1)S(1)}, bf16[64,2048]{1,0:T(8,128)(2,1)S(1)}, u32[]{:S(2)}, u32[]{:S(2)}) %collective-permute-start.1) | collective-permute-done | bytes 262176 | tf_op jit(solution)/shard_map/ppermute | solution.py:51
  34.6 3.6 %exponential_convert_fusion.1 = bf16[2048,2048]{1,0:T(8,128)(2,1)S(1)} fusion(bf16[64,2048]{1,0:T(8,128)(2,1)S(1)} %collective-permute-done.1, f32[2048]{0:T(1024)S(1)} %multiply_reduce_fusion.4, f32[2048]{0:T(1024)S(1)} %multiply_reduce_fusion.5, bf16[1,64,2048]{2,1,0:T(8,128)(2,1)S(1)} %all-gather), kind=kOutput, calls=%fused_computation.4 | convolution fusion | flops 557842432 | bytes 8929280 | tf_op jit(solution)/shard_map/dot_general | solution.py:19
  38.2 1.3 fusion.19
  39.8 0.7 collective-permute-start.4
  40.5 1.3 fusion.20
  42.1 0.7 collective-permute-start.5
  42.8 1.3 collective-permute-start.2
  44.1 0.7 collective-permute-start.3
  44.8 1.3 fusion.21
  46.3 10.6 %collective-permute-done.2 = bf16[64,2048]{1,0:T(8,128)(2,1)S(1)} collective-permute-done((bf16[64,2048]{1,0:T(8,128)(2,1)S(1)}, bf16[64,2048]{1,0:T(8,128)(2,1)S(1)}, u32[]{:S(2)}, u32[]{:S(2)}) %collective-permute-start.2) | collective-permute-done | bytes 262176 | tf_op jit(solution)/shard_map/ppermute | solution.py:64
  57.1 0.7 collective-permute-start.6
  57.8 3.6 %exponential_convert_fusion = bf16[2048,2048]{1,0:T(8,128)(2,1)S(1)} fusion(bf16[64,2048]{1,0:T(8,128)(2,1)S(1)} %broadcast_select_fusion, f32[2048]{0:T(1024)S(1)} %multiply_reduce_fusion.3, f32[2048]{0:T(1024)S(1)} %multiply_reduce_fusion.4, bf16[1,64,2048]{2,1,0:T(8,128)(2,1)S(1)} %all-gather), kind=kOutput, calls=%fused_computation.3 | convolution fusion | flops 557842432 | bytes 8929280 | tf_op jit(solution)/shard_map/dot_general | solution.py:19
  61.4 1.3 fusion.22
  63.0 0.7 collective-permute-start.7
  63.7 1.3 fusion.23
  65.3 0.8 collective-permute-start.8
  66.2 1.3 fusion.24
  67.8 1.3 collective-permute-start.9
  69.2 18.3 %collective-permute-done.9 = bf16[16,2048]{1,0:T(8,128)(2,1)S(1)} collective-permute-done((bf16[16,2048]{1,0:T(8,128)(2,1)S(1)}, bf16[16,2048]{1,0:T(8,128)(2,1)S(1)}, u32[]{:S(2)}, u32[]{:S(2)}) %collective-permute-start.9) | collective-permute-done | bytes 65568 | tf_op jit(solution)/shard_map/ppermute | solution.py:76
  87.4 1.3 fusion.25
  88.8 0.8 select_select_fusion
  91.7 13.5 %all-gather.3.cloned.1.call-done = f32[2,64,2048]{2,1,0:T(8,128)} async-done(((f32[2,16,2048]{2,1,0:T(8,128)}), f32[2,64,2048]{2,1,0:T(8,128)}) %all-gather.3.cloned.1.call-update) | async-done | bytes 1048592 | tf_op jit(solution)/shard_map/all_gather | solution.py:80
  105.2 1.3 fusion.1
  107.1 4.3 %multiply_reduce_fusion.1 = (f32[2048]{0:T(1024)S(1)}, f32[2048,2048]{1,0:T(8,128)S(1)}) fusion(f32[2048]{0:T(1024)S(1)} %get-tuple-element.12, f32[2048]{0:T(1024)S(1)} %multiply_reduce_fusion.2, f32[2048]{0:T(1024)S(1)} %multiply_reduce_fusion.4, bf16[1,64,2048]{2,1,0:T(8,128)(2,1)S(1)} %copy-done, bf16[1,64,2048]{2,1,0:T(8,128)(2,1)S(1)} %all-gather), kind=kOutput, calls=%fused_computation.1 | convolution fusion | flops 562034688 | bytes 17334272 | tf_op jit(solution)/shard_map/dot_general | solution.py:19
  112.0 5.0 %multiply_reduce_fusion = f32[2048]{0:T(1024)S(1)} fusion(f32[2048,2048]{1,0:T(8,128)S(1)} %get-tuple-element.30, f32[2048]{0:T(1024)S(1)} %select_divide_fusion, f32[2048]{0:T(1024)S(1)} %multiply_reduce_fusion.2, f32[2048]{0:T(1024)S(1)} %multiply_reduce_fusion.4), kind=kLoop, calls=%fused_computation | loop fusion | flops 25163776 | bytes 16809984 | tf_op jit(solution)/shard_map/reduce_sum | solution.py:98
  117.0 6.0 %all-reduce = f32[2048]{0:T(1024)S(1)} all-reduce(f32[2048]{0:T(1024)S(1)} %multiply_reduce_fusion), channel_id=3, replica_groups=mesh['day'=8,'pt'=4] {'pt'}, use_global_device_ids=true, to_apply=%region_15.16.clone | all-reduce | flops 2048 | bytes 16384
  123.7 1.7 %constant_dynamic-slice_fusion.1 = (f32[1,64,512]{2,1,0:T(8,128)}, f32[1,64,512]{2,1,0:T(8,128)}) fusion(f32[2,64,2048]{2,1,0:T(8,128)} %all-gather.3.cloned.1.call-done, s32[]{:T(128)S(6)} %add.77, s32[]{:T(128)S(6)} %select_n.133), kind=kLoop, calls=%fused_computation.71 | loop fusion | bytes 524296 | tf_op jit(solution)/shard_map/slice | solution.py:84
  (54 shorter events, 4.9 us)
Async XLA Ops:
  7.2 98.0 %all-gather.3.cloned.1.call-start = ((), (), s32[]{:S(2)}) async-start(), calls=%async_computation | async-start | bytes 1310720 | tf_op jit(solution)/shard_map/all_gather | solution.py:80
  17.5 20.7 %collective-permute-start = (bf16[16,2048]{1,0:T(8,128)(2,1)S(1)}, bf16[16,2048]{1,0:T(8,128)(2,1)S(1)}, u32[]{:S(2)}, u32[]{:S(2)}) collective-permute-start(bf16[16,2048]{1,0:T(8,128)(2,1)S(1)} %fusion.11), channel_id=1, source_target_pairs={{0,4},{28,24},{1,5},{29,25},{2,6},{30,26},{3,7},{31,27}} | collective-permute-start | bytes 196616 | tf_op jit(solution)/shard_map/ppermute | solution.py:76
  26.9 7.6 %collective-permute-start.1 = (bf16[64,2048]{1,0:T(8,128)(2,1)S(1)}, bf16[64,2048]{1,0:T(8,128)(2,1)S(1)}, u32[]{:S(2)}, u32[]{:S(2)}) collective-permute-start(bf16[64,2048]{1,0:T(8,128)(2,1)S(1)} %bitcast.78), channel_id=1, source_target_pairs={{0,4},{4,8},{8,12},{20,16},{24,20},{28,24},{1,5},{5,9},{9,13},{21,... | collective-permute-start | bytes 786440 | tf_op jit(solution)/shard_map/ppermute | solution.py:51
  39.8 0.8 collective-permute-start.4
  42.1 2.7 %collective-permute-start.5 = (bf16[16,2048]{1,0:T(8,128)(2,1)S(1)}, bf16[16,2048]{1,0:T(8,128)(2,1)S(1)}, u32[]{:S(2)}, u32[]{:S(2)}) collective-permute-start(bf16[16,2048]{1,0:T(8,128)(2,1)S(1)} %fusion.9), channel_id=1, source_target_pairs={{8,12},{20,16},{9,13},{21,17},{10,14},{22,18},{11,15},{23,19}} | collective-permute-start | bytes 196616 | tf_op jit(solution)/shard_map/ppermute | solution.py:76
  42.8 14.1 %collective-permute-start.2 = (bf16[64,2048]{1,0:T(8,128)(2,1)S(1)}, bf16[64,2048]{1,0:T(8,128)(2,1)S(1)}, u32[]{:S(2)}, u32[]{:S(2)}) collective-permute-start(bf16[64,2048]{1,0:T(8,128)(2,1)S(1)} %bitcast.79), channel_id=1, source_target_pairs={{4,0},{8,4},{12,8},{16,12},{5,1},{9,5},{13,9},{17,13},{6,2},{10,6}... | collective-permute-start | bytes 786440 | tf_op jit(solution)/shard_map/ppermute | solution.py:64
  44.1 12.8 %collective-permute-start.3 = (bf16[64,2048]{1,0:T(8,128)(2,1)S(1)}, bf16[64,2048]{1,0:T(8,128)(2,1)S(1)}, u32[]{:S(2)}, u32[]{:S(2)}) collective-permute-start(bf16[64,2048]{1,0:T(8,128)(2,1)S(1)} %bitcast.80), channel_id=1, source_target_pairs={{12,16},{16,20},{20,24},{24,28},{13,17},{17,21},{21,25},{25,29},{1... | collective-permute-start | bytes 786440 | tf_op jit(solution)/shard_map/ppermute | solution.py:65
  57.1 4.4 %collective-permute-start.6 = (bf16[16,2048]{1,0:T(8,128)(2,1)S(1)}, bf16[16,2048]{1,0:T(8,128)(2,1)S(1)}, u32[]{:S(2)}, u32[]{:S(2)}) collective-permute-start(bf16[16,2048]{1,0:T(8,128)(2,1)S(1)} %fusion.8), channel_id=1, source_target_pairs={{12,16},{16,12},{13,17},{17,13},{14,18},{18,14},{15,19},{19,15}} | collective-permute-start | bytes 196616 | tf_op jit(solution)/shard_map/ppermute | solution.py:76
  62.7 27.6 %copy-start.1 = (u32[32]{0:T(128)S(1)}, u32[32]{0:T(128)}, u32[]{:S(2)}) copy-start(u32[32]{0:T(128)} %constant.47) | copy-start | bytes 388
  62.7 28.9 %copy-start = (bf16[1,64,2048]{2,1,0:T(8,128)(2,1)S(1)}, bf16[1,64,2048]{2,1,0:T(8,128)(2,1)}, u32[]{:S(2)}) copy-start(bf16[1,64,2048]{2,1,0:T(8,128)(2,1)} %param.7) | copy-start | bytes 786436
  63.0 0.8 collective-permute-start.7
  65.3 0.9 collective-permute-start.8
  67.8 19.7 %collective-permute-start.9 = (bf16[16,2048]{1,0:T(8,128)(2,1)S(1)}, bf16[16,2048]{1,0:T(8,128)(2,1)S(1)}, u32[]{:S(2)}, u32[]{:S(2)}) collective-permute-start(bf16[16,2048]{1,0:T(8,128)(2,1)S(1)} %fusion.5), channel_id=1, source_target_pairs={{24,28},{4,0},{25,29},{5,1},{26,30},{6,2},{27,31},{7,3}} | collective-permute-start | bytes 196616 | tf_op jit(solution)/shard_map/ppermute | solution.py:76
Sparse Core Ops, SparseCore 0:
  89.8 15.3 all-gather.2

commit v6 on v4

--- a/solution.py
+++ b/solution.py
@@ -8,6 +8,20 @@
     devices = range(lax.axis_size(axis))
     route = [(i - distance, i) for i in devices if i - distance in devices]
     return lax.ppermute(block, axis, route)
+
+
+def swap_blocks(x, take_axis, put_axis, put_shape):
+    count = lax.axis_size("pt")
+    rank = lax.axis_index("pt")
+    take = x.shape[take_axis] // count
+    put = put_shape[put_axis] // count
+    out = jnp.zeros(put_shape, x.dtype)
+    for shift in range(count):
+        piece = lax.dynamic_slice_in_dim(x, ((rank + shift) % count) * take, take, take_axis)
+        if shift:
+            piece = lax.ppermute(piece, "pt", [(i, (i + shift) % count) for i in range(count)])
+        out = lax.dynamic_update_slice_in_dim(out, piece, ((rank - shift) % count) * put, put_axis)
+    return out
 
 
 def norm_of(coords):
@@ -31,8 +45,8 @@
     day_pts = lax.all_gather(own_pts, "pt", axis=1, tiled=True)
     support_total = day_pts.shape[1]
     own_weight = clone_weight[0] * potential[0][None, :]
-    block_weight = lax.all_to_all(own_weight, "pt", 0, 1, tiled=True)
-    block_rows = block_weight.shape[0]
+    block_rows = own_weight.shape[0] // lax.axis_size("pt")
+    block_weight = swap_blocks(own_weight, 0, 1, (block_rows, day_pts.shape[1]))
     live_total = support_count[0].astype(jnp.float32)
     live_all = (jnp.arange(support_total, dtype=jnp.int32) < support_count[0]).astype(jnp.float32)
     live_own = lax.dynamic_slice_in_dim(live_all, pt_rank * per_device, per_device)
@@ -78,7 +92,7 @@
         rows = jnp.where(keep[:, None, None], fresh[None], rows)
     forward_rows = rows[0]
     backward_rows = rows[1]
-    both_out = lax.all_to_all(rows, "pt", 2, 1, tiled=True)
+    both_out = swap_blocks(rows, 2, 1, (2, own_weight.shape[0], per_device))
     forward_out = both_out[0]
     backward_out = both_out[1]
     mass_part = jnp.sum(forward_rows * block_weight * backward_rows, axis=0)

time: 119 us -> 104 us (0.87)
  local copies, waits for them, and re-layouts: 11.6 us -> 2.2 us
  other arithmetic: 13.2 us -> 11.1 us
  blocking collectives: 20.3 us -> 18.4 us
  starting transfers between devices: 21.8 us -> 20.1 us
    all_to_all x2 -> x0, starting transfers between devices: 7.67 us -> none  [the longest x1 4.26 us: shards(): block_weight = lax.all_to_all(own_weight, 'pt', 0, 1, tiled=True)]
    ppermute x0 -> x6, starting transfers between devices: none -> 6.53 us  [swap_blocks(): lax.ppermute(piece, 'pt', [(i, (i + shift) % count) for i in range(count)])]
    unnamed x5 -> x3, local copies, waits for them, and re-layouts: 7.72 us -> 1.33 us
    all_to_all x2 -> x0, local copies, waits for them, and re-layouts: 1.39 us -> none  [shards(): both_out = lax.all_to_all(rows, 'pt', 2, 1, tiled=True)]
    all_to_all x1 -> x0, other arithmetic: 1.37 us -> none  [shards(): both_out = lax.all_to_all(rows, 'pt', 2, 1, tiled=True)]
    unnamed x1, blocking collectives: 7.69 us -> 6.5 us
  transfers between devices with their start and end apart: 12 -> 16, of which waited for: 2 -> 2; matrix products, arithmetic and copies ran while one was open for 19% -> 22% of each run, Pallas kernels for 0% -> 0%
where the time goes in v6:
time: 104 us; the launch traced here: 103 us
  waiting for transfers between devices  27.6 us (27%)
  matrix products  20.6 us (20%)
  starting transfers between devices  20.1 us (19%)
  blocking collectives  18.4 us (18%)
  other arithmetic  11.1 us (11%)
  between operations  3.3 us (3%)
  local copies, waits for them, and re-layouts  2.2 us (2%)
    ppermute x7, waiting for transfers between devices, shards(): incoming = lax.ppermute(outgoing, 'day', route)  18.3 us
    dot_general x3, matrix products, squared_dist(): lax.dot_general(left_pts, right_pts, (((0,), (0,)), ((), ())), preferred_...  11.5 us
    ppermute x1, waiting for transfers between devices, shards(): lax.ppermute(later_pts, 'day', [(d + 1, d) for d in range(half)])  9.27 us
    dot_general x7, matrix products, shards(): jnp.dot(incoming, kernel, preferred_element_type=jnp.float32)  9.15 us
    ppermute x7, starting transfers between devices, shards(): incoming = lax.ppermute(outgoing, 'day', route)  8.24 us
    ppermute x6, starting transfers between devices, swap_blocks(): lax.ppermute(piece, 'pt', [(i, (i + shift) % count) for i in range(count)])  6.53 us
    unnamed x1, blocking collectives  6.5 us
    psum x1, blocking collectives, shards(): full_mass = live_all * lax.psum(mass_part, 'pt')  5.97 us
  transfers between devices with their start and end apart: 16, of which 2 were waited for; matrix products, arithmetic and copies ran while one was open for 22% of the time, Pallas kernels for 0%

profile of v6, /device:TPU:0, one launch (start us, length us, event | category | flops | bytes accessed | tf_op | source)
XLA Modules:
  0.0 103.4 jit_solution(11661411998159053765)
XLA Ops:
  0.7 0.9 bitcast_multiply_fusion
  2.2 2.6 %collective-permute-start.1 = (f32[16,512]{1,0:T(8,128)S(1)}, f32[16,512]{1,0:T(8,128)S(1)}, u32[]{:S(2)}, u32[]{:S(2)}) collective-permute-start(f32[16,512]{1,0:T(8,128)S(1)} %get-tuple-element.20), channel_id=1, source_target_pairs={{0,2},{1,3},{2,0},{3,1},{4,6},{5,7},{6,4},{7,5},{8,10},{9,11},{10,... | collective-permute-start | bytes 98312 | tf_op jit(solution)/shard_map/ppermute | solution.py:22
  4.8 1.4 %collective-permute-start.2 = (f32[16,512]{1,0:T(8,128)S(1)}, f32[16,512]{1,0:T(8,128)S(1)}, u32[]{:S(2)}, u32[]{:S(2)}) collective-permute-start(f32[16,512]{1,0:T(8,128)S(1)} %get-tuple-element.19), channel_id=1, source_target_pairs={{0,3},{1,0},{2,1},{3,2},{4,7},{5,4},{6,5},{7,6},{8,11},{9,8},{10,9... | collective-permute-start | bytes 98312 | tf_op jit(solution)/shard_map/ppermute | solution.py:22
  6.2 6.0 %all-gather = bf16[1,64,2048]{2,1,0:T(8,128)(2,1)S(1)} all-gather(bf16[1,64,512]{2,1,0:T(8,128)(2,1)} %param.6), channel_id=2, replica_groups=mesh['day'=8,'pt'=4] {'pt'}, dimensions={2}, use_global_device_ids=true | all-gather | bytes 327680 | tf_op jit(solution)/shard_map/all_gather | solution.py:45
  12.2 3.4 %collective-permute-start.4 = (bf16[64,2048]{1,0:T(8,128)(2,1)S(1)}, bf16[64,2048]{1,0:T(8,128)(2,1)S(1)}, u32[]{:S(2)}, u32[]{:S(2)}) collective-permute-start(bf16[64,2048]{1,0:T(8,128)(2,1)S(1)} %bitcast.78), channel_id=1, source_target_pairs={{0,4},{4,8},{8,12},{20,16},{24,20},{28,24},{1,5},{5,9},{9,13},{21,... | collective-permute-start | bytes 786440 | tf_op jit(solution)/shard_map/ppermute | solution.py:64
  16.3 1.0 multiply_reduce_fusion.2
  18.2 1.3 %dynamic-slice = u32[1]{0:T(128)} dynamic-slice(u32[32]{0:T(128)} %constant.106, u32[]{:T(128)S(6)} %add.180), dynamic_slice_sizes={1} | dynamic-slice | bytes 12
  20.4 3.4 %collective-permute-start.3 = (bf16[16,2048]{1,0:T(8,128)(2,1)S(1)}, bf16[16,2048]{1,0:T(8,128)(2,1)S(1)}, u32[]{:S(2)}, u32[]{:S(2)}) collective-permute-start(bf16[16,2048]{1,0:T(8,128)(2,1)S(1)} %fusion.11), channel_id=1, source_target_pairs={{0,4},{28,24},{1,5},{29,25},{2,6},{30,26},{3,7},{31,27}} | collective-permute-start | bytes 196616 | tf_op jit(solution)/shard_map/ppermute | solution.py:89
  23.9 3.6 %exponential_convert_fusion.1 = bf16[2048,2048]{1,0:T(8,128)(2,1)S(1)} fusion(bf16[64,2048]{1,0:T(8,128)(2,1)S(1)} %collective-permute-done.4, f32[2048]{0:T(1024)S(1)} %multiply_reduce_fusion.4, f32[2048]{0:T(1024)S(1)} %multiply_reduce_fusion.5, bf16[1,64,2048]{2,1,0:T(8,128)(2,1)S(1)} %all-gather), kind=kOutput, calls=%fused_computation.4 | convolution fusion | flops 557842432 | bytes 8929280 | tf_op jit(solution)/shard_map/dot_general | solution.py:33
  27.5 1.3 %fusion.20 = (f32[16]{0:T(128)S(1)}, f32[16,2048]{1,0:T(8,128)S(1)}) fusion(f32[2048]{0:T(1024)S(1)} %fusion.13, bf16[16,2048]{1,0:T(8,128)(2,1)S(1)} %collective-permute-done.3, bf16[2048,2048]{1,0:T(8,128)(2,1)S(1)} %exponential_convert_fusion.1), kind=kOutput, calls=%fused_computation.89 | convolution fusion | flops 134283248 | bytes 8593472 | tf_op jit(solution)/shard_map/dot_general | solution.py:90
  29.1 0.7 collective-permute-start.7
  29.8 1.3 %fusion.21 = (f32[16]{0:T(128)S(1)}, f32[16,2048]{1,0:T(8,128)S(1)}) fusion(f32[2048]{0:T(1024)S(1)} %fusion.13, bf16[16,2048]{1,0:T(8,128)(2,1)S(1)} %collective-permute-done.7, bf16[2048,2048]{1,0:T(8,128)(2,1)S(1)} %exponential_convert_fusion.1), kind=kOutput, calls=%fused_computation.90 | convolution fusion | flops 134283248 | bytes 8593472 | tf_op jit(solution)/shard_map/dot_general | solution.py:90
  31.4 0.7 collective-permute-start.8
  32.1 1.3 %collective-permute-start.5 = (bf16[64,2048]{1,0:T(8,128)(2,1)S(1)}, bf16[64,2048]{1,0:T(8,128)(2,1)S(1)}, u32[]{:S(2)}, u32[]{:S(2)}) collective-permute-start(bf16[64,2048]{1,0:T(8,128)(2,1)S(1)} %bitcast.79), channel_id=1, source_target_pairs={{4,0},{8,4},{12,8},{16,12},{5,1},{9,5},{13,9},{17,13},{6,2},{10,6}... | collective-permute-start | bytes 786440 | tf_op jit(solution)/shard_map/ppermute | solution.py:77
  33.4 0.7 collective-permute-start.6
  34.1 1.3 %fusion.22 = (f32[16]{0:T(128)S(1)}, f32[16,2048]{1,0:T(8,128)S(1)}) fusion(f32[2048]{0:T(1024)S(1)} %fusion.13, bf16[16,2048]{1,0:T(8,128)(2,1)S(1)} %collective-permute-done.8, bf16[2048,2048]{1,0:T(8,128)(2,1)S(1)} %exponential_convert_fusion.1), kind=kOutput, calls=%fused_computation.91 | convolution fusion | flops 134283248 | bytes 8593472 | tf_op jit(solution)/shard_map/dot_general | solution.py:90
  35.6 9.3 %collective-permute-done.5 = bf16[64,2048]{1,0:T(8,128)(2,1)S(1)} collective-permute-done((bf16[64,2048]{1,0:T(8,128)(2,1)S(1)}, bf16[64,2048]{1,0:T(8,128)(2,1)S(1)}, u32[]{:S(2)}, u32[]{:S(2)}) %collective-permute-start.5) | collective-permute-done | bytes 262176 | tf_op jit(solution)/shard_map/ppermute | solution.py:77
  45.0 0.7 collective-permute-start.9
  45.7 3.6 %exponential_convert_fusion = bf16[2048,2048]{1,0:T(8,128)(2,1)S(1)} fusion(bf16[64,2048]{1,0:T(8,128)(2,1)S(1)} %broadcast_select_fusion, f32[2048]{0:T(1024)S(1)} %multiply_reduce_fusion.3, f32[2048]{0:T(1024)S(1)} %multiply_reduce_fusion.4, bf16[1,64,2048]{2,1,0:T(8,128)(2,1)S(1)} %all-gather), kind=kOutput, calls=%fused_computation.3 | convolution fusion | flops 557842432 | bytes 8929280 | tf_op jit(solution)/shard_map/dot_general | solution.py:33
  49.3 1.3 %fusion.23 = (f32[16]{0:T(128)S(1)}, f32[16,2048]{1,0:T(8,128)S(1)}) fusion(f32[2048]{0:T(1024)S(1)} %fusion.13, bf16[16,2048]{1,0:T(8,128)(2,1)S(1)} %collective-permute-done.9, bf16[2048,2048]{1,0:T(8,128)(2,1)S(1)} %exponential_convert_fusion), kind=kOutput, calls=%fused_computation.92 | convolution fusion | flops 134283248 | bytes 8593472 | tf_op jit(solution)/shard_map/dot_general | solution.py:90
  51.6 1.3 %fusion.24 = (f32[16]{0:T(128)S(1)}, f32[16,2048]{1,0:T(8,128)S(1)}) fusion(f32[2048]{0:T(1024)S(1)} %fusion.13, bf16[16,2048]{1,0:T(8,128)(2,1)S(1)} %collective-permute-done.10, bf16[2048,2048]{1,0:T(8,128)(2,1)S(1)} %exponential_convert_fusion), kind=kOutput, calls=%fused_computation.93 | convolution fusion | flops 134283248 | bytes 8593472 | tf_op jit(solution)/shard_map/dot_general | solution.py:90
  53.2 0.8 collective-permute-start.11
  54.1 1.3 %fusion.25 = (f32[16]{0:T(128)S(1)}, f32[16,2048]{1,0:T(8,128)S(1)}) fusion(f32[2048]{0:T(1024)S(1)} %fusion.13, bf16[16,2048]{1,0:T(8,128)(2,1)S(1)} %collective-permute-done.11, bf16[2048,2048]{1,0:T(8,128)(2,1)S(1)} %exponential_convert_fusion), kind=kOutput, calls=%fused_computation.94 | convolution fusion | flops 134283248 | bytes 8593472 | tf_op jit(solution)/shard_map/dot_general | solution.py:90
  55.7 1.3 %collective-permute-start.12 = (bf16[16,2048]{1,0:T(8,128)(2,1)S(1)}, bf16[16,2048]{1,0:T(8,128)(2,1)S(1)}, u32[]{:S(2)}, u32[]{:S(2)}) collective-permute-start(bf16[16,2048]{1,0:T(8,128)(2,1)S(1)} %fusion.5), channel_id=1, source_target_pairs={{24,28},{4,0},{25,29},{5,1},{26,30},{6,2},{27,31},{7,3}} | collective-permute-start | bytes 196616 | tf_op jit(solution)/shard_map/ppermute | solution.py:89
  57.0 18.3 %collective-permute-done.12 = bf16[16,2048]{1,0:T(8,128)(2,1)S(1)} collective-permute-done((bf16[16,2048]{1,0:T(8,128)(2,1)S(1)}, bf16[16,2048]{1,0:T(8,128)(2,1)S(1)}, u32[]{:S(2)}, u32[]{:S(2)}) %collective-permute-start.12) | collective-permute-done | bytes 65568 | tf_op jit(solution)/shard_map/ppermute | solution.py:89
  75.3 1.3 %fusion.26 = (f32[16]{0:T(128)S(1)}, f32[16,2048]{1,0:T(8,128)S(1)}) fusion(f32[2048]{0:T(1024)S(1)} %fusion.13, bf16[16,2048]{1,0:T(8,128)(2,1)S(1)} %collective-permute-done.12, bf16[2048,2048]{1,0:T(8,128)(2,1)S(1)} %exponential_convert_fusion), kind=kOutput, calls=%fused_computation.95 | convolution fusion | flops 134283248 | bytes 8593472 | tf_op jit(solution)/shard_map/dot_general | solution.py:90
  77.6 1.4 %collective-permute-start.15 = (f32[2,16,512]{2,1,0:T(8,128)S(1)}, f32[2,16,512]{2,1,0:T(8,128)S(1)}, u32[]{:S(2)}, u32[]{:S(2)}) collective-permute-start(f32[2,16,512]{2,1,0:T(8,128)S(1)} %get-tuple-element.15), channel_id=1, source_target_pairs={{0,3},{1,0},{2,1},{3,2},{4,7},{5,4},{6,5},{7,6},{8,11},{9,8},{10,9... | collective-permute-start | bytes 196616 | tf_op jit(solution)/shard_map/ppermute | solution.py:22
  79.0 6.0 %psum.7 = f32[2048]{0:T(1024)S(1)} all-reduce(f32[2048]{0:T(1024)S(1)} %fusion.3), channel_id=1, replica_groups=mesh['day'=8,'pt'=4] {'pt'}, use_global_device_ids=true, to_apply=%region_12.13 | all-reduce | flops 2048 | bytes 16384 | tf_op jit(solution)/shard_map/psum | solution.py:99
  85.6 4.3 %multiply_reduce_fusion.1 = (f32[2048]{0:T(1024)S(1)}, f32[2048,2048]{1,0:T(8,128)S(1)}) fusion(f32[2048]{0:T(1024)S(1)} %get-tuple-element.12, f32[2048]{0:T(1024)S(1)} %multiply_reduce_fusion.2, f32[2048]{0:T(1024)S(1)} %multiply_reduce_fusion.4, bf16[1,64,2048]{2,1,0:T(8,128)(2,1)S(1)} %copy-done, bf16[1,64,2048]{2,1,0:T(8,128)(2,1)S(1)} %all-gather), kind=kOutput, calls=%fused_computation.1 | convolution fusion | flops 562034688 | bytes 17334272 | tf_op jit(solution)/shard_map/dot_general | solution.py:33
  90.5 4.9 %multiply_reduce_fusion = f32[2048]{0:T(1024)S(1)} fusion(f32[2048,2048]{1,0:T(8,128)S(1)} %get-tuple-element.38, f32[2048]{0:T(1024)S(1)} %select_divide_fusion, f32[2048]{0:T(1024)S(1)} %multiply_reduce_fusion.2, f32[2048]{0:T(1024)S(1)} %multiply_reduce_fusion.4), kind=kLoop, calls=%fused_computation | loop fusion | flops 25163776 | bytes 16809984 | tf_op jit(solution)/shard_map/reduce_sum | solution.py:113
  95.4 6.5 %all-reduce = f32[2048]{0:T(1024)S(1)} all-reduce(f32[2048]{0:T(1024)S(1)} %multiply_reduce_fusion), channel_id=3, replica_groups=mesh['day'=8,'pt'=4] {'pt'}, use_global_device_ids=true, to_apply=%region_16.17.clone | all-reduce | flops 2048 | bytes 16384
  102.7 0.7 fusion.19
  (70 shorter events, 6.3 us)
Async XLA Ops:
  1.7 18.6 %collective-permute-start = (f32[16,512]{1,0:T(8,128)S(1)}, f32[16,512]{1,0:T(8,128)S(1)}, u32[]{:S(2)}, u32[]{:S(2)}) collective-permute-start(f32[16,512]{1,0:T(8,128)S(1)} %get-tuple-element.21), channel_id=1, source_target_pairs={{0,1},{1,2},{2,3},{3,0},{4,5},{5,6},{6,7},{7,4},{8,9},{9,10},{10,1... | collective-permute-start | bytes 98312 | tf_op jit(solution)/shard_map/ppermute | solution.py:22
  2.2 18.0 %collective-permute-start.1 = (f32[16,512]{1,0:T(8,128)S(1)}, f32[16,512]{1,0:T(8,128)S(1)}, u32[]{:S(2)}, u32[]{:S(2)}) collective-permute-start(f32[16,512]{1,0:T(8,128)S(1)} %get-tuple-element.20), channel_id=1, source_target_pairs={{0,2},{1,3},{2,0},{3,1},{4,6},{5,7},{6,4},{7,5},{8,10},{9,11},{10,... | collective-permute-start | bytes 98312 | tf_op jit(solution)/shard_map/ppermute | solution.py:22
  4.8 15.5 %collective-permute-start.2 = (f32[16,512]{1,0:T(8,128)S(1)}, f32[16,512]{1,0:T(8,128)S(1)}, u32[]{:S(2)}, u32[]{:S(2)}) collective-permute-start(f32[16,512]{1,0:T(8,128)S(1)} %get-tuple-element.19), channel_id=1, source_target_pairs={{0,3},{1,0},{2,1},{3,2},{4,7},{5,4},{6,5},{7,6},{8,11},{9,8},{10,9... | collective-permute-start | bytes 98312 | tf_op jit(solution)/shard_map/ppermute | solution.py:22
  12.2 11.6 %collective-permute-start.4 = (bf16[64,2048]{1,0:T(8,128)(2,1)S(1)}, bf16[64,2048]{1,0:T(8,128)(2,1)S(1)}, u32[]{:S(2)}, u32[]{:S(2)}) collective-permute-start(bf16[64,2048]{1,0:T(8,128)(2,1)S(1)} %bitcast.78), channel_id=1, source_target_pairs={{0,4},{4,8},{8,12},{20,16},{24,20},{28,24},{1,5},{5,9},{9,13},{21,... | collective-permute-start | bytes 786440 | tf_op jit(solution)/shard_map/ppermute | solution.py:64
  20.4 7.1 %collective-permute-start.3 = (bf16[16,2048]{1,0:T(8,128)(2,1)S(1)}, bf16[16,2048]{1,0:T(8,128)(2,1)S(1)}, u32[]{:S(2)}, u32[]{:S(2)}) collective-permute-start(bf16[16,2048]{1,0:T(8,128)(2,1)S(1)} %fusion.11), channel_id=1, source_target_pairs={{0,4},{28,24},{1,5},{29,25},{2,6},{30,26},{3,7},{31,27}} | collective-permute-start | bytes 196616 | tf_op jit(solution)/shard_map/ppermute | solution.py:89
  29.1 0.8 collective-permute-start.7
  31.4 2.7 %collective-permute-start.8 = (bf16[16,2048]{1,0:T(8,128)(2,1)S(1)}, bf16[16,2048]{1,0:T(8,128)(2,1)S(1)}, u32[]{:S(2)}, u32[]{:S(2)}) collective-permute-start(bf16[16,2048]{1,0:T(8,128)(2,1)S(1)} %fusion.9), channel_id=1, source_target_pairs={{8,12},{20,16},{9,13},{21,17},{10,14},{22,18},{11,15},{23,19}} | collective-permute-start | bytes 196616 | tf_op jit(solution)/shard_map/ppermute | solution.py:89
  32.1 12.8 %collective-permute-start.5 = (bf16[64,2048]{1,0:T(8,128)(2,1)S(1)}, bf16[64,2048]{1,0:T(8,128)(2,1)S(1)}, u32[]{:S(2)}, u32[]{:S(2)}) collective-permute-start(bf16[64,2048]{1,0:T(8,128)(2,1)S(1)} %bitcast.79), channel_id=1, source_target_pairs={{4,0},{8,4},{12,8},{16,12},{5,1},{9,5},{13,9},{17,13},{6,2},{10,6}... | collective-permute-start | bytes 786440 | tf_op jit(solution)/shard_map/ppermute | solution.py:77
  33.4 11.5 %collective-permute-start.6 = (bf16[64,2048]{1,0:T(8,128)(2,1)S(1)}, bf16[64,2048]{1,0:T(8,128)(2,1)S(1)}, u32[]{:S(2)}, u32[]{:S(2)}) collective-permute-start(bf16[64,2048]{1,0:T(8,128)(2,1)S(1)} %bitcast.80), channel_id=1, source_target_pairs={{12,16},{16,20},{20,24},{24,28},{13,17},{17,21},{21,25},{25,29},{1... | collective-permute-start | bytes 786440 | tf_op jit(solution)/shard_map/ppermute | solution.py:78
  45.0 4.4 %collective-permute-start.9 = (bf16[16,2048]{1,0:T(8,128)(2,1)S(1)}, bf16[16,2048]{1,0:T(8,128)(2,1)S(1)}, u32[]{:S(2)}, u32[]{:S(2)}) collective-permute-start(bf16[16,2048]{1,0:T(8,128)(2,1)S(1)} %fusion.8), channel_id=1, source_target_pairs={{12,16},{16,12},{13,17},{17,13},{14,18},{18,14},{15,19},{19,15}} | collective-permute-start | bytes 196616 | tf_op jit(solution)/shard_map/ppermute | solution.py:89
  50.6 34.9 %copy-start = (bf16[1,64,2048]{2,1,0:T(8,128)(2,1)S(1)}, bf16[1,64,2048]{2,1,0:T(8,128)(2,1)}, u32[]{:S(2)}) copy-start(bf16[1,64,2048]{2,1,0:T(8,128)(2,1)} %param.7) | copy-start | bytes 786436
  50.9 0.8 collective-permute-start.10
  53.2 0.9 collective-permute-start.11
  55.7 19.7 %collective-permute-start.12 = (bf16[16,2048]{1,0:T(8,128)(2,1)S(1)}, bf16[16,2048]{1,0:T(8,128)(2,1)S(1)}, u32[]{:S(2)}, u32[]{:S(2)}) collective-permute-start(bf16[16,2048]{1,0:T(8,128)(2,1)S(1)} %fusion.5), channel_id=1, source_target_pairs={{24,28},{4,0},{25,29},{5,1},{26,30},{6,2},{27,31},{7,3}} | collective-permute-start | bytes 196616 | tf_op jit(solution)/shard_map/ppermute | solution.py:89
  77.0 25.6 %collective-permute-start.13 = (f32[2,16,512]{2,1,0:T(8,128)S(1)}, f32[2,16,512]{2,1,0:T(8,128)S(1)}, u32[]{:S(2)}, u32[]{:S(2)}) collective-permute-start(f32[2,16,512]{2,1,0:T(8,128)S(1)} %get-tuple-element.17), channel_id=1, source_target_pairs={{0,1},{1,2},{2,3},{3,0},{4,5},{5,6},{6,7},{7,4},{8,9},{9,10},{10,1... | collective-permute-start | bytes 196616 | tf_op jit(solution)/shard_map/ppermute | solution.py:22
  77.0 25.6 %collective-permute-start.14 = (f32[2,16,512]{2,1,0:T(8,128)S(1)}, f32[2,16,512]{2,1,0:T(8,128)S(1)}, u32[]{:S(2)}, u32[]{:S(2)}) collective-permute-start(f32[2,16,512]{2,1,0:T(8,128)S(1)} %get-tuple-element.16), channel_id=1, source_target_pairs={{0,2},{1,3},{2,0},{3,1},{4,6},{5,7},{6,4},{7,5},{8,10},{9,11},{10,... | collective-permute-start | bytes 196616 | tf_op jit(solution)/shard_map/ppermute | solution.py:22
  77.6 25.0 %collective-permute-start.15 = (f32[2,16,512]{2,1,0:T(8,128)S(1)}, f32[2,16,512]{2,1,0:T(8,128)S(1)}, u32[]{:S(2)}, u32[]{:S(2)}) collective-permute-start(f32[2,16,512]{2,1,0:T(8,128)S(1)} %get-tuple-element.15), channel_id=1, source_target_pairs={{0,3},{1,0},{2,1},{3,2},{4,7},{5,4},{6,5},{7,6},{8,11},{9,8},{10,9... | collective-permute-start | bytes 196616 | tf_op jit(solution)/shard_map/ppermute | solution.py:22

commit v7 on v6

--- a/solution.py
+++ b/solution.py
@@ -22,6 +22,18 @@
             piece = lax.ppermute(piece, "pt", [(i, (i + shift) % count) for i in range(count)])
         out = lax.dynamic_update_slice_in_dim(out, piece, ((rank - shift) % count) * put, put_axis)
     return out
+
+
+def sum_over_pt(x):
+    count = lax.axis_size("pt")
+    every = swap_blocks(jnp.broadcast_to(x[None], (count,) + x.shape), 0, 0, (count,) + x.shape)
+    return jnp.sum(every, axis=0)
+
+
+def sum_scatter_over_pt(x):
+    count = lax.axis_size("pt")
+    every = swap_blocks(x, 0, 0, x.shape)
+    return jnp.sum(every.reshape((count, x.shape[0] // count) + x.shape[1:]), axis=0)
 
 
 def norm_of(coords):
@@ -96,7 +108,7 @@
     forward_out = both_out[0]
     backward_out = both_out[1]
     mass_part = jnp.sum(forward_rows * block_weight * backward_rows, axis=0)
-    full_mass = live_all * lax.psum(mass_part, "pt")
+    full_mass = live_all * sum_over_pt(mass_part)
     mass_total = jnp.sum(full_mass)
 
     cell_total = cell_count[0]
@@ -111,7 +123,7 @@
     )
     inverse = cell_live / density
     ratio_rows = jnp.sum(fit_kernel * inverse[None, :], axis=1)
-    summed = lax.psum_scatter(ratio_rows, "pt", scatter_dimension=0, tiled=True)
+    summed = sum_scatter_over_pt(ratio_rows)
     fit_rows_out = live_own / cell_total_f * summed
     return (forward_out[None], backward_out[None], fit_rows_out[None])
 

time: 104 us -> 100 us (0.962)
  blocking collectives: 18.4 us -> 5.97 us
  waiting for transfers between devices: 27.6 us -> 33.3 us
  starting transfers between devices: 20.1 us -> 25.1 us
    unnamed x1 -> x0, blocking collectives: 6.5 us -> none
    psum x1 -> x0, blocking collectives: 5.97 us -> none  [shards(): full_mass = live_all * lax.psum(mass_part, 'pt')]
    ppermute x6 -> x12, starting transfers between devices: 6.53 us -> 11.5 us  [swap_blocks(): lax.ppermute(piece, 'pt', [(i, (i + shift) % count) for i in range(count)])]
    ppermute x1, waiting for transfers between devices: 0.01 us -> 2.15 us  [shards(): first_kernel = chain_kernel(lax.ppermute(day_pts, 'day', first_route))]
    ppermute x6 -> x12, waiting for transfers between devices: 0.02 us -> 1.97 us  [swap_blocks(): lax.ppermute(piece, 'pt', [(i, (i + shift) % count) for i in range(count)])]
    ppermute x1, waiting for transfers between devices: 9.27 us -> 10.9 us  [shards(): lax.ppermute(later_pts, 'day', [(d + 1, d) for d in range(half)])]
    unnamed x3 -> x2, local copies, waits for them, and re-layouts: 1.33 us -> 0.01 us
    dynamic_update_slice x6 -> x13, local copies, waits for them, and re-layouts: 0.06 us -> 1.12 us  [swap_blocks(): lax.dynamic_update_slice_in_dim(out, piece, (rank - shift) % count * put,...]
  transfers between devices with their start and end apart: 16 -> 22, of which waited for: 2 -> 6; matrix products, arithmetic and copies ran while one was open for 22% -> 11% of each run, Pallas kernels for 0% -> 0%
where the time goes in v7:
time: 100 us
  waiting for transfers between devices  33.3 us (33%)
  starting transfers between devices  25.1 us (25%)
  matrix products  20.6 us (21%)
  other arithmetic  10.2 us (10%)
  blocking collectives  5.97 us (6%)
  between operations  2.68 us (3%)
  local copies, waits for them, and re-layouts  2.15 us (2%)
    ppermute x7, waiting for transfers between devices, shards(): incoming = lax.ppermute(outgoing, 'day', route)  18.3 us
    ppermute x12, starting transfers between devices, swap_blocks(): lax.ppermute(piece, 'pt', [(i, (i + shift) % count) for i in range(count)])  11.5 us
    dot_general x3, matrix products, squared_dist(): lax.dot_general(left_pts, right_pts, (((0,), (0,)), ((), ())), preferred_...  11.5 us
    ppermute x1, waiting for transfers between devices, shards(): lax.ppermute(later_pts, 'day', [(d + 1, d) for d in range(half)])  10.9 us
    dot_general x7, matrix products, shards(): jnp.dot(incoming, kernel, preferred_element_type=jnp.float32)  9.15 us
    ppermute x7, starting transfers between devices, shards(): incoming = lax.ppermute(outgoing, 'day', route)  8.24 us
    all_gather x1, blocking collectives, shards(): day_pts = lax.all_gather(own_pts, 'pt', axis=1, tiled=True)  5.97 us
    reduce_sum x1, other arithmetic, shards(): ratio_rows = jnp.sum(fit_kernel * inverse[None, :], axis=1)  4.9 us
  transfers between devices with their start and end apart: 22, of which 6 were waited for; matrix products, arithmetic and copies ran while one was open for 11% of the time, Pallas kernels for 0%

profile of v7, /device:TPU:0, one launch (start us, length us, event | category | flops | bytes accessed | tf_op | source)
XLA Modules:
  0.0 100.1 jit_solution(13250903983769557149)
XLA Ops:
  0.7 0.9 bitcast_multiply_fusion
  2.2 2.6 %collective-permute-start.1 = (f32[16,512]{1,0:T(8,128)S(1)}, f32[16,512]{1,0:T(8,128)S(1)}, u32[]{:S(2)}, u32[]{:S(2)}) collective-permute-start(f32[16,512]{1,0:T(8,128)S(1)} %get-tuple-element.20), channel_id=1, source_target_pairs={{0,2},{1,3},{2,0},{3,1},{4,6},{5,7},{6,4},{7,5},{8,10},{9,11},{10,... | collective-permute-start | bytes 98312 | tf_op jit(solution)/shard_map/ppermute | solution.py:22
  4.8 1.4 %collective-permute-start.2 = (f32[16,512]{1,0:T(8,128)S(1)}, f32[16,512]{1,0:T(8,128)S(1)}, u32[]{:S(2)}, u32[]{:S(2)}) collective-permute-start(f32[16,512]{1,0:T(8,128)S(1)} %get-tuple-element.19), channel_id=1, source_target_pairs={{0,3},{1,0},{2,1},{3,2},{4,7},{5,4},{6,5},{7,6},{8,11},{9,8},{10,9... | collective-permute-start | bytes 98312 | tf_op jit(solution)/shard_map/ppermute | solution.py:22
  6.2 6.0 %all-gather = bf16[1,64,2048]{2,1,0:T(8,128)(2,1)S(1)} all-gather(bf16[1,64,512]{2,1,0:T(8,128)(2,1)} %param.6), channel_id=2, replica_groups=mesh['day'=8,'pt'=4] {'pt'}, dimensions={2}, use_global_device_ids=true | all-gather | bytes 327680 | tf_op jit(solution)/shard_map/all_gather | solution.py:57
  12.2 3.4 %collective-permute-start.4 = (bf16[64,2048]{1,0:T(8,128)(2,1)S(1)}, bf16[64,2048]{1,0:T(8,128)(2,1)S(1)}, u32[]{:S(2)}, u32[]{:S(2)}) collective-permute-start(bf16[64,2048]{1,0:T(8,128)(2,1)S(1)} %bitcast.78), channel_id=1, source_target_pairs={{0,4},{4,8},{8,12},{20,16},{24,20},{28,24},{1,5},{5,9},{9,13},{21,... | collective-permute-start | bytes 786440 | tf_op jit(solution)/shard_map/ppermute | solution.py:76
  16.7 3.4 %collective-permute-start.3 = (bf16[16,2048]{1,0:T(8,128)(2,1)S(1)}, bf16[16,2048]{1,0:T(8,128)(2,1)S(1)}, u32[]{:S(2)}, u32[]{:S(2)}) collective-permute-start(bf16[16,2048]{1,0:T(8,128)(2,1)S(1)} %fusion.11), channel_id=1, source_target_pairs={{0,4},{28,24},{1,5},{29,25},{2,6},{30,26},{3,7},{31,27}} | collective-permute-start | bytes 196616 | tf_op jit(solution)/shard_map/ppermute | solution.py:101
  20.1 2.2 %collective-permute-done.4 = bf16[64,2048]{1,0:T(8,128)(2,1)S(1)} collective-permute-done((bf16[64,2048]{1,0:T(8,128)(2,1)S(1)}, bf16[64,2048]{1,0:T(8,128)(2,1)S(1)}, u32[]{:S(2)}, u32[]{:S(2)}) %collective-permute-start.4) | collective-permute-done | bytes 262176 | tf_op jit(solution)/shard_map/ppermute | solution.py:76
  22.3 3.6 %exponential_convert_fusion.1 = bf16[2048,2048]{1,0:T(8,128)(2,1)S(1)} fusion(bf16[64,2048]{1,0:T(8,128)(2,1)S(1)} %collective-permute-done.4, f32[2048]{0:T(1024)S(1)} %multiply_reduce_fusion.4, f32[2048]{0:T(1024)S(1)} %multiply_reduce_fusion.5, bf16[1,64,2048]{2,1,0:T(8,128)(2,1)S(1)} %all-gather), kind=kOutput, calls=%fused_computation.4 | convolution fusion | flops 557842432 | bytes 8929280 | tf_op jit(solution)/shard_map/dot_general | solution.py:45
  25.9 1.3 %fusion.21 = (f32[16]{0:T(128)S(1)}, f32[16,2048]{1,0:T(8,128)S(1)}) fusion(f32[2048]{0:T(1024)S(1)} %fusion.13, bf16[16,2048]{1,0:T(8,128)(2,1)S(1)} %collective-permute-done.3, bf16[2048,2048]{1,0:T(8,128)(2,1)S(1)} %exponential_convert_fusion.1), kind=kOutput, calls=%fused_computation.91 | convolution fusion | flops 134283248 | bytes 8593472 | tf_op jit(solution)/shard_map/dot_general | solution.py:102
  28.2 1.3 %fusion.22 = (f32[16]{0:T(128)S(1)}, f32[16,2048]{1,0:T(8,128)S(1)}) fusion(f32[2048]{0:T(1024)S(1)} %fusion.13, bf16[16,2048]{1,0:T(8,128)(2,1)S(1)} %collective-permute-done.7, bf16[2048,2048]{1,0:T(8,128)(2,1)S(1)} %exponential_convert_fusion.1), kind=kOutput, calls=%fused_computation.92 | convolution fusion | flops 134283248 | bytes 8593472 | tf_op jit(solution)/shard_map/dot_general | solution.py:102
  29.8 0.7 collective-permute-start.8
  30.5 1.3 %collective-permute-start.5 = (bf16[64,2048]{1,0:T(8,128)(2,1)S(1)}, bf16[64,2048]{1,0:T(8,128)(2,1)S(1)}, u32[]{:S(2)}, u32[]{:S(2)}) collective-permute-start(bf16[64,2048]{1,0:T(8,128)(2,1)S(1)} %bitcast.79), channel_id=1, source_target_pairs={{4,0},{8,4},{12,8},{16,12},{5,1},{9,5},{13,9},{17,13},{6,2},{10,6}... | collective-permute-start | bytes 786440 | tf_op jit(solution)/shard_map/ppermute | solution.py:89
  31.8 0.7 collective-permute-start.6
  32.5 1.3 %fusion.23 = (f32[16]{0:T(128)S(1)}, f32[16,2048]{1,0:T(8,128)S(1)}) fusion(f32[2048]{0:T(1024)S(1)} %fusion.13, bf16[16,2048]{1,0:T(8,128)(2,1)S(1)} %collective-permute-done.8, bf16[2048,2048]{1,0:T(8,128)(2,1)S(1)} %exponential_convert_fusion.1), kind=kOutput, calls=%fused_computation.93 | convolution fusion | flops 134283248 | bytes 8593472 | tf_op jit(solution)/shard_map/dot_general | solution.py:102
  34.0 10.9 %collective-permute-done.5 = bf16[64,2048]{1,0:T(8,128)(2,1)S(1)} collective-permute-done((bf16[64,2048]{1,0:T(8,128)(2,1)S(1)}, bf16[64,2048]{1,0:T(8,128)(2,1)S(1)}, u32[]{:S(2)}, u32[]{:S(2)}) %collective-permute-start.5) | collective-permute-done | bytes 262176 | tf_op jit(solution)/shard_map/ppermute | solution.py:89
  45.7 3.6 %exponential_convert_fusion = bf16[2048,2048]{1,0:T(8,128)(2,1)S(1)} fusion(bf16[64,2048]{1,0:T(8,128)(2,1)S(1)} %broadcast_select_fusion, f32[2048]{0:T(1024)S(1)} %multiply_reduce_fusion.3, f32[2048]{0:T(1024)S(1)} %multiply_reduce_fusion.4, bf16[1,64,2048]{2,1,0:T(8,128)(2,1)S(1)} %all-gather), kind=kOutput, calls=%fused_computation.3 | convolution fusion | flops 557842432 | bytes 8929280 | tf_op jit(solution)/shard_map/dot_general | solution.py:45
  49.3 1.3 %fusion.24 = (f32[16]{0:T(128)S(1)}, f32[16,2048]{1,0:T(8,128)S(1)}) fusion(f32[2048]{0:T(1024)S(1)} %fusion.13, bf16[16,2048]{1,0:T(8,128)(2,1)S(1)} %collective-permute-done.9, bf16[2048,2048]{1,0:T(8,128)(2,1)S(1)} %exponential_convert_fusion), kind=kOutput, calls=%fused_computation.94 | convolution fusion | flops 134283248 | bytes 8593472 | tf_op jit(solution)/shard_map/dot_general | solution.py:102
  51.6 1.3 %fusion.25 = (f32[16]{0:T(128)S(1)}, f32[16,2048]{1,0:T(8,128)S(1)}) fusion(f32[2048]{0:T(1024)S(1)} %fusion.13, bf16[16,2048]{1,0:T(8,128)(2,1)S(1)} %collective-permute-done.10, bf16[2048,2048]{1,0:T(8,128)(2,1)S(1)} %exponential_convert_fusion), kind=kOutput, calls=%fused_computation.95 | convolution fusion | flops 134283248 | bytes 8593472 | tf_op jit(solution)/shard_map/dot_general | solution.py:102
  53.2 0.8 collective-permute-start.11
  54.1 1.3 %fusion.26 = (f32[16]{0:T(128)S(1)}, f32[16,2048]{1,0:T(8,128)S(1)}) fusion(f32[2048]{0:T(1024)S(1)} %fusion.13, bf16[16,2048]{1,0:T(8,128)(2,1)S(1)} %collective-permute-done.11, bf16[2048,2048]{1,0:T(8,128)(2,1)S(1)} %exponential_convert_fusion), kind=kOutput, calls=%fused_computation.96 | convolution fusion | flops 134283248 | bytes 8593472 | tf_op jit(solution)/shard_map/dot_general | solution.py:102
  55.7 1.3 %collective-permute-start.12 = (bf16[16,2048]{1,0:T(8,128)(2,1)S(1)}, bf16[16,2048]{1,0:T(8,128)(2,1)S(1)}, u32[]{:S(2)}, u32[]{:S(2)}) collective-permute-start(bf16[16,2048]{1,0:T(8,128)(2,1)S(1)} %fusion.5), channel_id=1, source_target_pairs={{24,28},{4,0},{25,29},{5,1},{26,30},{6,2},{27,31},{7,3}} | collective-permute-start | bytes 196616 | tf_op jit(solution)/shard_map/ppermute | solution.py:101
  57.0 18.3 %collective-permute-done.12 = bf16[16,2048]{1,0:T(8,128)(2,1)S(1)} collective-permute-done((bf16[16,2048]{1,0:T(8,128)(2,1)S(1)}, bf16[16,2048]{1,0:T(8,128)(2,1)S(1)}, u32[]{:S(2)}, u32[]{:S(2)}) %collective-permute-start.12) | collective-permute-done | bytes 65568 | tf_op jit(solution)/shard_map/ppermute | solution.py:101
  75.3 1.3 %fusion.27 = (f32[16]{0:T(128)S(1)}, f32[16,2048]{1,0:T(8,128)S(1)}) fusion(f32[2048]{0:T(1024)S(1)} %fusion.13, bf16[16,2048]{1,0:T(8,128)(2,1)S(1)} %collective-permute-done.12, bf16[2048,2048]{1,0:T(8,128)(2,1)S(1)} %exponential_convert_fusion), kind=kOutput, calls=%fused_computation.97 | convolution fusion | flops 134283248 | bytes 8593472 | tf_op jit(solution)/shard_map/dot_general | solution.py:102
  77.5 1.4 %collective-permute-start.18 = (f32[1,2048]{1,0:T(1,128)S(1)}, f32[1,2048]{1,0:T(1,128)S(1)}, u32[]{:S(2)}, u32[]{:S(2)}) collective-permute-start(f32[1,2048]{1,0:T(1,128)S(1)} %bitcast.83), channel_id=1, source_target_pairs={{0,3},{1,0},{2,1},{3,2},{4,7},{5,4},{6,5},{7,6},{8,11},{9,8},{10,9... | collective-permute-start | bytes 24584 | tf_op jit(solution)/shard_map/ppermute | solution.py:22
  81.6 4.3 %multiply_reduce_fusion.1 = (f32[2048]{0:T(1024)S(1)}, f32[2048,2048]{1,0:T(8,128)S(1)}) fusion(f32[2048]{0:T(1024)S(1)} %get-tuple-element.12, f32[2048]{0:T(1024)S(1)} %multiply_reduce_fusion.2, f32[2048]{0:T(1024)S(1)} %multiply_reduce_fusion.4, bf16[1,64,2048]{2,1,0:T(8,128)(2,1)S(1)} %copy-done, bf16[1,64,2048]{2,1,0:T(8,128)(2,1)S(1)} %all-gather), kind=kOutput, calls=%fused_computation.1 | convolution fusion | flops 562034688 | bytes 17334272 | tf_op jit(solution)/shard_map/dot_general | solution.py:45
  86.5 4.9 %multiply_reduce_fusion = f32[2048]{0:T(1024)S(1)} fusion(f32[2048,2048]{1,0:T(8,128)S(1)} %get-tuple-element.42, f32[2048]{0:T(1024)S(1)} %select_divide_fusion, f32[2048]{0:T(1024)S(1)} %multiply_reduce_fusion.2, f32[2048]{0:T(1024)S(1)} %multiply_reduce_fusion.4), kind=kLoop, calls=%fused_computation | loop fusion | flops 25163776 | bytes 16809984 | tf_op jit(solution)/shard_map/reduce_sum | solution.py:125
  91.6 1.1 %collective-permute-start.19 = (f32[512]{0:T(512)S(1)}, f32[512]{0:T(512)S(1)}, u32[]{:S(2)}, u32[]{:S(2)}) collective-permute-start(f32[512]{0:T(512)S(1)} %get-tuple-element.25), channel_id=1, source_target_pairs={{0,1},{1,2},{2,3},{3,0},{4,5},{5,6},{6,7},{7,4},{8,9},{9,10},{10,1... | collective-permute-start | bytes 6152 | tf_op jit(solution)/shard_map/ppermute | solution.py:22
  93.2 0.9 collective-permute-start.21
  94.3 1.1 %collective-permute-start.14 = (f32[2,16,512]{2,1,0:T(8,128)S(1)}, f32[2,16,512]{2,1,0:T(8,128)S(1)}, u32[]{:S(2)}, u32[]{:S(2)}) collective-permute-start(f32[2,16,512]{2,1,0:T(8,128)S(1)} %get-tuple-element.16), channel_id=1, source_target_pairs={{0,2},{1,3},{2,0},{3,1},{4,6},{5,7},{6,4},{7,5},{8,10},{9,11},{10,... | collective-permute-start | bytes 196616 | tf_op jit(solution)/shard_map/ppermute | solution.py:22
  95.4 1.4 %collective-permute-start.15 = (f32[2,16,512]{2,1,0:T(8,128)S(1)}, f32[2,16,512]{2,1,0:T(8,128)S(1)}, u32[]{:S(2)}, u32[]{:S(2)}) collective-permute-start(f32[2,16,512]{2,1,0:T(8,128)S(1)} %get-tuple-element.15), channel_id=1, source_target_pairs={{0,3},{1,0},{2,1},{3,2},{4,7},{5,4},{6,5},{7,6},{8,11},{9,8},{10,9... | collective-permute-start | bytes 196616 | tf_op jit(solution)/shard_map/ppermute | solution.py:22
  98.1 1.2 %collective-permute-done.14 = f32[2,16,512]{2,1,0:T(8,128)S(1)} collective-permute-done((f32[2,16,512]{2,1,0:T(8,128)S(1)}, f32[2,16,512]{2,1,0:T(8,128)S(1)}, u32[]{:S(2)}, u32[]{:S(2)}) %collective-permute-start.14) | collective-permute-done | bytes 65568 | tf_op jit(solution)/shard_map/ppermute | solution.py:22
  99.3 0.7 fusion.19
  (92 shorter events, 10.3 us)
Async XLA Ops:
  1.7 14.8 %collective-permute-start = (f32[16,512]{1,0:T(8,128)S(1)}, f32[16,512]{1,0:T(8,128)S(1)}, u32[]{:S(2)}, u32[]{:S(2)}) collective-permute-start(f32[16,512]{1,0:T(8,128)S(1)} %get-tuple-element.21), channel_id=1, source_target_pairs={{0,1},{1,2},{2,3},{3,0},{4,5},{5,6},{6,7},{7,4},{8,9},{9,10},{10,1... | collective-permute-start | bytes 98312 | tf_op jit(solution)/shard_map/ppermute | solution.py:22
  2.2 14.3 %collective-permute-start.1 = (f32[16,512]{1,0:T(8,128)S(1)}, f32[16,512]{1,0:T(8,128)S(1)}, u32[]{:S(2)}, u32[]{:S(2)}) collective-permute-start(f32[16,512]{1,0:T(8,128)S(1)} %get-tuple-element.20), channel_id=1, source_target_pairs={{0,2},{1,3},{2,0},{3,1},{4,6},{5,7},{6,4},{7,5},{8,10},{9,11},{10,... | collective-permute-start | bytes 98312 | tf_op jit(solution)/shard_map/ppermute | solution.py:22
  4.8 11.8 %collective-permute-start.2 = (f32[16,512]{1,0:T(8,128)S(1)}, f32[16,512]{1,0:T(8,128)S(1)}, u32[]{:S(2)}, u32[]{:S(2)}) collective-permute-start(f32[16,512]{1,0:T(8,128)S(1)} %get-tuple-element.19), channel_id=1, source_target_pairs={{0,3},{1,0},{2,1},{3,2},{4,7},{5,4},{6,5},{7,6},{8,11},{9,8},{10,9... | collective-permute-start | bytes 98312 | tf_op jit(solution)/shard_map/ppermute | solution.py:22
  12.2 10.1 %collective-permute-start.4 = (bf16[64,2048]{1,0:T(8,128)(2,1)S(1)}, bf16[64,2048]{1,0:T(8,128)(2,1)S(1)}, u32[]{:S(2)}, u32[]{:S(2)}) collective-permute-start(bf16[64,2048]{1,0:T(8,128)(2,1)S(1)} %bitcast.78), channel_id=1, source_target_pairs={{0,4},{4,8},{8,12},{20,16},{24,20},{28,24},{1,5},{5,9},{9,13},{21,... | collective-permute-start | bytes 786440 | tf_op jit(solution)/shard_map/ppermute | solution.py:76
  16.7 9.3 %collective-permute-start.3 = (bf16[16,2048]{1,0:T(8,128)(2,1)S(1)}, bf16[16,2048]{1,0:T(8,128)(2,1)S(1)}, u32[]{:S(2)}, u32[]{:S(2)}) collective-permute-start(bf16[16,2048]{1,0:T(8,128)(2,1)S(1)} %fusion.11), channel_id=1, source_target_pairs={{0,4},{28,24},{1,5},{29,25},{2,6},{30,26},{3,7},{31,27}} | collective-permute-start | bytes 196616 | tf_op jit(solution)/shard_map/ppermute | solution.py:101
  27.5 0.8 collective-permute-start.7
  29.8 2.7 %collective-permute-start.8 = (bf16[16,2048]{1,0:T(8,128)(2,1)S(1)}, bf16[16,2048]{1,0:T(8,128)(2,1)S(1)}, u32[]{:S(2)}, u32[]{:S(2)}) collective-permute-start(bf16[16,2048]{1,0:T(8,128)(2,1)S(1)} %fusion.9), channel_id=1, source_target_pairs={{8,12},{20,16},{9,13},{21,17},{10,14},{22,18},{11,15},{23,19}} | collective-permute-start | bytes 196616 | tf_op jit(solution)/shard_map/ppermute | solution.py:101
  30.5 14.4 %collective-permute-start.5 = (bf16[64,2048]{1,0:T(8,128)(2,1)S(1)}, bf16[64,2048]{1,0:T(8,128)(2,1)S(1)}, u32[]{:S(2)}, u32[]{:S(2)}) collective-permute-start(bf16[64,2048]{1,0:T(8,128)(2,1)S(1)} %bitcast.79), channel_id=1, source_target_pairs={{4,0},{8,4},{12,8},{16,12},{5,1},{9,5},{13,9},{17,13},{6,2},{10,6}... | collective-permute-start | bytes 786440 | tf_op jit(solution)/shard_map/ppermute | solution.py:89
  31.8 13.1 %collective-permute-start.6 = (bf16[64,2048]{1,0:T(8,128)(2,1)S(1)}, bf16[64,2048]{1,0:T(8,128)(2,1)S(1)}, u32[]{:S(2)}, u32[]{:S(2)}) collective-permute-start(bf16[64,2048]{1,0:T(8,128)(2,1)S(1)} %bitcast.80), channel_id=1, source_target_pairs={{12,16},{16,20},{20,24},{24,28},{13,17},{17,21},{21,25},{25,29},{1... | collective-permute-start | bytes 786440 | tf_op jit(solution)/shard_map/ppermute | solution.py:90
  45.0 4.4 %collective-permute-start.9 = (bf16[16,2048]{1,0:T(8,128)(2,1)S(1)}, bf16[16,2048]{1,0:T(8,128)(2,1)S(1)}, u32[]{:S(2)}, u32[]{:S(2)}) collective-permute-start(bf16[16,2048]{1,0:T(8,128)(2,1)S(1)} %fusion.8), channel_id=1, source_target_pairs={{12,16},{16,12},{13,17},{17,13},{14,18},{18,14},{15,19},{19,15}} | collective-permute-start | bytes 196616 | tf_op jit(solution)/shard_map/ppermute | solution.py:101
  50.6 28.3 %copy-start = (bf16[1,64,2048]{2,1,0:T(8,128)(2,1)S(1)}, bf16[1,64,2048]{2,1,0:T(8,128)(2,1)}, u32[]{:S(2)}) copy-start(bf16[1,64,2048]{2,1,0:T(8,128)(2,1)} %param.7) | copy-start | bytes 786436
  50.9 0.8 collective-permute-start.10
  53.2 0.9 collective-permute-start.11
  55.7 19.7 %collective-permute-start.12 = (bf16[16,2048]{1,0:T(8,128)(2,1)S(1)}, bf16[16,2048]{1,0:T(8,128)(2,1)S(1)}, u32[]{:S(2)}, u32[]{:S(2)}) collective-permute-start(bf16[16,2048]{1,0:T(8,128)(2,1)S(1)} %fusion.5), channel_id=1, source_target_pairs={{24,28},{4,0},{25,29},{5,1},{26,30},{6,2},{27,31},{7,3}} | collective-permute-start | bytes 196616 | tf_op jit(solution)/shard_map/ppermute | solution.py:101
  76.9 3.1 %collective-permute-start.16 = (f32[1,2048]{1,0:T(1,128)S(1)}, f32[1,2048]{1,0:T(1,128)S(1)}, u32[]{:S(2)}, u32[]{:S(2)}) collective-permute-start(f32[1,2048]{1,0:T(1,128)S(1)} %bitcast.81), channel_id=1, source_target_pairs={{0,1},{1,2},{2,3},{3,0},{4,5},{5,6},{6,7},{7,4},{8,9},{9,10},{10,1... | collective-permute-start | bytes 24584 | tf_op jit(solution)/shard_map/ppermute | solution.py:22
  77.0 3.7 %collective-permute-start.17 = (f32[1,2048]{1,0:T(1,128)S(1)}, f32[1,2048]{1,0:T(1,128)S(1)}, u32[]{:S(2)}, u32[]{:S(2)}) collective-permute-start(f32[1,2048]{1,0:T(1,128)S(1)} %bitcast.82), channel_id=1, source_target_pairs={{0,2},{1,3},{2,0},{3,1},{4,6},{5,7},{6,4},{7,5},{8,10},{9,11},{10,... | collective-permute-start | bytes 24584 | tf_op jit(solution)/shard_map/ppermute | solution.py:22
  77.5 3.3 %collective-permute-start.18 = (f32[1,2048]{1,0:T(1,128)S(1)}, f32[1,2048]{1,0:T(1,128)S(1)}, u32[]{:S(2)}, u32[]{:S(2)}) collective-permute-start(f32[1,2048]{1,0:T(1,128)S(1)} %bitcast.83), channel_id=1, source_target_pairs={{0,3},{1,0},{2,1},{3,2},{4,7},{5,4},{6,5},{7,6},{8,11},{9,8},{10,9... | collective-permute-start | bytes 24584 | tf_op jit(solution)/shard_map/ppermute | solution.py:22
  91.6 3.7 %collective-permute-start.19 = (f32[512]{0:T(512)S(1)}, f32[512]{0:T(512)S(1)}, u32[]{:S(2)}, u32[]{:S(2)}) collective-permute-start(f32[512]{0:T(512)S(1)} %get-tuple-element.25), channel_id=1, source_target_pairs={{0,1},{1,2},{2,3},{3,0},{4,5},{5,6},{6,7},{7,4},{8,9},{9,10},{10,1... | collective-permute-start | bytes 6152 | tf_op jit(solution)/shard_map/ppermute | solution.py:22
  92.7 4.2 %collective-permute-start.20 = (f32[512]{0:T(512)S(1)}, f32[512]{0:T(512)S(1)}, u32[]{:S(2)}, u32[]{:S(2)}) collective-permute-start(f32[512]{0:T(512)S(1)} %get-tuple-element.24), channel_id=1, source_target_pairs={{0,2},{1,3},{2,0},{3,1},{4,6},{5,7},{6,4},{7,5},{8,10},{9,11},{10,... | collective-permute-start | bytes 6152 | tf_op jit(solution)/shard_map/ppermute | solution.py:22
  93.2 3.9 %collective-permute-start.21 = (f32[512]{0:T(512)S(1)}, f32[512]{0:T(512)S(1)}, u32[]{:S(2)}, u32[]{:S(2)}) collective-permute-start(f32[512]{0:T(512)S(1)} %get-tuple-element.23), channel_id=1, source_target_pairs={{0,3},{1,0},{2,1},{3,2},{4,7},{5,4},{6,5},{7,6},{8,11},{9,8},{10,9... | collective-permute-start | bytes 6152 | tf_op jit(solution)/shard_map/ppermute | solution.py:22
  94.2 3.9 %collective-permute-start.13 = (f32[2,16,512]{2,1,0:T(8,128)S(1)}, f32[2,16,512]{2,1,0:T(8,128)S(1)}, u32[]{:S(2)}, u32[]{:S(2)}) collective-permute-start(f32[2,16,512]{2,1,0:T(8,128)S(1)} %get-tuple-element.17), channel_id=1, source_target_pairs={{0,1},{1,2},{2,3},{3,0},{4,5},{5,6},{6,7},{7,4},{8,9},{9,10},{10,1... | collective-permute-start | bytes 196616 | tf_op jit(solution)/shard_map/ppermute | solution.py:22
  94.3 5.0 %collective-permute-start.14 = (f32[2,16,512]{2,1,0:T(8,128)S(1)}, f32[2,16,512]{2,1,0:T(8,128)S(1)}, u32[]{:S(2)}, u32[]{:S(2)}) collective-permute-start(f32[2,16,512]{2,1,0:T(8,128)S(1)} %get-tuple-element.16), channel_id=1, source_target_pairs={{0,2},{1,3},{2,0},{3,1},{4,6},{5,7},{6,4},{7,5},{8,10},{9,11},{10,... | collective-permute-start | bytes 196616 | tf_op jit(solution)/shard_map/ppermute | solution.py:22
  95.4 4.0 %collective-permute-start.15 = (f32[2,16,512]{2,1,0:T(8,128)S(1)}, f32[2,16,512]{2,1,0:T(8,128)S(1)}, u32[]{:S(2)}, u32[]{:S(2)}) collective-permute-start(f32[2,16,512]{2,1,0:T(8,128)S(1)} %get-tuple-element.15), channel_id=1, source_target_pairs={{0,3},{1,0},{2,1},{3,2},{4,7},{5,4},{6,5},{7,6},{8,11},{9,8},{10,9... | collective-permute-start | bytes 196616 | tf_op jit(solution)/shard_map/ppermute | solution.py:22

commit v8 on v7

--- a/solution.py
+++ b/solution.py
@@ -83,14 +83,14 @@
     later_kernel = None
     for step in range(day_count - 1):
         if step == min(1, switch_step):
-            later_pts, rows = lax.optimization_barrier((day_pts, rows))
+            later_pts = lax.optimization_barrier((day_pts, rows))[0]
             later_source = jnp.where(
                 first_forward,
                 lax.ppermute(later_pts, "day", [(d + 1, d) for d in range(half)]),
                 lax.ppermute(later_pts, "day", [(d - 1, d) for d in range(half, day_count)]),
             )
         if step == switch_step:
-            later_source, rows = lax.optimization_barrier((later_source, rows))
+            later_source = lax.optimization_barrier((later_source, rows))[0]
             later_kernel = chain_kernel(later_source)
         kernel = first_kernel if step < switch_step else later_kernel
         forward_from = step

time: 100 us -> 96 us (0.960)
  waiting for transfers between devices: 33.3 us -> 28.1 us
  blocking collectives: 5.97 us -> 7.46 us
    ppermute x1, waiting for transfers between devices: 10.9 us -> 0.01 us  [shards(): lax.ppermute(later_pts, 'day', [(d + 1, d) for d in range(half)])]
    ppermute x7, waiting for transfers between devices: 18.3 us -> 24.1 us  [shards(): incoming = lax.ppermute(outgoing, 'day', route)]
    ppermute x1, waiting for transfers between devices: 2.15 us -> 0.01 us  [shards(): first_kernel = chain_kernel(lax.ppermute(day_pts, 'day', first_route))]
    ppermute x12, waiting for transfers between devices: 1.97 us -> 3.95 us  [swap_blocks(): lax.ppermute(piece, 'pt', [(i, (i + shift) % count) for i in range(count)])]
    ppermute x12, starting transfers between devices: 11.5 us -> 9.65 us  [swap_blocks(): lax.ppermute(piece, 'pt', [(i, (i + shift) % count) for i in range(count)])]
    all_gather x1, blocking collectives: 5.97 us -> 7.46 us  [shards(): day_pts = lax.all_gather(own_pts, 'pt', axis=1, tiled=True)]
    ppermute x7, starting transfers between devices: 8.24 us -> 9.35 us  [shards(): incoming = lax.ppermute(outgoing, 'day', route)]
  transfers between devices with their start and end apart: 22 -> 22, of which waited for: 6 -> 5; matrix products, arithmetic and copies ran while one was open for 11% -> 13% of each run, Pallas kernels for 0% -> 0%
where the time goes in v8:
time: 96 us; the launch traced here: 95.6 us
  waiting for transfers between devices  28.1 us (29%)
  starting transfers between devices  24.4 us (25%)
  matrix products  20.7 us (22%)
  other arithmetic  10.2 us (11%)
  blocking collectives  7.46 us (8%)
  between operations  2.67 us (3%)
  local copies, waits for them, and re-layouts  2.18 us (2%)
    ppermute x7, waiting for transfers between devices, shards(): incoming = lax.ppermute(outgoing, 'day', route)  24.1 us
    dot_general x3, matrix products, squared_dist(): lax.dot_general(left_pts, right_pts, (((0,), (0,)), ((), ())), preferred_...  11.5 us
    ppermute x12, starting transfers between devices, swap_blocks(): lax.ppermute(piece, 'pt', [(i, (i + shift) % count) for i in range(count)])  9.65 us
    ppermute x7, starting transfers between devices, shards(): incoming = lax.ppermute(outgoing, 'day', route)  9.35 us
    dot_general x7, matrix products, shards(): jnp.dot(incoming, kernel, preferred_element_type=jnp.float32)  9.16 us
    all_gather x1, blocking collectives, shards(): day_pts = lax.all_gather(own_pts, 'pt', axis=1, tiled=True)  7.46 us
    reduce_sum x1, other arithmetic, shards(): ratio_rows = jnp.sum(fit_kernel * inverse[None, :], axis=1)  4.9 us
    ppermute x12, waiting for transfers between devices, swap_blocks(): lax.ppermute(piece, 'pt', [(i, (i + shift) % count) for i in range(count)])  3.95 us
  transfers between devices with their start and end apart: 22, of which 5 were waited for; matrix products, arithmetic and copies ran while one was open for 13% of the time, Pallas kernels for 0%

profile of v8, /device:TPU:0, one launch (start us, length us, event | category | flops | bytes accessed | tf_op | source)
XLA Modules:
  0.0 95.6 jit_solution(8012839953983855339)
XLA Ops:
  0.6 7.5 %all-gather = bf16[1,64,2048]{2,1,0:T(8,128)(2,1)S(1)} all-gather(bf16[1,64,512]{2,1,0:T(8,128)(2,1)} %param.6), channel_id=2, replica_groups=mesh['day'=8,'pt'=4] {'pt'}, dimensions={2}, use_global_device_ids=true | all-gather | bytes 327680 | tf_op jit(solution)/shard_map/all_gather | solution.py:57
  8.1 3.4 %collective-permute-start.4 = (bf16[64,2048]{1,0:T(8,128)(2,1)S(1)}, bf16[64,2048]{1,0:T(8,128)(2,1)S(1)}, u32[]{:S(2)}, u32[]{:S(2)}) collective-permute-start(bf16[64,2048]{1,0:T(8,128)(2,1)S(1)} %bitcast.78), channel_id=1, source_target_pairs={{0,4},{4,8},{8,12},{20,16},{24,20},{28,24},{1,5},{5,9},{9,13},{21,... | collective-permute-start | bytes 786440 | tf_op jit(solution)/shard_map/ppermute | solution.py:76
  11.5 1.3 %collective-permute-start.8 = (bf16[64,2048]{1,0:T(8,128)(2,1)S(1)}, bf16[64,2048]{1,0:T(8,128)(2,1)S(1)}, u32[]{:S(2)}, u32[]{:S(2)}) collective-permute-start(bf16[64,2048]{1,0:T(8,128)(2,1)S(1)} %bitcast.79), channel_id=1, source_target_pairs={{4,0},{8,4},{12,8},{16,12},{5,1},{9,5},{13,9},{17,13},{6,2},{10,6}... | collective-permute-start | bytes 786440 | tf_op jit(solution)/shard_map/ppermute | solution.py:89
  12.8 0.7 collective-permute-start.9
  13.5 0.9 bitcast_multiply_fusion
  14.7 1.5 %collective-permute-start.1 = (f32[16,512]{1,0:T(8,128)S(1)}, f32[16,512]{1,0:T(8,128)S(1)}, u32[]{:S(2)}, u32[]{:S(2)}) collective-permute-start(f32[16,512]{1,0:T(8,128)S(1)} %get-tuple-element.16), channel_id=1, source_target_pairs={{0,2},{1,3},{2,0},{3,1},{4,6},{5,7},{6,4},{7,5},{8,10},{9,11},{10,... | collective-permute-start | bytes 98312 | tf_op jit(solution)/shard_map/ppermute | solution.py:22
  17.2 0.7 collective-permute-done
  17.9 0.7 collective-permute-start.2
  18.7 1.6 %collective-permute-done.2 = f32[16,512]{1,0:T(8,128)S(1)} collective-permute-done((f32[16,512]{1,0:T(8,128)S(1)}, f32[16,512]{1,0:T(8,128)S(1)}, u32[]{:S(2)}, u32[]{:S(2)}) %collective-permute-start.2) | collective-permute-done | bytes 32800 | tf_op jit(solution)/shard_map/ppermute | solution.py:22
  20.3 4.5 %collective-permute-start.3 = (bf16[16,2048]{1,0:T(8,128)(2,1)S(1)}, bf16[16,2048]{1,0:T(8,128)(2,1)S(1)}, u32[]{:S(2)}, u32[]{:S(2)}) collective-permute-start(bf16[16,2048]{1,0:T(8,128)(2,1)S(1)} %fusion.11), channel_id=1, source_target_pairs={{0,4},{28,24},{1,5},{29,25},{2,6},{30,26},{3,7},{31,27}} | collective-permute-start | bytes 196616 | tf_op jit(solution)/shard_map/ppermute | solution.py:101
  24.9 3.6 %exponential_convert_fusion.1 = bf16[2048,2048]{1,0:T(8,128)(2,1)S(1)} fusion(bf16[64,2048]{1,0:T(8,128)(2,1)S(1)} %collective-permute-done.4, f32[2048]{0:T(1024)S(1)} %multiply_reduce_fusion.4, f32[2048]{0:T(1024)S(1)} %multiply_reduce_fusion.5, bf16[1,64,2048]{2,1,0:T(8,128)(2,1)S(1)} %all-gather), kind=kOutput, calls=%fused_computation.4 | convolution fusion | flops 557842432 | bytes 8929280 | tf_op jit(solution)/shard_map/dot_general | solution.py:45
  28.6 1.3 %fusion.21 = (f32[16]{0:T(128)S(1)}, f32[16,2048]{1,0:T(8,128)S(1)}) fusion(f32[2048]{0:T(1024)S(1)} %fusion.13, bf16[16,2048]{1,0:T(8,128)(2,1)S(1)} %collective-permute-done.3, bf16[2048,2048]{1,0:T(8,128)(2,1)S(1)} %exponential_convert_fusion.1), kind=kOutput, calls=%fused_computation.91 | convolution fusion | flops 134283248 | bytes 8593472 | tf_op jit(solution)/shard_map/dot_general | solution.py:102
  30.8 1.3 %fusion.22 = (f32[16]{0:T(128)S(1)}, f32[16,2048]{1,0:T(8,128)S(1)}) fusion(f32[2048]{0:T(1024)S(1)} %fusion.13, bf16[16,2048]{1,0:T(8,128)(2,1)S(1)} %collective-permute-done.5, bf16[2048,2048]{1,0:T(8,128)(2,1)S(1)} %exponential_convert_fusion.1), kind=kOutput, calls=%fused_computation.92 | convolution fusion | flops 134283248 | bytes 8593472 | tf_op jit(solution)/shard_map/dot_general | solution.py:102
  33.1 1.3 %fusion.23 = (f32[16]{0:T(128)S(1)}, f32[16,2048]{1,0:T(8,128)S(1)}) fusion(f32[2048]{0:T(1024)S(1)} %fusion.13, bf16[16,2048]{1,0:T(8,128)(2,1)S(1)} %collective-permute-done.6, bf16[2048,2048]{1,0:T(8,128)(2,1)S(1)} %exponential_convert_fusion.1), kind=kOutput, calls=%fused_computation.93 | convolution fusion | flops 134283248 | bytes 8593472 | tf_op jit(solution)/shard_map/dot_general | solution.py:102
  35.4 3.6 %exponential_convert_fusion = bf16[2048,2048]{1,0:T(8,128)(2,1)S(1)} fusion(bf16[64,2048]{1,0:T(8,128)(2,1)S(1)} %broadcast_select_fusion, f32[2048]{0:T(1024)S(1)} %multiply_reduce_fusion.3, f32[2048]{0:T(1024)S(1)} %multiply_reduce_fusion.4, bf16[1,64,2048]{2,1,0:T(8,128)(2,1)S(1)} %all-gather), kind=kOutput, calls=%fused_computation.3 | convolution fusion | flops 557842432 | bytes 8929280 | tf_op jit(solution)/shard_map/dot_general | solution.py:45
  39.0 1.3 %fusion.24 = (f32[16]{0:T(128)S(1)}, f32[16,2048]{1,0:T(8,128)S(1)}) fusion(f32[2048]{0:T(1024)S(1)} %fusion.13, bf16[16,2048]{1,0:T(8,128)(2,1)S(1)} %collective-permute-done.7, bf16[2048,2048]{1,0:T(8,128)(2,1)S(1)} %exponential_convert_fusion), kind=kOutput, calls=%fused_computation.94 | convolution fusion | flops 134283248 | bytes 8593472 | tf_op jit(solution)/shard_map/dot_general | solution.py:102
  41.3 1.3 %fusion.25 = (f32[16]{0:T(128)S(1)}, f32[16,2048]{1,0:T(8,128)S(1)}) fusion(f32[2048]{0:T(1024)S(1)} %fusion.13, bf16[16,2048]{1,0:T(8,128)(2,1)S(1)} %collective-permute-done.10, bf16[2048,2048]{1,0:T(8,128)(2,1)S(1)} %exponential_convert_fusion), kind=kOutput, calls=%fused_computation.95 | convolution fusion | flops 134283248 | bytes 8593472 | tf_op jit(solution)/shard_map/dot_general | solution.py:102
  42.9 0.8 collective-permute-start.11
  43.8 1.3 %fusion.26 = (f32[16]{0:T(128)S(1)}, f32[16,2048]{1,0:T(8,128)S(1)}) fusion(f32[2048]{0:T(1024)S(1)} %fusion.13, bf16[16,2048]{1,0:T(8,128)(2,1)S(1)} %collective-permute-done.11, bf16[2048,2048]{1,0:T(8,128)(2,1)S(1)} %exponential_convert_fusion), kind=kOutput, calls=%fused_computation.96 | convolution fusion | flops 134283248 | bytes 8593472 | tf_op jit(solution)/shard_map/dot_general | solution.py:102
  45.4 1.3 %collective-permute-start.12 = (bf16[16,2048]{1,0:T(8,128)(2,1)S(1)}, bf16[16,2048]{1,0:T(8,128)(2,1)S(1)}, u32[]{:S(2)}, u32[]{:S(2)}) collective-permute-start(bf16[16,2048]{1,0:T(8,128)(2,1)S(1)} %fusion.5), channel_id=1, source_target_pairs={{24,28},{4,0},{25,29},{5,1},{26,30},{6,2},{27,31},{7,3}} | collective-permute-start | bytes 196616 | tf_op jit(solution)/shard_map/ppermute | solution.py:101
  46.8 24.1 %collective-permute-done.12 = bf16[16,2048]{1,0:T(8,128)(2,1)S(1)} collective-permute-done((bf16[16,2048]{1,0:T(8,128)(2,1)S(1)}, bf16[16,2048]{1,0:T(8,128)(2,1)S(1)}, u32[]{:S(2)}, u32[]{:S(2)}) %collective-permute-start.12) | collective-permute-done | bytes 65568 | tf_op jit(solution)/shard_map/ppermute | solution.py:101
  70.8 1.3 %fusion.27 = (f32[16]{0:T(128)S(1)}, f32[16,2048]{1,0:T(8,128)S(1)}) fusion(f32[2048]{0:T(1024)S(1)} %fusion.13, bf16[16,2048]{1,0:T(8,128)(2,1)S(1)} %collective-permute-done.12, bf16[2048,2048]{1,0:T(8,128)(2,1)S(1)} %exponential_convert_fusion), kind=kOutput, calls=%fused_computation.97 | convolution fusion | flops 134283248 | bytes 8593472 | tf_op jit(solution)/shard_map/dot_general | solution.py:102
  72.5 0.8 collective-permute-start.17
  73.4 1.4 %collective-permute-start.18 = (f32[1,2048]{1,0:T(1,128)S(1)}, f32[1,2048]{1,0:T(1,128)S(1)}, u32[]{:S(2)}, u32[]{:S(2)}) collective-permute-start(f32[1,2048]{1,0:T(1,128)S(1)} %bitcast.83), channel_id=1, source_target_pairs={{0,3},{1,0},{2,1},{3,2},{4,7},{5,4},{6,5},{7,6},{8,11},{9,8},{10,9... | collective-permute-start | bytes 24584 | tf_op jit(solution)/shard_map/ppermute | solution.py:22
  77.1 4.3 %multiply_reduce_fusion.1 = (f32[2048]{0:T(1024)S(1)}, f32[2048,2048]{1,0:T(8,128)S(1)}) fusion(f32[2048]{0:T(1024)S(1)} %get-tuple-element.8, f32[2048]{0:T(1024)S(1)} %multiply_reduce_fusion.2, f32[2048]{0:T(1024)S(1)} %multiply_reduce_fusion.4, bf16[1,64,2048]{2,1,0:T(8,128)(2,1)S(1)} %copy-done, bf16[1,64,2048]{2,1,0:T(8,128)(2,1)S(1)} %all-gather), kind=kOutput, calls=%fused_computation.1 | convolution fusion | flops 562034688 | bytes 17334272 | tf_op jit(solution)/shard_map/dot_general | solution.py:45
  82.1 4.9 %multiply_reduce_fusion = f32[2048]{0:T(1024)S(1)} fusion(f32[2048,2048]{1,0:T(8,128)S(1)} %get-tuple-element.38, f32[2048]{0:T(1024)S(1)} %select_divide_fusion, f32[2048]{0:T(1024)S(1)} %multiply_reduce_fusion.2, f32[2048]{0:T(1024)S(1)} %multiply_reduce_fusion.4), kind=kLoop, calls=%fused_computation | loop fusion | flops 25163776 | bytes 16809984 | tf_op jit(solution)/shard_map/reduce_sum | solution.py:125
  87.2 1.1 %collective-permute-start.19 = (f32[512]{0:T(512)S(1)}, f32[512]{0:T(512)S(1)}, u32[]{:S(2)}, u32[]{:S(2)}) collective-permute-start(f32[512]{0:T(512)S(1)} %get-tuple-element.21), channel_id=1, source_target_pairs={{0,1},{1,2},{2,3},{3,0},{4,5},{5,6},{6,7},{7,4},{8,9},{9,10},{10,1... | collective-permute-start | bytes 6152 | tf_op jit(solution)/shard_map/ppermute | solution.py:22
  88.3 0.8 collective-permute-start.20
  89.8 1.1 %collective-permute-start.14 = (f32[2,16,512]{2,1,0:T(8,128)S(1)}, f32[2,16,512]{2,1,0:T(8,128)S(1)}, u32[]{:S(2)}, u32[]{:S(2)}) collective-permute-start(f32[2,16,512]{2,1,0:T(8,128)S(1)} %get-tuple-element.12), channel_id=1, source_target_pairs={{0,2},{1,3},{2,0},{3,1},{4,6},{5,7},{6,4},{7,5},{8,10},{9,11},{10,... | collective-permute-start | bytes 196616 | tf_op jit(solution)/shard_map/ppermute | solution.py:22
  90.9 1.4 %collective-permute-start.15 = (f32[2,16,512]{2,1,0:T(8,128)S(1)}, f32[2,16,512]{2,1,0:T(8,128)S(1)}, u32[]{:S(2)}, u32[]{:S(2)}) collective-permute-start(f32[2,16,512]{2,1,0:T(8,128)S(1)} %get-tuple-element.11), channel_id=1, source_target_pairs={{0,3},{1,0},{2,1},{3,2},{4,7},{5,4},{6,5},{7,6},{8,11},{9,8},{10,9... | collective-permute-start | bytes 196616 | tf_op jit(solution)/shard_map/ppermute | solution.py:22
  93.6 1.2 %collective-permute-done.14 = f32[2,16,512]{2,1,0:T(8,128)S(1)} collective-permute-done((f32[2,16,512]{2,1,0:T(8,128)S(1)}, f32[2,16,512]{2,1,0:T(8,128)S(1)}, u32[]{:S(2)}, u32[]{:S(2)}) %collective-permute-start.14) | collective-permute-done | bytes 65568 | tf_op jit(solution)/shard_map/ppermute | solution.py:22
  94.9 0.7 fusion.19
  (89 shorter events, 9.9 us)
Async XLA Ops:
  8.1 16.8 %collective-permute-start.4 = (bf16[64,2048]{1,0:T(8,128)(2,1)S(1)}, bf16[64,2048]{1,0:T(8,128)(2,1)S(1)}, u32[]{:S(2)}, u32[]{:S(2)}) collective-permute-start(bf16[64,2048]{1,0:T(8,128)(2,1)S(1)} %bitcast.78), channel_id=1, source_target_pairs={{0,4},{4,8},{8,12},{20,16},{24,20},{28,24},{1,5},{5,9},{9,13},{21,... | collective-permute-start | bytes 786440 | tf_op jit(solution)/shard_map/ppermute | solution.py:76
  11.5 19.3 %collective-permute-start.8 = (bf16[64,2048]{1,0:T(8,128)(2,1)S(1)}, bf16[64,2048]{1,0:T(8,128)(2,1)S(1)}, u32[]{:S(2)}, u32[]{:S(2)}) collective-permute-start(bf16[64,2048]{1,0:T(8,128)(2,1)S(1)} %bitcast.79), channel_id=1, source_target_pairs={{4,0},{8,4},{12,8},{16,12},{5,1},{9,5},{13,9},{17,13},{6,2},{10,6}... | collective-permute-start | bytes 786440 | tf_op jit(solution)/shard_map/ppermute | solution.py:89
  12.8 18.0 %collective-permute-start.9 = (bf16[64,2048]{1,0:T(8,128)(2,1)S(1)}, bf16[64,2048]{1,0:T(8,128)(2,1)S(1)}, u32[]{:S(2)}, u32[]{:S(2)}) collective-permute-start(bf16[64,2048]{1,0:T(8,128)(2,1)S(1)} %bitcast.80), channel_id=1, source_target_pairs={{12,16},{16,20},{20,24},{24,28},{13,17},{17,21},{21,25},{25,29},{1... | collective-permute-start | bytes 786440 | tf_op jit(solution)/shard_map/ppermute | solution.py:90
  14.6 3.4 %collective-permute-start = (f32[16,512]{1,0:T(8,128)S(1)}, f32[16,512]{1,0:T(8,128)S(1)}, u32[]{:S(2)}, u32[]{:S(2)}) collective-permute-start(f32[16,512]{1,0:T(8,128)S(1)} %get-tuple-element.17), channel_id=1, source_target_pairs={{0,1},{1,2},{2,3},{3,0},{4,5},{5,6},{6,7},{7,4},{8,9},{9,10},{10,1... | collective-permute-start | bytes 98312 | tf_op jit(solution)/shard_map/ppermute | solution.py:22
  14.7 4.0 %collective-permute-start.1 = (f32[16,512]{1,0:T(8,128)S(1)}, f32[16,512]{1,0:T(8,128)S(1)}, u32[]{:S(2)}, u32[]{:S(2)}) collective-permute-start(f32[16,512]{1,0:T(8,128)S(1)} %get-tuple-element.16), channel_id=1, source_target_pairs={{0,2},{1,3},{2,0},{3,1},{4,6},{5,7},{6,4},{7,5},{8,10},{9,11},{10,... | collective-permute-start | bytes 98312 | tf_op jit(solution)/shard_map/ppermute | solution.py:22
  17.9 2.3 %collective-permute-start.2 = (f32[16,512]{1,0:T(8,128)S(1)}, f32[16,512]{1,0:T(8,128)S(1)}, u32[]{:S(2)}, u32[]{:S(2)}) collective-permute-start(f32[16,512]{1,0:T(8,128)S(1)} %get-tuple-element.15), channel_id=1, source_target_pairs={{0,3},{1,0},{2,1},{3,2},{4,7},{5,4},{6,5},{7,6},{8,11},{9,8},{10,9... | collective-permute-start | bytes 98312 | tf_op jit(solution)/shard_map/ppermute | solution.py:22
  20.3 8.3 %collective-permute-start.3 = (bf16[16,2048]{1,0:T(8,128)(2,1)S(1)}, bf16[16,2048]{1,0:T(8,128)(2,1)S(1)}, u32[]{:S(2)}, u32[]{:S(2)}) collective-permute-start(bf16[16,2048]{1,0:T(8,128)(2,1)S(1)} %fusion.11), channel_id=1, source_target_pairs={{0,4},{28,24},{1,5},{29,25},{2,6},{30,26},{3,7},{31,27}} | collective-permute-start | bytes 196616 | tf_op jit(solution)/shard_map/ppermute | solution.py:101
  30.1 0.7 collective-permute-start.5
  32.4 0.8 collective-permute-start.6
  34.7 4.3 %collective-permute-start.7 = (bf16[16,2048]{1,0:T(8,128)(2,1)S(1)}, bf16[16,2048]{1,0:T(8,128)(2,1)S(1)}, u32[]{:S(2)}, u32[]{:S(2)}) collective-permute-start(bf16[16,2048]{1,0:T(8,128)(2,1)S(1)} %fusion.8), channel_id=1, source_target_pairs={{12,16},{16,12},{13,17},{17,13},{14,18},{18,14},{15,19},{19,15}} | collective-permute-start | bytes 196616 | tf_op jit(solution)/shard_map/ppermute | solution.py:101
  40.3 34.4 %copy-start = (bf16[1,64,2048]{2,1,0:T(8,128)(2,1)S(1)}, bf16[1,64,2048]{2,1,0:T(8,128)(2,1)}, u32[]{:S(2)}) copy-start(bf16[1,64,2048]{2,1,0:T(8,128)(2,1)} %param.7) | copy-start | bytes 786436
  40.5 0.8 collective-permute-start.10
  42.9 0.9 collective-permute-start.11
  45.4 25.5 %collective-permute-start.12 = (bf16[16,2048]{1,0:T(8,128)(2,1)S(1)}, bf16[16,2048]{1,0:T(8,128)(2,1)S(1)}, u32[]{:S(2)}, u32[]{:S(2)}) collective-permute-start(bf16[16,2048]{1,0:T(8,128)(2,1)S(1)} %fusion.5), channel_id=1, source_target_pairs={{24,28},{4,0},{25,29},{5,1},{26,30},{6,2},{27,31},{7,3}} | collective-permute-start | bytes 196616 | tf_op jit(solution)/shard_map/ppermute | solution.py:101
  72.5 3.2 %collective-permute-start.16 = (f32[1,2048]{1,0:T(1,128)S(1)}, f32[1,2048]{1,0:T(1,128)S(1)}, u32[]{:S(2)}, u32[]{:S(2)}) collective-permute-start(f32[1,2048]{1,0:T(1,128)S(1)} %bitcast.81), channel_id=1, source_target_pairs={{0,1},{1,2},{2,3},{3,0},{4,5},{5,6},{6,7},{7,4},{8,9},{9,10},{10,1... | collective-permute-start | bytes 24584 | tf_op jit(solution)/shard_map/ppermute | solution.py:22
  72.5 3.7 %collective-permute-start.17 = (f32[1,2048]{1,0:T(1,128)S(1)}, f32[1,2048]{1,0:T(1,128)S(1)}, u32[]{:S(2)}, u32[]{:S(2)}) collective-permute-start(f32[1,2048]{1,0:T(1,128)S(1)} %bitcast.82), channel_id=1, source_target_pairs={{0,2},{1,3},{2,0},{3,1},{4,6},{5,7},{6,4},{7,5},{8,10},{9,11},{10,... | collective-permute-start | bytes 24584 | tf_op jit(solution)/shard_map/ppermute | solution.py:22
  73.4 3.0 %collective-permute-start.18 = (f32[1,2048]{1,0:T(1,128)S(1)}, f32[1,2048]{1,0:T(1,128)S(1)}, u32[]{:S(2)}, u32[]{:S(2)}) collective-permute-start(f32[1,2048]{1,0:T(1,128)S(1)} %bitcast.83), channel_id=1, source_target_pairs={{0,3},{1,0},{2,1},{3,2},{4,7},{5,4},{6,5},{7,6},{8,11},{9,8},{10,9... | collective-permute-start | bytes 24584 | tf_op jit(solution)/shard_map/ppermute | solution.py:22
  87.2 3.7 %collective-permute-start.19 = (f32[512]{0:T(512)S(1)}, f32[512]{0:T(512)S(1)}, u32[]{:S(2)}, u32[]{:S(2)}) collective-permute-start(f32[512]{0:T(512)S(1)} %get-tuple-element.21), channel_id=1, source_target_pairs={{0,1},{1,2},{2,3},{3,0},{4,5},{5,6},{6,7},{7,4},{8,9},{9,10},{10,1... | collective-permute-start | bytes 6152 | tf_op jit(solution)/shard_map/ppermute | solution.py:22
  88.3 4.2 %collective-permute-start.20 = (f32[512]{0:T(512)S(1)}, f32[512]{0:T(512)S(1)}, u32[]{:S(2)}, u32[]{:S(2)}) collective-permute-start(f32[512]{0:T(512)S(1)} %get-tuple-element.20), channel_id=1, source_target_pairs={{0,2},{1,3},{2,0},{3,1},{4,6},{5,7},{6,4},{7,5},{8,10},{9,11},{10,... | collective-permute-start | bytes 6152 | tf_op jit(solution)/shard_map/ppermute | solution.py:22
  89.0 3.7 %collective-permute-start.21 = (f32[512]{0:T(512)S(1)}, f32[512]{0:T(512)S(1)}, u32[]{:S(2)}, u32[]{:S(2)}) collective-permute-start(f32[512]{0:T(512)S(1)} %get-tuple-element.19), channel_id=1, source_target_pairs={{0,3},{1,0},{2,1},{3,2},{4,7},{5,4},{6,5},{7,6},{8,11},{9,8},{10,9... | collective-permute-start | bytes 6152 | tf_op jit(solution)/shard_map/ppermute | solution.py:22
  89.7 3.9 %collective-permute-start.13 = (f32[2,16,512]{2,1,0:T(8,128)S(1)}, f32[2,16,512]{2,1,0:T(8,128)S(1)}, u32[]{:S(2)}, u32[]{:S(2)}) collective-permute-start(f32[2,16,512]{2,1,0:T(8,128)S(1)} %get-tuple-element.13), channel_id=1, source_target_pairs={{0,1},{1,2},{2,3},{3,0},{4,5},{5,6},{6,7},{7,4},{8,9},{9,10},{10,1... | collective-permute-start | bytes 196616 | tf_op jit(solution)/shard_map/ppermute | solution.py:22
  89.8 5.0 %collective-permute-start.14 = (f32[2,16,512]{2,1,0:T(8,128)S(1)}, f32[2,16,512]{2,1,0:T(8,128)S(1)}, u32[]{:S(2)}, u32[]{:S(2)}) collective-permute-start(f32[2,16,512]{2,1,0:T(8,128)S(1)} %get-tuple-element.12), channel_id=1, source_target_pairs={{0,2},{1,3},{2,0},{3,1},{4,6},{5,7},{6,4},{7,5},{8,10},{9,11},{10,... | collective-permute-start | bytes 196616 | tf_op jit(solution)/shard_map/ppermute | solution.py:22
  90.9 4.0 %collective-permute-start.15 = (f32[2,16,512]{2,1,0:T(8,128)S(1)}, f32[2,16,512]{2,1,0:T(8,128)S(1)}, u32[]{:S(2)}, u32[]{:S(2)}) collective-permute-start(f32[2,16,512]{2,1,0:T(8,128)S(1)} %get-tuple-element.11), channel_id=1, source_target_pairs={{0,3},{1,0},{2,1},{3,2},{4,7},{5,4},{6,5},{7,6},{8,11},{9,8},{10,9... | collective-permute-start | bytes 196616 | tf_op jit(solution)/shard_map/ppermute | solution.py:22

commit v9 on v8

--- a/solution.py
+++ b/solution.py
@@ -83,7 +83,7 @@
     later_kernel = None
     for step in range(day_count - 1):
         if step == min(1, switch_step):
-            later_pts = lax.optimization_barrier((day_pts, rows))[0]
+            later_pts, rows = lax.optimization_barrier((day_pts, rows))
             later_source = jnp.where(
                 first_forward,
                 lax.ppermute(later_pts, "day", [(d + 1, d) for d in range(half)]),

time: 96 us -> 96.9 us (level)
  waiting for transfers between devices: 28.1 us -> 29.8 us
  blocking collectives: 7.46 us -> 5.97 us
    ppermute x1, waiting for transfers between devices: 0.01 us -> 10.1 us  [shards(): lax.ppermute(later_pts, 'day', [(d + 1, d) for d in range(half)])]
    ppermute x7, waiting for transfers between devices: 24.1 us -> 15.5 us  [shards(): incoming = lax.ppermute(outgoing, 'day', route)]
    ppermute x1, waiting for transfers between devices: 0.01 us -> 2.23 us  [shards(): first_kernel = chain_kernel(lax.ppermute(day_pts, 'day', first_route))]
    ppermute x12, waiting for transfers between devices: 3.95 us -> 1.97 us  [swap_blocks(): lax.ppermute(piece, 'pt', [(i, (i + shift) % count) for i in range(count)])]
    ppermute x12, starting transfers between devices: 9.65 us -> 11.5 us  [swap_blocks(): lax.ppermute(piece, 'pt', [(i, (i + shift) % count) for i in range(count)])]
    all_gather x1, blocking collectives: 7.46 us -> 5.97 us  [shards(): day_pts = lax.all_gather(own_pts, 'pt', axis=1, tiled=True)]
    ppermute x7, starting transfers between devices: 9.35 us -> 8.24 us  [shards(): incoming = lax.ppermute(outgoing, 'day', route)]
  transfers between devices with their start and end apart: 22 -> 22, of which waited for: 5 -> 6; matrix products, arithmetic and copies ran while one was open for 13% -> 12% of each run, Pallas kernels for 0% -> 0%
where the time goes in v9:
time: 96.9 us; the launch traced here: 96.5 us
  waiting for transfers between devices  29.8 us (31%)
  starting transfers between devices  25.1 us (26%)
  matrix products  20.6 us (21%)
  other arithmetic  10.1 us (10%)
  blocking collectives  5.97 us (6%)
  between operations  2.67 us (3%)
  local copies, waits for them, and re-layouts  2.15 us (2%)
    ppermute x7, waiting for transfers between devices, shards(): incoming = lax.ppermute(outgoing, 'day', route)  15.5 us
    ppermute x12, starting transfers between devices, swap_blocks(): lax.ppermute(piece, 'pt', [(i, (i + shift) % count) for i in range(count)])  11.5 us
    dot_general x3, matrix products, squared_dist(): lax.dot_general(left_pts, right_pts, (((0,), (0,)), ((), ())), preferred_...  11.5 us
    ppermute x1, waiting for transfers between devices, shards(): lax.ppermute(later_pts, 'day', [(d + 1, d) for d in range(half)])  10.1 us
    dot_general x7, matrix products, shards(): jnp.dot(incoming, kernel, preferred_element_type=jnp.float32)  9.15 us
    ppermute x7, starting transfers between devices, shards(): incoming = lax.ppermute(outgoing, 'day', route)  8.24 us
    all_gather x1, blocking collectives, shards(): day_pts = lax.all_gather(own_pts, 'pt', axis=1, tiled=True)  5.97 us
    reduce_sum x1, other arithmetic, shards(): ratio_rows = jnp.sum(fit_kernel * inverse[None, :], axis=1)  4.9 us
  transfers between devices with their start and end apart: 22, of which 6 were waited for; matrix products, arithmetic and copies ran while one was open for 12% of the time, Pallas kernels for 0%

profile of v9, /device:TPU:0, one launch (start us, length us, event | category | flops | bytes accessed | tf_op | source)
XLA Modules:
  0.0 96.5 jit_solution(10012954205050375914)
XLA Ops:
  0.7 0.9 bitcast_multiply_fusion
  2.2 2.6 %collective-permute-start.1 = (f32[16,512]{1,0:T(8,128)S(1)}, f32[16,512]{1,0:T(8,128)S(1)}, u32[]{:S(2)}, u32[]{:S(2)}) collective-permute-start(f32[16,512]{1,0:T(8,128)S(1)} %get-tuple-element.20), channel_id=1, source_target_pairs={{0,2},{1,3},{2,0},{3,1},{4,6},{5,7},{6,4},{7,5},{8,10},{9,11},{10,... | collective-permute-start | bytes 98312 | tf_op jit(solution)/shard_map/ppermute | solution.py:22
  4.8 1.4 %collective-permute-start.2 = (f32[16,512]{1,0:T(8,128)S(1)}, f32[16,512]{1,0:T(8,128)S(1)}, u32[]{:S(2)}, u32[]{:S(2)}) collective-permute-start(f32[16,512]{1,0:T(8,128)S(1)} %get-tuple-element.19), channel_id=1, source_target_pairs={{0,3},{1,0},{2,1},{3,2},{4,7},{5,4},{6,5},{7,6},{8,11},{9,8},{10,9... | collective-permute-start | bytes 98312 | tf_op jit(solution)/shard_map/ppermute | solution.py:22
  6.2 6.0 %all-gather = bf16[1,64,2048]{2,1,0:T(8,128)(2,1)S(1)} all-gather(bf16[1,64,512]{2,1,0:T(8,128)(2,1)} %param.6), channel_id=2, replica_groups=mesh['day'=8,'pt'=4] {'pt'}, dimensions={2}, use_global_device_ids=true | all-gather | bytes 327680 | tf_op jit(solution)/shard_map/all_gather | solution.py:57
  12.2 3.4 %collective-permute-start.4 = (bf16[64,2048]{1,0:T(8,128)(2,1)S(1)}, bf16[64,2048]{1,0:T(8,128)(2,1)S(1)}, u32[]{:S(2)}, u32[]{:S(2)}) collective-permute-start(bf16[64,2048]{1,0:T(8,128)(2,1)S(1)} %bitcast.78), channel_id=1, source_target_pairs={{0,4},{4,8},{8,12},{20,16},{24,20},{28,24},{1,5},{5,9},{9,13},{21,... | collective-permute-start | bytes 786440 | tf_op jit(solution)/shard_map/ppermute | solution.py:76
  16.6 3.4 %collective-permute-start.3 = (bf16[16,2048]{1,0:T(8,128)(2,1)S(1)}, bf16[16,2048]{1,0:T(8,128)(2,1)S(1)}, u32[]{:S(2)}, u32[]{:S(2)}) collective-permute-start(bf16[16,2048]{1,0:T(8,128)(2,1)S(1)} %fusion.11), channel_id=1, source_target_pairs={{0,4},{28,24},{1,5},{29,25},{2,6},{30,26},{3,7},{31,27}} | collective-permute-start | bytes 196616 | tf_op jit(solution)/shard_map/ppermute | solution.py:101
  20.0 2.2 %collective-permute-done.4 = bf16[64,2048]{1,0:T(8,128)(2,1)S(1)} collective-permute-done((bf16[64,2048]{1,0:T(8,128)(2,1)S(1)}, bf16[64,2048]{1,0:T(8,128)(2,1)S(1)}, u32[]{:S(2)}, u32[]{:S(2)}) %collective-permute-start.4) | collective-permute-done | bytes 262176 | tf_op jit(solution)/shard_map/ppermute | solution.py:76
  22.3 3.6 %exponential_convert_fusion.1 = bf16[2048,2048]{1,0:T(8,128)(2,1)S(1)} fusion(bf16[64,2048]{1,0:T(8,128)(2,1)S(1)} %collective-permute-done.4, f32[2048]{0:T(1024)S(1)} %multiply_reduce_fusion.4, f32[2048]{0:T(1024)S(1)} %multiply_reduce_fusion.5, bf16[1,64,2048]{2,1,0:T(8,128)(2,1)S(1)} %all-gather), kind=kOutput, calls=%fused_computation.4 | convolution fusion | flops 557842432 | bytes 8929280 | tf_op jit(solution)/shard_map/dot_general | solution.py:45
  25.9 1.3 %fusion.21 = (f32[16]{0:T(128)S(1)}, f32[16,2048]{1,0:T(8,128)S(1)}) fusion(f32[2048]{0:T(1024)S(1)} %fusion.13, bf16[16,2048]{1,0:T(8,128)(2,1)S(1)} %collective-permute-done.3, bf16[2048,2048]{1,0:T(8,128)(2,1)S(1)} %exponential_convert_fusion.1), kind=kOutput, calls=%fused_computation.91 | convolution fusion | flops 134283248 | bytes 8593472 | tf_op jit(solution)/shard_map/dot_general | solution.py:102
  28.2 1.3 %fusion.22 = (f32[16]{0:T(128)S(1)}, f32[16,2048]{1,0:T(8,128)S(1)}) fusion(f32[2048]{0:T(1024)S(1)} %fusion.13, bf16[16,2048]{1,0:T(8,128)(2,1)S(1)} %collective-permute-done.5, bf16[2048,2048]{1,0:T(8,128)(2,1)S(1)} %exponential_convert_fusion.1), kind=kOutput, calls=%fused_computation.92 | convolution fusion | flops 134283248 | bytes 8593472 | tf_op jit(solution)/shard_map/dot_general | solution.py:102
  29.8 0.7 collective-permute-start.6
  30.5 1.3 %collective-permute-start.8 = (bf16[64,2048]{1,0:T(8,128)(2,1)S(1)}, bf16[64,2048]{1,0:T(8,128)(2,1)S(1)}, u32[]{:S(2)}, u32[]{:S(2)}) collective-permute-start(bf16[64,2048]{1,0:T(8,128)(2,1)S(1)} %bitcast.79), channel_id=1, source_target_pairs={{4,0},{8,4},{12,8},{16,12},{5,1},{9,5},{13,9},{17,13},{6,2},{10,6}... | collective-permute-start | bytes 786440 | tf_op jit(solution)/shard_map/ppermute | solution.py:89
  31.8 0.7 collective-permute-start.9
  32.5 1.3 %fusion.23 = (f32[16]{0:T(128)S(1)}, f32[16,2048]{1,0:T(8,128)S(1)}) fusion(f32[2048]{0:T(1024)S(1)} %fusion.13, bf16[16,2048]{1,0:T(8,128)(2,1)S(1)} %collective-permute-done.6, bf16[2048,2048]{1,0:T(8,128)(2,1)S(1)} %exponential_convert_fusion.1), kind=kOutput, calls=%fused_computation.93 | convolution fusion | flops 134283248 | bytes 8593472 | tf_op jit(solution)/shard_map/dot_general | solution.py:102
  34.7 10.1 %collective-permute-done.8 = bf16[64,2048]{1,0:T(8,128)(2,1)S(1)} collective-permute-done((bf16[64,2048]{1,0:T(8,128)(2,1)S(1)}, bf16[64,2048]{1,0:T(8,128)(2,1)S(1)}, u32[]{:S(2)}, u32[]{:S(2)}) %collective-permute-start.8) | collective-permute-done | bytes 262176 | tf_op jit(solution)/shard_map/ppermute | solution.py:89
  45.0 3.6 %exponential_convert_fusion = bf16[2048,2048]{1,0:T(8,128)(2,1)S(1)} fusion(bf16[64,2048]{1,0:T(8,128)(2,1)S(1)} %broadcast_select_fusion, f32[2048]{0:T(1024)S(1)} %multiply_reduce_fusion.3, f32[2048]{0:T(1024)S(1)} %multiply_reduce_fusion.4, bf16[1,64,2048]{2,1,0:T(8,128)(2,1)S(1)} %all-gather), kind=kOutput, calls=%fused_computation.3 | convolution fusion | flops 557842432 | bytes 8929280 | tf_op jit(solution)/shard_map/dot_general | solution.py:45
  48.6 1.3 %fusion.24 = (f32[16]{0:T(128)S(1)}, f32[16,2048]{1,0:T(8,128)S(1)}) fusion(f32[2048]{0:T(1024)S(1)} %fusion.13, bf16[16,2048]{1,0:T(8,128)(2,1)S(1)} %collective-permute-done.7, bf16[2048,2048]{1,0:T(8,128)(2,1)S(1)} %exponential_convert_fusion), kind=kOutput, calls=%fused_computation.94 | convolution fusion | flops 134283248 | bytes 8593472 | tf_op jit(solution)/shard_map/dot_general | solution.py:102
  50.9 1.3 %fusion.25 = (f32[16]{0:T(128)S(1)}, f32[16,2048]{1,0:T(8,128)S(1)}) fusion(f32[2048]{0:T(1024)S(1)} %fusion.13, bf16[16,2048]{1,0:T(8,128)(2,1)S(1)} %collective-permute-done.10, bf16[2048,2048]{1,0:T(8,128)(2,1)S(1)} %exponential_convert_fusion), kind=kOutput, calls=%fused_computation.95 | convolution fusion | flops 134283248 | bytes 8593472 | tf_op jit(solution)/shard_map/dot_general | solution.py:102
  52.4 0.8 collective-permute-start.11
  53.4 1.3 %fusion.26 = (f32[16]{0:T(128)S(1)}, f32[16,2048]{1,0:T(8,128)S(1)}) fusion(f32[2048]{0:T(1024)S(1)} %fusion.13, bf16[16,2048]{1,0:T(8,128)(2,1)S(1)} %collective-permute-done.11, bf16[2048,2048]{1,0:T(8,128)(2,1)S(1)} %exponential_convert_fusion), kind=kOutput, calls=%fused_computation.96 | convolution fusion | flops 134283248 | bytes 8593472 | tf_op jit(solution)/shard_map/dot_general | solution.py:102
  54.9 1.3 %collective-permute-start.12 = (bf16[16,2048]{1,0:T(8,128)(2,1)S(1)}, bf16[16,2048]{1,0:T(8,128)(2,1)S(1)}, u32[]{:S(2)}, u32[]{:S(2)}) collective-permute-start(bf16[16,2048]{1,0:T(8,128)(2,1)S(1)} %fusion.5), channel_id=1, source_target_pairs={{24,28},{4,0},{25,29},{5,1},{26,30},{6,2},{27,31},{7,3}} | collective-permute-start | bytes 196616 | tf_op jit(solution)/shard_map/ppermute | solution.py:101
  56.3 15.5 %collective-permute-done.12 = bf16[16,2048]{1,0:T(8,128)(2,1)S(1)} collective-permute-done((bf16[16,2048]{1,0:T(8,128)(2,1)S(1)}, bf16[16,2048]{1,0:T(8,128)(2,1)S(1)}, u32[]{:S(2)}, u32[]{:S(2)}) %collective-permute-start.12) | collective-permute-done | bytes 65568 | tf_op jit(solution)/shard_map/ppermute | solution.py:101
  71.8 1.3 %fusion.27 = (f32[16]{0:T(128)S(1)}, f32[16,2048]{1,0:T(8,128)S(1)}) fusion(f32[2048]{0:T(1024)S(1)} %fusion.13, bf16[16,2048]{1,0:T(8,128)(2,1)S(1)} %collective-permute-done.12, bf16[2048,2048]{1,0:T(8,128)(2,1)S(1)} %exponential_convert_fusion), kind=kOutput, calls=%fused_computation.97 | convolution fusion | flops 134283248 | bytes 8593472 | tf_op jit(solution)/shard_map/dot_general | solution.py:102
  74.0 1.4 %collective-permute-start.18 = (f32[1,2048]{1,0:T(1,128)S(1)}, f32[1,2048]{1,0:T(1,128)S(1)}, u32[]{:S(2)}, u32[]{:S(2)}) collective-permute-start(f32[1,2048]{1,0:T(1,128)S(1)} %bitcast.83), channel_id=1, source_target_pairs={{0,3},{1,0},{2,1},{3,2},{4,7},{5,4},{6,5},{7,6},{8,11},{9,8},{10,9... | collective-permute-start | bytes 24584 | tf_op jit(solution)/shard_map/ppermute | solution.py:22
  78.0 4.3 %multiply_reduce_fusion.1 = (f32[2048]{0:T(1024)S(1)}, f32[2048,2048]{1,0:T(8,128)S(1)}) fusion(f32[2048]{0:T(1024)S(1)} %get-tuple-element.10, f32[2048]{0:T(1024)S(1)} %multiply_reduce_fusion.2, f32[2048]{0:T(1024)S(1)} %multiply_reduce_fusion.4, bf16[1,64,2048]{2,1,0:T(8,128)(2,1)S(1)} %copy-done, bf16[1,64,2048]{2,1,0:T(8,128)(2,1)S(1)} %all-gather), kind=kOutput, calls=%fused_computation.1 | convolution fusion | flops 562034688 | bytes 17334272 | tf_op jit(solution)/shard_map/dot_general | solution.py:45
  83.0 4.9 %multiply_reduce_fusion = f32[2048]{0:T(1024)S(1)} fusion(f32[2048,2048]{1,0:T(8,128)S(1)} %get-tuple-element.42, f32[2048]{0:T(1024)S(1)} %select_divide_fusion, f32[2048]{0:T(1024)S(1)} %multiply_reduce_fusion.2, f32[2048]{0:T(1024)S(1)} %multiply_reduce_fusion.4), kind=kLoop, calls=%fused_computation | loop fusion | flops 25163776 | bytes 16809984 | tf_op jit(solution)/shard_map/reduce_sum | solution.py:125
  88.1 1.1 %collective-permute-start.19 = (f32[512]{0:T(512)S(1)}, f32[512]{0:T(512)S(1)}, u32[]{:S(2)}, u32[]{:S(2)}) collective-permute-start(f32[512]{0:T(512)S(1)} %get-tuple-element.25), channel_id=1, source_target_pairs={{0,1},{1,2},{2,3},{3,0},{4,5},{5,6},{6,7},{7,4},{8,9},{9,10},{10,1... | collective-permute-start | bytes 6152 | tf_op jit(solution)/shard_map/ppermute | solution.py:22
  89.7 0.9 collective-permute-start.21
  90.7 1.1 %collective-permute-start.14 = (f32[2,16,512]{2,1,0:T(8,128)S(1)}, f32[2,16,512]{2,1,0:T(8,128)S(1)}, u32[]{:S(2)}, u32[]{:S(2)}) collective-permute-start(f32[2,16,512]{2,1,0:T(8,128)S(1)} %get-tuple-element.16), channel_id=1, source_target_pairs={{0,2},{1,3},{2,0},{3,1},{4,6},{5,7},{6,4},{7,5},{8,10},{9,11},{10,... | collective-permute-start | bytes 196616 | tf_op jit(solution)/shard_map/ppermute | solution.py:22
  91.8 1.4 %collective-permute-start.15 = (f32[2,16,512]{2,1,0:T(8,128)S(1)}, f32[2,16,512]{2,1,0:T(8,128)S(1)}, u32[]{:S(2)}, u32[]{:S(2)}) collective-permute-start(f32[2,16,512]{2,1,0:T(8,128)S(1)} %get-tuple-element.15), channel_id=1, source_target_pairs={{0,3},{1,0},{2,1},{3,2},{4,7},{5,4},{6,5},{7,6},{8,11},{9,8},{10,9... | collective-permute-start | bytes 196616 | tf_op jit(solution)/shard_map/ppermute | solution.py:22
  94.5 1.2 %collective-permute-done.14 = f32[2,16,512]{2,1,0:T(8,128)S(1)} collective-permute-done((f32[2,16,512]{2,1,0:T(8,128)S(1)}, f32[2,16,512]{2,1,0:T(8,128)S(1)}, u32[]{:S(2)}, u32[]{:S(2)}) %collective-permute-start.14) | collective-permute-done | bytes 65568 | tf_op jit(solution)/shard_map/ppermute | solution.py:22
  95.8 0.7 fusion.19
  (90 shorter events, 10.2 us)
Async XLA Ops:
  1.7 14.8 %collective-permute-start = (f32[16,512]{1,0:T(8,128)S(1)}, f32[16,512]{1,0:T(8,128)S(1)}, u32[]{:S(2)}, u32[]{:S(2)}) collective-permute-start(f32[16,512]{1,0:T(8,128)S(1)} %get-tuple-element.21), channel_id=1, source_target_pairs={{0,1},{1,2},{2,3},{3,0},{4,5},{5,6},{6,7},{7,4},{8,9},{9,10},{10,1... | collective-permute-start | bytes 98312 | tf_op jit(solution)/shard_map/ppermute | solution.py:22
  2.2 14.2 %collective-permute-start.1 = (f32[16,512]{1,0:T(8,128)S(1)}, f32[16,512]{1,0:T(8,128)S(1)}, u32[]{:S(2)}, u32[]{:S(2)}) collective-permute-start(f32[16,512]{1,0:T(8,128)S(1)} %get-tuple-element.20), channel_id=1, source_target_pairs={{0,2},{1,3},{2,0},{3,1},{4,6},{5,7},{6,4},{7,5},{8,10},{9,11},{10,... | collective-permute-start | bytes 98312 | tf_op jit(solution)/shard_map/ppermute | solution.py:22
  4.8 11.7 %collective-permute-start.2 = (f32[16,512]{1,0:T(8,128)S(1)}, f32[16,512]{1,0:T(8,128)S(1)}, u32[]{:S(2)}, u32[]{:S(2)}) collective-permute-start(f32[16,512]{1,0:T(8,128)S(1)} %get-tuple-element.19), channel_id=1, source_target_pairs={{0,3},{1,0},{2,1},{3,2},{4,7},{5,4},{6,5},{7,6},{8,11},{9,8},{10,9... | collective-permute-start | bytes 98312 | tf_op jit(solution)/shard_map/ppermute | solution.py:22
  12.2 10.1 %collective-permute-start.4 = (bf16[64,2048]{1,0:T(8,128)(2,1)S(1)}, bf16[64,2048]{1,0:T(8,128)(2,1)S(1)}, u32[]{:S(2)}, u32[]{:S(2)}) collective-permute-start(bf16[64,2048]{1,0:T(8,128)(2,1)S(1)} %bitcast.78), channel_id=1, source_target_pairs={{0,4},{4,8},{8,12},{20,16},{24,20},{28,24},{1,5},{5,9},{9,13},{21,... | collective-permute-start | bytes 786440 | tf_op jit(solution)/shard_map/ppermute | solution.py:76
  16.6 9.4 %collective-permute-start.3 = (bf16[16,2048]{1,0:T(8,128)(2,1)S(1)}, bf16[16,2048]{1,0:T(8,128)(2,1)S(1)}, u32[]{:S(2)}, u32[]{:S(2)}) collective-permute-start(bf16[16,2048]{1,0:T(8,128)(2,1)S(1)} %fusion.11), channel_id=1, source_target_pairs={{0,4},{28,24},{1,5},{29,25},{2,6},{30,26},{3,7},{31,27}} | collective-permute-start | bytes 196616 | tf_op jit(solution)/shard_map/ppermute | solution.py:101
  27.5 0.8 collective-permute-start.5
  29.8 2.7 %collective-permute-start.6 = (bf16[16,2048]{1,0:T(8,128)(2,1)S(1)}, bf16[16,2048]{1,0:T(8,128)(2,1)S(1)}, u32[]{:S(2)}, u32[]{:S(2)}) collective-permute-start(bf16[16,2048]{1,0:T(8,128)(2,1)S(1)} %fusion.9), channel_id=1, source_target_pairs={{8,12},{20,16},{9,13},{21,17},{10,14},{22,18},{11,15},{23,19}} | collective-permute-start | bytes 196616 | tf_op jit(solution)/shard_map/ppermute | solution.py:101
  30.5 14.3 %collective-permute-start.8 = (bf16[64,2048]{1,0:T(8,128)(2,1)S(1)}, bf16[64,2048]{1,0:T(8,128)(2,1)S(1)}, u32[]{:S(2)}, u32[]{:S(2)}) collective-permute-start(bf16[64,2048]{1,0:T(8,128)(2,1)S(1)} %bitcast.79), channel_id=1, source_target_pairs={{4,0},{8,4},{12,8},{16,12},{5,1},{9,5},{13,9},{17,13},{6,2},{10,6}... | collective-permute-start | bytes 786440 | tf_op jit(solution)/shard_map/ppermute | solution.py:89
  31.8 13.1 %collective-permute-start.9 = (bf16[64,2048]{1,0:T(8,128)(2,1)S(1)}, bf16[64,2048]{1,0:T(8,128)(2,1)S(1)}, u32[]{:S(2)}, u32[]{:S(2)}) collective-permute-start(bf16[64,2048]{1,0:T(8,128)(2,1)S(1)} %bitcast.80), channel_id=1, source_target_pairs={{12,16},{16,20},{20,24},{24,28},{13,17},{17,21},{21,25},{25,29},{1... | collective-permute-start | bytes 786440 | tf_op jit(solution)/shard_map/ppermute | solution.py:90
  34.1 14.5 %collective-permute-start.7 = (bf16[16,2048]{1,0:T(8,128)(2,1)S(1)}, bf16[16,2048]{1,0:T(8,128)(2,1)S(1)}, u32[]{:S(2)}, u32[]{:S(2)}) collective-permute-start(bf16[16,2048]{1,0:T(8,128)(2,1)S(1)} %fusion.8), channel_id=1, source_target_pairs={{12,16},{16,12},{13,17},{17,13},{14,18},{18,14},{15,19},{19,15}} | collective-permute-start | bytes 196616 | tf_op jit(solution)/shard_map/ppermute | solution.py:101
  49.9 25.5 %copy-start = (bf16[1,64,2048]{2,1,0:T(8,128)(2,1)S(1)}, bf16[1,64,2048]{2,1,0:T(8,128)(2,1)}, u32[]{:S(2)}) copy-start(bf16[1,64,2048]{2,1,0:T(8,128)(2,1)} %param.7) | copy-start | bytes 786436
  50.1 0.8 collective-permute-start.10
  52.4 0.9 collective-permute-start.11
  54.9 16.8 %collective-permute-start.12 = (bf16[16,2048]{1,0:T(8,128)(2,1)S(1)}, bf16[16,2048]{1,0:T(8,128)(2,1)S(1)}, u32[]{:S(2)}, u32[]{:S(2)}) collective-permute-start(bf16[16,2048]{1,0:T(8,128)(2,1)S(1)} %fusion.5), channel_id=1, source_target_pairs={{24,28},{4,0},{25,29},{5,1},{26,30},{6,2},{27,31},{7,3}} | collective-permute-start | bytes 196616 | tf_op jit(solution)/shard_map/ppermute | solution.py:101
  73.4 3.1 %collective-permute-start.16 = (f32[1,2048]{1,0:T(1,128)S(1)}, f32[1,2048]{1,0:T(1,128)S(1)}, u32[]{:S(2)}, u32[]{:S(2)}) collective-permute-start(f32[1,2048]{1,0:T(1,128)S(1)} %bitcast.81), channel_id=1, source_target_pairs={{0,1},{1,2},{2,3},{3,0},{4,5},{5,6},{6,7},{7,4},{8,9},{9,10},{10,1... | collective-permute-start | bytes 24584 | tf_op jit(solution)/shard_map/ppermute | solution.py:22
  73.4 3.7 %collective-permute-start.17 = (f32[1,2048]{1,0:T(1,128)S(1)}, f32[1,2048]{1,0:T(1,128)S(1)}, u32[]{:S(2)}, u32[]{:S(2)}) collective-permute-start(f32[1,2048]{1,0:T(1,128)S(1)} %bitcast.82), channel_id=1, source_target_pairs={{0,2},{1,3},{2,0},{3,1},{4,6},{5,7},{6,4},{7,5},{8,10},{9,11},{10,... | collective-permute-start | bytes 24584 | tf_op jit(solution)/shard_map/ppermute | solution.py:22
  74.0 3.3 %collective-permute-start.18 = (f32[1,2048]{1,0:T(1,128)S(1)}, f32[1,2048]{1,0:T(1,128)S(1)}, u32[]{:S(2)}, u32[]{:S(2)}) collective-permute-start(f32[1,2048]{1,0:T(1,128)S(1)} %bitcast.83), channel_id=1, source_target_pairs={{0,3},{1,0},{2,1},{3,2},{4,7},{5,4},{6,5},{7,6},{8,11},{9,8},{10,9... | collective-permute-start | bytes 24584 | tf_op jit(solution)/shard_map/ppermute | solution.py:22
  88.1 3.7 %collective-permute-start.19 = (f32[512]{0:T(512)S(1)}, f32[512]{0:T(512)S(1)}, u32[]{:S(2)}, u32[]{:S(2)}) collective-permute-start(f32[512]{0:T(512)S(1)} %get-tuple-element.25), channel_id=1, source_target_pairs={{0,1},{1,2},{2,3},{3,0},{4,5},{5,6},{6,7},{7,4},{8,9},{9,10},{10,1... | collective-permute-start | bytes 6152 | tf_op jit(solution)/shard_map/ppermute | solution.py:22
  89.2 4.2 %collective-permute-start.20 = (f32[512]{0:T(512)S(1)}, f32[512]{0:T(512)S(1)}, u32[]{:S(2)}, u32[]{:S(2)}) collective-permute-start(f32[512]{0:T(512)S(1)} %get-tuple-element.24), channel_id=1, source_target_pairs={{0,2},{1,3},{2,0},{3,1},{4,6},{5,7},{6,4},{7,5},{8,10},{9,11},{10,... | collective-permute-start | bytes 6152 | tf_op jit(solution)/shard_map/ppermute | solution.py:22
  89.7 3.9 %collective-permute-start.21 = (f32[512]{0:T(512)S(1)}, f32[512]{0:T(512)S(1)}, u32[]{:S(2)}, u32[]{:S(2)}) collective-permute-start(f32[512]{0:T(512)S(1)} %get-tuple-element.23), channel_id=1, source_target_pairs={{0,3},{1,0},{2,1},{3,2},{4,7},{5,4},{6,5},{7,6},{8,11},{9,8},{10,9... | collective-permute-start | bytes 6152 | tf_op jit(solution)/shard_map/ppermute | solution.py:22
  90.7 3.9 %collective-permute-start.13 = (f32[2,16,512]{2,1,0:T(8,128)S(1)}, f32[2,16,512]{2,1,0:T(8,128)S(1)}, u32[]{:S(2)}, u32[]{:S(2)}) collective-permute-start(f32[2,16,512]{2,1,0:T(8,128)S(1)} %get-tuple-element.17), channel_id=1, source_target_pairs={{0,1},{1,2},{2,3},{3,0},{4,5},{5,6},{6,7},{7,4},{8,9},{9,10},{10,1... | collective-permute-start | bytes 196616 | tf_op jit(solution)/shard_map/ppermute | solution.py:22
  90.7 5.0 %collective-permute-start.14 = (f32[2,16,512]{2,1,0:T(8,128)S(1)}, f32[2,16,512]{2,1,0:T(8,128)S(1)}, u32[]{:S(2)}, u32[]{:S(2)}) collective-permute-start(f32[2,16,512]{2,1,0:T(8,128)S(1)} %get-tuple-element.16), channel_id=1, source_target_pairs={{0,2},{1,3},{2,0},{3,1},{4,6},{5,7},{6,4},{7,5},{8,10},{9,11},{10,... | collective-permute-start | bytes 196616 | tf_op jit(solution)/shard_map/ppermute | solution.py:22
  91.8 4.0 %collective-permute-start.15 = (f32[2,16,512]{2,1,0:T(8,128)S(1)}, f32[2,16,512]{2,1,0:T(8,128)S(1)}, u32[]{:S(2)}, u32[]{:S(2)}) collective-permute-start(f32[2,16,512]{2,1,0:T(8,128)S(1)} %get-tuple-element.15), channel_id=1, source_target_pairs={{0,3},{1,0},{2,1},{3,2},{4,7},{5,4},{6,5},{7,6},{8,11},{9,8},{10,9... | collective-permute-start | bytes 196616 | tf_op jit(solution)/shard_map/ppermute | solution.py:22

commit v10 on v9

--- a/solution.py
+++ b/solution.py
@@ -73,7 +73,8 @@
     first_forward = day_index < half
     first_route = [(d - 1, d) for d in range(1, half)]
     first_route += [(d + 1, d) for d in range(half, day_count - 1)]
-    first_kernel = chain_kernel(lax.ppermute(day_pts, "day", first_route))
+    first_quarter = lax.ppermute(own_pts, "day", first_route)
+    first_kernel = chain_kernel(lax.all_gather(first_quarter, "pt", axis=1, tiled=True))
 
     def settle(values):
         masked = values * live_all[None, :]

time: 96.9 us -> 97.9 us (1.010)
  blocking collectives: 5.97 us -> 11.8 us
  waiting for transfers between devices: 29.8 us -> 25 us
    all_gather x0 -> x1, blocking collectives: none -> 5.78 us  [shards(): lax.all_gather(first_quarter, 'pt', axis=1, tiled=True)]
    ppermute x1, waiting for transfers between devices: 10.1 us -> 7 us  [shards(): lax.ppermute(later_pts, 'day', [(d + 1, d) for d in range(half)])]
    ppermute x1, waiting for transfers between devices: 2.23 us -> 0.01 us  [shards(): first_quarter = lax.ppermute(own_pts, 'day', first_route)]
  transfers between devices with their start and end apart: 22 -> 22, of which waited for: 6 -> 5; matrix products, arithmetic and copies ran while one was open for 12% -> 12% of each run, Pallas kernels for 0% -> 0%
where the time goes in v10:
time: 97.9 us; the launch traced here: 97.5 us
  starting transfers between devices  25.1 us (26%)
  waiting for transfers between devices  25 us (26%)
  matrix products  20.6 us (21%)
  blocking collectives  11.8 us (12%)
  other arithmetic  10.1 us (10%)
  between operations  2.68 us (3%)
  local copies, waits for them, and re-layouts  2.15 us (2%)
    ppermute x7, waiting for transfers between devices, shards(): incoming = lax.ppermute(outgoing, 'day', route)  16 us
    ppermute x12, starting transfers between devices, swap_blocks(): lax.ppermute(piece, 'pt', [(i, (i + shift) % count) for i in range(count)])  11.5 us
    dot_general x3, matrix products, squared_dist(): lax.dot_general(left_pts, right_pts, (((0,), (0,)), ((), ())), preferred_...  11.5 us
    dot_general x7, matrix products, shards(): jnp.dot(incoming, kernel, preferred_element_type=jnp.float32)  9.15 us
    ppermute x7, starting transfers between devices, shards(): incoming = lax.ppermute(outgoing, 'day', route)  8.25 us
    ppermute x1, waiting for transfers between devices, shards(): lax.ppermute(later_pts, 'day', [(d + 1, d) for d in range(half)])  7 us
    all_gather x1, blocking collectives, shards(): day_pts = lax.all_gather(own_pts, 'pt', axis=1, tiled=True)  5.99 us
    all_gather x1, blocking collectives, shards(): lax.all_gather(first_quarter, 'pt', axis=1, tiled=True)  5.78 us
  transfers between devices with their start and end apart: 22, of which 5 were waited for; matrix products, arithmetic and copies ran while one was open for 12% of the time, Pallas kernels for 0%

profile of v10, /device:TPU:0, one launch (start us, length us, event | category | flops | bytes accessed | tf_op | source)
XLA Modules:
  0.0 97.5 jit_solution(2166340310961091341)
XLA Ops:
  0.7 0.9 bitcast_multiply_fusion
  2.2 2.6 %collective-permute-start.1 = (f32[16,512]{1,0:T(8,128)S(1)}, f32[16,512]{1,0:T(8,128)S(1)}, u32[]{:S(2)}, u32[]{:S(2)}) collective-permute-start(f32[16,512]{1,0:T(8,128)S(1)} %get-tuple-element.20), channel_id=1, source_target_pairs={{0,2},{1,3},{2,0},{3,1},{4,6},{5,7},{6,4},{7,5},{8,10},{9,11},{10,... | collective-permute-start | bytes 98312 | tf_op jit(solution)/shard_map/ppermute | solution.py:22
  4.8 1.4 %collective-permute-start.2 = (f32[16,512]{1,0:T(8,128)S(1)}, f32[16,512]{1,0:T(8,128)S(1)}, u32[]{:S(2)}, u32[]{:S(2)}) collective-permute-start(f32[16,512]{1,0:T(8,128)S(1)} %get-tuple-element.19), channel_id=1, source_target_pairs={{0,3},{1,0},{2,1},{3,2},{4,7},{5,4},{6,5},{7,6},{8,11},{9,8},{10,9... | collective-permute-start | bytes 98312 | tf_op jit(solution)/shard_map/ppermute | solution.py:22
  6.2 3.4 %collective-permute-start.4 = (bf16[64,512]{1,0:T(8,128)(2,1)}, bf16[64,512]{1,0:T(8,128)(2,1)S(1)}, u32[]{:S(2)}, u32[]{:S(2)}) collective-permute-start(bf16[64,512]{1,0:T(8,128)(2,1)} %bitcast.81), channel_id=1, source_target_pairs={{0,4},{4,8},{8,12},{20,16},{24,20},{28,24},{1,5},{5,9},{9,13},{21,... | collective-permute-start | bytes 196616 | tf_op jit(solution)/shard_map/ppermute | solution.py:76
  9.6 6.0 %all-gather = bf16[1,64,2048]{2,1,0:T(8,128)(2,1)S(1)} all-gather(bf16[1,64,512]{2,1,0:T(8,128)(2,1)} %param.6), channel_id=2, replica_groups=mesh['day'=8,'pt'=4] {'pt'}, dimensions={2}, use_global_device_ids=true | all-gather | bytes 327680 | tf_op jit(solution)/shard_map/all_gather | solution.py:57
  16.6 3.5 %collective-permute-start.3 = (bf16[16,2048]{1,0:T(8,128)(2,1)S(1)}, bf16[16,2048]{1,0:T(8,128)(2,1)S(1)}, u32[]{:S(2)}, u32[]{:S(2)}) collective-permute-start(bf16[16,2048]{1,0:T(8,128)(2,1)S(1)} %fusion.11), channel_id=1, source_target_pairs={{0,4},{28,24},{1,5},{29,25},{2,6},{30,26},{3,7},{31,27}} | collective-permute-start | bytes 196616 | tf_op jit(solution)/shard_map/ppermute | solution.py:102
  20.1 5.8 %all_gather.7 = bf16[64,2048]{1,0:T(8,128)(2,1)S(1)} all-gather(bf16[64,512]{1,0:T(8,128)(2,1)S(1)} %collective-permute-done.4), channel_id=1, replica_groups=mesh['day'=8,'pt'=4] {'pt'}, dimensions={1}, use_global_device_ids=true | all-gather | bytes 327680 | tf_op jit(solution)/shard_map/all_gather | solution.py:77
  25.9 3.6 %exponential_convert_fusion.1 = bf16[2048,2048]{1,0:T(8,128)(2,1)S(1)} fusion(bf16[64,2048]{1,0:T(8,128)(2,1)S(1)} %all_gather.7, f32[2048]{0:T(1024)S(1)} %multiply_reduce_fusion.4, f32[2048]{0:T(1024)S(1)} %multiply_reduce_fusion.5, bf16[1,64,2048]{2,1,0:T(8,128)(2,1)S(1)} %all-gather), kind=kOutput, calls=%fused_computation.4 | convolution fusion | flops 557842432 | bytes 8929280 | tf_op jit(solution)/shard_map/dot_general | solution.py:45
  29.5 1.3 %fusion.21 = (f32[16]{0:T(128)S(1)}, f32[16,2048]{1,0:T(8,128)S(1)}) fusion(f32[2048]{0:T(1024)S(1)} %fusion.13, bf16[16,2048]{1,0:T(8,128)(2,1)S(1)} %collective-permute-done.3, bf16[2048,2048]{1,0:T(8,128)(2,1)S(1)} %exponential_convert_fusion.1), kind=kOutput, calls=%fused_computation.91 | convolution fusion | flops 134283248 | bytes 8593472 | tf_op jit(solution)/shard_map/dot_general | solution.py:103
  31.1 0.7 collective-permute-start.5
  31.8 1.3 %fusion.22 = (f32[16]{0:T(128)S(1)}, f32[16,2048]{1,0:T(8,128)S(1)}) fusion(f32[2048]{0:T(1024)S(1)} %fusion.13, bf16[16,2048]{1,0:T(8,128)(2,1)S(1)} %collective-permute-done.5, bf16[2048,2048]{1,0:T(8,128)(2,1)S(1)} %exponential_convert_fusion.1), kind=kOutput, calls=%fused_computation.92 | convolution fusion | flops 134283248 | bytes 8593472 | tf_op jit(solution)/shard_map/dot_general | solution.py:103
  34.1 1.3 %collective-permute-start.8 = (bf16[64,2048]{1,0:T(8,128)(2,1)S(1)}, bf16[64,2048]{1,0:T(8,128)(2,1)S(1)}, u32[]{:S(2)}, u32[]{:S(2)}) collective-permute-start(bf16[64,2048]{1,0:T(8,128)(2,1)S(1)} %bitcast.79), channel_id=1, source_target_pairs={{4,0},{8,4},{12,8},{16,12},{5,1},{9,5},{13,9},{17,13},{6,2},{10,6}... | collective-permute-start | bytes 786440 | tf_op jit(solution)/shard_map/ppermute | solution.py:90
  35.4 0.7 collective-permute-start.9
  36.1 1.3 %fusion.23 = (f32[16]{0:T(128)S(1)}, f32[16,2048]{1,0:T(8,128)S(1)}) fusion(f32[2048]{0:T(1024)S(1)} %fusion.13, bf16[16,2048]{1,0:T(8,128)(2,1)S(1)} %collective-permute-done.6, bf16[2048,2048]{1,0:T(8,128)(2,1)S(1)} %exponential_convert_fusion.1), kind=kOutput, calls=%fused_computation.93 | convolution fusion | flops 134283248 | bytes 8593472 | tf_op jit(solution)/shard_map/dot_general | solution.py:103
  38.3 7.0 %collective-permute-done.8 = bf16[64,2048]{1,0:T(8,128)(2,1)S(1)} collective-permute-done((bf16[64,2048]{1,0:T(8,128)(2,1)S(1)}, bf16[64,2048]{1,0:T(8,128)(2,1)S(1)}, u32[]{:S(2)}, u32[]{:S(2)}) %collective-permute-start.8) | collective-permute-done | bytes 262176 | tf_op jit(solution)/shard_map/ppermute | solution.py:90
  45.5 3.6 %exponential_convert_fusion = bf16[2048,2048]{1,0:T(8,128)(2,1)S(1)} fusion(bf16[64,2048]{1,0:T(8,128)(2,1)S(1)} %broadcast_select_fusion, f32[2048]{0:T(1024)S(1)} %multiply_reduce_fusion.3, f32[2048]{0:T(1024)S(1)} %multiply_reduce_fusion.4, bf16[1,64,2048]{2,1,0:T(8,128)(2,1)S(1)} %all-gather), kind=kOutput, calls=%fused_computation.3 | convolution fusion | flops 557842432 | bytes 8929280 | tf_op jit(solution)/shard_map/dot_general | solution.py:45
  49.1 1.3 %fusion.24 = (f32[16]{0:T(128)S(1)}, f32[16,2048]{1,0:T(8,128)S(1)}) fusion(f32[2048]{0:T(1024)S(1)} %fusion.13, bf16[16,2048]{1,0:T(8,128)(2,1)S(1)} %collective-permute-done.7, bf16[2048,2048]{1,0:T(8,128)(2,1)S(1)} %exponential_convert_fusion), kind=kOutput, calls=%fused_computation.94 | convolution fusion | flops 134283248 | bytes 8593472 | tf_op jit(solution)/shard_map/dot_general | solution.py:103
  51.4 1.3 %fusion.25 = (f32[16]{0:T(128)S(1)}, f32[16,2048]{1,0:T(8,128)S(1)}) fusion(f32[2048]{0:T(1024)S(1)} %fusion.13, bf16[16,2048]{1,0:T(8,128)(2,1)S(1)} %collective-permute-done.10, bf16[2048,2048]{1,0:T(8,128)(2,1)S(1)} %exponential_convert_fusion), kind=kOutput, calls=%fused_computation.95 | convolution fusion | flops 134283248 | bytes 8593472 | tf_op jit(solution)/shard_map/dot_general | solution.py:103
  52.9 0.8 collective-permute-start.11
  53.9 1.3 %fusion.26 = (f32[16]{0:T(128)S(1)}, f32[16,2048]{1,0:T(8,128)S(1)}) fusion(f32[2048]{0:T(1024)S(1)} %fusion.13, bf16[16,2048]{1,0:T(8,128)(2,1)S(1)} %collective-permute-done.11, bf16[2048,2048]{1,0:T(8,128)(2,1)S(1)} %exponential_convert_fusion), kind=kOutput, calls=%fused_computation.96 | convolution fusion | flops 134283248 | bytes 8593472 | tf_op jit(solution)/shard_map/dot_general | solution.py:103
  55.4 1.3 %collective-permute-start.12 = (bf16[16,2048]{1,0:T(8,128)(2,1)S(1)}, bf16[16,2048]{1,0:T(8,128)(2,1)S(1)}, u32[]{:S(2)}, u32[]{:S(2)}) collective-permute-start(bf16[16,2048]{1,0:T(8,128)(2,1)S(1)} %fusion.5), channel_id=1, source_target_pairs={{24,28},{4,0},{25,29},{5,1},{26,30},{6,2},{27,31},{7,3}} | collective-permute-start | bytes 196616 | tf_op jit(solution)/shard_map/ppermute | solution.py:102
  56.8 16.0 %collective-permute-done.12 = bf16[16,2048]{1,0:T(8,128)(2,1)S(1)} collective-permute-done((bf16[16,2048]{1,0:T(8,128)(2,1)S(1)}, bf16[16,2048]{1,0:T(8,128)(2,1)S(1)}, u32[]{:S(2)}, u32[]{:S(2)}) %collective-permute-start.12) | collective-permute-done | bytes 65568 | tf_op jit(solution)/shard_map/ppermute | solution.py:102
  72.8 1.3 %fusion.27 = (f32[16]{0:T(128)S(1)}, f32[16,2048]{1,0:T(8,128)S(1)}) fusion(f32[2048]{0:T(1024)S(1)} %fusion.13, bf16[16,2048]{1,0:T(8,128)(2,1)S(1)} %collective-permute-done.12, bf16[2048,2048]{1,0:T(8,128)(2,1)S(1)} %exponential_convert_fusion), kind=kOutput, calls=%fused_computation.97 | convolution fusion | flops 134283248 | bytes 8593472 | tf_op jit(solution)/shard_map/dot_general | solution.py:103
  75.0 1.4 %collective-permute-start.18 = (f32[1,2048]{1,0:T(1,128)S(1)}, f32[1,2048]{1,0:T(1,128)S(1)}, u32[]{:S(2)}, u32[]{:S(2)}) collective-permute-start(f32[1,2048]{1,0:T(1,128)S(1)} %bitcast.84), channel_id=1, source_target_pairs={{0,3},{1,0},{2,1},{3,2},{4,7},{5,4},{6,5},{7,6},{8,11},{9,8},{10,9... | collective-permute-start | bytes 24584 | tf_op jit(solution)/shard_map/ppermute | solution.py:22
  79.0 4.3 %multiply_reduce_fusion.1 = (f32[2048]{0:T(1024)S(1)}, f32[2048,2048]{1,0:T(8,128)S(1)}) fusion(f32[2048]{0:T(1024)S(1)} %get-tuple-element.10, f32[2048]{0:T(1024)S(1)} %multiply_reduce_fusion.2, f32[2048]{0:T(1024)S(1)} %multiply_reduce_fusion.4, bf16[1,64,2048]{2,1,0:T(8,128)(2,1)S(1)} %copy-done, bf16[1,64,2048]{2,1,0:T(8,128)(2,1)S(1)} %all-gather), kind=kOutput, calls=%fused_computation.1 | convolution fusion | flops 562034688 | bytes 17334272 | tf_op jit(solution)/shard_map/dot_general | solution.py:45
  84.0 4.9 %multiply_reduce_fusion = f32[2048]{0:T(1024)S(1)} fusion(f32[2048,2048]{1,0:T(8,128)S(1)} %get-tuple-element.42, f32[2048]{0:T(1024)S(1)} %select_divide_fusion, f32[2048]{0:T(1024)S(1)} %multiply_reduce_fusion.2, f32[2048]{0:T(1024)S(1)} %multiply_reduce_fusion.4), kind=kLoop, calls=%fused_computation | loop fusion | flops 25163776 | bytes 16809984 | tf_op jit(solution)/shard_map/reduce_sum | solution.py:126
  89.1 1.1 %collective-permute-start.19 = (f32[512]{0:T(512)S(1)}, f32[512]{0:T(512)S(1)}, u32[]{:S(2)}, u32[]{:S(2)}) collective-permute-start(f32[512]{0:T(512)S(1)} %get-tuple-element.25), channel_id=1, source_target_pairs={{0,1},{1,2},{2,3},{3,0},{4,5},{5,6},{6,7},{7,4},{8,9},{9,10},{10,1... | collective-permute-start | bytes 6152 | tf_op jit(solution)/shard_map/ppermute | solution.py:22
  90.6 0.9 collective-permute-start.21
  91.7 1.1 %collective-permute-start.14 = (f32[2,16,512]{2,1,0:T(8,128)S(1)}, f32[2,16,512]{2,1,0:T(8,128)S(1)}, u32[]{:S(2)}, u32[]{:S(2)}) collective-permute-start(f32[2,16,512]{2,1,0:T(8,128)S(1)} %get-tuple-element.16), channel_id=1, source_target_pairs={{0,2},{1,3},{2,0},{3,1},{4,6},{5,7},{6,4},{7,5},{8,10},{9,11},{10,... | collective-permute-start | bytes 196616 | tf_op jit(solution)/shard_map/ppermute | solution.py:22
  92.8 1.4 %collective-permute-start.15 = (f32[2,16,512]{2,1,0:T(8,128)S(1)}, f32[2,16,512]{2,1,0:T(8,128)S(1)}, u32[]{:S(2)}, u32[]{:S(2)}) collective-permute-start(f32[2,16,512]{2,1,0:T(8,128)S(1)} %get-tuple-element.15), channel_id=1, source_target_pairs={{0,3},{1,0},{2,1},{3,2},{4,7},{5,4},{6,5},{7,6},{8,11},{9,8},{10,9... | collective-permute-start | bytes 196616 | tf_op jit(solution)/shard_map/ppermute | solution.py:22
  95.5 1.2 %collective-permute-done.14 = f32[2,16,512]{2,1,0:T(8,128)S(1)} collective-permute-done((f32[2,16,512]{2,1,0:T(8,128)S(1)}, f32[2,16,512]{2,1,0:T(8,128)S(1)}, u32[]{:S(2)}, u32[]{:S(2)}) %collective-permute-start.14) | collective-permute-done | bytes 65568 | tf_op jit(solution)/shard_map/ppermute | solution.py:22
  96.8 0.7 fusion.19
  (91 shorter events, 10.2 us)
Async XLA Ops:
  1.7 14.8 %collective-permute-start = (f32[16,512]{1,0:T(8,128)S(1)}, f32[16,512]{1,0:T(8,128)S(1)}, u32[]{:S(2)}, u32[]{:S(2)}) collective-permute-start(f32[16,512]{1,0:T(8,128)S(1)} %get-tuple-element.21), channel_id=1, source_target_pairs={{0,1},{1,2},{2,3},{3,0},{4,5},{5,6},{6,7},{7,4},{8,9},{9,10},{10,1... | collective-permute-start | bytes 98312 | tf_op jit(solution)/shard_map/ppermute | solution.py:22
  2.2 14.2 %collective-permute-start.1 = (f32[16,512]{1,0:T(8,128)S(1)}, f32[16,512]{1,0:T(8,128)S(1)}, u32[]{:S(2)}, u32[]{:S(2)}) collective-permute-start(f32[16,512]{1,0:T(8,128)S(1)} %get-tuple-element.20), channel_id=1, source_target_pairs={{0,2},{1,3},{2,0},{3,1},{4,6},{5,7},{6,4},{7,5},{8,10},{9,11},{10,... | collective-permute-start | bytes 98312 | tf_op jit(solution)/shard_map/ppermute | solution.py:22
  4.8 11.7 %collective-permute-start.2 = (f32[16,512]{1,0:T(8,128)S(1)}, f32[16,512]{1,0:T(8,128)S(1)}, u32[]{:S(2)}, u32[]{:S(2)}) collective-permute-start(f32[16,512]{1,0:T(8,128)S(1)} %get-tuple-element.19), channel_id=1, source_target_pairs={{0,3},{1,0},{2,1},{3,2},{4,7},{5,4},{6,5},{7,6},{8,11},{9,8},{10,9... | collective-permute-start | bytes 98312 | tf_op jit(solution)/shard_map/ppermute | solution.py:22
  6.2 13.8 %collective-permute-start.4 = (bf16[64,512]{1,0:T(8,128)(2,1)}, bf16[64,512]{1,0:T(8,128)(2,1)S(1)}, u32[]{:S(2)}, u32[]{:S(2)}) collective-permute-start(bf16[64,512]{1,0:T(8,128)(2,1)} %bitcast.81), channel_id=1, source_target_pairs={{0,4},{4,8},{8,12},{20,16},{24,20},{28,24},{1,5},{5,9},{9,13},{21,... | collective-permute-start | bytes 196616 | tf_op jit(solution)/shard_map/ppermute | solution.py:76
  16.6 12.9 %collective-permute-start.3 = (bf16[16,2048]{1,0:T(8,128)(2,1)S(1)}, bf16[16,2048]{1,0:T(8,128)(2,1)S(1)}, u32[]{:S(2)}, u32[]{:S(2)}) collective-permute-start(bf16[16,2048]{1,0:T(8,128)(2,1)S(1)} %fusion.11), channel_id=1, source_target_pairs={{0,4},{28,24},{1,5},{29,25},{2,6},{30,26},{3,7},{31,27}} | collective-permute-start | bytes 196616 | tf_op jit(solution)/shard_map/ppermute | solution.py:102
  31.1 0.8 collective-permute-start.5
  33.4 2.7 %collective-permute-start.6 = (bf16[16,2048]{1,0:T(8,128)(2,1)S(1)}, bf16[16,2048]{1,0:T(8,128)(2,1)S(1)}, u32[]{:S(2)}, u32[]{:S(2)}) collective-permute-start(bf16[16,2048]{1,0:T(8,128)(2,1)S(1)} %fusion.9), channel_id=1, source_target_pairs={{8,12},{20,16},{9,13},{21,17},{10,14},{22,18},{11,15},{23,19}} | collective-permute-start | bytes 196616 | tf_op jit(solution)/shard_map/ppermute | solution.py:102
  34.1 11.2 %collective-permute-start.8 = (bf16[64,2048]{1,0:T(8,128)(2,1)S(1)}, bf16[64,2048]{1,0:T(8,128)(2,1)S(1)}, u32[]{:S(2)}, u32[]{:S(2)}) collective-permute-start(bf16[64,2048]{1,0:T(8,128)(2,1)S(1)} %bitcast.79), channel_id=1, source_target_pairs={{4,0},{8,4},{12,8},{16,12},{5,1},{9,5},{13,9},{17,13},{6,2},{10,6}... | collective-permute-start | bytes 786440 | tf_op jit(solution)/shard_map/ppermute | solution.py:90
  35.4 9.9 %collective-permute-start.9 = (bf16[64,2048]{1,0:T(8,128)(2,1)S(1)}, bf16[64,2048]{1,0:T(8,128)(2,1)S(1)}, u32[]{:S(2)}, u32[]{:S(2)}) collective-permute-start(bf16[64,2048]{1,0:T(8,128)(2,1)S(1)} %bitcast.80), channel_id=1, source_target_pairs={{12,16},{16,20},{20,24},{24,28},{13,17},{17,21},{21,25},{25,29},{1... | collective-permute-start | bytes 786440 | tf_op jit(solution)/shard_map/ppermute | solution.py:91
  37.7 11.4 %collective-permute-start.7 = (bf16[16,2048]{1,0:T(8,128)(2,1)S(1)}, bf16[16,2048]{1,0:T(8,128)(2,1)S(1)}, u32[]{:S(2)}, u32[]{:S(2)}) collective-permute-start(bf16[16,2048]{1,0:T(8,128)(2,1)S(1)} %fusion.8), channel_id=1, source_target_pairs={{12,16},{16,12},{13,17},{17,13},{14,18},{18,14},{15,19},{19,15}} | collective-permute-start | bytes 196616 | tf_op jit(solution)/shard_map/ppermute | solution.py:102
  50.4 26.0 %copy-start = (bf16[1,64,2048]{2,1,0:T(8,128)(2,1)S(1)}, bf16[1,64,2048]{2,1,0:T(8,128)(2,1)}, u32[]{:S(2)}) copy-start(bf16[1,64,2048]{2,1,0:T(8,128)(2,1)} %param.7) | copy-start | bytes 786436
  50.6 0.8 collective-permute-start.10
  52.9 0.9 collective-permute-start.11
  55.4 17.4 %collective-permute-start.12 = (bf16[16,2048]{1,0:T(8,128)(2,1)S(1)}, bf16[16,2048]{1,0:T(8,128)(2,1)S(1)}, u32[]{:S(2)}, u32[]{:S(2)}) collective-permute-start(bf16[16,2048]{1,0:T(8,128)(2,1)S(1)} %fusion.5), channel_id=1, source_target_pairs={{24,28},{4,0},{25,29},{5,1},{26,30},{6,2},{27,31},{7,3}} | collective-permute-start | bytes 196616 | tf_op jit(solution)/shard_map/ppermute | solution.py:102
  74.4 3.1 %collective-permute-start.16 = (f32[1,2048]{1,0:T(1,128)S(1)}, f32[1,2048]{1,0:T(1,128)S(1)}, u32[]{:S(2)}, u32[]{:S(2)}) collective-permute-start(f32[1,2048]{1,0:T(1,128)S(1)} %bitcast.82), channel_id=1, source_target_pairs={{0,1},{1,2},{2,3},{3,0},{4,5},{5,6},{6,7},{7,4},{8,9},{9,10},{10,1... | collective-permute-start | bytes 24584 | tf_op jit(solution)/shard_map/ppermute | solution.py:22
  74.4 3.7 %collective-permute-start.17 = (f32[1,2048]{1,0:T(1,128)S(1)}, f32[1,2048]{1,0:T(1,128)S(1)}, u32[]{:S(2)}, u32[]{:S(2)}) collective-permute-start(f32[1,2048]{1,0:T(1,128)S(1)} %bitcast.83), channel_id=1, source_target_pairs={{0,2},{1,3},{2,0},{3,1},{4,6},{5,7},{6,4},{7,5},{8,10},{9,11},{10,... | collective-permute-start | bytes 24584 | tf_op jit(solution)/shard_map/ppermute | solution.py:22
  75.0 3.3 %collective-permute-start.18 = (f32[1,2048]{1,0:T(1,128)S(1)}, f32[1,2048]{1,0:T(1,128)S(1)}, u32[]{:S(2)}, u32[]{:S(2)}) collective-permute-start(f32[1,2048]{1,0:T(1,128)S(1)} %bitcast.84), channel_id=1, source_target_pairs={{0,3},{1,0},{2,1},{3,2},{4,7},{5,4},{6,5},{7,6},{8,11},{9,8},{10,9... | collective-permute-start | bytes 24584 | tf_op jit(solution)/shard_map/ppermute | solution.py:22
  89.1 3.7 %collective-permute-start.19 = (f32[512]{0:T(512)S(1)}, f32[512]{0:T(512)S(1)}, u32[]{:S(2)}, u32[]{:S(2)}) collective-permute-start(f32[512]{0:T(512)S(1)} %get-tuple-element.25), channel_id=1, source_target_pairs={{0,1},{1,2},{2,3},{3,0},{4,5},{5,6},{6,7},{7,4},{8,9},{9,10},{10,1... | collective-permute-start | bytes 6152 | tf_op jit(solution)/shard_map/ppermute | solution.py:22
  90.2 4.2 %collective-permute-start.20 = (f32[512]{0:T(512)S(1)}, f32[512]{0:T(512)S(1)}, u32[]{:S(2)}, u32[]{:S(2)}) collective-permute-start(f32[512]{0:T(512)S(1)} %get-tuple-element.24), channel_id=1, source_target_pairs={{0,2},{1,3},{2,0},{3,1},{4,6},{5,7},{6,4},{7,5},{8,10},{9,11},{10,... | collective-permute-start | bytes 6152 | tf_op jit(solution)/shard_map/ppermute | solution.py:22
  90.6 3.9 %collective-permute-start.21 = (f32[512]{0:T(512)S(1)}, f32[512]{0:T(512)S(1)}, u32[]{:S(2)}, u32[]{:S(2)}) collective-permute-start(f32[512]{0:T(512)S(1)} %get-tuple-element.23), channel_id=1, source_target_pairs={{0,3},{1,0},{2,1},{3,2},{4,7},{5,4},{6,5},{7,6},{8,11},{9,8},{10,9... | collective-permute-start | bytes 6152 | tf_op jit(solution)/shard_map/ppermute | solution.py:22
  91.6 3.9 %collective-permute-start.13 = (f32[2,16,512]{2,1,0:T(8,128)S(1)}, f32[2,16,512]{2,1,0:T(8,128)S(1)}, u32[]{:S(2)}, u32[]{:S(2)}) collective-permute-start(f32[2,16,512]{2,1,0:T(8,128)S(1)} %get-tuple-element.17), channel_id=1, source_target_pairs={{0,1},{1,2},{2,3},{3,0},{4,5},{5,6},{6,7},{7,4},{8,9},{9,10},{10,1... | collective-permute-start | bytes 196616 | tf_op jit(solution)/shard_map/ppermute | solution.py:22
  91.7 5.0 %collective-permute-start.14 = (f32[2,16,512]{2,1,0:T(8,128)S(1)}, f32[2,16,512]{2,1,0:T(8,128)S(1)}, u32[]{:S(2)}, u32[]{:S(2)}) collective-permute-start(f32[2,16,512]{2,1,0:T(8,128)S(1)} %get-tuple-element.16), channel_id=1, source_target_pairs={{0,2},{1,3},{2,0},{3,1},{4,6},{5,7},{6,4},{7,5},{8,10},{9,11},{10,... | collective-permute-start | bytes 196616 | tf_op jit(solution)/shard_map/ppermute | solution.py:22
  92.8 4.0 %collective-permute-start.15 = (f32[2,16,512]{2,1,0:T(8,128)S(1)}, f32[2,16,512]{2,1,0:T(8,128)S(1)}, u32[]{:S(2)}, u32[]{:S(2)}) collective-permute-start(f32[2,16,512]{2,1,0:T(8,128)S(1)} %get-tuple-element.15), channel_id=1, source_target_pairs={{0,3},{1,0},{2,1},{3,2},{4,7},{5,4},{6,5},{7,6},{8,11},{9,8},{10,9... | collective-permute-start | bytes 196616 | tf_op jit(solution)/shard_map/ppermute | solution.py:22

commit v11 on v9

--- a/solution.py
+++ b/solution.py
@@ -21,6 +21,30 @@
         if shift:
             piece = lax.ppermute(piece, "pt", [(i, (i + shift) % count) for i in range(count)])
         out = lax.dynamic_update_slice_in_dim(out, piece, ((rank - shift) % count) * put, put_axis)
+    return out
+
+
+def gather_over_pt(x, axis, route=None):
+    count = lax.axis_size("pt")
+    rank = lax.axis_index("pt")
+    shape = list(x.shape)
+    shape[axis] *= count
+    out = jnp.zeros(shape, x.dtype)
+    for shift in range(count):
+        if route is None:
+            piece = x if shift == 0 else lax.ppermute(
+                x, "pt", [((i + shift) % count, i) for i in range(count)]
+            )
+        else:
+            pairs = [
+                (src * count + (p + shift) % count, dst * count + p)
+                for src, dst in route
+                for p in range(count)
+            ]
+            piece = lax.ppermute(x, ("day", "pt"), pairs)
+        out = lax.dynamic_update_slice_in_dim(
+            out, piece, ((rank + shift) % count) * x.shape[axis], axis
+        )
     return out
 
 
@@ -54,7 +78,7 @@
     day_count = lax.axis_size("day")
     own_pts = points[0]
     per_device = own_pts.shape[1]
-    day_pts = lax.all_gather(own_pts, "pt", axis=1, tiled=True)
+    day_pts = gather_over_pt(own_pts, 1)
     support_total = day_pts.shape[1]
     own_weight = clone_weight[0] * potential[0][None, :]
     block_rows = own_weight.shape[0] // lax.axis_size("pt")
@@ -73,7 +97,7 @@
     first_forward = day_index < half
     first_route = [(d - 1, d) for d in range(1, half)]
     first_route += [(d + 1, d) for d in range(half, day_count - 1)]
-    first_kernel = chain_kernel(lax.ppermute(day_pts, "day", first_route))
+    first_kernel = chain_kernel(gather_over_pt(own_pts, 1, first_route))
 
     def settle(values):
         masked = values * live_all[None, :]

time: 96.9 us -> 104 us (1.073)
  starting transfers between devices: 25.1 us -> 35.1 us
  blocking collectives: 5.97 us -> 0 us
  waiting for transfers between devices: 29.8 us -> 31.8 us
    ppermute x1 -> x7, starting transfers between devices: 3.4 us -> 16.7 us  [the longest x4 13.4 us: gather_over_pt(): piece = lax.ppermute(x, ('day', 'pt'), pairs)]
    all_gather x1 -> x0, blocking collectives: 5.97 us -> none  [shards(): day_pts = lax.all_gather(own_pts, 'pt', axis=1, tiled=True)]
    ppermute x12, waiting for transfers between devices: 1.97 us -> 6.31 us  [swap_blocks(): lax.ppermute(piece, 'pt', [(i, (i + shift) % count) for i in range(count)])]
    ppermute x12, starting transfers between devices: 11.5 us -> 9.79 us  [swap_blocks(): lax.ppermute(piece, 'pt', [(i, (i + shift) % count) for i in range(count)])]
    ppermute x1 -> x7, waiting for transfers between devices: 2.23 us -> 0.57 us  [the longest x4 0.56 us: gather_over_pt(): piece = lax.ppermute(x, ('day', 'pt'), pairs)]
    ppermute x7, starting transfers between devices: 8.24 us -> 6.72 us  [shards(): incoming = lax.ppermute(outgoing, 'day', route)]
  transfers between devices with their start and end apart: 22 -> 28, of which waited for: 6 -> 8; matrix products, arithmetic and copies ran while one was open for 12% -> 13% of each run, Pallas kernels for 0% -> 0%
where the time goes in v11:
time: 104 us
  starting transfers between devices  35.1 us (34%)
  waiting for transfers between devices  31.8 us (31%)
  matrix products  20.6 us (20%)
  other arithmetic  10.1 us (10%)
  local copies, waits for them, and re-layouts  3.15 us (3%)
  between operations  2.78 us (3%)
    ppermute x7, waiting for transfers between devices, shards(): incoming = lax.ppermute(outgoing, 'day', route)  15.6 us
    ppermute x4, starting transfers between devices, gather_over_pt(): piece = lax.ppermute(x, ('day', 'pt'), pairs)  13.4 us
    dot_general x3, matrix products, squared_dist(): lax.dot_general(left_pts, right_pts, (((0,), (0,)), ((), ())), preferred_...  11.5 us
    ppermute x12, starting transfers between devices, swap_blocks(): lax.ppermute(piece, 'pt', [(i, (i + shift) % count) for i in range(count)])  9.79 us
    ppermute x1, waiting for transfers between devices, shards(): lax.ppermute(later_pts, 'day', [(d + 1, d) for d in range(half)])  9.23 us
    dot_general x7, matrix products, shards(): jnp.dot(incoming, kernel, preferred_element_type=jnp.float32)  9.15 us
    ppermute x7, starting transfers between devices, shards(): incoming = lax.ppermute(outgoing, 'day', route)  6.72 us
    ppermute x12, waiting for transfers between devices, swap_blocks(): lax.ppermute(piece, 'pt', [(i, (i + shift) % count) for i in range(count)])  6.31 us
  transfers between devices with their start and end apart: 28, of which 8 were waited for; matrix products, arithmetic and copies ran while one was open for 13% of the time, Pallas kernels for 0%

profile of v11, /device:TPU:0, one launch (start us, length us, event | category | flops | bytes accessed | tf_op | source)
XLA Modules:
  0.0 103.6 jit_solution(13592853995756985953)
XLA Ops:
  0.6 2.5 %collective-permute-start = (bf16[64,512]{1,0:T(8,128)(2,1)}, bf16[64,512]{1,0:T(8,128)(2,1)S(1)}, u32[]{:S(2)}, u32[]{:S(2)}) collective-permute-start(bf16[64,512]{1,0:T(8,128)(2,1)} %bitcast.73), channel_id=1, source_target_pairs={{1,0},{2,1},{3,2},{0,3},{5,4},{6,5},{7,6},{4,7},{9,8},{10,9},{11,1... | collective-permute-start | bytes 196616 | tf_op jit(solution)/shard_map/ppermute | solution.py:35
  3.9 3.4 %collective-permute-start.7 = (bf16[64,512]{1,0:T(8,128)(2,1)}, bf16[64,512]{1,0:T(8,128)(2,1)S(1)}, u32[]{:S(2)}, u32[]{:S(2)}) collective-permute-start(bf16[64,512]{1,0:T(8,128)(2,1)} %bitcast.76), channel_id=1, source_target_pairs={{0,4},{1,5},{2,6},{3,7},{4,8},{5,9},{6,10},{7,11},{8,12},{9,13},{1... | collective-permute-start | bytes 196616 | tf_op jit(solution)/shard_map/ppermute | solution.py:44
  7.4 0.9 bitcast_multiply_fusion
  8.4 1.1 %collective-permute-start.3 = (f32[16,512]{1,0:T(8,128)S(1)}, f32[16,512]{1,0:T(8,128)S(1)}, u32[]{:S(2)}, u32[]{:S(2)}) collective-permute-start(f32[16,512]{1,0:T(8,128)S(1)} %get-tuple-element.21), channel_id=1, source_target_pairs={{0,1},{1,2},{2,3},{3,0},{4,5},{5,6},{6,7},{7,4},{8,9},{9,10},{10,1... | collective-permute-start | bytes 98312 | tf_op jit(solution)/shard_map/ppermute | solution.py:22
  11.8 1.2 %collective-permute-start.4 = (f32[16,512]{1,0:T(8,128)S(1)}, f32[16,512]{1,0:T(8,128)S(1)}, u32[]{:S(2)}, u32[]{:S(2)}) collective-permute-start(f32[16,512]{1,0:T(8,128)S(1)} %get-tuple-element.20), channel_id=1, source_target_pairs={{0,2},{1,3},{2,0},{3,1},{4,6},{5,7},{6,4},{7,5},{8,10},{9,11},{10,... | collective-permute-start | bytes 98312 | tf_op jit(solution)/shard_map/ppermute | solution.py:22
  13.0 2.7 %collective-permute-done.4 = f32[16,512]{1,0:T(8,128)S(1)} collective-permute-done((f32[16,512]{1,0:T(8,128)S(1)}, f32[16,512]{1,0:T(8,128)S(1)}, u32[]{:S(2)}, u32[]{:S(2)}) %collective-permute-start.4) | collective-permute-done | bytes 32800 | tf_op jit(solution)/shard_map/ppermute | solution.py:22
  15.7 1.6 %collective-permute-done.5 = f32[16,512]{1,0:T(8,128)S(1)} collective-permute-done((f32[16,512]{1,0:T(8,128)S(1)}, f32[16,512]{1,0:T(8,128)S(1)}, u32[]{:S(2)}, u32[]{:S(2)}) %collective-permute-start.5) | collective-permute-done | bytes 32800 | tf_op jit(solution)/shard_map/ppermute | solution.py:22
  17.3 4.6 %collective-permute-start.8 = (bf16[64,512]{1,0:T(8,128)(2,1)}, bf16[64,512]{1,0:T(8,128)(2,1)S(1)}, u32[]{:S(2)}, u32[]{:S(2)}) collective-permute-start(bf16[64,512]{1,0:T(8,128)(2,1)} %bitcast.77), channel_id=1, source_target_pairs={{1,4},{2,5},{3,6},{0,7},{5,8},{6,9},{7,10},{4,11},{9,12},{10,13},{... | collective-permute-start | bytes 196616 | tf_op jit(solution)/shard_map/ppermute | solution.py:44
  22.0 4.1 %collective-permute-start.9 = (bf16[64,512]{1,0:T(8,128)(2,1)}, bf16[64,512]{1,0:T(8,128)(2,1)S(1)}, u32[]{:S(2)}, u32[]{:S(2)}) collective-permute-start(bf16[64,512]{1,0:T(8,128)(2,1)} %bitcast.78), channel_id=1, source_target_pairs={{2,4},{3,5},{0,6},{1,7},{6,8},{7,9},{4,10},{5,11},{10,12},{11,13},... | collective-permute-start | bytes 196616 | tf_op jit(solution)/shard_map/ppermute | solution.py:44
  26.1 1.3 %collective-permute-start.10 = (bf16[64,512]{1,0:T(8,128)(2,1)}, bf16[64,512]{1,0:T(8,128)(2,1)S(1)}, u32[]{:S(2)}, u32[]{:S(2)}) collective-permute-start(bf16[64,512]{1,0:T(8,128)(2,1)} %bitcast.79), channel_id=1, source_target_pairs={{3,4},{0,5},{1,6},{2,7},{7,8},{4,9},{5,10},{6,11},{11,12},{8,13},{... | collective-permute-start | bytes 196616 | tf_op jit(solution)/shard_map/ppermute | solution.py:44
  27.4 1.9 %collective-permute-start.6 = (bf16[16,2048]{1,0:T(8,128)(2,1)S(1)}, bf16[16,2048]{1,0:T(8,128)(2,1)S(1)}, u32[]{:S(2)}, u32[]{:S(2)}) collective-permute-start(bf16[16,2048]{1,0:T(8,128)(2,1)S(1)} %fusion.11), channel_id=1, source_target_pairs={{0,4},{28,24},{1,5},{29,25},{2,6},{30,26},{3,7},{31,27}} | collective-permute-start | bytes 196616 | tf_op jit(solution)/shard_map/ppermute | solution.py:125
  30.2 3.6 %exponential_convert_fusion.1 = bf16[2048,2048]{1,0:T(8,128)(2,1)S(1)} fusion(bf16[64,2048]{1,0:T(8,128)(2,1)S(1)} %constant_dynamic-update-slice_fusion.3, bf16[64,2048]{1,0:T(8,128)(2,1)S(1)} %constant_dynamic-update-slice_fusion.10, f32[2048]{0:T(1024)S(1)} %multiply_reduce_fusion.4, f32[2048]{0:T(1024)S(1)} %multiply_reduce_fusion.5), kind=kOutput, calls=%fused_computation.4 | convolution fusion | flops 557842432 | bytes 8929280 | tf_op jit(solution)/shard_map/dot_general | solution.py:69
  33.8 1.3 %fusion.18 = (f32[16]{0:T(128)S(1)}, f32[16,2048]{1,0:T(8,128)S(1)}) fusion(f32[2048]{0:T(1024)S(1)} %fusion.13, bf16[16,2048]{1,0:T(8,128)(2,1)S(1)} %collective-permute-done.6, bf16[2048,2048]{1,0:T(8,128)(2,1)S(1)} %exponential_convert_fusion.1), kind=kOutput, calls=%fused_computation.96 | convolution fusion | flops 134283248 | bytes 8593472 | tf_op jit(solution)/shard_map/dot_general | solution.py:126
  36.1 1.3 %fusion.19 = (f32[16]{0:T(128)S(1)}, f32[16,2048]{1,0:T(8,128)S(1)}) fusion(f32[2048]{0:T(1024)S(1)} %fusion.13, bf16[16,2048]{1,0:T(8,128)(2,1)S(1)} %collective-permute-done.11, bf16[2048,2048]{1,0:T(8,128)(2,1)S(1)} %exponential_convert_fusion.1), kind=kOutput, calls=%fused_computation.97 | convolution fusion | flops 134283248 | bytes 8593472 | tf_op jit(solution)/shard_map/dot_general | solution.py:126
  38.4 1.3 %collective-permute-start.14 = (bf16[64,2048]{1,0:T(8,128)(2,1)S(1)}, bf16[64,2048]{1,0:T(8,128)(2,1)S(1)}, u32[]{:S(2)}, u32[]{:S(2)}) collective-permute-start(bf16[64,2048]{1,0:T(8,128)(2,1)S(1)} %constant_dynamic-update-slice_fusion.10), channel_id=1, source_target_pairs={{4,0},{8,4},{12,8},{16,12},{5,1},{9,5},{13,9},{17,13},{6,2},{10,6}... | collective-permute-start | bytes 786440 | tf_op jit(solution)/shard_map/ppermute | solution.py:113
  40.4 1.3 %fusion.20 = (f32[16]{0:T(128)S(1)}, f32[16,2048]{1,0:T(8,128)S(1)}) fusion(f32[2048]{0:T(1024)S(1)} %fusion.13, bf16[16,2048]{1,0:T(8,128)(2,1)S(1)} %collective-permute-done.12, bf16[2048,2048]{1,0:T(8,128)(2,1)S(1)} %exponential_convert_fusion.1), kind=kOutput, calls=%fused_computation.98 | convolution fusion | flops 134283248 | bytes 8593472 | tf_op jit(solution)/shard_map/dot_general | solution.py:126
  42.6 9.2 %collective-permute-done.14 = bf16[64,2048]{1,0:T(8,128)(2,1)S(1)} collective-permute-done((bf16[64,2048]{1,0:T(8,128)(2,1)S(1)}, bf16[64,2048]{1,0:T(8,128)(2,1)S(1)}, u32[]{:S(2)}, u32[]{:S(2)}) %collective-permute-start.14) | collective-permute-done | bytes 262176 | tf_op jit(solution)/shard_map/ppermute | solution.py:113
  52.0 3.6 %exponential_convert_fusion = bf16[2048,2048]{1,0:T(8,128)(2,1)S(1)} fusion(bf16[64,2048]{1,0:T(8,128)(2,1)S(1)} %broadcast_select_fusion, bf16[64,2048]{1,0:T(8,128)(2,1)S(1)} %constant_dynamic-update-slice_fusion.10, f32[2048]{0:T(1024)S(1)} %multiply_reduce_fusion.3, f32[2048]{0:T(1024)S(1)} %multiply_reduce_fusion.4), kind=kOutput, calls=%fused_computation.3 | convolution fusion | flops 557842432 | bytes 8929280 | tf_op jit(solution)/shard_map/dot_general | solution.py:69
  55.6 1.3 %fusion.21 = (f32[16]{0:T(128)S(1)}, f32[16,2048]{1,0:T(8,128)S(1)}) fusion(f32[2048]{0:T(1024)S(1)} %fusion.13, bf16[16,2048]{1,0:T(8,128)(2,1)S(1)} %collective-permute-done.13, bf16[2048,2048]{1,0:T(8,128)(2,1)S(1)} %exponential_convert_fusion), kind=kOutput, calls=%fused_computation.99 | convolution fusion | flops 134283248 | bytes 8593472 | tf_op jit(solution)/shard_map/dot_general | solution.py:126
  57.9 1.3 %fusion.22 = (f32[16]{0:T(128)S(1)}, f32[16,2048]{1,0:T(8,128)S(1)}) fusion(f32[2048]{0:T(1024)S(1)} %fusion.13, bf16[16,2048]{1,0:T(8,128)(2,1)S(1)} %collective-permute-done.16, bf16[2048,2048]{1,0:T(8,128)(2,1)S(1)} %exponential_convert_fusion), kind=kOutput, calls=%fused_computation.100 | convolution fusion | flops 134283248 | bytes 8593472 | tf_op jit(solution)/shard_map/dot_general | solution.py:126
  60.4 1.3 %fusion.23 = (f32[16]{0:T(128)S(1)}, f32[16,2048]{1,0:T(8,128)S(1)}) fusion(f32[2048]{0:T(1024)S(1)} %fusion.13, bf16[16,2048]{1,0:T(8,128)(2,1)S(1)} %collective-permute-done.17, bf16[2048,2048]{1,0:T(8,128)(2,1)S(1)} %exponential_convert_fusion), kind=kOutput, calls=%fused_computation.101 | convolution fusion | flops 134283248 | bytes 8593472 | tf_op jit(solution)/shard_map/dot_general | solution.py:126
  61.9 1.3 %collective-permute-start.18 = (bf16[16,2048]{1,0:T(8,128)(2,1)S(1)}, bf16[16,2048]{1,0:T(8,128)(2,1)S(1)}, u32[]{:S(2)}, u32[]{:S(2)}) collective-permute-start(bf16[16,2048]{1,0:T(8,128)(2,1)S(1)} %fusion.5), channel_id=1, source_target_pairs={{24,28},{4,0},{25,29},{5,1},{26,30},{6,2},{27,31},{7,3}} | collective-permute-start | bytes 196616 | tf_op jit(solution)/shard_map/ppermute | solution.py:125
  63.3 15.6 %collective-permute-done.18 = bf16[16,2048]{1,0:T(8,128)(2,1)S(1)} collective-permute-done((bf16[16,2048]{1,0:T(8,128)(2,1)S(1)}, bf16[16,2048]{1,0:T(8,128)(2,1)S(1)}, u32[]{:S(2)}, u32[]{:S(2)}) %collective-permute-start.18) | collective-permute-done | bytes 65568 | tf_op jit(solution)/shard_map/ppermute | solution.py:125
  78.9 1.3 %fusion.24 = (f32[16]{0:T(128)S(1)}, f32[16,2048]{1,0:T(8,128)S(1)}) fusion(f32[2048]{0:T(1024)S(1)} %fusion.13, bf16[16,2048]{1,0:T(8,128)(2,1)S(1)} %collective-permute-done.18, bf16[2048,2048]{1,0:T(8,128)(2,1)S(1)} %exponential_convert_fusion), kind=kOutput, calls=%fused_computation.102 | convolution fusion | flops 134283248 | bytes 8593472 | tf_op jit(solution)/shard_map/dot_general | solution.py:126
  80.6 1.0 collective-permute-start.23
  81.6 1.4 %collective-permute-start.24 = (f32[1,2048]{1,0:T(1,128)S(1)}, f32[1,2048]{1,0:T(1,128)S(1)}, u32[]{:S(2)}, u32[]{:S(2)}) collective-permute-start(f32[1,2048]{1,0:T(1,128)S(1)} %bitcast.82), channel_id=1, source_target_pairs={{0,3},{1,0},{2,1},{3,2},{4,7},{5,4},{6,5},{7,6},{8,11},{9,8},{10,9... | collective-permute-start | bytes 24584 | tf_op jit(solution)/shard_map/ppermute | solution.py:22
  85.2 4.3 %multiply_reduce_fusion.1 = (f32[2048]{0:T(1024)S(1)}, f32[2048,2048]{1,0:T(8,128)S(1)}) fusion(f32[2048]{0:T(1024)S(1)} %get-tuple-element.10, f32[2048]{0:T(1024)S(1)} %multiply_reduce_fusion.2, f32[2048]{0:T(1024)S(1)} %multiply_reduce_fusion.4, bf16[64,2048]{1,0:T(8,128)(2,1)S(1)} %constant_dynamic-update-slice_fusion.10, ...), kind=kOutput, calls=%fused_computation.1 | convolution fusion | flops 562034688 | bytes 17334272 | tf_op jit(solution)/shard_map/dot_general | solution.py:69
  90.2 4.9 %multiply_reduce_fusion = f32[2048]{0:T(1024)S(1)} fusion(f32[2048,2048]{1,0:T(8,128)S(1)} %get-tuple-element.42, f32[2048]{0:T(1024)S(1)} %select_divide_fusion, f32[2048]{0:T(1024)S(1)} %multiply_reduce_fusion.2, f32[2048]{0:T(1024)S(1)} %multiply_reduce_fusion.4), kind=kLoop, calls=%fused_computation | loop fusion | flops 25163776 | bytes 16809984 | tf_op jit(solution)/shard_map/reduce_sum | solution.py:149
  95.3 1.0 collective-permute-start.25
  97.8 1.1 %collective-permute-start.20 = (f32[2,16,512]{2,1,0:T(8,128)S(1)}, f32[2,16,512]{2,1,0:T(8,128)S(1)}, u32[]{:S(2)}, u32[]{:S(2)}) collective-permute-start(f32[2,16,512]{2,1,0:T(8,128)S(1)} %get-tuple-element.16), channel_id=1, source_target_pairs={{0,2},{1,3},{2,0},{3,1},{4,6},{5,7},{6,4},{7,5},{8,10},{9,11},{10,... | collective-permute-start | bytes 196616 | tf_op jit(solution)/shard_map/ppermute | solution.py:22
  99.0 1.4 %collective-permute-start.21 = (f32[2,16,512]{2,1,0:T(8,128)S(1)}, f32[2,16,512]{2,1,0:T(8,128)S(1)}, u32[]{:S(2)}, u32[]{:S(2)}) collective-permute-start(f32[2,16,512]{2,1,0:T(8,128)S(1)} %get-tuple-element.15), channel_id=1, source_target_pairs={{0,3},{1,0},{2,1},{3,2},{4,7},{5,4},{6,5},{7,6},{8,11},{9,8},{10,9... | collective-permute-start | bytes 196616 | tf_op jit(solution)/shard_map/ppermute | solution.py:22
  101.7 1.1 %collective-permute-done.20 = f32[2,16,512]{2,1,0:T(8,128)S(1)} collective-permute-done((f32[2,16,512]{2,1,0:T(8,128)S(1)}, f32[2,16,512]{2,1,0:T(8,128)S(1)}, u32[]{:S(2)}, u32[]{:S(2)}) %collective-permute-start.20) | collective-permute-done | bytes 65568 | tf_op jit(solution)/shard_map/ppermute | solution.py:22
  (111 shorter events, 15.5 us)
Async XLA Ops:
  0.6 21.3 %collective-permute-start = (bf16[64,512]{1,0:T(8,128)(2,1)}, bf16[64,512]{1,0:T(8,128)(2,1)S(1)}, u32[]{:S(2)}, u32[]{:S(2)}) collective-permute-start(bf16[64,512]{1,0:T(8,128)(2,1)} %bitcast.73), channel_id=1, source_target_pairs={{1,0},{2,1},{3,2},{0,3},{5,4},{6,5},{7,6},{4,7},{9,8},{10,9},{11,1... | collective-permute-start | bytes 196616 | tf_op jit(solution)/shard_map/ppermute | solution.py:35
  3.1 23.0 %collective-permute-start.1 = (bf16[64,512]{1,0:T(8,128)(2,1)}, bf16[64,512]{1,0:T(8,128)(2,1)S(1)}, u32[]{:S(2)}, u32[]{:S(2)}) collective-permute-start(bf16[64,512]{1,0:T(8,128)(2,1)} %bitcast.74), channel_id=1, source_target_pairs={{2,0},{3,1},{0,2},{1,3},{6,4},{7,5},{4,6},{5,7},{10,8},{11,9},{8,1... | collective-permute-start | bytes 196616 | tf_op jit(solution)/shard_map/ppermute | solution.py:35
  3.8 23.7 %collective-permute-start.2 = (bf16[64,512]{1,0:T(8,128)(2,1)}, bf16[64,512]{1,0:T(8,128)(2,1)S(1)}, u32[]{:S(2)}, u32[]{:S(2)}) collective-permute-start(bf16[64,512]{1,0:T(8,128)(2,1)} %bitcast.75), channel_id=1, source_target_pairs={{3,0},{0,1},{1,2},{2,3},{7,4},{4,5},{5,6},{6,7},{11,8},{8,9},{9,10... | collective-permute-start | bytes 196616 | tf_op jit(solution)/shard_map/ppermute | solution.py:35
  3.9 25.5 %collective-permute-start.7 = (bf16[64,512]{1,0:T(8,128)(2,1)}, bf16[64,512]{1,0:T(8,128)(2,1)S(1)}, u32[]{:S(2)}, u32[]{:S(2)}) collective-permute-start(bf16[64,512]{1,0:T(8,128)(2,1)} %bitcast.76), channel_id=1, source_target_pairs={{0,4},{1,5},{2,6},{3,7},{4,8},{5,9},{6,10},{7,11},{8,12},{9,13},{1... | collective-permute-start | bytes 196616 | tf_op jit(solution)/shard_map/ppermute | solution.py:44
  8.4 3.4 %collective-permute-start.3 = (f32[16,512]{1,0:T(8,128)S(1)}, f32[16,512]{1,0:T(8,128)S(1)}, u32[]{:S(2)}, u32[]{:S(2)}) collective-permute-start(f32[16,512]{1,0:T(8,128)S(1)} %get-tuple-element.21), channel_id=1, source_target_pairs={{0,1},{1,2},{2,3},{3,0},{4,5},{5,6},{6,7},{7,4},{8,9},{9,10},{10,1... | collective-permute-start | bytes 98312 | tf_op jit(solution)/shard_map/ppermute | solution.py:22
  11.8 3.9 %collective-permute-start.4 = (f32[16,512]{1,0:T(8,128)S(1)}, f32[16,512]{1,0:T(8,128)S(1)}, u32[]{:S(2)}, u32[]{:S(2)}) collective-permute-start(f32[16,512]{1,0:T(8,128)S(1)} %get-tuple-element.20), channel_id=1, source_target_pairs={{0,2},{1,3},{2,0},{3,1},{4,6},{5,7},{6,4},{7,5},{8,10},{9,11},{10,... | collective-permute-start | bytes 98312 | tf_op jit(solution)/shard_map/ppermute | solution.py:22
  15.7 1.6 %collective-permute-start.5 = (f32[16,512]{1,0:T(8,128)S(1)}, f32[16,512]{1,0:T(8,128)S(1)}, u32[]{:S(2)}, u32[]{:S(2)}) collective-permute-start(f32[16,512]{1,0:T(8,128)S(1)} %get-tuple-element.19), channel_id=1, source_target_pairs={{0,3},{1,0},{2,1},{3,2},{4,7},{5,4},{6,5},{7,6},{8,11},{9,8},{10,9... | collective-permute-start | bytes 98312 | tf_op jit(solution)/shard_map/ppermute | solution.py:22
  17.3 12.2 %collective-permute-start.8 = (bf16[64,512]{1,0:T(8,128)(2,1)}, bf16[64,512]{1,0:T(8,128)(2,1)S(1)}, u32[]{:S(2)}, u32[]{:S(2)}) collective-permute-start(bf16[64,512]{1,0:T(8,128)(2,1)} %bitcast.77), channel_id=1, source_target_pairs={{1,4},{2,5},{3,6},{0,7},{5,8},{6,9},{7,10},{4,11},{9,12},{10,13},{... | collective-permute-start | bytes 196616 | tf_op jit(solution)/shard_map/ppermute | solution.py:44
  22.0 7.6 %collective-permute-start.9 = (bf16[64,512]{1,0:T(8,128)(2,1)}, bf16[64,512]{1,0:T(8,128)(2,1)S(1)}, u32[]{:S(2)}, u32[]{:S(2)}) collective-permute-start(bf16[64,512]{1,0:T(8,128)(2,1)} %bitcast.78), channel_id=1, source_target_pairs={{2,4},{3,5},{0,6},{1,7},{6,8},{7,9},{4,10},{5,11},{10,12},{11,13},... | collective-permute-start | bytes 196616 | tf_op jit(solution)/shard_map/ppermute | solution.py:44
  26.1 4.0 %collective-permute-start.10 = (bf16[64,512]{1,0:T(8,128)(2,1)}, bf16[64,512]{1,0:T(8,128)(2,1)S(1)}, u32[]{:S(2)}, u32[]{:S(2)}) collective-permute-start(bf16[64,512]{1,0:T(8,128)(2,1)} %bitcast.79), channel_id=1, source_target_pairs={{3,4},{0,5},{1,6},{2,7},{7,8},{4,9},{5,10},{6,11},{11,12},{8,13},{... | collective-permute-start | bytes 196616 | tf_op jit(solution)/shard_map/ppermute | solution.py:44
  27.4 6.4 %collective-permute-start.6 = (bf16[16,2048]{1,0:T(8,128)(2,1)S(1)}, bf16[16,2048]{1,0:T(8,128)(2,1)S(1)}, u32[]{:S(2)}, u32[]{:S(2)}) collective-permute-start(bf16[16,2048]{1,0:T(8,128)(2,1)S(1)} %fusion.11), channel_id=1, source_target_pairs={{0,4},{28,24},{1,5},{29,25},{2,6},{30,26},{3,7},{31,27}} | collective-permute-start | bytes 196616 | tf_op jit(solution)/shard_map/ppermute | solution.py:125
  35.4 0.8 collective-permute-start.11
  37.7 2.7 %collective-permute-start.12 = (bf16[16,2048]{1,0:T(8,128)(2,1)S(1)}, bf16[16,2048]{1,0:T(8,128)(2,1)S(1)}, u32[]{:S(2)}, u32[]{:S(2)}) collective-permute-start(bf16[16,2048]{1,0:T(8,128)(2,1)S(1)} %fusion.9), channel_id=1, source_target_pairs={{8,12},{20,16},{9,13},{21,17},{10,14},{22,18},{11,15},{23,19}} | collective-permute-start | bytes 196616 | tf_op jit(solution)/shard_map/ppermute | solution.py:125
  38.4 13.4 %collective-permute-start.14 = (bf16[64,2048]{1,0:T(8,128)(2,1)S(1)}, bf16[64,2048]{1,0:T(8,128)(2,1)S(1)}, u32[]{:S(2)}, u32[]{:S(2)}) collective-permute-start(bf16[64,2048]{1,0:T(8,128)(2,1)S(1)} %constant_dynamic-update-slice_fusion.10), channel_id=1, source_target_pairs={{4,0},{8,4},{12,8},{16,12},{5,1},{9,5},{13,9},{17,13},{6,2},{10,6}... | collective-permute-start | bytes 786440 | tf_op jit(solution)/shard_map/ppermute | solution.py:113
  39.7 12.2 %collective-permute-start.15 = (bf16[64,2048]{1,0:T(8,128)(2,1)S(1)}, bf16[64,2048]{1,0:T(8,128)(2,1)S(1)}, u32[]{:S(2)}, u32[]{:S(2)}) collective-permute-start(bf16[64,2048]{1,0:T(8,128)(2,1)S(1)} %constant_dynamic-update-slice_fusion.10), channel_id=1, source_target_pairs={{12,16},{16,20},{20,24},{24,28},{13,17},{17,21},{21,25},{25,29},{1... | collective-permute-start | bytes 786440 | tf_op jit(solution)/shard_map/ppermute | solution.py:114
  41.9 13.6 %collective-permute-start.13 = (bf16[16,2048]{1,0:T(8,128)(2,1)S(1)}, bf16[16,2048]{1,0:T(8,128)(2,1)S(1)}, u32[]{:S(2)}, u32[]{:S(2)}) collective-permute-start(bf16[16,2048]{1,0:T(8,128)(2,1)S(1)} %fusion.8), channel_id=1, source_target_pairs={{12,16},{16,12},{13,17},{17,13},{14,18},{18,14},{15,19},{19,15}} | collective-permute-start | bytes 196616 | tf_op jit(solution)/shard_map/ppermute | solution.py:125
  56.9 26.0 %copy-start = (bf16[1,64,2048]{2,1,0:T(8,128)(2,1)S(1)}, bf16[1,64,2048]{2,1,0:T(8,128)(2,1)}, u32[]{:S(2)}) copy-start(bf16[1,64,2048]{2,1,0:T(8,128)(2,1)} %param.7) | copy-start | bytes 786436
  57.1 0.8 collective-permute-start.16
  59.4 0.9 collective-permute-start.17
  61.9 17.0 %collective-permute-start.18 = (bf16[16,2048]{1,0:T(8,128)(2,1)S(1)}, bf16[16,2048]{1,0:T(8,128)(2,1)S(1)}, u32[]{:S(2)}, u32[]{:S(2)}) collective-permute-start(bf16[16,2048]{1,0:T(8,128)(2,1)S(1)} %fusion.5), channel_id=1, source_target_pairs={{24,28},{4,0},{25,29},{5,1},{26,30},{6,2},{27,31},{7,3}} | collective-permute-start | bytes 196616 | tf_op jit(solution)/shard_map/ppermute | solution.py:125
  80.5 3.3 %collective-permute-start.22 = (f32[1,2048]{1,0:T(1,128)S(1)}, f32[1,2048]{1,0:T(1,128)S(1)}, u32[]{:S(2)}, u32[]{:S(2)}) collective-permute-start(f32[1,2048]{1,0:T(1,128)S(1)} %bitcast.80), channel_id=1, source_target_pairs={{0,1},{1,2},{2,3},{3,0},{4,5},{5,6},{6,7},{7,4},{8,9},{9,10},{10,1... | collective-permute-start | bytes 24584 | tf_op jit(solution)/shard_map/ppermute | solution.py:22
  80.6 3.8 %collective-permute-start.23 = (f32[1,2048]{1,0:T(1,128)S(1)}, f32[1,2048]{1,0:T(1,128)S(1)}, u32[]{:S(2)}, u32[]{:S(2)}) collective-permute-start(f32[1,2048]{1,0:T(1,128)S(1)} %bitcast.81), channel_id=1, source_target_pairs={{0,2},{1,3},{2,0},{3,1},{4,6},{5,7},{6,4},{7,5},{8,10},{9,11},{10,... | collective-permute-start | bytes 24584 | tf_op jit(solution)/shard_map/ppermute | solution.py:22
  81.6 2.9 %collective-permute-start.24 = (f32[1,2048]{1,0:T(1,128)S(1)}, f32[1,2048]{1,0:T(1,128)S(1)}, u32[]{:S(2)}, u32[]{:S(2)}) collective-permute-start(f32[1,2048]{1,0:T(1,128)S(1)} %bitcast.82), channel_id=1, source_target_pairs={{0,3},{1,0},{2,1},{3,2},{4,7},{5,4},{6,5},{7,6},{8,11},{9,8},{10,9... | collective-permute-start | bytes 24584 | tf_op jit(solution)/shard_map/ppermute | solution.py:22
  95.3 3.7 %collective-permute-start.25 = (f32[512]{0:T(512)S(1)}, f32[512]{0:T(512)S(1)}, u32[]{:S(2)}, u32[]{:S(2)}) collective-permute-start(f32[512]{0:T(512)S(1)} %get-tuple-element.25), channel_id=1, source_target_pairs={{0,1},{1,2},{2,3},{3,0},{4,5},{5,6},{6,7},{7,4},{8,9},{9,10},{10,1... | collective-permute-start | bytes 6152 | tf_op jit(solution)/shard_map/ppermute | solution.py:22
  96.3 4.3 %collective-permute-start.26 = (f32[512]{0:T(512)S(1)}, f32[512]{0:T(512)S(1)}, u32[]{:S(2)}, u32[]{:S(2)}) collective-permute-start(f32[512]{0:T(512)S(1)} %get-tuple-element.24), channel_id=1, source_target_pairs={{0,2},{1,3},{2,0},{3,1},{4,6},{5,7},{6,4},{7,5},{8,10},{9,11},{10,... | collective-permute-start | bytes 6152 | tf_op jit(solution)/shard_map/ppermute | solution.py:22
  97.2 3.6 %collective-permute-start.27 = (f32[512]{0:T(512)S(1)}, f32[512]{0:T(512)S(1)}, u32[]{:S(2)}, u32[]{:S(2)}) collective-permute-start(f32[512]{0:T(512)S(1)} %get-tuple-element.23), channel_id=1, source_target_pairs={{0,3},{1,0},{2,1},{3,2},{4,7},{5,4},{6,5},{7,6},{8,11},{9,8},{10,9... | collective-permute-start | bytes 6152 | tf_op jit(solution)/shard_map/ppermute | solution.py:22
  97.8 3.9 %collective-permute-start.19 = (f32[2,16,512]{2,1,0:T(8,128)S(1)}, f32[2,16,512]{2,1,0:T(8,128)S(1)}, u32[]{:S(2)}, u32[]{:S(2)}) collective-permute-start(f32[2,16,512]{2,1,0:T(8,128)S(1)} %get-tuple-element.17), channel_id=1, source_target_pairs={{0,1},{1,2},{2,3},{3,0},{4,5},{5,6},{6,7},{7,4},{8,9},{9,10},{10,1... | collective-permute-start | bytes 196616 | tf_op jit(solution)/shard_map/ppermute | solution.py:22
  97.8 5.0 %collective-permute-start.20 = (f32[2,16,512]{2,1,0:T(8,128)S(1)}, f32[2,16,512]{2,1,0:T(8,128)S(1)}, u32[]{:S(2)}, u32[]{:S(2)}) collective-permute-start(f32[2,16,512]{2,1,0:T(8,128)S(1)} %get-tuple-element.16), channel_id=1, source_target_pairs={{0,2},{1,3},{2,0},{3,1},{4,6},{5,7},{6,4},{7,5},{8,10},{9,11},{10,... | collective-permute-start | bytes 196616 | tf_op jit(solution)/shard_map/ppermute | solution.py:22
  99.0 3.8 %collective-permute-start.21 = (f32[2,16,512]{2,1,0:T(8,128)S(1)}, f32[2,16,512]{2,1,0:T(8,128)S(1)}, u32[]{:S(2)}, u32[]{:S(2)}) collective-permute-start(f32[2,16,512]{2,1,0:T(8,128)S(1)} %get-tuple-element.15), channel_id=1, source_target_pairs={{0,3},{1,0},{2,1},{3,2},{4,7},{5,4},{6,5},{7,6},{8,11},{9,8},{10,9... | collective-permute-start | bytes 196616 | tf_op jit(solution)/shard_map/ppermute | solution.py:22

commit v12 on v10

--- a/solution.py
+++ b/solution.py
@@ -21,6 +21,22 @@
         if shift:
             piece = lax.ppermute(piece, "pt", [(i, (i + shift) % count) for i in range(count)])
         out = lax.dynamic_update_slice_in_dim(out, piece, ((rank - shift) % count) * put, put_axis)
+    return out
+
+
+def gather_over_pt(x, axis):
+    count = lax.axis_size("pt")
+    rank = lax.axis_index("pt")
+    shape = list(x.shape)
+    shape[axis] *= count
+    out = jnp.zeros(shape, x.dtype)
+    for shift in range(count):
+        piece = x if shift == 0 else lax.ppermute(
+            x, "pt", [((i + shift) % count, i) for i in range(count)]
+        )
+        out = lax.dynamic_update_slice_in_dim(
+            out, piece, ((rank + shift) % count) * x.shape[axis], axis
+        )
     return out
 
 
@@ -74,7 +90,7 @@
     first_route = [(d - 1, d) for d in range(1, half)]
     first_route += [(d + 1, d) for d in range(half, day_count - 1)]
     first_quarter = lax.ppermute(own_pts, "day", first_route)
-    first_kernel = chain_kernel(lax.all_gather(first_quarter, "pt", axis=1, tiled=True))
+    first_kernel = chain_kernel(gather_over_pt(first_quarter, 1))
 
     def settle(values):
         masked = values * live_all[None, :]

time: 97.9 us -> 96.4 us (0.985)
  blocking collectives: 11.8 us -> 5.99 us
  starting transfers between devices: 25.1 us -> 27.4 us
  waiting for transfers between devices: 25 us -> 27 us
    all_gather x1 -> x0, blocking collectives: 5.78 us -> none  [shards(): lax.all_gather(first_quarter, 'pt', axis=1, tiled=True)]
    ppermute x0 -> x3, waiting for transfers between devices: none -> 4.15 us  [gather_over_pt(): lax.ppermute(x, 'pt', [((i + shift) % count, i) for i in range(count)])]
    ppermute x0 -> x3, starting transfers between devices: none -> 1.75 us  [gather_over_pt(): lax.ppermute(x, 'pt', [((i + shift) % count, i) for i in range(count)])]
    ppermute x1, waiting for transfers between devices: 7 us -> 5.31 us  [shards(): lax.ppermute(later_pts, 'day', [(d + 1, d) for d in range(half)])]
  transfers between devices with their start and end apart: 22 -> 25, of which waited for: 5 -> 7; matrix products, arithmetic and copies ran while one was open for 12% -> 12% of each run, Pallas kernels for 0% -> 0%
where the time goes in v12:
time: 96.4 us; the launch traced here: 96.1 us
  starting transfers between devices  27.4 us (28%)
  waiting for transfers between devices  27 us (28%)
  matrix products  20.6 us (21%)
  other arithmetic  10.1 us (10%)
  blocking collectives  5.99 us (6%)
  between operations  2.71 us (3%)
  local copies, waits for them, and re-layouts  2.25 us (2%)
    ppermute x7, waiting for transfers between devices, shards(): incoming = lax.ppermute(outgoing, 'day', route)  16 us
    ppermute x12, starting transfers between devices, swap_blocks(): lax.ppermute(piece, 'pt', [(i, (i + shift) % count) for i in range(count)])  12 us
    dot_general x3, matrix products, squared_dist(): lax.dot_general(left_pts, right_pts, (((0,), (0,)), ((), ())), preferred_...  11.5 us
    dot_general x7, matrix products, shards(): jnp.dot(incoming, kernel, preferred_element_type=jnp.float32)  9.15 us
    ppermute x7, starting transfers between devices, shards(): incoming = lax.ppermute(outgoing, 'day', route)  8.25 us
    all_gather x1, blocking collectives, shards(): day_pts = lax.all_gather(own_pts, 'pt', axis=1, tiled=True)  5.99 us
    ppermute x1, waiting for transfers between devices, shards(): lax.ppermute(later_pts, 'day', [(d + 1, d) for d in range(half)])  5.31 us
    reduce_sum x1, other arithmetic, shards(): ratio_rows = jnp.sum(fit_kernel * inverse[None, :], axis=1)  4.9 us
  transfers between devices with their start and end apart: 25, of which 7 were waited for; matrix products, arithmetic and copies ran while one was open for 12% of the time, Pallas kernels for 0%

profile of v12, /device:TPU:0, one launch (start us, length us, event | category | flops | bytes accessed | tf_op | source)
XLA Modules:
  0.0 96.1 jit_solution(8470221108973929365)
XLA Ops:
  0.7 0.9 bitcast_multiply_fusion
  2.2 2.6 %collective-permute-start.1 = (f32[16,512]{1,0:T(8,128)S(1)}, f32[16,512]{1,0:T(8,128)S(1)}, u32[]{:S(2)}, u32[]{:S(2)}) collective-permute-start(f32[16,512]{1,0:T(8,128)S(1)} %get-tuple-element.20), channel_id=1, source_target_pairs={{0,2},{1,3},{2,0},{3,1},{4,6},{5,7},{6,4},{7,5},{8,10},{9,11},{10,... | collective-permute-start | bytes 98312 | tf_op jit(solution)/shard_map/ppermute | solution.py:22
  4.8 1.4 %collective-permute-start.2 = (f32[16,512]{1,0:T(8,128)S(1)}, f32[16,512]{1,0:T(8,128)S(1)}, u32[]{:S(2)}, u32[]{:S(2)}) collective-permute-start(f32[16,512]{1,0:T(8,128)S(1)} %get-tuple-element.19), channel_id=1, source_target_pairs={{0,3},{1,0},{2,1},{3,2},{4,7},{5,4},{6,5},{7,6},{8,11},{9,8},{10,9... | collective-permute-start | bytes 98312 | tf_op jit(solution)/shard_map/ppermute | solution.py:22
  6.2 3.4 %collective-permute-start.4 = (bf16[64,512]{1,0:T(8,128)(2,1)}, bf16[64,512]{1,0:T(8,128)(2,1)S(1)}, u32[]{:S(2)}, u32[]{:S(2)}) collective-permute-start(bf16[64,512]{1,0:T(8,128)(2,1)} %bitcast.81), channel_id=1, source_target_pairs={{0,4},{4,8},{8,12},{20,16},{24,20},{28,24},{1,5},{5,9},{9,13},{21,... | collective-permute-start | bytes 196616 | tf_op jit(solution)/shard_map/ppermute | solution.py:92
  9.6 6.0 %all-gather = bf16[1,64,2048]{2,1,0:T(8,128)(2,1)S(1)} all-gather(bf16[1,64,512]{2,1,0:T(8,128)(2,1)} %param.6), channel_id=2, replica_groups=mesh['day'=8,'pt'=4] {'pt'}, dimensions={2}, use_global_device_ids=true | all-gather | bytes 327680 | tf_op jit(solution)/shard_map/all_gather | solution.py:73
  16.6 3.5 %collective-permute-start.3 = (bf16[16,2048]{1,0:T(8,128)(2,1)S(1)}, bf16[16,2048]{1,0:T(8,128)(2,1)S(1)}, u32[]{:S(2)}, u32[]{:S(2)}) collective-permute-start(bf16[16,2048]{1,0:T(8,128)(2,1)S(1)} %fusion.11), channel_id=1, source_target_pairs={{0,4},{28,24},{1,5},{29,25},{2,6},{30,26},{3,7},{31,27}} | collective-permute-start | bytes 196616 | tf_op jit(solution)/shard_map/ppermute | solution.py:118
  20.3 1.5 %collective-permute-start.6 = (bf16[64,512]{1,0:T(8,128)(2,1)S(1)}, bf16[64,512]{1,0:T(8,128)(2,1)S(1)}, u32[]{:S(2)}, u32[]{:S(2)}) collective-permute-start(bf16[64,512]{1,0:T(8,128)(2,1)S(1)} %collective-permute-done.4), channel_id=1, source_target_pairs={{2,0},{3,1},{0,2},{1,3},{6,4},{7,5},{4,6},{5,7},{10,8},{11,9},{8,1... | collective-permute-start | bytes 196616 | tf_op jit(solution)/shard_map/ppermute | solution.py:34
  21.9 0.8 collective-permute-done.5
  22.7 3.2 %collective-permute-done.6 = bf16[64,512]{1,0:T(8,128)(2,1)S(1)} collective-permute-done((bf16[64,512]{1,0:T(8,128)(2,1)S(1)}, bf16[64,512]{1,0:T(8,128)(2,1)S(1)}, u32[]{:S(2)}, u32[]{:S(2)}) %collective-permute-start.6) | collective-permute-done | bytes 65568 | tf_op jit(solution)/shard_map/ppermute | solution.py:34
  26.1 3.6 %exponential_convert_fusion.1 = bf16[2048,2048]{1,0:T(8,128)(2,1)S(1)} fusion(bf16[64,2048]{1,0:T(8,128)(2,1)S(1)} %constant_dynamic-update-slice_fusion.3, f32[2048]{0:T(1024)S(1)} %multiply_reduce_fusion.4, f32[2048]{0:T(1024)S(1)} %multiply_reduce_fusion.5, bf16[1,64,2048]{2,1,0:T(8,128)(2,1)S(1)} %all-gather), kind=kOutput, calls=%fused_computation.4 | convolution fusion | flops 557842432 | bytes 8929280 | tf_op jit(solution)/shard_map/dot_general | solution.py:61
  29.8 1.3 %fusion.21 = (f32[16]{0:T(128)S(1)}, f32[16,2048]{1,0:T(8,128)S(1)}) fusion(f32[2048]{0:T(1024)S(1)} %fusion.13, bf16[16,2048]{1,0:T(8,128)(2,1)S(1)} %collective-permute-done.3, bf16[2048,2048]{1,0:T(8,128)(2,1)S(1)} %exponential_convert_fusion.1), kind=kOutput, calls=%fused_computation.95 | convolution fusion | flops 134283248 | bytes 8593472 | tf_op jit(solution)/shard_map/dot_general | solution.py:119
  32.1 1.3 %fusion.22 = (f32[16]{0:T(128)S(1)}, f32[16,2048]{1,0:T(8,128)S(1)}) fusion(f32[2048]{0:T(1024)S(1)} %fusion.13, bf16[16,2048]{1,0:T(8,128)(2,1)S(1)} %collective-permute-done.8, bf16[2048,2048]{1,0:T(8,128)(2,1)S(1)} %exponential_convert_fusion.1), kind=kOutput, calls=%fused_computation.96 | convolution fusion | flops 134283248 | bytes 8593472 | tf_op jit(solution)/shard_map/dot_general | solution.py:119
  34.4 1.3 %collective-permute-start.11 = (bf16[64,2048]{1,0:T(8,128)(2,1)S(1)}, bf16[64,2048]{1,0:T(8,128)(2,1)S(1)}, u32[]{:S(2)}, u32[]{:S(2)}) collective-permute-start(bf16[64,2048]{1,0:T(8,128)(2,1)S(1)} %bitcast.79), channel_id=1, source_target_pairs={{4,0},{8,4},{12,8},{16,12},{5,1},{9,5},{13,9},{17,13},{6,2},{10,6}... | collective-permute-start | bytes 786440 | tf_op jit(solution)/shard_map/ppermute | solution.py:106
  36.3 1.3 %fusion.23 = (f32[16]{0:T(128)S(1)}, f32[16,2048]{1,0:T(8,128)S(1)}) fusion(f32[2048]{0:T(1024)S(1)} %fusion.13, bf16[16,2048]{1,0:T(8,128)(2,1)S(1)} %collective-permute-done.9, bf16[2048,2048]{1,0:T(8,128)(2,1)S(1)} %exponential_convert_fusion.1), kind=kOutput, calls=%fused_computation.97 | convolution fusion | flops 134283248 | bytes 8593472 | tf_op jit(solution)/shard_map/dot_general | solution.py:119
  38.6 5.3 %collective-permute-done.11 = bf16[64,2048]{1,0:T(8,128)(2,1)S(1)} collective-permute-done((bf16[64,2048]{1,0:T(8,128)(2,1)S(1)}, bf16[64,2048]{1,0:T(8,128)(2,1)S(1)}, u32[]{:S(2)}, u32[]{:S(2)}) %collective-permute-start.11) | collective-permute-done | bytes 262176 | tf_op jit(solution)/shard_map/ppermute | solution.py:106
  44.0 3.6 %exponential_convert_fusion = bf16[2048,2048]{1,0:T(8,128)(2,1)S(1)} fusion(bf16[64,2048]{1,0:T(8,128)(2,1)S(1)} %broadcast_select_fusion, f32[2048]{0:T(1024)S(1)} %multiply_reduce_fusion.3, f32[2048]{0:T(1024)S(1)} %multiply_reduce_fusion.4, bf16[1,64,2048]{2,1,0:T(8,128)(2,1)S(1)} %all-gather), kind=kOutput, calls=%fused_computation.3 | convolution fusion | flops 557842432 | bytes 8929280 | tf_op jit(solution)/shard_map/dot_general | solution.py:61
  47.6 1.3 %fusion.24 = (f32[16]{0:T(128)S(1)}, f32[16,2048]{1,0:T(8,128)S(1)}) fusion(f32[2048]{0:T(1024)S(1)} %fusion.13, bf16[16,2048]{1,0:T(8,128)(2,1)S(1)} %collective-permute-done.10, bf16[2048,2048]{1,0:T(8,128)(2,1)S(1)} %exponential_convert_fusion), kind=kOutput, calls=%fused_computation.98 | convolution fusion | flops 134283248 | bytes 8593472 | tf_op jit(solution)/shard_map/dot_general | solution.py:119
  49.2 0.8 collective-permute-start.13
  50.1 1.3 %fusion.25 = (f32[16]{0:T(128)S(1)}, f32[16,2048]{1,0:T(8,128)S(1)}) fusion(f32[2048]{0:T(1024)S(1)} %fusion.13, bf16[16,2048]{1,0:T(8,128)(2,1)S(1)} %collective-permute-done.13, bf16[2048,2048]{1,0:T(8,128)(2,1)S(1)} %exponential_convert_fusion), kind=kOutput, calls=%fused_computation.99 | convolution fusion | flops 134283248 | bytes 8593472 | tf_op jit(solution)/shard_map/dot_general | solution.py:119
  52.4 1.3 %fusion.26 = (f32[16]{0:T(128)S(1)}, f32[16,2048]{1,0:T(8,128)S(1)}) fusion(f32[2048]{0:T(1024)S(1)} %fusion.13, bf16[16,2048]{1,0:T(8,128)(2,1)S(1)} %collective-permute-done.14, bf16[2048,2048]{1,0:T(8,128)(2,1)S(1)} %exponential_convert_fusion), kind=kOutput, calls=%fused_computation.100 | convolution fusion | flops 134283248 | bytes 8593472 | tf_op jit(solution)/shard_map/dot_general | solution.py:119
  53.9 1.3 %collective-permute-start.15 = (bf16[16,2048]{1,0:T(8,128)(2,1)S(1)}, bf16[16,2048]{1,0:T(8,128)(2,1)S(1)}, u32[]{:S(2)}, u32[]{:S(2)}) collective-permute-start(bf16[16,2048]{1,0:T(8,128)(2,1)S(1)} %fusion.5), channel_id=1, source_target_pairs={{24,28},{4,0},{25,29},{5,1},{26,30},{6,2},{27,31},{7,3}} | collective-permute-start | bytes 196616 | tf_op jit(solution)/shard_map/ppermute | solution.py:118
  55.3 16.0 %collective-permute-done.15 = bf16[16,2048]{1,0:T(8,128)(2,1)S(1)} collective-permute-done((bf16[16,2048]{1,0:T(8,128)(2,1)S(1)}, bf16[16,2048]{1,0:T(8,128)(2,1)S(1)}, u32[]{:S(2)}, u32[]{:S(2)}) %collective-permute-start.15) | collective-permute-done | bytes 65568 | tf_op jit(solution)/shard_map/ppermute | solution.py:118
  71.3 1.3 %fusion.27 = (f32[16]{0:T(128)S(1)}, f32[16,2048]{1,0:T(8,128)S(1)}) fusion(f32[2048]{0:T(1024)S(1)} %fusion.13, bf16[16,2048]{1,0:T(8,128)(2,1)S(1)} %collective-permute-done.15, bf16[2048,2048]{1,0:T(8,128)(2,1)S(1)} %exponential_convert_fusion), kind=kOutput, calls=%fused_computation.101 | convolution fusion | flops 134283248 | bytes 8593472 | tf_op jit(solution)/shard_map/dot_general | solution.py:119
  73.0 1.1 %collective-permute-start.20 = (f32[1,2048]{1,0:T(1,128)S(1)}, f32[1,2048]{1,0:T(1,128)S(1)}, u32[]{:S(2)}, u32[]{:S(2)}) collective-permute-start(f32[1,2048]{1,0:T(1,128)S(1)} %bitcast.83), channel_id=1, source_target_pairs={{0,2},{1,3},{2,0},{3,1},{4,6},{5,7},{6,4},{7,5},{8,10},{9,11},{10,... | collective-permute-start | bytes 24584 | tf_op jit(solution)/shard_map/ppermute | solution.py:22
  74.0 1.4 %collective-permute-start.21 = (f32[1,2048]{1,0:T(1,128)S(1)}, f32[1,2048]{1,0:T(1,128)S(1)}, u32[]{:S(2)}, u32[]{:S(2)}) collective-permute-start(f32[1,2048]{1,0:T(1,128)S(1)} %bitcast.84), channel_id=1, source_target_pairs={{0,3},{1,0},{2,1},{3,2},{4,7},{5,4},{6,5},{7,6},{8,11},{9,8},{10,9... | collective-permute-start | bytes 24584 | tf_op jit(solution)/shard_map/ppermute | solution.py:22
  77.6 4.3 %multiply_reduce_fusion.1 = (f32[2048]{0:T(1024)S(1)}, f32[2048,2048]{1,0:T(8,128)S(1)}) fusion(f32[2048]{0:T(1024)S(1)} %get-tuple-element.10, f32[2048]{0:T(1024)S(1)} %multiply_reduce_fusion.2, f32[2048]{0:T(1024)S(1)} %multiply_reduce_fusion.4, bf16[1,64,2048]{2,1,0:T(8,128)(2,1)S(1)} %copy-done, bf16[1,64,2048]{2,1,0:T(8,128)(2,1)S(1)} %all-gather), kind=kOutput, calls=%fused_computation.1 | convolution fusion | flops 562034688 | bytes 17334272 | tf_op jit(solution)/shard_map/dot_general | solution.py:61
  82.6 4.9 %multiply_reduce_fusion = f32[2048]{0:T(1024)S(1)} fusion(f32[2048,2048]{1,0:T(8,128)S(1)} %get-tuple-element.42, f32[2048]{0:T(1024)S(1)} %select_divide_fusion, f32[2048]{0:T(1024)S(1)} %multiply_reduce_fusion.2, f32[2048]{0:T(1024)S(1)} %multiply_reduce_fusion.4), kind=kLoop, calls=%fused_computation | loop fusion | flops 25163776 | bytes 16809984 | tf_op jit(solution)/shard_map/reduce_sum | solution.py:142
  87.7 1.1 %collective-permute-start.22 = (f32[512]{0:T(512)S(1)}, f32[512]{0:T(512)S(1)}, u32[]{:S(2)}, u32[]{:S(2)}) collective-permute-start(f32[512]{0:T(512)S(1)} %get-tuple-element.25), channel_id=1, source_target_pairs={{0,1},{1,2},{2,3},{3,0},{4,5},{5,6},{6,7},{7,4},{8,9},{9,10},{10,1... | collective-permute-start | bytes 6152 | tf_op jit(solution)/shard_map/ppermute | solution.py:22
  88.7 1.0 %collective-permute-start.23 = (f32[512]{0:T(512)S(1)}, f32[512]{0:T(512)S(1)}, u32[]{:S(2)}, u32[]{:S(2)}) collective-permute-start(f32[512]{0:T(512)S(1)} %get-tuple-element.24), channel_id=1, source_target_pairs={{0,2},{1,3},{2,0},{3,1},{4,6},{5,7},{6,4},{7,5},{8,10},{9,11},{10,... | collective-permute-start | bytes 6152 | tf_op jit(solution)/shard_map/ppermute | solution.py:22
  90.4 1.0 %collective-permute-start.17 = (f32[2,16,512]{2,1,0:T(8,128)S(1)}, f32[2,16,512]{2,1,0:T(8,128)S(1)}, u32[]{:S(2)}, u32[]{:S(2)}) collective-permute-start(f32[2,16,512]{2,1,0:T(8,128)S(1)} %get-tuple-element.16), channel_id=1, source_target_pairs={{0,2},{1,3},{2,0},{3,1},{4,6},{5,7},{6,4},{7,5},{8,10},{9,11},{10,... | collective-permute-start | bytes 196616 | tf_op jit(solution)/shard_map/ppermute | solution.py:22
  91.4 1.4 %collective-permute-start.18 = (f32[2,16,512]{2,1,0:T(8,128)S(1)}, f32[2,16,512]{2,1,0:T(8,128)S(1)}, u32[]{:S(2)}, u32[]{:S(2)}) collective-permute-start(f32[2,16,512]{2,1,0:T(8,128)S(1)} %get-tuple-element.15), channel_id=1, source_target_pairs={{0,3},{1,0},{2,1},{3,2},{4,7},{5,4},{6,5},{7,6},{8,11},{9,8},{10,9... | collective-permute-start | bytes 196616 | tf_op jit(solution)/shard_map/ppermute | solution.py:22
  94.1 1.2 %collective-permute-done.17 = f32[2,16,512]{2,1,0:T(8,128)S(1)} collective-permute-done((f32[2,16,512]{2,1,0:T(8,128)S(1)}, f32[2,16,512]{2,1,0:T(8,128)S(1)}, u32[]{:S(2)}, u32[]{:S(2)}) %collective-permute-start.17) | collective-permute-done | bytes 65568 | tf_op jit(solution)/shard_map/ppermute | solution.py:22
  (101 shorter events, 11.7 us)
Async XLA Ops:
  1.7 14.8 %collective-permute-start = (f32[16,512]{1,0:T(8,128)S(1)}, f32[16,512]{1,0:T(8,128)S(1)}, u32[]{:S(2)}, u32[]{:S(2)}) collective-permute-start(f32[16,512]{1,0:T(8,128)S(1)} %get-tuple-element.21), channel_id=1, source_target_pairs={{0,1},{1,2},{2,3},{3,0},{4,5},{5,6},{6,7},{7,4},{8,9},{9,10},{10,1... | collective-permute-start | bytes 98312 | tf_op jit(solution)/shard_map/ppermute | solution.py:22
  2.2 14.3 %collective-permute-start.1 = (f32[16,512]{1,0:T(8,128)S(1)}, f32[16,512]{1,0:T(8,128)S(1)}, u32[]{:S(2)}, u32[]{:S(2)}) collective-permute-start(f32[16,512]{1,0:T(8,128)S(1)} %get-tuple-element.20), channel_id=1, source_target_pairs={{0,2},{1,3},{2,0},{3,1},{4,6},{5,7},{6,4},{7,5},{8,10},{9,11},{10,... | collective-permute-start | bytes 98312 | tf_op jit(solution)/shard_map/ppermute | solution.py:22
  4.8 11.7 %collective-permute-start.2 = (f32[16,512]{1,0:T(8,128)S(1)}, f32[16,512]{1,0:T(8,128)S(1)}, u32[]{:S(2)}, u32[]{:S(2)}) collective-permute-start(f32[16,512]{1,0:T(8,128)S(1)} %get-tuple-element.19), channel_id=1, source_target_pairs={{0,3},{1,0},{2,1},{3,2},{4,7},{5,4},{6,5},{7,6},{8,11},{9,8},{10,9... | collective-permute-start | bytes 98312 | tf_op jit(solution)/shard_map/ppermute | solution.py:22
  6.2 13.9 %collective-permute-start.4 = (bf16[64,512]{1,0:T(8,128)(2,1)}, bf16[64,512]{1,0:T(8,128)(2,1)S(1)}, u32[]{:S(2)}, u32[]{:S(2)}) collective-permute-start(bf16[64,512]{1,0:T(8,128)(2,1)} %bitcast.81), channel_id=1, source_target_pairs={{0,4},{4,8},{8,12},{20,16},{24,20},{28,24},{1,5},{5,9},{9,13},{21,... | collective-permute-start | bytes 196616 | tf_op jit(solution)/shard_map/ppermute | solution.py:92
  16.6 13.1 %collective-permute-start.3 = (bf16[16,2048]{1,0:T(8,128)(2,1)S(1)}, bf16[16,2048]{1,0:T(8,128)(2,1)S(1)}, u32[]{:S(2)}, u32[]{:S(2)}) collective-permute-start(bf16[16,2048]{1,0:T(8,128)(2,1)S(1)} %fusion.11), channel_id=1, source_target_pairs={{0,4},{28,24},{1,5},{29,25},{2,6},{30,26},{3,7},{31,27}} | collective-permute-start | bytes 196616 | tf_op jit(solution)/shard_map/ppermute | solution.py:118
  20.1 2.6 %collective-permute-start.5 = (bf16[64,512]{1,0:T(8,128)(2,1)S(1)}, bf16[64,512]{1,0:T(8,128)(2,1)S(1)}, u32[]{:S(2)}, u32[]{:S(2)}) collective-permute-start(bf16[64,512]{1,0:T(8,128)(2,1)S(1)} %collective-permute-done.4), channel_id=1, source_target_pairs={{1,0},{2,1},{3,2},{0,3},{5,4},{6,5},{7,6},{4,7},{9,8},{10,9},{11,1... | collective-permute-start | bytes 196616 | tf_op jit(solution)/shard_map/ppermute | solution.py:34
  20.3 5.6 %collective-permute-start.6 = (bf16[64,512]{1,0:T(8,128)(2,1)S(1)}, bf16[64,512]{1,0:T(8,128)(2,1)S(1)}, u32[]{:S(2)}, u32[]{:S(2)}) collective-permute-start(bf16[64,512]{1,0:T(8,128)(2,1)S(1)} %collective-permute-done.4), channel_id=1, source_target_pairs={{2,0},{3,1},{0,2},{1,3},{6,4},{7,5},{4,6},{5,7},{10,8},{11,9},{8,1... | collective-permute-start | bytes 196616 | tf_op jit(solution)/shard_map/ppermute | solution.py:34
  21.8 4.2 %collective-permute-start.7 = (bf16[64,512]{1,0:T(8,128)(2,1)S(1)}, bf16[64,512]{1,0:T(8,128)(2,1)S(1)}, u32[]{:S(2)}, u32[]{:S(2)}) collective-permute-start(bf16[64,512]{1,0:T(8,128)(2,1)S(1)} %collective-permute-done.4), channel_id=1, source_target_pairs={{3,0},{0,1},{1,2},{2,3},{7,4},{4,5},{5,6},{6,7},{11,8},{8,9},{9,10... | collective-permute-start | bytes 196616 | tf_op jit(solution)/shard_map/ppermute | solution.py:34
  31.3 0.8 collective-permute-start.8
  33.6 2.7 %collective-permute-start.9 = (bf16[16,2048]{1,0:T(8,128)(2,1)S(1)}, bf16[16,2048]{1,0:T(8,128)(2,1)S(1)}, u32[]{:S(2)}, u32[]{:S(2)}) collective-permute-start(bf16[16,2048]{1,0:T(8,128)(2,1)S(1)} %fusion.9), channel_id=1, source_target_pairs={{8,12},{20,16},{9,13},{21,17},{10,14},{22,18},{11,15},{23,19}} | collective-permute-start | bytes 196616 | tf_op jit(solution)/shard_map/ppermute | solution.py:118
  34.4 9.5 %collective-permute-start.11 = (bf16[64,2048]{1,0:T(8,128)(2,1)S(1)}, bf16[64,2048]{1,0:T(8,128)(2,1)S(1)}, u32[]{:S(2)}, u32[]{:S(2)}) collective-permute-start(bf16[64,2048]{1,0:T(8,128)(2,1)S(1)} %bitcast.79), channel_id=1, source_target_pairs={{4,0},{8,4},{12,8},{16,12},{5,1},{9,5},{13,9},{17,13},{6,2},{10,6}... | collective-permute-start | bytes 786440 | tf_op jit(solution)/shard_map/ppermute | solution.py:106
  35.6 8.2 %collective-permute-start.12 = (bf16[64,2048]{1,0:T(8,128)(2,1)S(1)}, bf16[64,2048]{1,0:T(8,128)(2,1)S(1)}, u32[]{:S(2)}, u32[]{:S(2)}) collective-permute-start(bf16[64,2048]{1,0:T(8,128)(2,1)S(1)} %bitcast.80), channel_id=1, source_target_pairs={{12,16},{16,20},{20,24},{24,28},{13,17},{17,21},{21,25},{25,29},{1... | collective-permute-start | bytes 786440 | tf_op jit(solution)/shard_map/ppermute | solution.py:107
  37.9 9.7 %collective-permute-start.10 = (bf16[16,2048]{1,0:T(8,128)(2,1)S(1)}, bf16[16,2048]{1,0:T(8,128)(2,1)S(1)}, u32[]{:S(2)}, u32[]{:S(2)}) collective-permute-start(bf16[16,2048]{1,0:T(8,128)(2,1)S(1)} %fusion.8), channel_id=1, source_target_pairs={{12,16},{16,12},{13,17},{17,13},{14,18},{18,14},{15,19},{19,15}} | collective-permute-start | bytes 196616 | tf_op jit(solution)/shard_map/ppermute | solution.py:118
  48.9 26.5 %copy-start = (bf16[1,64,2048]{2,1,0:T(8,128)(2,1)S(1)}, bf16[1,64,2048]{2,1,0:T(8,128)(2,1)}, u32[]{:S(2)}) copy-start(bf16[1,64,2048]{2,1,0:T(8,128)(2,1)} %param.7) | copy-start | bytes 786436
  49.2 0.9 collective-permute-start.13
  51.6 0.8 collective-permute-start.14
  53.9 17.4 %collective-permute-start.15 = (bf16[16,2048]{1,0:T(8,128)(2,1)S(1)}, bf16[16,2048]{1,0:T(8,128)(2,1)S(1)}, u32[]{:S(2)}, u32[]{:S(2)}) collective-permute-start(bf16[16,2048]{1,0:T(8,128)(2,1)S(1)} %fusion.5), channel_id=1, source_target_pairs={{24,28},{4,0},{25,29},{5,1},{26,30},{6,2},{27,31},{7,3}} | collective-permute-start | bytes 196616 | tf_op jit(solution)/shard_map/ppermute | solution.py:118
  72.9 3.4 %collective-permute-start.19 = (f32[1,2048]{1,0:T(1,128)S(1)}, f32[1,2048]{1,0:T(1,128)S(1)}, u32[]{:S(2)}, u32[]{:S(2)}) collective-permute-start(f32[1,2048]{1,0:T(1,128)S(1)} %bitcast.82), channel_id=1, source_target_pairs={{0,1},{1,2},{2,3},{3,0},{4,5},{5,6},{6,7},{7,4},{8,9},{9,10},{10,1... | collective-permute-start | bytes 24584 | tf_op jit(solution)/shard_map/ppermute | solution.py:22
  73.0 3.7 %collective-permute-start.20 = (f32[1,2048]{1,0:T(1,128)S(1)}, f32[1,2048]{1,0:T(1,128)S(1)}, u32[]{:S(2)}, u32[]{:S(2)}) collective-permute-start(f32[1,2048]{1,0:T(1,128)S(1)} %bitcast.83), channel_id=1, source_target_pairs={{0,2},{1,3},{2,0},{3,1},{4,6},{5,7},{6,4},{7,5},{8,10},{9,11},{10,... | collective-permute-start | bytes 24584 | tf_op jit(solution)/shard_map/ppermute | solution.py:22
  74.0 2.8 %collective-permute-start.21 = (f32[1,2048]{1,0:T(1,128)S(1)}, f32[1,2048]{1,0:T(1,128)S(1)}, u32[]{:S(2)}, u32[]{:S(2)}) collective-permute-start(f32[1,2048]{1,0:T(1,128)S(1)} %bitcast.84), channel_id=1, source_target_pairs={{0,3},{1,0},{2,1},{3,2},{4,7},{5,4},{6,5},{7,6},{8,11},{9,8},{10,9... | collective-permute-start | bytes 24584 | tf_op jit(solution)/shard_map/ppermute | solution.py:22
  87.7 3.7 %collective-permute-start.22 = (f32[512]{0:T(512)S(1)}, f32[512]{0:T(512)S(1)}, u32[]{:S(2)}, u32[]{:S(2)}) collective-permute-start(f32[512]{0:T(512)S(1)} %get-tuple-element.25), channel_id=1, source_target_pairs={{0,1},{1,2},{2,3},{3,0},{4,5},{5,6},{6,7},{7,4},{8,9},{9,10},{10,1... | collective-permute-start | bytes 6152 | tf_op jit(solution)/shard_map/ppermute | solution.py:22
  88.7 4.2 %collective-permute-start.23 = (f32[512]{0:T(512)S(1)}, f32[512]{0:T(512)S(1)}, u32[]{:S(2)}, u32[]{:S(2)}) collective-permute-start(f32[512]{0:T(512)S(1)} %get-tuple-element.24), channel_id=1, source_target_pairs={{0,2},{1,3},{2,0},{3,1},{4,6},{5,7},{6,4},{7,5},{8,10},{9,11},{10,... | collective-permute-start | bytes 6152 | tf_op jit(solution)/shard_map/ppermute | solution.py:22
  89.7 3.4 %collective-permute-start.24 = (f32[512]{0:T(512)S(1)}, f32[512]{0:T(512)S(1)}, u32[]{:S(2)}, u32[]{:S(2)}) collective-permute-start(f32[512]{0:T(512)S(1)} %get-tuple-element.23), channel_id=1, source_target_pairs={{0,3},{1,0},{2,1},{3,2},{4,7},{5,4},{6,5},{7,6},{8,11},{9,8},{10,9... | collective-permute-start | bytes 6152 | tf_op jit(solution)/shard_map/ppermute | solution.py:22
  90.2 3.8 %collective-permute-start.16 = (f32[2,16,512]{2,1,0:T(8,128)S(1)}, f32[2,16,512]{2,1,0:T(8,128)S(1)}, u32[]{:S(2)}, u32[]{:S(2)}) collective-permute-start(f32[2,16,512]{2,1,0:T(8,128)S(1)} %get-tuple-element.17), channel_id=1, source_target_pairs={{0,1},{1,2},{2,3},{3,0},{4,5},{5,6},{6,7},{7,4},{8,9},{9,10},{10,1... | collective-permute-start | bytes 196616 | tf_op jit(solution)/shard_map/ppermute | solution.py:22
  90.4 5.0 %collective-permute-start.17 = (f32[2,16,512]{2,1,0:T(8,128)S(1)}, f32[2,16,512]{2,1,0:T(8,128)S(1)}, u32[]{:S(2)}, u32[]{:S(2)}) collective-permute-start(f32[2,16,512]{2,1,0:T(8,128)S(1)} %get-tuple-element.16), channel_id=1, source_target_pairs={{0,2},{1,3},{2,0},{3,1},{4,6},{5,7},{6,4},{7,5},{8,10},{9,11},{10,... | collective-permute-start | bytes 196616 | tf_op jit(solution)/shard_map/ppermute | solution.py:22
  91.4 4.0 %collective-permute-start.18 = (f32[2,16,512]{2,1,0:T(8,128)S(1)}, f32[2,16,512]{2,1,0:T(8,128)S(1)}, u32[]{:S(2)}, u32[]{:S(2)}) collective-permute-start(f32[2,16,512]{2,1,0:T(8,128)S(1)} %get-tuple-element.15), channel_id=1, source_target_pairs={{0,3},{1,0},{2,1},{3,2},{4,7},{5,4},{6,5},{7,6},{8,11},{9,8},{10,9... | collective-permute-start | bytes 196616 | tf_op jit(solution)/shard_map/ppermute | solution.py:22

commit v13 on v12

--- a/solution.py
+++ b/solution.py
@@ -121,11 +121,30 @@
         rows = jnp.where(keep[:, None, None], fresh[None], rows)
     forward_rows = rows[0]
     backward_rows = rows[1]
-    both_out = swap_blocks(rows, 2, 1, (2, own_weight.shape[0], per_device))
+    mass_part = jnp.sum(forward_rows * block_weight * backward_rows, axis=0)
+    pt_count = lax.axis_size("pt")
+    mass_rows = mass_part.reshape(pt_count, per_device)
+    both_out = jnp.zeros((2 * pt_count, block_rows, per_device), jnp.float32)
+    every_mass = jnp.zeros((pt_count, support_total), jnp.float32)
+    for shift in range(pt_count):
+        block = lax.dynamic_slice_in_dim(rows, ((pt_rank + shift) % pt_count) * per_device, per_device, 2)
+        packed = jnp.concatenate([block.reshape(2 * block_rows, per_device), mass_rows], axis=0)
+        if shift:
+            packed = lax.ppermute(
+                packed, "pt", [(i, (i + shift) % pt_count) for i in range(pt_count)]
+            )
+        origin = (pt_rank - shift) % pt_count
+        piece = packed[: 2 * block_rows].reshape(2, 1, block_rows, per_device)
+        both_out = lax.dynamic_update_slice_in_dim(
+            both_out.reshape(2, pt_count, block_rows, per_device), piece, origin, 1
+        ).reshape(2 * pt_count, block_rows, per_device)
+        every_mass = lax.dynamic_update_slice_in_dim(
+            every_mass, packed[2 * block_rows:].reshape(1, support_total), origin, 0
+        )
+    both_out = both_out.reshape(2, pt_count * block_rows, per_device)
     forward_out = both_out[0]
     backward_out = both_out[1]
-    mass_part = jnp.sum(forward_rows * block_weight * backward_rows, axis=0)
-    full_mass = live_all * sum_over_pt(mass_part)
+    full_mass = live_all * jnp.sum(every_mass, axis=0)
     mass_total = jnp.sum(full_mass)
 
     cell_total = cell_count[0]

time: 96.4 us -> 97.2 us (level)
  starting transfers between devices: 27.4 us -> 24.8 us
  waiting for transfers between devices: 27 us -> 29.3 us
  other arithmetic: 10.1 us -> 11.1 us
    ppermute x12 -> x6, starting transfers between devices: 12 us -> 6.97 us  [swap_blocks(): lax.ppermute(piece, 'pt', [(i, (i + shift) % count) for i in range(count)])]
    ppermute x0 -> x3, waiting for transfers between devices: none -> 2.76 us  [shards(): lax.ppermute(packed, 'pt', [(i, (i + shift) % pt_count) for i in range(pt...]
    ppermute x0 -> x3, starting transfers between devices: none -> 2.51 us  [shards(): lax.ppermute(packed, 'pt', [(i, (i + shift) % pt_count) for i in range(pt...]
  transfers between devices with their start and end apart: 25 -> 22, of which waited for: 7 -> 8; matrix products, arithmetic and copies ran while one was open for 12% -> 12% of each run, Pallas kernels for 0% -> 0%
where the time goes in v13:
time: 97.2 us; the launch traced here: 96.9 us
  waiting for transfers between devices  29.3 us (30%)
  starting transfers between devices  24.8 us (26%)
  matrix products  20.6 us (21%)
  other arithmetic  11.1 us (11%)
  blocking collectives  5.99 us (6%)
  between operations  2.72 us (3%)
  local copies, waits for them, and re-layouts  2.31 us (2%)
    ppermute x7, waiting for transfers between devices, shards(): incoming = lax.ppermute(outgoing, 'day', route)  16.1 us
    dot_general x3, matrix products, squared_dist(): lax.dot_general(left_pts, right_pts, (((0,), (0,)), ((), ())), preferred_...  11.5 us
    dot_general x7, matrix products, shards(): jnp.dot(incoming, kernel, preferred_element_type=jnp.float32)  9.15 us
    ppermute x7, starting transfers between devices, shards(): incoming = lax.ppermute(outgoing, 'day', route)  8.25 us
    ppermute x6, starting transfers between devices, swap_blocks(): lax.ppermute(piece, 'pt', [(i, (i + shift) % count) for i in range(count)])  6.97 us
    all_gather x1, blocking collectives, shards(): day_pts = lax.all_gather(own_pts, 'pt', axis=1, tiled=True)  5.99 us
    ppermute x1, waiting for transfers between devices, shards(): lax.ppermute(later_pts, 'day', [(d + 1, d) for d in range(half)])  5.33 us
    reduce_sum x1, other arithmetic, shards(): ratio_rows = jnp.sum(fit_kernel * inverse[None, :], axis=1)  4.9 us
  transfers between devices with their start and end apart: 22, of which 8 were waited for; matrix products, arithmetic and copies ran while one was open for 12% of the time, Pallas kernels for 0%

profile of v13, /device:TPU:0, one launch (start us, length us, event | category | flops | bytes accessed | tf_op | source)
XLA Modules:
  0.0 96.9 jit_solution(17301347073763639130)
XLA Ops:
  0.7 0.9 bitcast_multiply_fusion
  2.2 2.6 %collective-permute-start.1 = (f32[16,512]{1,0:T(8,128)S(1)}, f32[16,512]{1,0:T(8,128)S(1)}, u32[]{:S(2)}, u32[]{:S(2)}) collective-permute-start(f32[16,512]{1,0:T(8,128)S(1)} %get-tuple-element.19), channel_id=1, source_target_pairs={{0,2},{1,3},{2,0},{3,1},{4,6},{5,7},{6,4},{7,5},{8,10},{9,11},{10,... | collective-permute-start | bytes 98312 | tf_op jit(solution)/shard_map/ppermute | solution.py:22
  4.8 1.4 %collective-permute-start.2 = (f32[16,512]{1,0:T(8,128)S(1)}, f32[16,512]{1,0:T(8,128)S(1)}, u32[]{:S(2)}, u32[]{:S(2)}) collective-permute-start(f32[16,512]{1,0:T(8,128)S(1)} %get-tuple-element.18), channel_id=1, source_target_pairs={{0,3},{1,0},{2,1},{3,2},{4,7},{5,4},{6,5},{7,6},{8,11},{9,8},{10,9... | collective-permute-start | bytes 98312 | tf_op jit(solution)/shard_map/ppermute | solution.py:22
  6.2 3.4 %collective-permute-start.4 = (bf16[64,512]{1,0:T(8,128)(2,1)}, bf16[64,512]{1,0:T(8,128)(2,1)S(1)}, u32[]{:S(2)}, u32[]{:S(2)}) collective-permute-start(bf16[64,512]{1,0:T(8,128)(2,1)} %bitcast.112), channel_id=1, source_target_pairs={{0,4},{4,8},{8,12},{20,16},{24,20},{28,24},{1,5},{5,9},{9,13},{21,... | collective-permute-start | bytes 196616 | tf_op jit(solution)/shard_map/ppermute | solution.py:92
  9.6 6.0 %all-gather = bf16[1,64,2048]{2,1,0:T(8,128)(2,1)S(1)} all-gather(bf16[1,64,512]{2,1,0:T(8,128)(2,1)} %param.6), channel_id=2, replica_groups=mesh['day'=8,'pt'=4] {'pt'}, dimensions={2}, use_global_device_ids=true | all-gather | bytes 327680 | tf_op jit(solution)/shard_map/all_gather | solution.py:73
  16.4 1.0 %multiply_reduce_fusion.2 = f32[2048]{0:T(1024)S(1)} fusion(bf16[1,64,2048]{2,1,0:T(8,128)(2,1)} %param.7), kind=kLoop, calls=%fused_computation.12 | loop fusion | flops 391168 | bytes 270336 | tf_op jit(solution)/shard_map/reduce_sum | solution.py:57
  18.3 3.5 %collective-permute-start.3 = (bf16[16,2048]{1,0:T(8,128)(2,1)S(1)}, bf16[16,2048]{1,0:T(8,128)(2,1)S(1)}, u32[]{:S(2)}, u32[]{:S(2)}) collective-permute-start(bf16[16,2048]{1,0:T(8,128)(2,1)S(1)} %fusion.11), channel_id=1, source_target_pairs={{0,4},{28,24},{1,5},{29,25},{2,6},{30,26},{3,7},{31,27}} | collective-permute-start | bytes 196616 | tf_op jit(solution)/shard_map/ppermute | solution.py:118
  22.0 1.5 %collective-permute-start.6 = (bf16[64,512]{1,0:T(8,128)(2,1)S(1)}, bf16[64,512]{1,0:T(8,128)(2,1)S(1)}, u32[]{:S(2)}, u32[]{:S(2)}) collective-permute-start(bf16[64,512]{1,0:T(8,128)(2,1)S(1)} %collective-permute-done.4), channel_id=1, source_target_pairs={{2,0},{3,1},{0,2},{1,3},{6,4},{7,5},{4,6},{5,7},{10,8},{11,9},{8,1... | collective-permute-start | bytes 196616 | tf_op jit(solution)/shard_map/ppermute | solution.py:34
  24.4 3.2 %collective-permute-done.6 = bf16[64,512]{1,0:T(8,128)(2,1)S(1)} collective-permute-done((bf16[64,512]{1,0:T(8,128)(2,1)S(1)}, bf16[64,512]{1,0:T(8,128)(2,1)S(1)}, u32[]{:S(2)}, u32[]{:S(2)}) %collective-permute-start.6) | collective-permute-done | bytes 65568 | tf_op jit(solution)/shard_map/ppermute | solution.py:34
  27.8 3.6 %exponential_convert_fusion.1 = bf16[2048,2048]{1,0:T(8,128)(2,1)S(1)} fusion(bf16[64,2048]{1,0:T(8,128)(2,1)S(1)} %constant_dynamic-update-slice_fusion.3, f32[2048]{0:T(1024)S(1)} %multiply_reduce_fusion.4, f32[2048]{0:T(1024)S(1)} %multiply_reduce_fusion.5, bf16[1,64,2048]{2,1,0:T(8,128)(2,1)S(1)} %all-gather), kind=kOutput, calls=%fused_computation.4 | convolution fusion | flops 557842432 | bytes 8929280 | tf_op jit(solution)/shard_map/dot_general | solution.py:61
  31.4 1.3 %fusion.21 = (f32[16]{0:T(128)S(1)}, f32[16,2048]{1,0:T(8,128)S(1)}) fusion(f32[2048]{0:T(1024)S(1)} %fusion.13, bf16[16,2048]{1,0:T(8,128)(2,1)S(1)} %collective-permute-done.3, bf16[2048,2048]{1,0:T(8,128)(2,1)S(1)} %exponential_convert_fusion.1), kind=kOutput, calls=%fused_computation.101 | convolution fusion | flops 134283248 | bytes 8593472 | tf_op jit(solution)/shard_map/dot_general | solution.py:119
  33.7 1.3 %fusion.22 = (f32[16]{0:T(128)S(1)}, f32[16,2048]{1,0:T(8,128)S(1)}) fusion(f32[2048]{0:T(1024)S(1)} %fusion.13, bf16[16,2048]{1,0:T(8,128)(2,1)S(1)} %collective-permute-done.8, bf16[2048,2048]{1,0:T(8,128)(2,1)S(1)} %exponential_convert_fusion.1), kind=kOutput, calls=%fused_computation.102 | convolution fusion | flops 134283248 | bytes 8593472 | tf_op jit(solution)/shard_map/dot_general | solution.py:119
  36.0 1.3 %collective-permute-start.11 = (bf16[64,2048]{1,0:T(8,128)(2,1)S(1)}, bf16[64,2048]{1,0:T(8,128)(2,1)S(1)}, u32[]{:S(2)}, u32[]{:S(2)}) collective-permute-start(bf16[64,2048]{1,0:T(8,128)(2,1)S(1)} %bitcast.101), channel_id=1, source_target_pairs={{4,0},{8,4},{12,8},{16,12},{5,1},{9,5},{13,9},{17,13},{6,2},{10,6}... | collective-permute-start | bytes 786440 | tf_op jit(solution)/shard_map/ppermute | solution.py:106
  38.0 1.3 %fusion.23 = (f32[16]{0:T(128)S(1)}, f32[16,2048]{1,0:T(8,128)S(1)}) fusion(f32[2048]{0:T(1024)S(1)} %fusion.13, bf16[16,2048]{1,0:T(8,128)(2,1)S(1)} %collective-permute-done.9, bf16[2048,2048]{1,0:T(8,128)(2,1)S(1)} %exponential_convert_fusion.1), kind=kOutput, calls=%fused_computation.103 | convolution fusion | flops 134283248 | bytes 8593472 | tf_op jit(solution)/shard_map/dot_general | solution.py:119
  40.2 5.3 %collective-permute-done.11 = bf16[64,2048]{1,0:T(8,128)(2,1)S(1)} collective-permute-done((bf16[64,2048]{1,0:T(8,128)(2,1)S(1)}, bf16[64,2048]{1,0:T(8,128)(2,1)S(1)}, u32[]{:S(2)}, u32[]{:S(2)}) %collective-permute-start.11) | collective-permute-done | bytes 262176 | tf_op jit(solution)/shard_map/ppermute | solution.py:106
  45.7 3.6 %exponential_convert_fusion = bf16[2048,2048]{1,0:T(8,128)(2,1)S(1)} fusion(bf16[64,2048]{1,0:T(8,128)(2,1)S(1)} %broadcast_select_fusion, f32[2048]{0:T(1024)S(1)} %multiply_reduce_fusion.3, f32[2048]{0:T(1024)S(1)} %multiply_reduce_fusion.4, bf16[1,64,2048]{2,1,0:T(8,128)(2,1)S(1)} %all-gather), kind=kOutput, calls=%fused_computation.3 | convolution fusion | flops 557842432 | bytes 8929280 | tf_op jit(solution)/shard_map/dot_general | solution.py:61
  49.3 1.3 %fusion.24 = (f32[16]{0:T(128)S(1)}, f32[16,2048]{1,0:T(8,128)S(1)}) fusion(f32[2048]{0:T(1024)S(1)} %fusion.13, bf16[16,2048]{1,0:T(8,128)(2,1)S(1)} %collective-permute-done.10, bf16[2048,2048]{1,0:T(8,128)(2,1)S(1)} %exponential_convert_fusion), kind=kOutput, calls=%fused_computation.104 | convolution fusion | flops 134283248 | bytes 8593472 | tf_op jit(solution)/shard_map/dot_general | solution.py:119
  50.8 0.8 collective-permute-start.13
  51.8 1.3 %fusion.25 = (f32[16]{0:T(128)S(1)}, f32[16,2048]{1,0:T(8,128)S(1)}) fusion(f32[2048]{0:T(1024)S(1)} %fusion.13, bf16[16,2048]{1,0:T(8,128)(2,1)S(1)} %collective-permute-done.13, bf16[2048,2048]{1,0:T(8,128)(2,1)S(1)} %exponential_convert_fusion), kind=kOutput, calls=%fused_computation.105 | convolution fusion | flops 134283248 | bytes 8593472 | tf_op jit(solution)/shard_map/dot_general | solution.py:119
  54.1 1.3 %fusion.26 = (f32[16]{0:T(128)S(1)}, f32[16,2048]{1,0:T(8,128)S(1)}) fusion(f32[2048]{0:T(1024)S(1)} %fusion.13, bf16[16,2048]{1,0:T(8,128)(2,1)S(1)} %collective-permute-done.14, bf16[2048,2048]{1,0:T(8,128)(2,1)S(1)} %exponential_convert_fusion), kind=kOutput, calls=%fused_computation.106 | convolution fusion | flops 134283248 | bytes 8593472 | tf_op jit(solution)/shard_map/dot_general | solution.py:119
  55.6 1.3 %collective-permute-start.15 = (bf16[16,2048]{1,0:T(8,128)(2,1)S(1)}, bf16[16,2048]{1,0:T(8,128)(2,1)S(1)}, u32[]{:S(2)}, u32[]{:S(2)}) collective-permute-start(bf16[16,2048]{1,0:T(8,128)(2,1)S(1)} %fusion.5), channel_id=1, source_target_pairs={{24,28},{4,0},{25,29},{5,1},{26,30},{6,2},{27,31},{7,3}} | collective-permute-start | bytes 196616 | tf_op jit(solution)/shard_map/ppermute | solution.py:118
  57.0 16.0 %collective-permute-done.15 = bf16[16,2048]{1,0:T(8,128)(2,1)S(1)} collective-permute-done((bf16[16,2048]{1,0:T(8,128)(2,1)S(1)}, bf16[16,2048]{1,0:T(8,128)(2,1)S(1)}, u32[]{:S(2)}, u32[]{:S(2)}) %collective-permute-start.15) | collective-permute-done | bytes 65568 | tf_op jit(solution)/shard_map/ppermute | solution.py:118
  73.0 1.3 %fusion.27 = (f32[16]{0:T(128)S(1)}, f32[16,2048]{1,0:T(8,128)S(1)}) fusion(f32[2048]{0:T(1024)S(1)} %fusion.13, bf16[16,2048]{1,0:T(8,128)(2,1)S(1)} %collective-permute-done.15, bf16[2048,2048]{1,0:T(8,128)(2,1)S(1)} %exponential_convert_fusion), kind=kOutput, calls=%fused_computation.107 | convolution fusion | flops 134283248 | bytes 8593472 | tf_op jit(solution)/shard_map/dot_general | solution.py:119
  74.8 1.1 %collective-permute-start.17 = (f32[36,512]{1,0:T(8,128)S(1)}, f32[36,512]{1,0:T(8,128)S(1)}, u32[]{:S(2)}, u32[]{:S(2)}) collective-permute-start(f32[36,512]{1,0:T(8,128)S(1)} %get-tuple-element.27), channel_id=1, source_target_pairs={{0,2},{1,3},{2,0},{3,1},{4,6},{5,7},{6,4},{7,5},{8,10},{9,11},{10,... | collective-permute-start | bytes 221192 | tf_op jit(solution)/shard_map/ppermute | solution.py:133
  75.8 1.4 %collective-permute-start.18 = (f32[36,512]{1,0:T(8,128)S(1)}, f32[36,512]{1,0:T(8,128)S(1)}, u32[]{:S(2)}, u32[]{:S(2)}) collective-permute-start(f32[36,512]{1,0:T(8,128)S(1)} %get-tuple-element.26), channel_id=1, source_target_pairs={{0,3},{1,0},{2,1},{3,2},{4,7},{5,4},{6,5},{7,6},{8,11},{9,8},{10,9... | collective-permute-start | bytes 221192 | tf_op jit(solution)/shard_map/ppermute | solution.py:133
  77.4 1.4 %collective-permute-done.16 = f32[36,512]{1,0:T(8,128)S(1)} collective-permute-done((f32[36,512]{1,0:T(8,128)S(1)}, f32[36,512]{1,0:T(8,128)S(1)}, u32[]{:S(2)}, u32[]{:S(2)}) %collective-permute-start.16) | collective-permute-done | bytes 73760 | tf_op jit(solution)/shard_map/ppermute | solution.py:133
  78.8 1.3 %collective-permute-done.17 = f32[36,512]{1,0:T(8,128)S(1)} collective-permute-done((f32[36,512]{1,0:T(8,128)S(1)}, f32[36,512]{1,0:T(8,128)S(1)}, u32[]{:S(2)}, u32[]{:S(2)}) %collective-permute-start.17) | collective-permute-done | bytes 73760 | tf_op jit(solution)/shard_map/ppermute | solution.py:133
  81.3 4.3 %multiply_reduce_fusion.1 = (f32[2048]{0:T(1024)S(1)}, f32[2048,2048]{1,0:T(8,128)S(1)}) fusion(f32[2048]{0:T(1024)S(1)} %get-tuple-element.10, f32[2048]{0:T(1024)S(1)} %multiply_reduce_fusion.2, f32[2048]{0:T(1024)S(1)} %multiply_reduce_fusion.4, bf16[1,64,2048]{2,1,0:T(8,128)(2,1)S(1)} %copy-done, bf16[1,64,2048]{2,1,0:T(8,128)(2,1)S(1)} %all-gather), kind=kOutput, calls=%fused_computation.1 | convolution fusion | flops 562034688 | bytes 17334272 | tf_op jit(solution)/shard_map/dot_general | solution.py:61
  86.2 4.9 %multiply_reduce_fusion = f32[2048]{0:T(1024)S(1)} fusion(f32[2048,2048]{1,0:T(8,128)S(1)} %get-tuple-element.44, f32[2048]{0:T(1024)S(1)} %select_divide_fusion, f32[2048]{0:T(1024)S(1)} %multiply_reduce_fusion.2, f32[2048]{0:T(1024)S(1)} %multiply_reduce_fusion.4), kind=kLoop, calls=%fused_computation | loop fusion | flops 25163776 | bytes 16809984 | tf_op jit(solution)/shard_map/reduce_sum | solution.py:161
  91.3 0.9 collective-permute-start.19
  92.2 1.0 %collective-permute-start.20 = (f32[512]{0:T(512)S(1)}, f32[512]{0:T(512)S(1)}, u32[]{:S(2)}, u32[]{:S(2)}) collective-permute-start(f32[512]{0:T(512)S(1)} %get-tuple-element.23), channel_id=1, source_target_pairs={{0,2},{1,3},{2,0},{3,1},{4,6},{5,7},{6,4},{7,5},{8,10},{9,11},{10,... | collective-permute-start | bytes 6152 | tf_op jit(solution)/shard_map/ppermute | solution.py:22
  94.8 1.0 %collective-permute-done.20 = f32[512]{0:T(512)S(1)} collective-permute-done((f32[512]{0:T(512)S(1)}, f32[512]{0:T(512)S(1)}, u32[]{:S(2)}, u32[]{:S(2)}) %collective-permute-start.20) | collective-permute-done | bytes 2080 | tf_op jit(solution)/shard_map/ppermute | solution.py:22
  (107 shorter events, 12.3 us)
Async XLA Ops:
  1.7 16.5 %collective-permute-start = (f32[16,512]{1,0:T(8,128)S(1)}, f32[16,512]{1,0:T(8,128)S(1)}, u32[]{:S(2)}, u32[]{:S(2)}) collective-permute-start(f32[16,512]{1,0:T(8,128)S(1)} %get-tuple-element.20), channel_id=1, source_target_pairs={{0,1},{1,2},{2,3},{3,0},{4,5},{5,6},{6,7},{7,4},{8,9},{9,10},{10,1... | collective-permute-start | bytes 98312 | tf_op jit(solution)/shard_map/ppermute | solution.py:22
  2.2 16.0 %collective-permute-start.1 = (f32[16,512]{1,0:T(8,128)S(1)}, f32[16,512]{1,0:T(8,128)S(1)}, u32[]{:S(2)}, u32[]{:S(2)}) collective-permute-start(f32[16,512]{1,0:T(8,128)S(1)} %get-tuple-element.19), channel_id=1, source_target_pairs={{0,2},{1,3},{2,0},{3,1},{4,6},{5,7},{6,4},{7,5},{8,10},{9,11},{10,... | collective-permute-start | bytes 98312 | tf_op jit(solution)/shard_map/ppermute | solution.py:22
  4.8 13.4 %collective-permute-start.2 = (f32[16,512]{1,0:T(8,128)S(1)}, f32[16,512]{1,0:T(8,128)S(1)}, u32[]{:S(2)}, u32[]{:S(2)}) collective-permute-start(f32[16,512]{1,0:T(8,128)S(1)} %get-tuple-element.18), channel_id=1, source_target_pairs={{0,3},{1,0},{2,1},{3,2},{4,7},{5,4},{6,5},{7,6},{8,11},{9,8},{10,9... | collective-permute-start | bytes 98312 | tf_op jit(solution)/shard_map/ppermute | solution.py:22
  6.2 15.6 %collective-permute-start.4 = (bf16[64,512]{1,0:T(8,128)(2,1)}, bf16[64,512]{1,0:T(8,128)(2,1)S(1)}, u32[]{:S(2)}, u32[]{:S(2)}) collective-permute-start(bf16[64,512]{1,0:T(8,128)(2,1)} %bitcast.112), channel_id=1, source_target_pairs={{0,4},{4,8},{8,12},{20,16},{24,20},{28,24},{1,5},{5,9},{9,13},{21,... | collective-permute-start | bytes 196616 | tf_op jit(solution)/shard_map/ppermute | solution.py:92
  18.3 13.1 %collective-permute-start.3 = (bf16[16,2048]{1,0:T(8,128)(2,1)S(1)}, bf16[16,2048]{1,0:T(8,128)(2,1)S(1)}, u32[]{:S(2)}, u32[]{:S(2)}) collective-permute-start(bf16[16,2048]{1,0:T(8,128)(2,1)S(1)} %fusion.11), channel_id=1, source_target_pairs={{0,4},{28,24},{1,5},{29,25},{2,6},{30,26},{3,7},{31,27}} | collective-permute-start | bytes 196616 | tf_op jit(solution)/shard_map/ppermute | solution.py:118
  21.8 2.6 %collective-permute-start.5 = (bf16[64,512]{1,0:T(8,128)(2,1)S(1)}, bf16[64,512]{1,0:T(8,128)(2,1)S(1)}, u32[]{:S(2)}, u32[]{:S(2)}) collective-permute-start(bf16[64,512]{1,0:T(8,128)(2,1)S(1)} %collective-permute-done.4), channel_id=1, source_target_pairs={{1,0},{2,1},{3,2},{0,3},{5,4},{6,5},{7,6},{4,7},{9,8},{10,9},{11,1... | collective-permute-start | bytes 196616 | tf_op jit(solution)/shard_map/ppermute | solution.py:34
  22.0 5.6 %collective-permute-start.6 = (bf16[64,512]{1,0:T(8,128)(2,1)S(1)}, bf16[64,512]{1,0:T(8,128)(2,1)S(1)}, u32[]{:S(2)}, u32[]{:S(2)}) collective-permute-start(bf16[64,512]{1,0:T(8,128)(2,1)S(1)} %collective-permute-done.4), channel_id=1, source_target_pairs={{2,0},{3,1},{0,2},{1,3},{6,4},{7,5},{4,6},{5,7},{10,8},{11,9},{8,1... | collective-permute-start | bytes 196616 | tf_op jit(solution)/shard_map/ppermute | solution.py:34
  23.5 4.2 %collective-permute-start.7 = (bf16[64,512]{1,0:T(8,128)(2,1)S(1)}, bf16[64,512]{1,0:T(8,128)(2,1)S(1)}, u32[]{:S(2)}, u32[]{:S(2)}) collective-permute-start(bf16[64,512]{1,0:T(8,128)(2,1)S(1)} %collective-permute-done.4), channel_id=1, source_target_pairs={{3,0},{0,1},{1,2},{2,3},{7,4},{4,5},{5,6},{6,7},{11,8},{8,9},{9,10... | collective-permute-start | bytes 196616 | tf_op jit(solution)/shard_map/ppermute | solution.py:34
  33.0 0.8 collective-permute-start.8
  35.3 2.7 %collective-permute-start.9 = (bf16[16,2048]{1,0:T(8,128)(2,1)S(1)}, bf16[16,2048]{1,0:T(8,128)(2,1)S(1)}, u32[]{:S(2)}, u32[]{:S(2)}) collective-permute-start(bf16[16,2048]{1,0:T(8,128)(2,1)S(1)} %fusion.9), channel_id=1, source_target_pairs={{8,12},{20,16},{9,13},{21,17},{10,14},{22,18},{11,15},{23,19}} | collective-permute-start | bytes 196616 | tf_op jit(solution)/shard_map/ppermute | solution.py:118
  36.0 9.5 %collective-permute-start.11 = (bf16[64,2048]{1,0:T(8,128)(2,1)S(1)}, bf16[64,2048]{1,0:T(8,128)(2,1)S(1)}, u32[]{:S(2)}, u32[]{:S(2)}) collective-permute-start(bf16[64,2048]{1,0:T(8,128)(2,1)S(1)} %bitcast.101), channel_id=1, source_target_pairs={{4,0},{8,4},{12,8},{16,12},{5,1},{9,5},{13,9},{17,13},{6,2},{10,6}... | collective-permute-start | bytes 786440 | tf_op jit(solution)/shard_map/ppermute | solution.py:106
  37.3 8.2 %collective-permute-start.12 = (bf16[64,2048]{1,0:T(8,128)(2,1)S(1)}, bf16[64,2048]{1,0:T(8,128)(2,1)S(1)}, u32[]{:S(2)}, u32[]{:S(2)}) collective-permute-start(bf16[64,2048]{1,0:T(8,128)(2,1)S(1)} %bitcast.102), channel_id=1, source_target_pairs={{12,16},{16,20},{20,24},{24,28},{13,17},{17,21},{21,25},{25,29},{1... | collective-permute-start | bytes 786440 | tf_op jit(solution)/shard_map/ppermute | solution.py:107
  39.6 9.7 %collective-permute-start.10 = (bf16[16,2048]{1,0:T(8,128)(2,1)S(1)}, bf16[16,2048]{1,0:T(8,128)(2,1)S(1)}, u32[]{:S(2)}, u32[]{:S(2)}) collective-permute-start(bf16[16,2048]{1,0:T(8,128)(2,1)S(1)} %fusion.8), channel_id=1, source_target_pairs={{12,16},{16,12},{13,17},{17,13},{14,18},{18,14},{15,19},{19,15}} | collective-permute-start | bytes 196616 | tf_op jit(solution)/shard_map/ppermute | solution.py:118
  50.6 30.7 %copy-start = (bf16[1,64,2048]{2,1,0:T(8,128)(2,1)S(1)}, bf16[1,64,2048]{2,1,0:T(8,128)(2,1)}, u32[]{:S(2)}) copy-start(bf16[1,64,2048]{2,1,0:T(8,128)(2,1)} %param.7) | copy-start | bytes 786436
  50.8 0.9 collective-permute-start.13
  53.3 0.8 collective-permute-start.14
  55.6 17.4 %collective-permute-start.15 = (bf16[16,2048]{1,0:T(8,128)(2,1)S(1)}, bf16[16,2048]{1,0:T(8,128)(2,1)S(1)}, u32[]{:S(2)}, u32[]{:S(2)}) collective-permute-start(bf16[16,2048]{1,0:T(8,128)(2,1)S(1)} %fusion.5), channel_id=1, source_target_pairs={{24,28},{4,0},{25,29},{5,1},{26,30},{6,2},{27,31},{7,3}} | collective-permute-start | bytes 196616 | tf_op jit(solution)/shard_map/ppermute | solution.py:118
  74.7 4.1 %collective-permute-start.16 = (f32[36,512]{1,0:T(8,128)S(1)}, f32[36,512]{1,0:T(8,128)S(1)}, u32[]{:S(2)}, u32[]{:S(2)}) collective-permute-start(f32[36,512]{1,0:T(8,128)S(1)} %get-tuple-element.28), channel_id=1, source_target_pairs={{0,1},{1,2},{2,3},{3,0},{4,5},{5,6},{6,7},{7,4},{8,9},{9,10},{10,1... | collective-permute-start | bytes 221192 | tf_op jit(solution)/shard_map/ppermute | solution.py:133
  74.8 5.4 %collective-permute-start.17 = (f32[36,512]{1,0:T(8,128)S(1)}, f32[36,512]{1,0:T(8,128)S(1)}, u32[]{:S(2)}, u32[]{:S(2)}) collective-permute-start(f32[36,512]{1,0:T(8,128)S(1)} %get-tuple-element.27), channel_id=1, source_target_pairs={{0,2},{1,3},{2,0},{3,1},{4,6},{5,7},{6,4},{7,5},{8,10},{9,11},{10,... | collective-permute-start | bytes 221192 | tf_op jit(solution)/shard_map/ppermute | solution.py:133
  75.8 4.4 %collective-permute-start.18 = (f32[36,512]{1,0:T(8,128)S(1)}, f32[36,512]{1,0:T(8,128)S(1)}, u32[]{:S(2)}, u32[]{:S(2)}) collective-permute-start(f32[36,512]{1,0:T(8,128)S(1)} %get-tuple-element.26), channel_id=1, source_target_pairs={{0,3},{1,0},{2,1},{3,2},{4,7},{5,4},{6,5},{7,6},{8,11},{9,8},{10,9... | collective-permute-start | bytes 221192 | tf_op jit(solution)/shard_map/ppermute | solution.py:133
  91.3 3.3 %collective-permute-start.19 = (f32[512]{0:T(512)S(1)}, f32[512]{0:T(512)S(1)}, u32[]{:S(2)}, u32[]{:S(2)}) collective-permute-start(f32[512]{0:T(512)S(1)} %get-tuple-element.24), channel_id=1, source_target_pairs={{0,1},{1,2},{2,3},{3,0},{4,5},{5,6},{6,7},{7,4},{8,9},{9,10},{10,1... | collective-permute-start | bytes 6152 | tf_op jit(solution)/shard_map/ppermute | solution.py:22
  92.2 3.6 %collective-permute-start.20 = (f32[512]{0:T(512)S(1)}, f32[512]{0:T(512)S(1)}, u32[]{:S(2)}, u32[]{:S(2)}) collective-permute-start(f32[512]{0:T(512)S(1)} %get-tuple-element.23), channel_id=1, source_target_pairs={{0,2},{1,3},{2,0},{3,1},{4,6},{5,7},{6,4},{7,5},{8,10},{9,11},{10,... | collective-permute-start | bytes 6152 | tf_op jit(solution)/shard_map/ppermute | solution.py:22
  93.2 2.8 %collective-permute-start.21 = (f32[512]{0:T(512)S(1)}, f32[512]{0:T(512)S(1)}, u32[]{:S(2)}, u32[]{:S(2)}) collective-permute-start(f32[512]{0:T(512)S(1)} %get-tuple-element.22), channel_id=1, source_target_pairs={{0,3},{1,0},{2,1},{3,2},{4,7},{5,4},{6,5},{7,6},{8,11},{9,8},{10,9... | collective-permute-start | bytes 6152 | tf_op jit(solution)/shard_map/ppermute | solution.py:22

commit v14 on v8

--- a/solution.py
+++ b/solution.py
@@ -116,13 +116,13 @@
     own_cells = cells[0]
     own_slots = own_cells.shape[1]
     cell_norm = norm_of(own_cells)
-    fit_kernel = jnp.exp(-squared_dist(day_pts, day_norm, own_cells, cell_norm))
-    density = jnp.sum(full_mass[:, None] * fit_kernel, axis=0) / mass_total
+    fit_kernel = jnp.exp(-squared_dist(own_cells, cell_norm, day_pts, day_norm))
+    density = jnp.sum(fit_kernel * full_mass[None, :], axis=1) / mass_total
     cell_live = (pt_rank * own_slots + jnp.arange(own_slots, dtype=jnp.int32) < cell_total).astype(
         jnp.float32
     )
     inverse = cell_live / density
-    ratio_rows = jnp.sum(fit_kernel * inverse[None, :], axis=1)
+    ratio_rows = jnp.sum(fit_kernel * inverse[:, None], axis=0)
     summed = sum_scatter_over_pt(ratio_rows)
     fit_rows_out = live_own / cell_total_f * summed
     return (forward_out[None], backward_out[None], fit_rows_out[None])

time: 96 us -> 95.8 us (level)
  no operation moved by 1% of the time
where the time goes in v14:
time: 95.8 us; the launch traced here: 95.5 us
  waiting for transfers between devices  28.1 us (29%)
  starting transfers between devices  24.4 us (25%)
  matrix products  20.7 us (22%)
  other arithmetic  10 us (10%)
  blocking collectives  7.46 us (8%)
  between operations  2.67 us (3%)
  local copies, waits for them, and re-layouts  2.18 us (2%)
    ppermute x7, waiting for transfers between devices, shards(): incoming = lax.ppermute(outgoing, 'day', route)  24.1 us
    dot_general x3, matrix products, squared_dist(): lax.dot_general(left_pts, right_pts, (((0,), (0,)), ((), ())), preferred_...  11.6 us
    ppermute x12, starting transfers between devices, swap_blocks(): lax.ppermute(piece, 'pt', [(i, (i + shift) % count) for i in range(count)])  9.65 us
    ppermute x7, starting transfers between devices, shards(): incoming = lax.ppermute(outgoing, 'day', route)  9.35 us
    dot_general x7, matrix products, shards(): jnp.dot(incoming, kernel, preferred_element_type=jnp.float32)  9.16 us
    all_gather x1, blocking collectives, shards(): day_pts = lax.all_gather(own_pts, 'pt', axis=1, tiled=True)  7.46 us
    reduce_sum x1, other arithmetic, shards(): ratio_rows = jnp.sum(fit_kernel * inverse[:, None], axis=0)  4.73 us
    ppermute x12, waiting for transfers between devices, swap_blocks(): lax.ppermute(piece, 'pt', [(i, (i + shift) % count) for i in range(count)])  3.95 us
  transfers between devices with their start and end apart: 22, of which 5 were waited for; matrix products, arithmetic and copies ran while one was open for 13% of the time, Pallas kernels for 0%

profile of v14, /device:TPU:0, one launch (start us, length us, event | category | flops | bytes accessed | tf_op | source)
XLA Modules:
  0.0 95.5 jit_solution(4421748903322537276)
XLA Ops:
  0.6 7.5 %all-gather = bf16[1,64,2048]{2,1,0:T(8,128)(2,1)S(1)} all-gather(bf16[1,64,512]{2,1,0:T(8,128)(2,1)} %param.6), channel_id=2, replica_groups=mesh['day'=8,'pt'=4] {'pt'}, dimensions={2}, use_global_device_ids=true | all-gather | bytes 327680 | tf_op jit(solution)/shard_map/all_gather | solution.py:57
  8.1 3.4 %collective-permute-start.4 = (bf16[64,2048]{1,0:T(8,128)(2,1)S(1)}, bf16[64,2048]{1,0:T(8,128)(2,1)S(1)}, u32[]{:S(2)}, u32[]{:S(2)}) collective-permute-start(bf16[64,2048]{1,0:T(8,128)(2,1)S(1)} %bitcast.78), channel_id=1, source_target_pairs={{0,4},{4,8},{8,12},{20,16},{24,20},{28,24},{1,5},{5,9},{9,13},{21,... | collective-permute-start | bytes 786440 | tf_op jit(solution)/shard_map/ppermute | solution.py:76
  11.5 1.3 %collective-permute-start.8 = (bf16[64,2048]{1,0:T(8,128)(2,1)S(1)}, bf16[64,2048]{1,0:T(8,128)(2,1)S(1)}, u32[]{:S(2)}, u32[]{:S(2)}) collective-permute-start(bf16[64,2048]{1,0:T(8,128)(2,1)S(1)} %bitcast.79), channel_id=1, source_target_pairs={{4,0},{8,4},{12,8},{16,12},{5,1},{9,5},{13,9},{17,13},{6,2},{10,6}... | collective-permute-start | bytes 786440 | tf_op jit(solution)/shard_map/ppermute | solution.py:89
  12.8 0.7 collective-permute-start.9
  13.5 0.9 bitcast_multiply_fusion
  14.7 1.5 %collective-permute-start.1 = (f32[16,512]{1,0:T(8,128)S(1)}, f32[16,512]{1,0:T(8,128)S(1)}, u32[]{:S(2)}, u32[]{:S(2)}) collective-permute-start(f32[16,512]{1,0:T(8,128)S(1)} %get-tuple-element.16), channel_id=1, source_target_pairs={{0,2},{1,3},{2,0},{3,1},{4,6},{5,7},{6,4},{7,5},{8,10},{9,11},{10,... | collective-permute-start | bytes 98312 | tf_op jit(solution)/shard_map/ppermute | solution.py:22
  17.2 0.7 collective-permute-done
  17.9 0.7 collective-permute-start.2
  18.7 1.6 %collective-permute-done.2 = f32[16,512]{1,0:T(8,128)S(1)} collective-permute-done((f32[16,512]{1,0:T(8,128)S(1)}, f32[16,512]{1,0:T(8,128)S(1)}, u32[]{:S(2)}, u32[]{:S(2)}) %collective-permute-start.2) | collective-permute-done | bytes 32800 | tf_op jit(solution)/shard_map/ppermute | solution.py:22
  20.3 4.5 %collective-permute-start.3 = (bf16[16,2048]{1,0:T(8,128)(2,1)S(1)}, bf16[16,2048]{1,0:T(8,128)(2,1)S(1)}, u32[]{:S(2)}, u32[]{:S(2)}) collective-permute-start(bf16[16,2048]{1,0:T(8,128)(2,1)S(1)} %fusion.11), channel_id=1, source_target_pairs={{0,4},{28,24},{1,5},{29,25},{2,6},{30,26},{3,7},{31,27}} | collective-permute-start | bytes 196616 | tf_op jit(solution)/shard_map/ppermute | solution.py:101
  24.9 3.6 %exponential_convert_fusion.1 = bf16[2048,2048]{1,0:T(8,128)(2,1)S(1)} fusion(bf16[64,2048]{1,0:T(8,128)(2,1)S(1)} %collective-permute-done.4, f32[2048]{0:T(1024)S(1)} %multiply_reduce_fusion.4, f32[2048]{0:T(1024)S(1)} %multiply_reduce_fusion.5, bf16[1,64,2048]{2,1,0:T(8,128)(2,1)S(1)} %all-gather), kind=kOutput, calls=%fused_computation.4 | convolution fusion | flops 557842432 | bytes 8929280 | tf_op jit(solution)/shard_map/dot_general | solution.py:45
  28.6 1.3 %fusion.21 = (f32[16]{0:T(128)S(1)}, f32[16,2048]{1,0:T(8,128)S(1)}) fusion(f32[2048]{0:T(1024)S(1)} %fusion.13, bf16[16,2048]{1,0:T(8,128)(2,1)S(1)} %collective-permute-done.3, bf16[2048,2048]{1,0:T(8,128)(2,1)S(1)} %exponential_convert_fusion.1), kind=kOutput, calls=%fused_computation.91 | convolution fusion | flops 134283248 | bytes 8593472 | tf_op jit(solution)/shard_map/dot_general | solution.py:102
  30.8 1.3 %fusion.22 = (f32[16]{0:T(128)S(1)}, f32[16,2048]{1,0:T(8,128)S(1)}) fusion(f32[2048]{0:T(1024)S(1)} %fusion.13, bf16[16,2048]{1,0:T(8,128)(2,1)S(1)} %collective-permute-done.5, bf16[2048,2048]{1,0:T(8,128)(2,1)S(1)} %exponential_convert_fusion.1), kind=kOutput, calls=%fused_computation.92 | convolution fusion | flops 134283248 | bytes 8593472 | tf_op jit(solution)/shard_map/dot_general | solution.py:102
  33.1 1.3 %fusion.23 = (f32[16]{0:T(128)S(1)}, f32[16,2048]{1,0:T(8,128)S(1)}) fusion(f32[2048]{0:T(1024)S(1)} %fusion.13, bf16[16,2048]{1,0:T(8,128)(2,1)S(1)} %collective-permute-done.6, bf16[2048,2048]{1,0:T(8,128)(2,1)S(1)} %exponential_convert_fusion.1), kind=kOutput, calls=%fused_computation.93 | convolution fusion | flops 134283248 | bytes 8593472 | tf_op jit(solution)/shard_map/dot_general | solution.py:102
  35.4 3.6 %exponential_convert_fusion = bf16[2048,2048]{1,0:T(8,128)(2,1)S(1)} fusion(bf16[64,2048]{1,0:T(8,128)(2,1)S(1)} %broadcast_select_fusion, f32[2048]{0:T(1024)S(1)} %multiply_reduce_fusion.3, f32[2048]{0:T(1024)S(1)} %multiply_reduce_fusion.4, bf16[1,64,2048]{2,1,0:T(8,128)(2,1)S(1)} %all-gather), kind=kOutput, calls=%fused_computation.3 | convolution fusion | flops 557842432 | bytes 8929280 | tf_op jit(solution)/shard_map/dot_general | solution.py:45
  39.0 1.3 %fusion.24 = (f32[16]{0:T(128)S(1)}, f32[16,2048]{1,0:T(8,128)S(1)}) fusion(f32[2048]{0:T(1024)S(1)} %fusion.13, bf16[16,2048]{1,0:T(8,128)(2,1)S(1)} %collective-permute-done.7, bf16[2048,2048]{1,0:T(8,128)(2,1)S(1)} %exponential_convert_fusion), kind=kOutput, calls=%fused_computation.94 | convolution fusion | flops 134283248 | bytes 8593472 | tf_op jit(solution)/shard_map/dot_general | solution.py:102
  41.3 1.3 %fusion.25 = (f32[16]{0:T(128)S(1)}, f32[16,2048]{1,0:T(8,128)S(1)}) fusion(f32[2048]{0:T(1024)S(1)} %fusion.13, bf16[16,2048]{1,0:T(8,128)(2,1)S(1)} %collective-permute-done.10, bf16[2048,2048]{1,0:T(8,128)(2,1)S(1)} %exponential_convert_fusion), kind=kOutput, calls=%fused_computation.95 | convolution fusion | flops 134283248 | bytes 8593472 | tf_op jit(solution)/shard_map/dot_general | solution.py:102
  42.9 0.8 collective-permute-start.11
  43.8 1.3 %fusion.26 = (f32[16]{0:T(128)S(1)}, f32[16,2048]{1,0:T(8,128)S(1)}) fusion(f32[2048]{0:T(1024)S(1)} %fusion.13, bf16[16,2048]{1,0:T(8,128)(2,1)S(1)} %collective-permute-done.11, bf16[2048,2048]{1,0:T(8,128)(2,1)S(1)} %exponential_convert_fusion), kind=kOutput, calls=%fused_computation.96 | convolution fusion | flops 134283248 | bytes 8593472 | tf_op jit(solution)/shard_map/dot_general | solution.py:102
  45.4 1.3 %collective-permute-start.12 = (bf16[16,2048]{1,0:T(8,128)(2,1)S(1)}, bf16[16,2048]{1,0:T(8,128)(2,1)S(1)}, u32[]{:S(2)}, u32[]{:S(2)}) collective-permute-start(bf16[16,2048]{1,0:T(8,128)(2,1)S(1)} %fusion.5), channel_id=1, source_target_pairs={{24,28},{4,0},{25,29},{5,1},{26,30},{6,2},{27,31},{7,3}} | collective-permute-start | bytes 196616 | tf_op jit(solution)/shard_map/ppermute | solution.py:101
  46.8 24.1 %collective-permute-done.12 = bf16[16,2048]{1,0:T(8,128)(2,1)S(1)} collective-permute-done((bf16[16,2048]{1,0:T(8,128)(2,1)S(1)}, bf16[16,2048]{1,0:T(8,128)(2,1)S(1)}, u32[]{:S(2)}, u32[]{:S(2)}) %collective-permute-start.12) | collective-permute-done | bytes 65568 | tf_op jit(solution)/shard_map/ppermute | solution.py:101
  70.8 1.3 %fusion.27 = (f32[16]{0:T(128)S(1)}, f32[16,2048]{1,0:T(8,128)S(1)}) fusion(f32[2048]{0:T(1024)S(1)} %fusion.13, bf16[16,2048]{1,0:T(8,128)(2,1)S(1)} %collective-permute-done.12, bf16[2048,2048]{1,0:T(8,128)(2,1)S(1)} %exponential_convert_fusion), kind=kOutput, calls=%fused_computation.97 | convolution fusion | flops 134283248 | bytes 8593472 | tf_op jit(solution)/shard_map/dot_general | solution.py:102
  72.5 0.8 collective-permute-start.17
  73.4 1.4 %collective-permute-start.18 = (f32[1,2048]{1,0:T(1,128)S(1)}, f32[1,2048]{1,0:T(1,128)S(1)}, u32[]{:S(2)}, u32[]{:S(2)}) collective-permute-start(f32[1,2048]{1,0:T(1,128)S(1)} %bitcast.83), channel_id=1, source_target_pairs={{0,3},{1,0},{2,1},{3,2},{4,7},{5,4},{6,5},{7,6},{8,11},{9,8},{10,9... | collective-permute-start | bytes 24584 | tf_op jit(solution)/shard_map/ppermute | solution.py:22
  77.1 4.3 %multiply_reduce_fusion.1 = (f32[2048]{0:T(1024)S(1)}, f32[2048,2048]{1,0:T(8,128)S(1)}) fusion(f32[2048]{0:T(1024)S(1)} %get-tuple-element.8, f32[2048]{0:T(1024)S(1)} %multiply_reduce_fusion.2, f32[2048]{0:T(1024)S(1)} %multiply_reduce_fusion.4, bf16[1,64,2048]{2,1,0:T(8,128)(2,1)S(1)} %all-gather, bf16[1,64,2048]{2,1,0:T(8,128)(2,1)S(1)} %copy-done), kind=kOutput, calls=%fused_computation.1 | convolution fusion | flops 562034688 | bytes 17334272 | tf_op jit(solution)/shard_map/dot_general | solution.py:45
  82.1 4.7 %multiply_reduce_fusion = f32[2048]{0:T(1024)S(1)} fusion(f32[2048,2048]{1,0:T(8,128)S(1)} %get-tuple-element.38, f32[2048]{0:T(1024)S(1)} %select_divide_fusion, f32[2048]{0:T(1024)S(1)} %multiply_reduce_fusion.2, f32[2048]{0:T(1024)S(1)} %multiply_reduce_fusion.4), kind=kLoop, calls=%fused_computation | loop fusion | flops 25163776 | bytes 16809984 | tf_op jit(solution)/shard_map/reduce_sum | solution.py:125
  87.1 1.1 %collective-permute-start.19 = (f32[512]{0:T(512)S(1)}, f32[512]{0:T(512)S(1)}, u32[]{:S(2)}, u32[]{:S(2)}) collective-permute-start(f32[512]{0:T(512)S(1)} %get-tuple-element.21), channel_id=1, source_target_pairs={{0,1},{1,2},{2,3},{3,0},{4,5},{5,6},{6,7},{7,4},{8,9},{9,10},{10,1... | collective-permute-start | bytes 6152 | tf_op jit(solution)/shard_map/ppermute | solution.py:22
  88.1 0.8 collective-permute-start.20
  89.7 1.1 %collective-permute-start.14 = (f32[2,16,512]{2,1,0:T(8,128)S(1)}, f32[2,16,512]{2,1,0:T(8,128)S(1)}, u32[]{:S(2)}, u32[]{:S(2)}) collective-permute-start(f32[2,16,512]{2,1,0:T(8,128)S(1)} %get-tuple-element.12), channel_id=1, source_target_pairs={{0,2},{1,3},{2,0},{3,1},{4,6},{5,7},{6,4},{7,5},{8,10},{9,11},{10,... | collective-permute-start | bytes 196616 | tf_op jit(solution)/shard_map/ppermute | solution.py:22
  90.8 1.4 %collective-permute-start.15 = (f32[2,16,512]{2,1,0:T(8,128)S(1)}, f32[2,16,512]{2,1,0:T(8,128)S(1)}, u32[]{:S(2)}, u32[]{:S(2)}) collective-permute-start(f32[2,16,512]{2,1,0:T(8,128)S(1)} %get-tuple-element.11), channel_id=1, source_target_pairs={{0,3},{1,0},{2,1},{3,2},{4,7},{5,4},{6,5},{7,6},{8,11},{9,8},{10,9... | collective-permute-start | bytes 196616 | tf_op jit(solution)/shard_map/ppermute | solution.py:22
  93.5 1.2 %collective-permute-done.14 = f32[2,16,512]{2,1,0:T(8,128)S(1)} collective-permute-done((f32[2,16,512]{2,1,0:T(8,128)S(1)}, f32[2,16,512]{2,1,0:T(8,128)S(1)}, u32[]{:S(2)}, u32[]{:S(2)}) %collective-permute-start.14) | collective-permute-done | bytes 65568 | tf_op jit(solution)/shard_map/ppermute | solution.py:22
  94.8 0.7 fusion.19
  (89 shorter events, 9.9 us)
Async XLA Ops:
  8.1 16.8 %collective-permute-start.4 = (bf16[64,2048]{1,0:T(8,128)(2,1)S(1)}, bf16[64,2048]{1,0:T(8,128)(2,1)S(1)}, u32[]{:S(2)}, u32[]{:S(2)}) collective-permute-start(bf16[64,2048]{1,0:T(8,128)(2,1)S(1)} %bitcast.78), channel_id=1, source_target_pairs={{0,4},{4,8},{8,12},{20,16},{24,20},{28,24},{1,5},{5,9},{9,13},{21,... | collective-permute-start | bytes 786440 | tf_op jit(solution)/shard_map/ppermute | solution.py:76
  11.5 19.3 %collective-permute-start.8 = (bf16[64,2048]{1,0:T(8,128)(2,1)S(1)}, bf16[64,2048]{1,0:T(8,128)(2,1)S(1)}, u32[]{:S(2)}, u32[]{:S(2)}) collective-permute-start(bf16[64,2048]{1,0:T(8,128)(2,1)S(1)} %bitcast.79), channel_id=1, source_target_pairs={{4,0},{8,4},{12,8},{16,12},{5,1},{9,5},{13,9},{17,13},{6,2},{10,6}... | collective-permute-start | bytes 786440 | tf_op jit(solution)/shard_map/ppermute | solution.py:89
  12.8 18.0 %collective-permute-start.9 = (bf16[64,2048]{1,0:T(8,128)(2,1)S(1)}, bf16[64,2048]{1,0:T(8,128)(2,1)S(1)}, u32[]{:S(2)}, u32[]{:S(2)}) collective-permute-start(bf16[64,2048]{1,0:T(8,128)(2,1)S(1)} %bitcast.80), channel_id=1, source_target_pairs={{12,16},{16,20},{20,24},{24,28},{13,17},{17,21},{21,25},{25,29},{1... | collective-permute-start | bytes 786440 | tf_op jit(solution)/shard_map/ppermute | solution.py:90
  14.6 3.4 %collective-permute-start = (f32[16,512]{1,0:T(8,128)S(1)}, f32[16,512]{1,0:T(8,128)S(1)}, u32[]{:S(2)}, u32[]{:S(2)}) collective-permute-start(f32[16,512]{1,0:T(8,128)S(1)} %get-tuple-element.17), channel_id=1, source_target_pairs={{0,1},{1,2},{2,3},{3,0},{4,5},{5,6},{6,7},{7,4},{8,9},{9,10},{10,1... | collective-permute-start | bytes 98312 | tf_op jit(solution)/shard_map/ppermute | solution.py:22
  14.7 4.0 %collective-permute-start.1 = (f32[16,512]{1,0:T(8,128)S(1)}, f32[16,512]{1,0:T(8,128)S(1)}, u32[]{:S(2)}, u32[]{:S(2)}) collective-permute-start(f32[16,512]{1,0:T(8,128)S(1)} %get-tuple-element.16), channel_id=1, source_target_pairs={{0,2},{1,3},{2,0},{3,1},{4,6},{5,7},{6,4},{7,5},{8,10},{9,11},{10,... | collective-permute-start | bytes 98312 | tf_op jit(solution)/shard_map/ppermute | solution.py:22
  17.9 2.3 %collective-permute-start.2 = (f32[16,512]{1,0:T(8,128)S(1)}, f32[16,512]{1,0:T(8,128)S(1)}, u32[]{:S(2)}, u32[]{:S(2)}) collective-permute-start(f32[16,512]{1,0:T(8,128)S(1)} %get-tuple-element.15), channel_id=1, source_target_pairs={{0,3},{1,0},{2,1},{3,2},{4,7},{5,4},{6,5},{7,6},{8,11},{9,8},{10,9... | collective-permute-start | bytes 98312 | tf_op jit(solution)/shard_map/ppermute | solution.py:22
  20.3 8.3 %collective-permute-start.3 = (bf16[16,2048]{1,0:T(8,128)(2,1)S(1)}, bf16[16,2048]{1,0:T(8,128)(2,1)S(1)}, u32[]{:S(2)}, u32[]{:S(2)}) collective-permute-start(bf16[16,2048]{1,0:T(8,128)(2,1)S(1)} %fusion.11), channel_id=1, source_target_pairs={{0,4},{28,24},{1,5},{29,25},{2,6},{30,26},{3,7},{31,27}} | collective-permute-start | bytes 196616 | tf_op jit(solution)/shard_map/ppermute | solution.py:101
  30.1 0.7 collective-permute-start.5
  32.4 0.8 collective-permute-start.6
  34.7 4.3 %collective-permute-start.7 = (bf16[16,2048]{1,0:T(8,128)(2,1)S(1)}, bf16[16,2048]{1,0:T(8,128)(2,1)S(1)}, u32[]{:S(2)}, u32[]{:S(2)}) collective-permute-start(bf16[16,2048]{1,0:T(8,128)(2,1)S(1)} %fusion.8), channel_id=1, source_target_pairs={{12,16},{16,12},{13,17},{17,13},{14,18},{18,14},{15,19},{19,15}} | collective-permute-start | bytes 196616 | tf_op jit(solution)/shard_map/ppermute | solution.py:101
  40.3 34.4 %copy-start = (bf16[1,64,2048]{2,1,0:T(8,128)(2,1)S(1)}, bf16[1,64,2048]{2,1,0:T(8,128)(2,1)}, u32[]{:S(2)}) copy-start(bf16[1,64,2048]{2,1,0:T(8,128)(2,1)} %param.7) | copy-start | bytes 786436
  40.5 0.8 collective-permute-start.10
  42.9 0.9 collective-permute-start.11
  45.4 25.5 %collective-permute-start.12 = (bf16[16,2048]{1,0:T(8,128)(2,1)S(1)}, bf16[16,2048]{1,0:T(8,128)(2,1)S(1)}, u32[]{:S(2)}, u32[]{:S(2)}) collective-permute-start(bf16[16,2048]{1,0:T(8,128)(2,1)S(1)} %fusion.5), channel_id=1, source_target_pairs={{24,28},{4,0},{25,29},{5,1},{26,30},{6,2},{27,31},{7,3}} | collective-permute-start | bytes 196616 | tf_op jit(solution)/shard_map/ppermute | solution.py:101
  72.5 3.2 %collective-permute-start.16 = (f32[1,2048]{1,0:T(1,128)S(1)}, f32[1,2048]{1,0:T(1,128)S(1)}, u32[]{:S(2)}, u32[]{:S(2)}) collective-permute-start(f32[1,2048]{1,0:T(1,128)S(1)} %bitcast.81), channel_id=1, source_target_pairs={{0,1},{1,2},{2,3},{3,0},{4,5},{5,6},{6,7},{7,4},{8,9},{9,10},{10,1... | collective-permute-start | bytes 24584 | tf_op jit(solution)/shard_map/ppermute | solution.py:22
  72.5 3.7 %collective-permute-start.17 = (f32[1,2048]{1,0:T(1,128)S(1)}, f32[1,2048]{1,0:T(1,128)S(1)}, u32[]{:S(2)}, u32[]{:S(2)}) collective-permute-start(f32[1,2048]{1,0:T(1,128)S(1)} %bitcast.82), channel_id=1, source_target_pairs={{0,2},{1,3},{2,0},{3,1},{4,6},{5,7},{6,4},{7,5},{8,10},{9,11},{10,... | collective-permute-start | bytes 24584 | tf_op jit(solution)/shard_map/ppermute | solution.py:22
  73.4 3.0 %collective-permute-start.18 = (f32[1,2048]{1,0:T(1,128)S(1)}, f32[1,2048]{1,0:T(1,128)S(1)}, u32[]{:S(2)}, u32[]{:S(2)}) collective-permute-start(f32[1,2048]{1,0:T(1,128)S(1)} %bitcast.83), channel_id=1, source_target_pairs={{0,3},{1,0},{2,1},{3,2},{4,7},{5,4},{6,5},{7,6},{8,11},{9,8},{10,9... | collective-permute-start | bytes 24584 | tf_op jit(solution)/shard_map/ppermute | solution.py:22
  87.1 3.7 %collective-permute-start.19 = (f32[512]{0:T(512)S(1)}, f32[512]{0:T(512)S(1)}, u32[]{:S(2)}, u32[]{:S(2)}) collective-permute-start(f32[512]{0:T(512)S(1)} %get-tuple-element.21), channel_id=1, source_target_pairs={{0,1},{1,2},{2,3},{3,0},{4,5},{5,6},{6,7},{7,4},{8,9},{9,10},{10,1... | collective-permute-start | bytes 6152 | tf_op jit(solution)/shard_map/ppermute | solution.py:22
  88.1 4.2 %collective-permute-start.20 = (f32[512]{0:T(512)S(1)}, f32[512]{0:T(512)S(1)}, u32[]{:S(2)}, u32[]{:S(2)}) collective-permute-start(f32[512]{0:T(512)S(1)} %get-tuple-element.20), channel_id=1, source_target_pairs={{0,2},{1,3},{2,0},{3,1},{4,6},{5,7},{6,4},{7,5},{8,10},{9,11},{10,... | collective-permute-start | bytes 6152 | tf_op jit(solution)/shard_map/ppermute | solution.py:22
  88.9 3.7 %collective-permute-start.21 = (f32[512]{0:T(512)S(1)}, f32[512]{0:T(512)S(1)}, u32[]{:S(2)}, u32[]{:S(2)}) collective-permute-start(f32[512]{0:T(512)S(1)} %get-tuple-element.19), channel_id=1, source_target_pairs={{0,3},{1,0},{2,1},{3,2},{4,7},{5,4},{6,5},{7,6},{8,11},{9,8},{10,9... | collective-permute-start | bytes 6152 | tf_op jit(solution)/shard_map/ppermute | solution.py:22
  89.6 3.9 %collective-permute-start.13 = (f32[2,16,512]{2,1,0:T(8,128)S(1)}, f32[2,16,512]{2,1,0:T(8,128)S(1)}, u32[]{:S(2)}, u32[]{:S(2)}) collective-permute-start(f32[2,16,512]{2,1,0:T(8,128)S(1)} %get-tuple-element.13), channel_id=1, source_target_pairs={{0,1},{1,2},{2,3},{3,0},{4,5},{5,6},{6,7},{7,4},{8,9},{9,10},{10,1... | collective-permute-start | bytes 196616 | tf_op jit(solution)/shard_map/ppermute | solution.py:22
  89.7 5.0 %collective-permute-start.14 = (f32[2,16,512]{2,1,0:T(8,128)S(1)}, f32[2,16,512]{2,1,0:T(8,128)S(1)}, u32[]{:S(2)}, u32[]{:S(2)}) collective-permute-start(f32[2,16,512]{2,1,0:T(8,128)S(1)} %get-tuple-element.12), channel_id=1, source_target_pairs={{0,2},{1,3},{2,0},{3,1},{4,6},{5,7},{6,4},{7,5},{8,10},{9,11},{10,... | collective-permute-start | bytes 196616 | tf_op jit(solution)/shard_map/ppermute | solution.py:22
  90.8 4.0 %collective-permute-start.15 = (f32[2,16,512]{2,1,0:T(8,128)S(1)}, f32[2,16,512]{2,1,0:T(8,128)S(1)}, u32[]{:S(2)}, u32[]{:S(2)}) collective-permute-start(f32[2,16,512]{2,1,0:T(8,128)S(1)} %get-tuple-element.11), channel_id=1, source_target_pairs={{0,3},{1,0},{2,1},{3,2},{4,7},{5,4},{6,5},{7,6},{8,11},{9,8},{10,9... | collective-permute-start | bytes 196616 | tf_op jit(solution)/shard_map/ppermute | solution.py:22

commit v15 on v9

--- a/solution.py
+++ b/solution.py
@@ -69,39 +69,65 @@
         return jnp.exp(-dist).astype(jnp.bfloat16)
 
     half = day_count // 2
-    switch_step = half - 1
-    first_forward = day_index < half
-    first_route = [(d - 1, d) for d in range(1, half)]
-    first_route += [(d + 1, d) for d in range(half, day_count - 1)]
-    first_kernel = chain_kernel(lax.ppermute(day_pts, "day", first_route))
+    even_day = day_index % 2 == 0
+    pair_route = [(d + 1, d) if d % 2 == 0 else (d - 1, d) for d in range(day_count)]
+    link_route = [(d - 1, d) if d % 2 == 0 else (d + 1, d) for d in range(1, day_count - 1)]
+    other_kernel = chain_kernel(lax.ppermute(day_pts, "day", pair_route))
+    other_weight = lax.ppermute(block_weight, "day", pair_route)
+    other_count = lax.ppermute(support_count, "day", pair_route)[0]
+    other_total = other_count.astype(jnp.float32)
+    other_live = (jnp.arange(support_total, dtype=jnp.int32) < other_count).astype(jnp.float32)
+    link_pts = lax.ppermute(day_pts, "day", link_route)
 
-    def settle(values):
-        masked = values * live_all[None, :]
-        return masked * live_total / jnp.sum(masked, axis=1, keepdims=True)
+    def settle(values, live, total):
+        masked = values * live[None, :]
+        return masked * total / jnp.sum(masked, axis=1, keepdims=True)
 
-    rows = jnp.broadcast_to(live_all[None, None, :], (2, block_rows, support_total))
-    later_kernel = None
-    for step in range(day_count - 1):
-        if step == min(1, switch_step):
-            later_pts, rows = lax.optimization_barrier((day_pts, rows))
-            later_source = jnp.where(
-                first_forward,
-                lax.ppermute(later_pts, "day", [(d + 1, d) for d in range(half)]),
-                lax.ppermute(later_pts, "day", [(d - 1, d) for d in range(half, day_count)]),
+    seed_rows = jnp.broadcast_to(live_all[None, :], (block_rows, support_total))
+    own_rows = seed_rows
+    handed_rows = jnp.zeros_like(seed_rows)
+    incoming = None
+    link_kernel = None
+    for round_index in range(half):
+        forward_day = 2 * round_index
+        backward_day = day_count - 1 - 2 * round_index
+        if round_index == 0:
+            current = seed_rows
+        else:
+            current = settle(
+                jnp.dot(incoming, link_kernel, preferred_element_type=jnp.float32),
+                live_all,
+                live_total,
             )
-        if step == switch_step:
-            later_source = lax.optimization_barrier((later_source, rows))[0]
-            later_kernel = chain_kernel(later_source)
-        kernel = first_kernel if step < switch_step else later_kernel
-        forward_from = step
-        backward_from = day_count - 1 - step
-        sent = (rows * block_weight[None]).astype(jnp.bfloat16)
-        outgoing = jnp.where(day_index == forward_from, sent[0], sent[1])
-        route = [(forward_from, forward_from + 1), (backward_from, backward_from - 1)]
-        incoming = lax.ppermute(outgoing, "day", route)
-        fresh = settle(jnp.dot(incoming, kernel, preferred_element_type=jnp.float32))
-        keep = jnp.stack([day_index == step + 1, day_index == day_count - 2 - step])
-        rows = jnp.where(keep[:, None, None], fresh[None], rows)
+            active = (day_index == forward_day) | (day_index == backward_day)
+            own_rows = jnp.where(active, current, own_rows)
+        sent = (current * block_weight).astype(jnp.bfloat16)
+        following = settle(
+            lax.dot_general(
+                sent, other_kernel, (((1,), (1,)), ((), ())), preferred_element_type=jnp.float32
+            ),
+            other_live,
+            other_total,
+        )
+        if round_index == 0:
+            link_pts = lax.optimization_barrier((link_pts, following))[0]
+            link_kernel = chain_kernel(link_pts)
+        if round_index < half - 1:
+            outgoing = (following * other_weight).astype(jnp.bfloat16)
+            incoming = lax.ppermute(
+                outgoing, "day", [(forward_day, forward_day + 2), (backward_day, backward_day - 2)]
+            )
+        handed = lax.ppermute(
+            following, "day", [(forward_day, forward_day + 1), (backward_day, backward_day - 1)]
+        )
+        receiver = (day_index == forward_day + 1) | (day_index == backward_day - 1)
+        handed_rows = jnp.where(receiver, handed, handed_rows)
+    rows = jnp.stack(
+        [
+            jnp.where(even_day, own_rows, handed_rows),
+            jnp.where(even_day, handed_rows, own_rows),
+        ]
+    )
     forward_rows = rows[0]
     backward_rows = rows[1]
     both_out = swap_blocks(rows, 2, 1, (2, own_weight.shape[0], per_device))

time: 96.9 us -> 96.5 us (level)
  waiting for transfers between devices: 29.8 us -> 13.9 us
  matrix products: 20.6 us -> 31.8 us
  starting transfers between devices: 25.1 us -> 27.9 us
  blocking collectives: 5.97 us -> 7.46 us
    ppermute x10 -> x11, waiting for transfers between devices: 27.9 us -> 11.5 us  [the longest x4 8.11 us: shards(): lax.ppermute(following, 'day', [(forward_day, forward_day + 1), (backward...]
    dot_general x7, matrix products: 9.15 us -> 20.3 us  [the longest x4 13 us: shards(): lax.dot_general(sent, other_kernel, (((1,), (1,)), ((), ())), preferred_e...]
    ppermute x10 -> x11, starting transfers between devices: 13.6 us -> 17.9 us  [the longest x3 5.11 us: shards(): lax.ppermute(outgoing, 'day', [(forward_day, forward_day + 2), (backward_...]
    ppermute x12, starting transfers between devices: 11.5 us -> 9.97 us  [swap_blocks(): lax.ppermute(piece, 'pt', [(i, (i + shift) % count) for i in range(count)])]
    all_gather x1, blocking collectives: 5.97 us -> 7.46 us  [shards(): day_pts = lax.all_gather(own_pts, 'pt', axis=1, tiled=True)]
  transfers between devices with their start and end apart: 22 -> 23, of which waited for: 6 -> 7; matrix products, arithmetic and copies ran while one was open for 12% -> 25% of each run, Pallas kernels for 0% -> 0%
where the time goes in v15:
time: 96.5 us; the launch traced here: 96.1 us
  matrix products  31.8 us (33%)
  starting transfers between devices  27.9 us (29%)
  waiting for transfers between devices  13.9 us (14%)
  other arithmetic  9.46 us (10%)
  blocking collectives  7.46 us (8%)
  between operations  3.31 us (3%)
  local copies, waits for them, and re-layouts  2.3 us (2%)
    dot_general x4, matrix products, shards(): lax.dot_general(sent, other_kernel, (((1,), (1,)), ((), ())), preferred_e...  13 us
    dot_general x3, matrix products, squared_dist(): lax.dot_general(left_pts, right_pts, (((0,), (0,)), ((), ())), preferred_...  11.5 us
    ppermute x12, starting transfers between devices, swap_blocks(): lax.ppermute(piece, 'pt', [(i, (i + shift) % count) for i in range(count)])  9.97 us
    ppermute x4, waiting for transfers between devices, shards(): lax.ppermute(following, 'day', [(forward_day, forward_day + 1), (backward...  8.11 us
    all_gather x1, blocking collectives, shards(): day_pts = lax.all_gather(own_pts, 'pt', axis=1, tiled=True)  7.46 us
    dot_general x3, matrix products, shards(): jnp.dot(incoming, link_kernel, preferred_element_type=jnp.float32)  7.31 us
    ppermute x3, starting transfers between devices, shards(): lax.ppermute(outgoing, 'day', [(forward_day, forward_day + 2), (backward_...  5.11 us
    reduce_sum x1, other arithmetic, shards(): ratio_rows = jnp.sum(fit_kernel * inverse[None, :], axis=1)  5.03 us
  transfers between devices with their start and end apart: 23, of which 7 were waited for; matrix products, arithmetic and copies ran while one was open for 25% of the time, Pallas kernels for 0%

profile of v15, /device:TPU:0, one launch (start us, length us, event | category | flops | bytes accessed | tf_op | source)
XLA Modules:
  0.0 96.1 jit_solution(9451725298130748449)
XLA Ops:
  0.6 7.5 %all-gather = bf16[1,64,2048]{2,1,0:T(8,128)(2,1)S(1)} all-gather(bf16[1,64,512]{2,1,0:T(8,128)(2,1)} %param.6), channel_id=2, replica_groups=mesh['day'=8,'pt'=4] {'pt'}, dimensions={2}, use_global_device_ids=true | all-gather | bytes 327680 | tf_op jit(solution)/shard_map/all_gather | solution.py:57
  8.1 1.5 %collective-permute-start.3 = (bf16[64,2048]{1,0:T(8,128)(2,1)S(1)}, bf16[64,2048]{1,0:T(8,128)(2,1)S(1)}, u32[]{:S(2)}, u32[]{:S(2)}) collective-permute-start(bf16[64,2048]{1,0:T(8,128)(2,1)S(1)} %bitcast.45), channel_id=1, source_target_pairs={{4,0},{0,4},{12,8},{8,12},{20,16},{16,20},{28,24},{24,28},{5,1},{1... | collective-permute-start | bytes 786440 | tf_op jit(solution)/shard_map/ppermute | solution.py:75
  10.3 0.9 bitcast_multiply_fusion
  11.4 1.5 %collective-permute-start.1 = (f32[16,512]{1,0:T(8,128)S(1)}, f32[16,512]{1,0:T(8,128)S(1)}, u32[]{:S(2)}, u32[]{:S(2)}) collective-permute-start(f32[16,512]{1,0:T(8,128)S(1)} %get-tuple-element.25), channel_id=1, source_target_pairs={{0,2},{1,3},{2,0},{3,1},{4,6},{5,7},{6,4},{7,5},{8,10},{9,11},{10,... | collective-permute-start | bytes 98312 | tf_op jit(solution)/shard_map/ppermute | solution.py:22
  13.0 4.3 %collective-permute-start.4 = (s32[1]{0:T(128)}, s32[1]{0:T(128)}, u32[]{:S(2)}, u32[]{:S(2)}) collective-permute-start(s32[1]{0:T(128)} %param.10), channel_id=1, source_target_pairs={{4,0},{0,4},{12,8},{8,12},{20,16},{16,20},{28,24},{24,28},{5,1},{1... | collective-permute-start | bytes 20 | tf_op jit(solution)/shard_map/ppermute | solution.py:77
  18.0 3.3 %collective-permute-done.4 = s32[1]{0:T(128)} collective-permute-done((s32[1]{0:T(128)}, s32[1]{0:T(128)}, u32[]{:S(2)}, u32[]{:S(2)}) %collective-permute-start.4) | collective-permute-done | bytes 36 | tf_op jit(solution)/shard_map/ppermute | solution.py:77
  21.9 0.7 fusion.12
  23.5 2.4 %collective-permute-start.5 = (f32[16,2048]{1,0:T(8,128)S(1)}, f32[16,2048]{1,0:T(8,128)S(1)}, u32[]{:S(2)}, u32[]{:S(2)}) collective-permute-start(f32[16,2048]{1,0:T(8,128)S(1)} %constant_dynamic-update-slice_fusion.3), channel_id=1, source_target_pairs={{4,0},{0,4},{12,8},{8,12},{20,16},{16,20},{28,24},{24,28},{5,1},{1... | collective-permute-start | bytes 393224 | tf_op jit(solution)/shard_map/ppermute | solution.py:76
  26.1 3.6 %exponential_convert_fusion.1 = bf16[2048,2048]{1,0:T(8,128)(2,1)S(1)} fusion(bf16[64,2048]{1,0:T(8,128)(2,1)S(1)} %collective-permute-done.3, f32[2048]{0:T(1024)S(1)} %multiply_reduce_fusion.4, f32[2048]{0:T(1024)S(1)} %multiply_reduce_fusion.5, bf16[1,64,2048]{2,1,0:T(8,128)(2,1)S(1)} %all-gather), kind=kOutput, calls=%fused_computation.4 | convolution fusion | flops 557842432 | bytes 8929280 | tf_op jit(solution)/shard_map/dot_general | solution.py:45
  29.7 2.4 %fusion.20 = (f32[16]{0:T(128)S(1)}, f32[16,2048]{1,0:T(8,128)S(1)}) fusion(f32[2048]{0:T(1024)S(1)} %fusion.12, bf16[2048,2048]{1,0:T(8,128)(2,1)S(1)} %exponential_convert_fusion.1, f32[16,2048]{1,0:T(8,128)S(1)} %constant_dynamic-update-slice_fusion.3, f32[2048]{0:T(1024)S(1)} %fusion.11), kind=kOutput, calls=%fused_computation.79 | convolution fusion | flops 134348784 | bytes 8667200 | tf_op jit(solution)/shard_map/dot_general | solution.py:106
  32.3 3.5 %collective-permute-start.6 = (bf16[16,2048]{1,0:T(8,128)(2,1)S(1)}, bf16[16,2048]{1,0:T(8,128)(2,1)S(1)}, u32[]{:S(2)}, u32[]{:S(2)}) collective-permute-start(bf16[16,2048]{1,0:T(8,128)(2,1)S(1)} %get-tuple-element.14), channel_id=1, source_target_pairs={{0,8},{28,20},{1,9},{29,21},{2,10},{30,22},{3,11},{31,23}} | collective-permute-start | bytes 196616 | tf_op jit(solution)/shard_map/ppermute | solution.py:117
  35.7 3.6 %exponential_convert_fusion = bf16[2048,2048]{1,0:T(8,128)(2,1)S(1)} fusion(bf16[64,2048]{1,0:T(8,128)(2,1)S(1)} %collective-permute-done.7, f32[2048]{0:T(1024)S(1)} %multiply_reduce_fusion.3, f32[2048]{0:T(1024)S(1)} %multiply_reduce_fusion.4, bf16[1,64,2048]{2,1,0:T(8,128)(2,1)S(1)} %all-gather), kind=kOutput, calls=%fused_computation.3 | convolution fusion | flops 557842432 | bytes 8929280 | tf_op jit(solution)/shard_map/dot_general | solution.py:45
  39.4 1.3 %fusion.21 = (f32[16]{0:T(128)S(1)}, f32[16,2048]{1,0:T(8,128)S(1)}) fusion(f32[2048]{0:T(1024)S(1)} %fusion.11, bf16[16,2048]{1,0:T(8,128)(2,1)S(1)} %collective-permute-done.6, bf16[2048,2048]{1,0:T(8,128)(2,1)S(1)} %exponential_convert_fusion), kind=kOutput, calls=%fused_computation.80 | convolution fusion | flops 134283248 | bytes 8593472 | tf_op jit(solution)/shard_map/dot_general | solution.py:98
  40.7 2.4 %fusion.22 = (f32[16]{0:T(128)S(1)}, f32[16,2048]{1,0:T(8,128)S(1)}) fusion(f32[2048]{0:T(1024)S(1)} %fusion.12, bf16[2048,2048]{1,0:T(8,128)(2,1)S(1)} %exponential_convert_fusion.1, f32[16,2048]{1,0:T(8,128)S(1)} %constant_dynamic-update-slice_fusion.3, f32[16]{0:T(128)S(1)} %get-tuple-element.34, f32[16,2048]{1,0:T(8,128)S(1)} %get-tuple-element.35, ...), kind=kOutput, calls=%fused_computation.81 | convolution fusion | flops 134414320 | bytes 8790148 | tf_op jit(solution)/shard_map/dot_general | solution.py:106
  43.2 1.0 %collective-permute-start.8 = (bf16[16,2048]{1,0:T(8,128)(2,1)S(1)}, bf16[16,2048]{1,0:T(8,128)(2,1)S(1)}, u32[]{:S(2)}, u32[]{:S(2)}) collective-permute-start(bf16[16,2048]{1,0:T(8,128)(2,1)S(1)} %get-tuple-element.12), channel_id=1, source_target_pairs={{8,16},{20,12},{9,17},{21,13},{10,18},{22,14},{11,19},{23,15}} | collective-permute-start | bytes 196616 | tf_op jit(solution)/shard_map/ppermute | solution.py:117
  44.2 1.3 %fusion.23 = (f32[16]{0:T(128)S(1)}, f32[16,2048]{1,0:T(8,128)S(1)}) fusion(f32[2048]{0:T(1024)S(1)} %fusion.11, bf16[16,2048]{1,0:T(8,128)(2,1)S(1)} %collective-permute-done.8, bf16[2048,2048]{1,0:T(8,128)(2,1)S(1)} %exponential_convert_fusion), kind=kOutput, calls=%fused_computation.82 | convolution fusion | flops 134283248 | bytes 8593472 | tf_op jit(solution)/shard_map/dot_general | solution.py:98
  45.5 2.4 %fusion.24 = (f32[16]{0:T(128)S(1)}, f32[16,2048]{1,0:T(8,128)S(1)}) fusion(f32[2048]{0:T(1024)S(1)} %fusion.12, bf16[2048,2048]{1,0:T(8,128)(2,1)S(1)} %exponential_convert_fusion.1, f32[16,2048]{1,0:T(8,128)S(1)} %constant_dynamic-update-slice_fusion.3, f32[16]{0:T(128)S(1)} %get-tuple-element.38, f32[16,2048]{1,0:T(8,128)S(1)} %get-tuple-element.39, ...), kind=kOutput, calls=%fused_computation.83 | convolution fusion | flops 134414320 | bytes 8790148 | tf_op jit(solution)/shard_map/dot_general | solution.py:106
  48.7 1.3 %collective-permute-start.13 = (f32[16,2048]{1,0:T(8,128)S(1)}, f32[16,2048]{1,0:T(8,128)S(1)}, u32[]{:S(2)}, u32[]{:S(2)}) collective-permute-start(f32[16,2048]{1,0:T(8,128)S(1)} %get-tuple-element.15), channel_id=1, source_target_pairs={{0,4},{28,24},{1,5},{29,25},{2,6},{30,26},{3,7},{31,27}} | collective-permute-start | bytes 393224 | tf_op jit(solution)/shard_map/ppermute | solution.py:120
  51.4 4.7 %fusion.25 = (f32[16]{0:T(128)S(1)}, f32[16,2048]{1,0:T(8,128)S(1)}) fusion(f32[2048]{0:T(1024)S(1)} %fusion.11, bf16[16,2048]{1,0:T(8,128)(2,1)S(1)} %collective-permute-done.9, bf16[2048,2048]{1,0:T(8,128)(2,1)} %copy-done.1), kind=kOutput, calls=%fused_computation.84 | convolution fusion | flops 134283248 | bytes 8593472 | tf_op jit(solution)/shard_map/dot_general | solution.py:98
  56.1 5.8 %fusion.26 = (f32[16]{0:T(128)S(1)}, f32[16,2048]{1,0:T(8,128)S(1)}) fusion(f32[2048]{0:T(1024)S(1)} %fusion.12, bf16[2048,2048]{1,0:T(8,128)(2,1)} %copy-done, f32[16,2048]{1,0:T(8,128)S(1)} %constant_dynamic-update-slice_fusion.3, f32[16]{0:T(128)S(1)} %get-tuple-element.42, f32[16,2048]{1,0:T(8,128)S(1)} %get-tuple-element.43, f32[]{:T(128)S(6)} %convert_element_type.74), kind=kOutput, calls=%fused_computation.85 | convolution fusion | flops 134414320 | bytes 8790148 | tf_op jit(solution)/shard_map/dot_general | solution.py:106
  62.0 1.3 %collective-permute-start.10 = (f32[16,2048]{1,0:T(8,128)S(1)}, f32[16,2048]{1,0:T(8,128)S(1)}, u32[]{:S(2)}, u32[]{:S(2)}) collective-permute-start(f32[16,2048]{1,0:T(8,128)S(1)} %multiply_divide_fusion), channel_id=1, source_target_pairs={{24,28},{4,0},{25,29},{5,1},{26,30},{6,2},{27,31},{7,3}} | collective-permute-start | bytes 393224 | tf_op jit(solution)/shard_map/ppermute | solution.py:120
  64.2 8.1 %collective-permute-done.10 = f32[16,2048]{1,0:T(8,128)S(1)} collective-permute-done((f32[16,2048]{1,0:T(8,128)S(1)}, f32[16,2048]{1,0:T(8,128)S(1)}, u32[]{:S(2)}, u32[]{:S(2)}) %collective-permute-start.10) | collective-permute-done | bytes 131104 | tf_op jit(solution)/shard_map/ppermute | solution.py:120
  72.5 1.2 %collective-permute-start.18 = (f32[1,2048]{1,0:T(1,128)S(1)}, f32[1,2048]{1,0:T(1,128)S(1)}, u32[]{:S(2)}, u32[]{:S(2)}) collective-permute-start(f32[1,2048]{1,0:T(1,128)S(1)} %bitcast.48), channel_id=1, source_target_pairs={{0,2},{1,3},{2,0},{3,1},{4,6},{5,7},{6,4},{7,5},{8,10},{9,11},{10,... | collective-permute-start | bytes 24584 | tf_op jit(solution)/shard_map/ppermute | solution.py:22
  73.7 1.4 %collective-permute-start.19 = (f32[1,2048]{1,0:T(1,128)S(1)}, f32[1,2048]{1,0:T(1,128)S(1)}, u32[]{:S(2)}, u32[]{:S(2)}) collective-permute-start(f32[1,2048]{1,0:T(1,128)S(1)} %bitcast.49), channel_id=1, source_target_pairs={{0,3},{1,0},{2,1},{3,2},{4,7},{5,4},{6,5},{7,6},{8,11},{9,8},{10,9... | collective-permute-start | bytes 24584 | tf_op jit(solution)/shard_map/ppermute | solution.py:22
  77.4 4.3 %multiply_reduce_fusion.1 = (f32[2048]{0:T(1024)S(1)}, f32[2048,2048]{1,0:T(8,128)S(1)}) fusion(f32[2048]{0:T(1024)S(1)} %get-tuple-element.6, f32[2048]{0:T(1024)S(1)} %multiply_reduce_fusion.2, f32[2048]{0:T(1024)S(1)} %multiply_reduce_fusion.4, bf16[1,64,2048]{2,1,0:T(8,128)(2,1)S(1)} %copy-done.2, bf16[1,64,2048]{2,1,0:T(8,128)(2,1)S(1)} %all-gather), kind=kOutput, calls=%fused_computation.1 | convolution fusion | flops 562034688 | bytes 17334272 | tf_op jit(solution)/shard_map/dot_general | solution.py:45
  82.4 5.0 %multiply_reduce_fusion = f32[2048]{0:T(1024)S(1)} fusion(f32[2048,2048]{1,0:T(8,128)S(1)} %get-tuple-element.47, f32[2048]{0:T(1024)S(1)} %select_divide_fusion, f32[2048]{0:T(1024)S(1)} %multiply_reduce_fusion.2, f32[2048]{0:T(1024)S(1)} %multiply_reduce_fusion.4), kind=kLoop, calls=%fused_computation | loop fusion | flops 25163776 | bytes 16809984 | tf_op jit(solution)/shard_map/reduce_sum | solution.py:151
  87.6 1.0 %collective-permute-start.20 = (f32[512]{0:T(512)S(1)}, f32[512]{0:T(512)S(1)}, u32[]{:S(2)}, u32[]{:S(2)}) collective-permute-start(f32[512]{0:T(512)S(1)} %get-tuple-element.30), channel_id=1, source_target_pairs={{0,1},{1,2},{2,3},{3,0},{4,5},{5,6},{6,7},{7,4},{8,9},{9,10},{10,1... | collective-permute-start | bytes 6152 | tf_op jit(solution)/shard_map/ppermute | solution.py:22
  88.6 1.1 %collective-permute-start.21 = (f32[512]{0:T(512)S(1)}, f32[512]{0:T(512)S(1)}, u32[]{:S(2)}, u32[]{:S(2)}) collective-permute-start(f32[512]{0:T(512)S(1)} %get-tuple-element.29), channel_id=1, source_target_pairs={{0,2},{1,3},{2,0},{3,1},{4,6},{5,7},{6,4},{7,5},{8,10},{9,11},{10,... | collective-permute-start | bytes 6152 | tf_op jit(solution)/shard_map/ppermute | solution.py:22
  90.3 1.0 %collective-permute-start.15 = (f32[2,16,512]{2,1,0:T(8,128)S(1)}, f32[2,16,512]{2,1,0:T(8,128)S(1)}, u32[]{:S(2)}, u32[]{:S(2)}) collective-permute-start(f32[2,16,512]{2,1,0:T(8,128)S(1)} %get-tuple-element.21), channel_id=1, source_target_pairs={{0,2},{1,3},{2,0},{3,1},{4,6},{5,7},{6,4},{7,5},{8,10},{9,11},{10,... | collective-permute-start | bytes 196616 | tf_op jit(solution)/shard_map/ppermute | solution.py:22
  91.3 1.4 %collective-permute-start.16 = (f32[2,16,512]{2,1,0:T(8,128)S(1)}, f32[2,16,512]{2,1,0:T(8,128)S(1)}, u32[]{:S(2)}, u32[]{:S(2)}) collective-permute-start(f32[2,16,512]{2,1,0:T(8,128)S(1)} %get-tuple-element.18), channel_id=1, source_target_pairs={{0,3},{1,0},{2,1},{3,2},{4,7},{5,4},{6,5},{7,6},{8,11},{9,8},{10,9... | collective-permute-start | bytes 196616 | tf_op jit(solution)/shard_map/ppermute | solution.py:22
  94.1 1.2 %collective-permute-done.15 = f32[2,16,512]{2,1,0:T(8,128)S(1)} collective-permute-done((f32[2,16,512]{2,1,0:T(8,128)S(1)}, f32[2,16,512]{2,1,0:T(8,128)S(1)}, u32[]{:S(2)}, u32[]{:S(2)}) %collective-permute-start.15) | collective-permute-done | bytes 65568 | tf_op jit(solution)/shard_map/ppermute | solution.py:22
  95.4 0.7 fusion.18
  (72 shorter events, 9.6 us)
Async XLA Ops:
  8.1 17.9 %collective-permute-start.3 = (bf16[64,2048]{1,0:T(8,128)(2,1)S(1)}, bf16[64,2048]{1,0:T(8,128)(2,1)S(1)}, u32[]{:S(2)}, u32[]{:S(2)}) collective-permute-start(bf16[64,2048]{1,0:T(8,128)(2,1)S(1)} %bitcast.45), channel_id=1, source_target_pairs={{4,0},{0,4},{12,8},{8,12},{20,16},{16,20},{28,24},{24,28},{5,1},{1... | collective-permute-start | bytes 786440 | tf_op jit(solution)/shard_map/ppermute | solution.py:75
  9.6 22.6 %collective-permute-start.7 = (bf16[64,2048]{1,0:T(8,128)(2,1)S(1)}, bf16[64,2048]{1,0:T(8,128)(2,1)S(1)}, u32[]{:S(2)}, u32[]{:S(2)}) collective-permute-start(bf16[64,2048]{1,0:T(8,128)(2,1)S(1)} %bitcast.46), channel_id=1, source_target_pairs={{8,4},{4,8},{16,12},{12,16},{24,20},{20,24},{9,5},{5,9},{17,13},{1... | collective-permute-start | bytes 786440 | tf_op jit(solution)/shard_map/ppermute | solution.py:80
  11.3 12.0 %collective-permute-start = (f32[16,512]{1,0:T(8,128)S(1)}, f32[16,512]{1,0:T(8,128)S(1)}, u32[]{:S(2)}, u32[]{:S(2)}) collective-permute-start(f32[16,512]{1,0:T(8,128)S(1)} %get-tuple-element.26), channel_id=1, source_target_pairs={{0,1},{1,2},{2,3},{3,0},{4,5},{5,6},{6,7},{7,4},{8,9},{9,10},{10,1... | collective-permute-start | bytes 98312 | tf_op jit(solution)/shard_map/ppermute | solution.py:22
  11.4 11.9 %collective-permute-start.1 = (f32[16,512]{1,0:T(8,128)S(1)}, f32[16,512]{1,0:T(8,128)S(1)}, u32[]{:S(2)}, u32[]{:S(2)}) collective-permute-start(f32[16,512]{1,0:T(8,128)S(1)} %get-tuple-element.25), channel_id=1, source_target_pairs={{0,2},{1,3},{2,0},{3,1},{4,6},{5,7},{6,4},{7,5},{8,10},{9,11},{10,... | collective-permute-start | bytes 98312 | tf_op jit(solution)/shard_map/ppermute | solution.py:22
  13.0 8.4 %collective-permute-start.4 = (s32[1]{0:T(128)}, s32[1]{0:T(128)}, u32[]{:S(2)}, u32[]{:S(2)}) collective-permute-start(s32[1]{0:T(128)} %param.10), channel_id=1, source_target_pairs={{4,0},{0,4},{12,8},{8,12},{20,16},{16,20},{28,24},{24,28},{5,1},{1... | collective-permute-start | bytes 20 | tf_op jit(solution)/shard_map/ppermute | solution.py:77
  21.3 2.2 %collective-permute-start.2 = (f32[16,512]{1,0:T(8,128)S(1)}, f32[16,512]{1,0:T(8,128)S(1)}, u32[]{:S(2)}, u32[]{:S(2)}) collective-permute-start(f32[16,512]{1,0:T(8,128)S(1)} %get-tuple-element.24), channel_id=1, source_target_pairs={{0,3},{1,0},{2,1},{3,2},{4,7},{5,4},{6,5},{7,6},{8,11},{9,8},{10,9... | collective-permute-start | bytes 98312 | tf_op jit(solution)/shard_map/ppermute | solution.py:22
  23.5 8.5 %collective-permute-start.5 = (f32[16,2048]{1,0:T(8,128)S(1)}, f32[16,2048]{1,0:T(8,128)S(1)}, u32[]{:S(2)}, u32[]{:S(2)}) collective-permute-start(f32[16,2048]{1,0:T(8,128)S(1)} %constant_dynamic-update-slice_fusion.3), channel_id=1, source_target_pairs={{4,0},{0,4},{12,8},{8,12},{20,16},{16,20},{28,24},{24,28},{5,1},{1... | collective-permute-start | bytes 393224 | tf_op jit(solution)/shard_map/ppermute | solution.py:76
  29.7 15.8 %copy-start = (bf16[2048,2048]{1,0:T(8,128)(2,1)}, bf16[2048,2048]{1,0:T(8,128)(2,1)S(1)}, u32[]{:S(2)}) copy-start(bf16[2048,2048]{1,0:T(8,128)(2,1)S(1)} %exponential_convert_fusion.1) | copy-start | bytes 25165828
  32.3 7.1 %collective-permute-start.6 = (bf16[16,2048]{1,0:T(8,128)(2,1)S(1)}, bf16[16,2048]{1,0:T(8,128)(2,1)S(1)}, u32[]{:S(2)}, u32[]{:S(2)}) collective-permute-start(bf16[16,2048]{1,0:T(8,128)(2,1)S(1)} %get-tuple-element.14), channel_id=1, source_target_pairs={{0,8},{28,20},{1,9},{29,21},{2,10},{30,22},{3,11},{31,23}} | collective-permute-start | bytes 196616 | tf_op jit(solution)/shard_map/ppermute | solution.py:117
  39.3 8.6 %copy-start.1 = (bf16[2048,2048]{1,0:T(8,128)(2,1)}, bf16[2048,2048]{1,0:T(8,128)(2,1)S(1)}, u32[]{:S(2)}) copy-start(bf16[2048,2048]{1,0:T(8,128)(2,1)S(1)} %exponential_convert_fusion) | copy-start | bytes 25165828
  43.2 20.8 %copy-start.2 = (bf16[1,64,2048]{2,1,0:T(8,128)(2,1)S(1)}, bf16[1,64,2048]{2,1,0:T(8,128)(2,1)}, u32[]{:S(2)}) copy-start(bf16[1,64,2048]{2,1,0:T(8,128)(2,1)} %param.7) | copy-start | bytes 786436
  43.2 1.0 %collective-permute-start.8 = (bf16[16,2048]{1,0:T(8,128)(2,1)S(1)}, bf16[16,2048]{1,0:T(8,128)(2,1)S(1)}, u32[]{:S(2)}, u32[]{:S(2)}) collective-permute-start(bf16[16,2048]{1,0:T(8,128)(2,1)S(1)} %get-tuple-element.12), channel_id=1, source_target_pairs={{8,16},{20,12},{9,17},{21,13},{10,18},{22,14},{11,19},{23,15}} | collective-permute-start | bytes 196616 | tf_op jit(solution)/shard_map/ppermute | solution.py:117
  48.0 3.4 %collective-permute-start.9 = (bf16[16,2048]{1,0:T(8,128)(2,1)S(1)}, bf16[16,2048]{1,0:T(8,128)(2,1)S(1)}, u32[]{:S(2)}, u32[]{:S(2)}) collective-permute-start(bf16[16,2048]{1,0:T(8,128)(2,1)S(1)} %get-tuple-element.10), channel_id=1, source_target_pairs={{16,24},{12,4},{17,25},{13,5},{18,26},{14,6},{19,27},{15,7}} | collective-permute-start | bytes 196616 | tf_op jit(solution)/shard_map/ppermute | solution.py:117
  48.7 15.4 %collective-permute-start.13 = (f32[16,2048]{1,0:T(8,128)S(1)}, f32[16,2048]{1,0:T(8,128)S(1)}, u32[]{:S(2)}, u32[]{:S(2)}) collective-permute-start(f32[16,2048]{1,0:T(8,128)S(1)} %get-tuple-element.15), channel_id=1, source_target_pairs={{0,4},{28,24},{1,5},{29,25},{2,6},{30,26},{3,7},{31,27}} | collective-permute-start | bytes 393224 | tf_op jit(solution)/shard_map/ppermute | solution.py:120
  50.0 14.1 %collective-permute-start.12 = (f32[16,2048]{1,0:T(8,128)S(1)}, f32[16,2048]{1,0:T(8,128)S(1)}, u32[]{:S(2)}, u32[]{:S(2)}) collective-permute-start(f32[16,2048]{1,0:T(8,128)S(1)} %get-tuple-element.13), channel_id=1, source_target_pairs={{8,12},{20,16},{9,13},{21,17},{10,14},{22,18},{11,15},{23,19}} | collective-permute-start | bytes 393224 | tf_op jit(solution)/shard_map/ppermute | solution.py:120
  50.7 13.4 %collective-permute-start.11 = (f32[16,2048]{1,0:T(8,128)S(1)}, f32[16,2048]{1,0:T(8,128)S(1)}, u32[]{:S(2)}, u32[]{:S(2)}) collective-permute-start(f32[16,2048]{1,0:T(8,128)S(1)} %get-tuple-element.11), channel_id=1, source_target_pairs={{16,20},{12,8},{17,21},{13,9},{18,22},{14,10},{19,23},{15,11}} | collective-permute-start | bytes 393224 | tf_op jit(solution)/shard_map/ppermute | solution.py:120
  62.0 10.3 %collective-permute-start.10 = (f32[16,2048]{1,0:T(8,128)S(1)}, f32[16,2048]{1,0:T(8,128)S(1)}, u32[]{:S(2)}, u32[]{:S(2)}) collective-permute-start(f32[16,2048]{1,0:T(8,128)S(1)} %multiply_divide_fusion), channel_id=1, source_target_pairs={{24,28},{4,0},{25,29},{5,1},{26,30},{6,2},{27,31},{7,3}} | collective-permute-start | bytes 393224 | tf_op jit(solution)/shard_map/ppermute | solution.py:120
  72.4 3.1 %collective-permute-start.17 = (f32[1,2048]{1,0:T(1,128)S(1)}, f32[1,2048]{1,0:T(1,128)S(1)}, u32[]{:S(2)}, u32[]{:S(2)}) collective-permute-start(f32[1,2048]{1,0:T(1,128)S(1)} %bitcast.47), channel_id=1, source_target_pairs={{0,1},{1,2},{2,3},{3,0},{4,5},{5,6},{6,7},{7,4},{8,9},{9,10},{10,1... | collective-permute-start | bytes 24584 | tf_op jit(solution)/shard_map/ppermute | solution.py:22
  72.5 3.7 %collective-permute-start.18 = (f32[1,2048]{1,0:T(1,128)S(1)}, f32[1,2048]{1,0:T(1,128)S(1)}, u32[]{:S(2)}, u32[]{:S(2)}) collective-permute-start(f32[1,2048]{1,0:T(1,128)S(1)} %bitcast.48), channel_id=1, source_target_pairs={{0,2},{1,3},{2,0},{3,1},{4,6},{5,7},{6,4},{7,5},{8,10},{9,11},{10,... | collective-permute-start | bytes 24584 | tf_op jit(solution)/shard_map/ppermute | solution.py:22
  73.7 2.8 %collective-permute-start.19 = (f32[1,2048]{1,0:T(1,128)S(1)}, f32[1,2048]{1,0:T(1,128)S(1)}, u32[]{:S(2)}, u32[]{:S(2)}) collective-permute-start(f32[1,2048]{1,0:T(1,128)S(1)} %bitcast.49), channel_id=1, source_target_pairs={{0,3},{1,0},{2,1},{3,2},{4,7},{5,4},{6,5},{7,6},{8,11},{9,8},{10,9... | collective-permute-start | bytes 24584 | tf_op jit(solution)/shard_map/ppermute | solution.py:22
  87.6 3.7 %collective-permute-start.20 = (f32[512]{0:T(512)S(1)}, f32[512]{0:T(512)S(1)}, u32[]{:S(2)}, u32[]{:S(2)}) collective-permute-start(f32[512]{0:T(512)S(1)} %get-tuple-element.30), channel_id=1, source_target_pairs={{0,1},{1,2},{2,3},{3,0},{4,5},{5,6},{6,7},{7,4},{8,9},{9,10},{10,1... | collective-permute-start | bytes 6152 | tf_op jit(solution)/shard_map/ppermute | solution.py:22
  88.6 4.3 %collective-permute-start.21 = (f32[512]{0:T(512)S(1)}, f32[512]{0:T(512)S(1)}, u32[]{:S(2)}, u32[]{:S(2)}) collective-permute-start(f32[512]{0:T(512)S(1)} %get-tuple-element.29), channel_id=1, source_target_pairs={{0,2},{1,3},{2,0},{3,1},{4,6},{5,7},{6,4},{7,5},{8,10},{9,11},{10,... | collective-permute-start | bytes 6152 | tf_op jit(solution)/shard_map/ppermute | solution.py:22
  89.7 3.4 %collective-permute-start.22 = (f32[512]{0:T(512)S(1)}, f32[512]{0:T(512)S(1)}, u32[]{:S(2)}, u32[]{:S(2)}) collective-permute-start(f32[512]{0:T(512)S(1)} %get-tuple-element.28), channel_id=1, source_target_pairs={{0,3},{1,0},{2,1},{3,2},{4,7},{5,4},{6,5},{7,6},{8,11},{9,8},{10,9... | collective-permute-start | bytes 6152 | tf_op jit(solution)/shard_map/ppermute | solution.py:22
  90.2 3.8 %collective-permute-start.14 = (f32[2,16,512]{2,1,0:T(8,128)S(1)}, f32[2,16,512]{2,1,0:T(8,128)S(1)}, u32[]{:S(2)}, u32[]{:S(2)}) collective-permute-start(f32[2,16,512]{2,1,0:T(8,128)S(1)} %get-tuple-element.20), channel_id=1, source_target_pairs={{0,1},{1,2},{2,3},{3,0},{4,5},{5,6},{6,7},{7,4},{8,9},{9,10},{10,1... | collective-permute-start | bytes 196616 | tf_op jit(solution)/shard_map/ppermute | solution.py:22
  90.3 5.0 %collective-permute-start.15 = (f32[2,16,512]{2,1,0:T(8,128)S(1)}, f32[2,16,512]{2,1,0:T(8,128)S(1)}, u32[]{:S(2)}, u32[]{:S(2)}) collective-permute-start(f32[2,16,512]{2,1,0:T(8,128)S(1)} %get-tuple-element.21), channel_id=1, source_target_pairs={{0,2},{1,3},{2,0},{3,1},{4,6},{5,7},{6,4},{7,5},{8,10},{9,11},{10,... | collective-permute-start | bytes 196616 | tf_op jit(solution)/shard_map/ppermute | solution.py:22
  91.3 4.0 %collective-permute-start.16 = (f32[2,16,512]{2,1,0:T(8,128)S(1)}, f32[2,16,512]{2,1,0:T(8,128)S(1)}, u32[]{:S(2)}, u32[]{:S(2)}) collective-permute-start(f32[2,16,512]{2,1,0:T(8,128)S(1)} %get-tuple-element.18), channel_id=1, source_target_pairs={{0,3},{1,0},{2,1},{3,2},{4,7},{5,4},{6,5},{7,6},{8,11},{9,8},{10,9... | collective-permute-start | bytes 196616 | tf_op jit(solution)/shard_map/ppermute | solution.py:22

commit v16 on v15

--- a/solution.py
+++ b/solution.py
@@ -72,7 +72,10 @@
     even_day = day_index % 2 == 0
     pair_route = [(d + 1, d) if d % 2 == 0 else (d - 1, d) for d in range(day_count)]
     link_route = [(d - 1, d) if d % 2 == 0 else (d + 1, d) for d in range(1, day_count - 1)]
-    other_kernel = chain_kernel(lax.ppermute(day_pts, "day", pair_route))
+    other_pts = lax.ppermute(day_pts, "day", pair_route)
+    other_kernel = jnp.exp(
+        -squared_dist(day_pts, day_norm, other_pts, norm_of(other_pts))
+    ).astype(jnp.bfloat16)
     other_weight = lax.ppermute(block_weight, "day", pair_route)
     other_count = lax.ppermute(support_count, "day", pair_route)[0]
     other_total = other_count.astype(jnp.float32)
@@ -103,9 +106,7 @@
             own_rows = jnp.where(active, current, own_rows)
         sent = (current * block_weight).astype(jnp.bfloat16)
         following = settle(
-            lax.dot_general(
-                sent, other_kernel, (((1,), (1,)), ((), ())), preferred_element_type=jnp.float32
-            ),
+            jnp.dot(sent, other_kernel, preferred_element_type=jnp.float32),
             other_live,
             other_total,
         )

time: 96.5 us -> 92.2 us (0.955)
  matrix products: 31.8 us -> 27.6 us
    dot_general x4, matrix products: 13 us -> 8.77 us  [shards(): jnp.dot(sent, other_kernel, preferred_element_type=jnp.float32)]
  transfers between devices with their start and end apart: 23 -> 23, of which waited for: 7 -> 6; matrix products, arithmetic and copies ran while one was open for 25% -> 24% of each run, Pallas kernels for 0% -> 0%
where the time goes in v16:
time: 92.2 us; the launch traced here: 91.7 us
  starting transfers between devices  27.6 us (30%)
  matrix products  27.6 us (30%)
  waiting for transfers between devices  14.2 us (15%)
  other arithmetic  9.46 us (10%)
  blocking collectives  7.46 us (8%)
  between operations  3.31 us (4%)
  local copies, waits for them, and re-layouts  2.12 us (2%)
    dot_general x3, matrix products, squared_dist(): lax.dot_general(left_pts, right_pts, (((0,), (0,)), ((), ())), preferred_...  11.5 us
    ppermute x12, starting transfers between devices, swap_blocks(): lax.ppermute(piece, 'pt', [(i, (i + shift) % count) for i in range(count)])  9.63 us
    dot_general x4, matrix products, shards(): jnp.dot(sent, other_kernel, preferred_element_type=jnp.float32)  8.77 us
    ppermute x4, waiting for transfers between devices, shards(): lax.ppermute(following, 'day', [(forward_day, forward_day + 1), (backward...  8.33 us
    all_gather x1, blocking collectives, shards(): day_pts = lax.all_gather(own_pts, 'pt', axis=1, tiled=True)  7.46 us
    dot_general x3, matrix products, shards(): jnp.dot(incoming, link_kernel, preferred_element_type=jnp.float32)  7.31 us
    reduce_sum x1, other arithmetic, shards(): ratio_rows = jnp.sum(fit_kernel * inverse[None, :], axis=1)  5.03 us
    ppermute x3, starting transfers between devices, shards(): lax.ppermute(outgoing, 'day', [(forward_day, forward_day + 2), (backward_...  4.96 us
  transfers between devices with their start and end apart: 23, of which 6 were waited for; matrix products, arithmetic and copies ran while one was open for 24% of the time, Pallas kernels for 0%

profile of v16, /device:TPU:0, one launch (start us, length us, event | category | flops | bytes accessed | tf_op | source)
XLA Modules:
  0.0 91.7 jit_solution(4884440785368029963)
XLA Ops:
  0.6 7.5 %all-gather = bf16[1,64,2048]{2,1,0:T(8,128)(2,1)S(1)} all-gather(bf16[1,64,512]{2,1,0:T(8,128)(2,1)} %param.6), channel_id=2, replica_groups=mesh['day'=8,'pt'=4] {'pt'}, dimensions={2}, use_global_device_ids=true | all-gather | bytes 327680 | tf_op jit(solution)/shard_map/all_gather | solution.py:57
  8.1 1.5 %collective-permute-start.3 = (bf16[64,2048]{1,0:T(8,128)(2,1)S(1)}, bf16[64,2048]{1,0:T(8,128)(2,1)S(1)}, u32[]{:S(2)}, u32[]{:S(2)}) collective-permute-start(bf16[64,2048]{1,0:T(8,128)(2,1)S(1)} %bitcast.45), channel_id=1, source_target_pairs={{4,0},{0,4},{12,8},{8,12},{20,16},{16,20},{28,24},{24,28},{5,1},{1... | collective-permute-start | bytes 786440 | tf_op jit(solution)/shard_map/ppermute | solution.py:75
  10.3 0.9 %bitcast_multiply_fusion = f32[64,512]{1,0:T(8,128)S(1)} fusion(f32[1,64,512]{2,1,0:T(8,128)} %param.8, f32[512]{0:T(512)} %bitcast.51), kind=kLoop, calls=%fused_computation.26 | loop fusion | flops 32768 | bytes 264192 | tf_op jit(solution)/shard_map/mul | solution.py:59
  11.4 1.5 %collective-permute-start.1 = (f32[16,512]{1,0:T(8,128)S(1)}, f32[16,512]{1,0:T(8,128)S(1)}, u32[]{:S(2)}, u32[]{:S(2)}) collective-permute-start(f32[16,512]{1,0:T(8,128)S(1)} %get-tuple-element.25), channel_id=1, source_target_pairs={{0,2},{1,3},{2,0},{3,1},{4,6},{5,7},{6,4},{7,5},{8,10},{9,11},{10,... | collective-permute-start | bytes 98312 | tf_op jit(solution)/shard_map/ppermute | solution.py:22
  13.0 4.3 %collective-permute-start.4 = (s32[1]{0:T(128)}, s32[1]{0:T(128)}, u32[]{:S(2)}, u32[]{:S(2)}) collective-permute-start(s32[1]{0:T(128)} %param.10), channel_id=1, source_target_pairs={{4,0},{0,4},{12,8},{8,12},{20,16},{16,20},{28,24},{24,28},{5,1},{1... | collective-permute-start | bytes 20 | tf_op jit(solution)/shard_map/ppermute | solution.py:80
  18.0 3.3 %collective-permute-done.4 = s32[1]{0:T(128)} collective-permute-done((s32[1]{0:T(128)}, s32[1]{0:T(128)}, u32[]{:S(2)}, u32[]{:S(2)}) %collective-permute-start.4) | collective-permute-done | bytes 36 | tf_op jit(solution)/shard_map/ppermute | solution.py:80
  23.5 2.4 %collective-permute-start.5 = (f32[16,2048]{1,0:T(8,128)S(1)}, f32[16,2048]{1,0:T(8,128)S(1)}, u32[]{:S(2)}, u32[]{:S(2)}) collective-permute-start(f32[16,2048]{1,0:T(8,128)S(1)} %constant_dynamic-update-slice_fusion.3), channel_id=1, source_target_pairs={{4,0},{0,4},{12,8},{8,12},{20,16},{16,20},{28,24},{24,28},{5,1},{1... | collective-permute-start | bytes 393224 | tf_op jit(solution)/shard_map/ppermute | solution.py:79
  26.1 3.6 %exponential_convert_fusion.1 = bf16[2048,2048]{1,0:T(8,128)(2,1)S(1)} fusion(bf16[64,2048]{1,0:T(8,128)(2,1)S(1)} %collective-permute-done.3, f32[2048]{0:T(1024)S(1)} %multiply_reduce_fusion.4, f32[2048]{0:T(1024)S(1)} %multiply_reduce_fusion.5, bf16[1,64,2048]{2,1,0:T(8,128)(2,1)S(1)} %all-gather), kind=kOutput, calls=%fused_computation.4 | convolution fusion | flops 557842432 | bytes 8929280 | tf_op jit(solution)/shard_map/dot_general | solution.py:45
  29.7 1.3 %fusion.20 = (f32[16]{0:T(128)S(1)}, f32[16,2048]{1,0:T(8,128)S(1)}) fusion(f32[2048]{0:T(1024)S(1)} %fusion.12, bf16[2048,2048]{1,0:T(8,128)(2,1)S(1)} %exponential_convert_fusion.1, f32[16,2048]{1,0:T(8,128)S(1)} %constant_dynamic-update-slice_fusion.3, f32[2048]{0:T(1024)S(1)} %fusion.11), kind=kOutput, calls=%fused_computation.79 | convolution fusion | flops 134348784 | bytes 8667200 | tf_op jit(solution)/shard_map/dot_general | solution.py:109
  31.2 3.5 %collective-permute-start.6 = (bf16[16,2048]{1,0:T(8,128)(2,1)S(1)}, bf16[16,2048]{1,0:T(8,128)(2,1)S(1)}, u32[]{:S(2)}, u32[]{:S(2)}) collective-permute-start(bf16[16,2048]{1,0:T(8,128)(2,1)S(1)} %get-tuple-element.14), channel_id=1, source_target_pairs={{0,8},{28,20},{1,9},{29,21},{2,10},{30,22},{3,11},{31,23}} | collective-permute-start | bytes 196616 | tf_op jit(solution)/shard_map/ppermute | solution.py:118
  34.7 3.6 %exponential_convert_fusion = bf16[2048,2048]{1,0:T(8,128)(2,1)S(1)} fusion(bf16[64,2048]{1,0:T(8,128)(2,1)S(1)} %collective-permute-done.7, f32[2048]{0:T(1024)S(1)} %multiply_reduce_fusion.5, f32[2048]{0:T(1024)S(1)} %multiply_reduce_fusion.3, bf16[1,64,2048]{2,1,0:T(8,128)(2,1)S(1)} %all-gather), kind=kOutput, calls=%fused_computation.3 | convolution fusion | flops 557842432 | bytes 8929280 | tf_op jit(solution)/shard_map/dot_general | solution.py:45
  38.3 1.3 %fusion.21 = (f32[16]{0:T(128)S(1)}, f32[16,2048]{1,0:T(8,128)S(1)}) fusion(f32[2048]{0:T(1024)S(1)} %fusion.11, bf16[16,2048]{1,0:T(8,128)(2,1)S(1)} %collective-permute-done.6, bf16[2048,2048]{1,0:T(8,128)(2,1)S(1)} %exponential_convert_fusion), kind=kOutput, calls=%fused_computation.80 | convolution fusion | flops 134283248 | bytes 8593472 | tf_op jit(solution)/shard_map/dot_general | solution.py:101
  39.6 1.4 %fusion.22 = (f32[16]{0:T(128)S(1)}, f32[16,2048]{1,0:T(8,128)S(1)}) fusion(f32[2048]{0:T(1024)S(1)} %fusion.12, bf16[2048,2048]{1,0:T(8,128)(2,1)S(1)} %exponential_convert_fusion.1, f32[16,2048]{1,0:T(8,128)S(1)} %constant_dynamic-update-slice_fusion.3, f32[16]{0:T(128)S(1)} %get-tuple-element.34, f32[16,2048]{1,0:T(8,128)S(1)} %get-tuple-element.35, ...), kind=kOutput, calls=%fused_computation.81 | convolution fusion | flops 134414320 | bytes 8790148 | tf_op jit(solution)/shard_map/dot_general | solution.py:109
  41.1 0.8 collective-permute-start.8
  41.9 1.3 %fusion.23 = (f32[16]{0:T(128)S(1)}, f32[16,2048]{1,0:T(8,128)S(1)}) fusion(f32[2048]{0:T(1024)S(1)} %fusion.11, bf16[16,2048]{1,0:T(8,128)(2,1)S(1)} %collective-permute-done.8, bf16[2048,2048]{1,0:T(8,128)(2,1)S(1)} %exponential_convert_fusion), kind=kOutput, calls=%fused_computation.82 | convolution fusion | flops 134283248 | bytes 8593472 | tf_op jit(solution)/shard_map/dot_general | solution.py:101
  43.2 1.4 %fusion.24 = (f32[16]{0:T(128)S(1)}, f32[16,2048]{1,0:T(8,128)S(1)}) fusion(f32[2048]{0:T(1024)S(1)} %fusion.12, bf16[2048,2048]{1,0:T(8,128)(2,1)S(1)} %exponential_convert_fusion.1, f32[16,2048]{1,0:T(8,128)S(1)} %constant_dynamic-update-slice_fusion.3, f32[16]{0:T(128)S(1)} %get-tuple-element.38, f32[16,2048]{1,0:T(8,128)S(1)} %get-tuple-element.39, ...), kind=kOutput, calls=%fused_computation.83 | convolution fusion | flops 134414320 | bytes 8790148 | tf_op jit(solution)/shard_map/dot_general | solution.py:109
  45.4 1.3 %collective-permute-start.13 = (f32[16,2048]{1,0:T(8,128)S(1)}, f32[16,2048]{1,0:T(8,128)S(1)}, u32[]{:S(2)}, u32[]{:S(2)}) collective-permute-start(f32[16,2048]{1,0:T(8,128)S(1)} %get-tuple-element.15), channel_id=1, source_target_pairs={{0,4},{28,24},{1,5},{29,25},{2,6},{30,26},{3,7},{31,27}} | collective-permute-start | bytes 393224 | tf_op jit(solution)/shard_map/ppermute | solution.py:121
  47.4 0.8 collective-permute-start.11
  48.2 4.7 %fusion.25 = (f32[16]{0:T(128)S(1)}, f32[16,2048]{1,0:T(8,128)S(1)}) fusion(f32[2048]{0:T(1024)S(1)} %fusion.11, bf16[16,2048]{1,0:T(8,128)(2,1)S(1)} %collective-permute-done.9, bf16[2048,2048]{1,0:T(8,128)(2,1)} %copy-done.1), kind=kOutput, calls=%fused_computation.84 | convolution fusion | flops 134283248 | bytes 8593472 | tf_op jit(solution)/shard_map/dot_general | solution.py:101
  52.9 4.7 %fusion.26 = (f32[16]{0:T(128)S(1)}, f32[16,2048]{1,0:T(8,128)S(1)}) fusion(f32[2048]{0:T(1024)S(1)} %fusion.12, bf16[2048,2048]{1,0:T(8,128)(2,1)} %copy-done, f32[16,2048]{1,0:T(8,128)S(1)} %constant_dynamic-update-slice_fusion.3, f32[16]{0:T(128)S(1)} %get-tuple-element.42, f32[16,2048]{1,0:T(8,128)S(1)} %get-tuple-element.43, f32[]{:T(128)S(6)} %convert_element_type.74), kind=kOutput, calls=%fused_computation.85 | convolution fusion | flops 134414320 | bytes 8790148 | tf_op jit(solution)/shard_map/dot_general | solution.py:109
  57.8 1.3 %collective-permute-start.10 = (f32[16,2048]{1,0:T(8,128)S(1)}, f32[16,2048]{1,0:T(8,128)S(1)}, u32[]{:S(2)}, u32[]{:S(2)}) collective-permute-start(f32[16,2048]{1,0:T(8,128)S(1)} %multiply_divide_fusion), channel_id=1, source_target_pairs={{24,28},{4,0},{25,29},{5,1},{26,30},{6,2},{27,31},{7,3}} | collective-permute-start | bytes 393224 | tf_op jit(solution)/shard_map/ppermute | solution.py:121
  59.9 8.3 %collective-permute-done.10 = f32[16,2048]{1,0:T(8,128)S(1)} collective-permute-done((f32[16,2048]{1,0:T(8,128)S(1)}, f32[16,2048]{1,0:T(8,128)S(1)}, u32[]{:S(2)}, u32[]{:S(2)}) %collective-permute-start.10) | collective-permute-done | bytes 131104 | tf_op jit(solution)/shard_map/ppermute | solution.py:121
  68.5 0.9 collective-permute-start.18
  69.4 1.4 %collective-permute-start.19 = (f32[1,2048]{1,0:T(1,128)S(1)}, f32[1,2048]{1,0:T(1,128)S(1)}, u32[]{:S(2)}, u32[]{:S(2)}) collective-permute-start(f32[1,2048]{1,0:T(1,128)S(1)} %bitcast.49), channel_id=1, source_target_pairs={{0,3},{1,0},{2,1},{3,2},{4,7},{5,4},{6,5},{7,6},{8,11},{9,8},{10,9... | collective-permute-start | bytes 24584 | tf_op jit(solution)/shard_map/ppermute | solution.py:22
  73.1 4.3 %multiply_reduce_fusion.1 = (f32[2048]{0:T(1024)S(1)}, f32[2048,2048]{1,0:T(8,128)S(1)}) fusion(f32[2048]{0:T(1024)S(1)} %get-tuple-element.6, f32[2048]{0:T(1024)S(1)} %multiply_reduce_fusion.2, f32[2048]{0:T(1024)S(1)} %multiply_reduce_fusion.5, bf16[1,64,2048]{2,1,0:T(8,128)(2,1)S(1)} %copy-done.2, bf16[1,64,2048]{2,1,0:T(8,128)(2,1)S(1)} %all-gather), kind=kOutput, calls=%fused_computation.1 | convolution fusion | flops 562034688 | bytes 17334272 | tf_op jit(solution)/shard_map/dot_general | solution.py:45
  78.1 5.0 %multiply_reduce_fusion = f32[2048]{0:T(1024)S(1)} fusion(f32[2048,2048]{1,0:T(8,128)S(1)} %get-tuple-element.47, f32[2048]{0:T(1024)S(1)} %select_divide_fusion, f32[2048]{0:T(1024)S(1)} %multiply_reduce_fusion.2, f32[2048]{0:T(1024)S(1)} %multiply_reduce_fusion.5), kind=kLoop, calls=%fused_computation | loop fusion | flops 25163776 | bytes 16809984 | tf_op jit(solution)/shard_map/reduce_sum | solution.py:152
  83.3 1.0 %collective-permute-start.20 = (f32[512]{0:T(512)S(1)}, f32[512]{0:T(512)S(1)}, u32[]{:S(2)}, u32[]{:S(2)}) collective-permute-start(f32[512]{0:T(512)S(1)} %get-tuple-element.30), channel_id=1, source_target_pairs={{0,1},{1,2},{2,3},{3,0},{4,5},{5,6},{6,7},{7,4},{8,9},{9,10},{10,1... | collective-permute-start | bytes 6152 | tf_op jit(solution)/shard_map/ppermute | solution.py:22
  84.4 0.8 collective-permute-start.21
  85.9 1.1 %collective-permute-start.15 = (f32[2,16,512]{2,1,0:T(8,128)S(1)}, f32[2,16,512]{2,1,0:T(8,128)S(1)}, u32[]{:S(2)}, u32[]{:S(2)}) collective-permute-start(f32[2,16,512]{2,1,0:T(8,128)S(1)} %get-tuple-element.21), channel_id=1, source_target_pairs={{0,2},{1,3},{2,0},{3,1},{4,6},{5,7},{6,4},{7,5},{8,10},{9,11},{10,... | collective-permute-start | bytes 196616 | tf_op jit(solution)/shard_map/ppermute | solution.py:22
  87.0 1.4 %collective-permute-start.16 = (f32[2,16,512]{2,1,0:T(8,128)S(1)}, f32[2,16,512]{2,1,0:T(8,128)S(1)}, u32[]{:S(2)}, u32[]{:S(2)}) collective-permute-start(f32[2,16,512]{2,1,0:T(8,128)S(1)} %get-tuple-element.18), channel_id=1, source_target_pairs={{0,3},{1,0},{2,1},{3,2},{4,7},{5,4},{6,5},{7,6},{8,11},{9,8},{10,9... | collective-permute-start | bytes 196616 | tf_op jit(solution)/shard_map/ppermute | solution.py:22
  89.8 1.2 %collective-permute-done.15 = f32[2,16,512]{2,1,0:T(8,128)S(1)} collective-permute-done((f32[2,16,512]{2,1,0:T(8,128)S(1)}, f32[2,16,512]{2,1,0:T(8,128)S(1)}, u32[]{:S(2)}, u32[]{:S(2)}) %collective-permute-start.15) | collective-permute-done | bytes 65568 | tf_op jit(solution)/shard_map/ppermute | solution.py:22
  91.0 0.7 fusion.18
  (72 shorter events, 9.7 us)
Async XLA Ops:
  8.1 17.9 %collective-permute-start.3 = (bf16[64,2048]{1,0:T(8,128)(2,1)S(1)}, bf16[64,2048]{1,0:T(8,128)(2,1)S(1)}, u32[]{:S(2)}, u32[]{:S(2)}) collective-permute-start(bf16[64,2048]{1,0:T(8,128)(2,1)S(1)} %bitcast.45), channel_id=1, source_target_pairs={{4,0},{0,4},{12,8},{8,12},{20,16},{16,20},{28,24},{24,28},{5,1},{1... | collective-permute-start | bytes 786440 | tf_op jit(solution)/shard_map/ppermute | solution.py:75
  9.6 21.5 %collective-permute-start.7 = (bf16[64,2048]{1,0:T(8,128)(2,1)S(1)}, bf16[64,2048]{1,0:T(8,128)(2,1)S(1)}, u32[]{:S(2)}, u32[]{:S(2)}) collective-permute-start(bf16[64,2048]{1,0:T(8,128)(2,1)S(1)} %bitcast.46), channel_id=1, source_target_pairs={{8,4},{4,8},{16,12},{12,16},{24,20},{20,24},{9,5},{5,9},{17,13},{1... | collective-permute-start | bytes 786440 | tf_op jit(solution)/shard_map/ppermute | solution.py:83
  11.3 12.0 %collective-permute-start = (f32[16,512]{1,0:T(8,128)S(1)}, f32[16,512]{1,0:T(8,128)S(1)}, u32[]{:S(2)}, u32[]{:S(2)}) collective-permute-start(f32[16,512]{1,0:T(8,128)S(1)} %get-tuple-element.26), channel_id=1, source_target_pairs={{0,1},{1,2},{2,3},{3,0},{4,5},{5,6},{6,7},{7,4},{8,9},{9,10},{10,1... | collective-permute-start | bytes 98312 | tf_op jit(solution)/shard_map/ppermute | solution.py:22
  11.4 11.9 %collective-permute-start.1 = (f32[16,512]{1,0:T(8,128)S(1)}, f32[16,512]{1,0:T(8,128)S(1)}, u32[]{:S(2)}, u32[]{:S(2)}) collective-permute-start(f32[16,512]{1,0:T(8,128)S(1)} %get-tuple-element.25), channel_id=1, source_target_pairs={{0,2},{1,3},{2,0},{3,1},{4,6},{5,7},{6,4},{7,5},{8,10},{9,11},{10,... | collective-permute-start | bytes 98312 | tf_op jit(solution)/shard_map/ppermute | solution.py:22
  13.0 8.4 %collective-permute-start.4 = (s32[1]{0:T(128)}, s32[1]{0:T(128)}, u32[]{:S(2)}, u32[]{:S(2)}) collective-permute-start(s32[1]{0:T(128)} %param.10), channel_id=1, source_target_pairs={{4,0},{0,4},{12,8},{8,12},{20,16},{16,20},{28,24},{24,28},{5,1},{1... | collective-permute-start | bytes 20 | tf_op jit(solution)/shard_map/ppermute | solution.py:80
  21.3 2.2 %collective-permute-start.2 = (f32[16,512]{1,0:T(8,128)S(1)}, f32[16,512]{1,0:T(8,128)S(1)}, u32[]{:S(2)}, u32[]{:S(2)}) collective-permute-start(f32[16,512]{1,0:T(8,128)S(1)} %get-tuple-element.24), channel_id=1, source_target_pairs={{0,3},{1,0},{2,1},{3,2},{4,7},{5,4},{6,5},{7,6},{8,11},{9,8},{10,9... | collective-permute-start | bytes 98312 | tf_op jit(solution)/shard_map/ppermute | solution.py:22
  23.5 7.4 %collective-permute-start.5 = (f32[16,2048]{1,0:T(8,128)S(1)}, f32[16,2048]{1,0:T(8,128)S(1)}, u32[]{:S(2)}, u32[]{:S(2)}) collective-permute-start(f32[16,2048]{1,0:T(8,128)S(1)} %constant_dynamic-update-slice_fusion.3), channel_id=1, source_target_pairs={{4,0},{0,4},{12,8},{8,12},{20,16},{16,20},{28,24},{24,28},{5,1},{1... | collective-permute-start | bytes 393224 | tf_op jit(solution)/shard_map/ppermute | solution.py:79
  29.7 13.6 %copy-start = (bf16[2048,2048]{1,0:T(8,128)(2,1)}, bf16[2048,2048]{1,0:T(8,128)(2,1)S(1)}, u32[]{:S(2)}) copy-start(bf16[2048,2048]{1,0:T(8,128)(2,1)S(1)} %exponential_convert_fusion.1) | copy-start | bytes 25165828
  31.2 7.1 %collective-permute-start.6 = (bf16[16,2048]{1,0:T(8,128)(2,1)S(1)}, bf16[16,2048]{1,0:T(8,128)(2,1)S(1)}, u32[]{:S(2)}, u32[]{:S(2)}) collective-permute-start(bf16[16,2048]{1,0:T(8,128)(2,1)S(1)} %get-tuple-element.14), channel_id=1, source_target_pairs={{0,8},{28,20},{1,9},{29,21},{2,10},{30,22},{3,11},{31,23}} | collective-permute-start | bytes 196616 | tf_op jit(solution)/shard_map/ppermute | solution.py:118
  38.3 6.3 %copy-start.1 = (bf16[2048,2048]{1,0:T(8,128)(2,1)}, bf16[2048,2048]{1,0:T(8,128)(2,1)S(1)}, u32[]{:S(2)}) copy-start(bf16[2048,2048]{1,0:T(8,128)(2,1)S(1)} %exponential_convert_fusion) | copy-start | bytes 25165828
  41.1 18.7 %copy-start.2 = (bf16[1,64,2048]{2,1,0:T(8,128)(2,1)S(1)}, bf16[1,64,2048]{2,1,0:T(8,128)(2,1)}, u32[]{:S(2)}) copy-start(bf16[1,64,2048]{2,1,0:T(8,128)(2,1)} %param.7) | copy-start | bytes 786436
  41.1 0.8 collective-permute-start.8
  44.7 3.5 %collective-permute-start.9 = (bf16[16,2048]{1,0:T(8,128)(2,1)S(1)}, bf16[16,2048]{1,0:T(8,128)(2,1)S(1)}, u32[]{:S(2)}, u32[]{:S(2)}) collective-permute-start(bf16[16,2048]{1,0:T(8,128)(2,1)S(1)} %get-tuple-element.10), channel_id=1, source_target_pairs={{16,24},{12,4},{17,25},{13,5},{18,26},{14,6},{19,27},{15,7}} | collective-permute-start | bytes 196616 | tf_op jit(solution)/shard_map/ppermute | solution.py:118
  45.4 14.5 %collective-permute-start.13 = (f32[16,2048]{1,0:T(8,128)S(1)}, f32[16,2048]{1,0:T(8,128)S(1)}, u32[]{:S(2)}, u32[]{:S(2)}) collective-permute-start(f32[16,2048]{1,0:T(8,128)S(1)} %get-tuple-element.15), channel_id=1, source_target_pairs={{0,4},{28,24},{1,5},{29,25},{2,6},{30,26},{3,7},{31,27}} | collective-permute-start | bytes 393224 | tf_op jit(solution)/shard_map/ppermute | solution.py:121
  46.7 13.2 %collective-permute-start.12 = (f32[16,2048]{1,0:T(8,128)S(1)}, f32[16,2048]{1,0:T(8,128)S(1)}, u32[]{:S(2)}, u32[]{:S(2)}) collective-permute-start(f32[16,2048]{1,0:T(8,128)S(1)} %get-tuple-element.13), channel_id=1, source_target_pairs={{8,12},{20,16},{9,13},{21,17},{10,14},{22,18},{11,15},{23,19}} | collective-permute-start | bytes 393224 | tf_op jit(solution)/shard_map/ppermute | solution.py:121
  47.4 12.6 %collective-permute-start.11 = (f32[16,2048]{1,0:T(8,128)S(1)}, f32[16,2048]{1,0:T(8,128)S(1)}, u32[]{:S(2)}, u32[]{:S(2)}) collective-permute-start(f32[16,2048]{1,0:T(8,128)S(1)} %get-tuple-element.11), channel_id=1, source_target_pairs={{16,20},{12,8},{17,21},{13,9},{18,22},{14,10},{19,23},{15,11}} | collective-permute-start | bytes 393224 | tf_op jit(solution)/shard_map/ppermute | solution.py:121
  57.8 10.5 %collective-permute-start.10 = (f32[16,2048]{1,0:T(8,128)S(1)}, f32[16,2048]{1,0:T(8,128)S(1)}, u32[]{:S(2)}, u32[]{:S(2)}) collective-permute-start(f32[16,2048]{1,0:T(8,128)S(1)} %multiply_divide_fusion), channel_id=1, source_target_pairs={{24,28},{4,0},{25,29},{5,1},{26,30},{6,2},{27,31},{7,3}} | collective-permute-start | bytes 393224 | tf_op jit(solution)/shard_map/ppermute | solution.py:121
  68.4 3.1 %collective-permute-start.17 = (f32[1,2048]{1,0:T(1,128)S(1)}, f32[1,2048]{1,0:T(1,128)S(1)}, u32[]{:S(2)}, u32[]{:S(2)}) collective-permute-start(f32[1,2048]{1,0:T(1,128)S(1)} %bitcast.47), channel_id=1, source_target_pairs={{0,1},{1,2},{2,3},{3,0},{4,5},{5,6},{6,7},{7,4},{8,9},{9,10},{10,1... | collective-permute-start | bytes 24584 | tf_op jit(solution)/shard_map/ppermute | solution.py:22
  68.5 3.7 %collective-permute-start.18 = (f32[1,2048]{1,0:T(1,128)S(1)}, f32[1,2048]{1,0:T(1,128)S(1)}, u32[]{:S(2)}, u32[]{:S(2)}) collective-permute-start(f32[1,2048]{1,0:T(1,128)S(1)} %bitcast.48), channel_id=1, source_target_pairs={{0,2},{1,3},{2,0},{3,1},{4,6},{5,7},{6,4},{7,5},{8,10},{9,11},{10,... | collective-permute-start | bytes 24584 | tf_op jit(solution)/shard_map/ppermute | solution.py:22
  69.4 2.9 %collective-permute-start.19 = (f32[1,2048]{1,0:T(1,128)S(1)}, f32[1,2048]{1,0:T(1,128)S(1)}, u32[]{:S(2)}, u32[]{:S(2)}) collective-permute-start(f32[1,2048]{1,0:T(1,128)S(1)} %bitcast.49), channel_id=1, source_target_pairs={{0,3},{1,0},{2,1},{3,2},{4,7},{5,4},{6,5},{7,6},{8,11},{9,8},{10,9... | collective-permute-start | bytes 24584 | tf_op jit(solution)/shard_map/ppermute | solution.py:22
  83.3 3.7 %collective-permute-start.20 = (f32[512]{0:T(512)S(1)}, f32[512]{0:T(512)S(1)}, u32[]{:S(2)}, u32[]{:S(2)}) collective-permute-start(f32[512]{0:T(512)S(1)} %get-tuple-element.30), channel_id=1, source_target_pairs={{0,1},{1,2},{2,3},{3,0},{4,5},{5,6},{6,7},{7,4},{8,9},{9,10},{10,1... | collective-permute-start | bytes 6152 | tf_op jit(solution)/shard_map/ppermute | solution.py:22
  84.4 4.2 %collective-permute-start.21 = (f32[512]{0:T(512)S(1)}, f32[512]{0:T(512)S(1)}, u32[]{:S(2)}, u32[]{:S(2)}) collective-permute-start(f32[512]{0:T(512)S(1)} %get-tuple-element.29), channel_id=1, source_target_pairs={{0,2},{1,3},{2,0},{3,1},{4,6},{5,7},{6,4},{7,5},{8,10},{9,11},{10,... | collective-permute-start | bytes 6152 | tf_op jit(solution)/shard_map/ppermute | solution.py:22
  85.2 3.6 %collective-permute-start.22 = (f32[512]{0:T(512)S(1)}, f32[512]{0:T(512)S(1)}, u32[]{:S(2)}, u32[]{:S(2)}) collective-permute-start(f32[512]{0:T(512)S(1)} %get-tuple-element.28), channel_id=1, source_target_pairs={{0,3},{1,0},{2,1},{3,2},{4,7},{5,4},{6,5},{7,6},{8,11},{9,8},{10,9... | collective-permute-start | bytes 6152 | tf_op jit(solution)/shard_map/ppermute | solution.py:22
  85.9 3.9 %collective-permute-start.14 = (f32[2,16,512]{2,1,0:T(8,128)S(1)}, f32[2,16,512]{2,1,0:T(8,128)S(1)}, u32[]{:S(2)}, u32[]{:S(2)}) collective-permute-start(f32[2,16,512]{2,1,0:T(8,128)S(1)} %get-tuple-element.20), channel_id=1, source_target_pairs={{0,1},{1,2},{2,3},{3,0},{4,5},{5,6},{6,7},{7,4},{8,9},{9,10},{10,1... | collective-permute-start | bytes 196616 | tf_op jit(solution)/shard_map/ppermute | solution.py:22
  85.9 5.0 %collective-permute-start.15 = (f32[2,16,512]{2,1,0:T(8,128)S(1)}, f32[2,16,512]{2,1,0:T(8,128)S(1)}, u32[]{:S(2)}, u32[]{:S(2)}) collective-permute-start(f32[2,16,512]{2,1,0:T(8,128)S(1)} %get-tuple-element.21), channel_id=1, source_target_pairs={{0,2},{1,3},{2,0},{3,1},{4,6},{5,7},{6,4},{7,5},{8,10},{9,11},{10,... | collective-permute-start | bytes 196616 | tf_op jit(solution)/shard_map/ppermute | solution.py:22
  87.0 4.0 %collective-permute-start.16 = (f32[2,16,512]{2,1,0:T(8,128)S(1)}, f32[2,16,512]{2,1,0:T(8,128)S(1)}, u32[]{:S(2)}, u32[]{:S(2)}) collective-permute-start(f32[2,16,512]{2,1,0:T(8,128)S(1)} %get-tuple-element.18), channel_id=1, source_target_pairs={{0,3},{1,0},{2,1},{3,2},{4,7},{5,4},{6,5},{7,6},{8,11},{9,8},{10,9... | collective-permute-start | bytes 196616 | tf_op jit(solution)/shard_map/ppermute | solution.py:22

commit v17 on v16

--- a/solution.py
+++ b/solution.py
@@ -143,13 +143,19 @@
     own_cells = cells[0]
     own_slots = own_cells.shape[1]
     cell_norm = norm_of(own_cells)
-    fit_kernel = jnp.exp(-squared_dist(day_pts, day_norm, own_cells, cell_norm))
-    density = jnp.sum(full_mass[:, None] * fit_kernel, axis=0) / mass_total
     cell_live = (pt_rank * own_slots + jnp.arange(own_slots, dtype=jnp.int32) < cell_total).astype(
         jnp.float32
     )
-    inverse = cell_live / density
-    ratio_rows = jnp.sum(fit_kernel * inverse[None, :], axis=1)
+    cell_span = own_slots // 2
+    ratio_rows = 0.0
+    for part in range(2):
+        part_cells = lax.slice_in_dim(own_cells, part * cell_span, (part + 1) * cell_span, axis=1)
+        part_norm = lax.slice_in_dim(cell_norm, part * cell_span, (part + 1) * cell_span)
+        fit_kernel = jnp.exp(-squared_dist(day_pts, day_norm, part_cells, part_norm))
+        density = jnp.sum(full_mass[:, None] * fit_kernel, axis=0) / mass_total
+        part_live = lax.slice_in_dim(cell_live, part * cell_span, (part + 1) * cell_span)
+        inverse = part_live / density
+        ratio_rows = ratio_rows + jnp.sum(fit_kernel * inverse[None, :], axis=1)
     summed = sum_scatter_over_pt(ratio_rows)
     fit_rows_out = live_own / cell_total_f * summed
     return (forward_out[None], backward_out[None], fit_rows_out[None])

time: 92.2 us -> 91.2 us (0.989)
  waiting for transfers between devices: 14.2 us -> 11.5 us
  other arithmetic: 9.46 us -> 10.8 us
    dot_general x3 -> x4, matrix products: 11.5 us -> 18.6 us  [squared_dist(): lax.dot_general(left_pts, right_pts, (((0,), (0,)), ((), ())), preferred_...]
    dot_general x3, matrix products: 7.31 us -> 3.92 us  [shards(): jnp.dot(incoming, link_kernel, preferred_element_type=jnp.float32)]
    dot_general x4, matrix products: 8.77 us -> 5.4 us  [shards(): jnp.dot(sent, other_kernel, preferred_element_type=jnp.float32)]
    ppermute x4, waiting for transfers between devices: 8.33 us -> 5.68 us  [shards(): lax.ppermute(following, 'day', [(forward_day, forward_day + 1), (backward...]
    reduce_sum x1, other arithmetic: 5.03 us -> 6.38 us  [shards(): ratio_rows = ratio_rows + jnp.sum(fit_kernel * inverse[None, :], axis=1)]
  transfers between devices with their start and end apart: 23 -> 23, of which waited for: 6 -> 7; matrix products, arithmetic and copies ran while one was open for 24% -> 21% of each run, Pallas kernels for 0% -> 0%
where the time goes in v17:
time: 91.2 us; the launch traced here: 90.8 us
  matrix products  28 us (31%)
  starting transfers between devices  27.7 us (30%)
  waiting for transfers between devices  11.5 us (13%)
  other arithmetic  10.8 us (12%)
  blocking collectives  7.46 us (8%)
  between operations  3.26 us (4%)
  local copies, waits for them, and re-layouts  2.07 us (2%)
    dot_general x4, matrix products, squared_dist(): lax.dot_general(left_pts, right_pts, (((0,), (0,)), ((), ())), preferred_...  18.6 us
    ppermute x12, starting transfers between devices, swap_blocks(): lax.ppermute(piece, 'pt', [(i, (i + shift) % count) for i in range(count)])  9.92 us
    all_gather x1, blocking collectives, shards(): day_pts = lax.all_gather(own_pts, 'pt', axis=1, tiled=True)  7.46 us
    reduce_sum x1, other arithmetic, shards(): ratio_rows = ratio_rows + jnp.sum(fit_kernel * inverse[None, :], axis=1)  6.38 us
    ppermute x4, waiting for transfers between devices, shards(): lax.ppermute(following, 'day', [(forward_day, forward_day + 1), (backward...  5.68 us
    dot_general x4, matrix products, shards(): jnp.dot(sent, other_kernel, preferred_element_type=jnp.float32)  5.4 us
    ppermute x3, starting transfers between devices, shards(): lax.ppermute(outgoing, 'day', [(forward_day, forward_day + 2), (backward_...  4.98 us
    ppermute x1, starting transfers between devices, shards(): other_count = lax.ppermute(support_count, 'day', pair_route)[0]  4.27 us
  transfers between devices with their start and end apart: 23, of which 7 were waited for; matrix products, arithmetic and copies ran while one was open for 21% of the time, Pallas kernels for 0%

profile of v17, /device:TPU:0, one launch (start us, length us, event | category | flops | bytes accessed | tf_op | source)
XLA Modules:
  0.0 90.8 jit_solution(18357264149444044881)
XLA Ops:
  0.6 7.5 %all-gather = bf16[1,64,2048]{2,1,0:T(8,128)(2,1)S(1)} all-gather(bf16[1,64,512]{2,1,0:T(8,128)(2,1)} %param.6), channel_id=2, replica_groups=mesh['day'=8,'pt'=4] {'pt'}, dimensions={2}, use_global_device_ids=true | all-gather | bytes 327680 | tf_op jit(solution)/shard_map/all_gather | solution.py:57
  8.1 1.5 %collective-permute-start.3 = (bf16[64,2048]{1,0:T(8,128)(2,1)S(1)}, bf16[64,2048]{1,0:T(8,128)(2,1)S(1)}, u32[]{:S(2)}, u32[]{:S(2)}) collective-permute-start(bf16[64,2048]{1,0:T(8,128)(2,1)S(1)} %bitcast.43), channel_id=1, source_target_pairs={{4,0},{0,4},{12,8},{8,12},{20,16},{16,20},{28,24},{24,28},{5,1},{1... | collective-permute-start | bytes 786440 | tf_op jit(solution)/shard_map/ppermute | solution.py:75
  10.3 0.9 %bitcast_multiply_fusion = f32[64,512]{1,0:T(8,128)S(1)} fusion(f32[1,64,512]{2,1,0:T(8,128)} %param.8, f32[512]{0:T(512)} %bitcast.51), kind=kLoop, calls=%fused_computation.31 | loop fusion | flops 32768 | bytes 264192 | tf_op jit(solution)/shard_map/mul | solution.py:59
  11.4 1.5 %collective-permute-start.1 = (f32[16,512]{1,0:T(8,128)S(1)}, f32[16,512]{1,0:T(8,128)S(1)}, u32[]{:S(2)}, u32[]{:S(2)}) collective-permute-start(f32[16,512]{1,0:T(8,128)S(1)} %get-tuple-element.29), channel_id=1, source_target_pairs={{0,2},{1,3},{2,0},{3,1},{4,6},{5,7},{6,4},{7,5},{8,10},{9,11},{10,... | collective-permute-start | bytes 98312 | tf_op jit(solution)/shard_map/ppermute | solution.py:22
  13.0 4.3 %collective-permute-start.4 = (s32[1]{0:T(128)}, s32[1]{0:T(128)}, u32[]{:S(2)}, u32[]{:S(2)}) collective-permute-start(s32[1]{0:T(128)} %param.10), channel_id=1, source_target_pairs={{4,0},{0,4},{12,8},{8,12},{20,16},{16,20},{28,24},{24,28},{5,1},{1... | collective-permute-start | bytes 20 | tf_op jit(solution)/shard_map/ppermute | solution.py:80
  18.0 3.3 %collective-permute-done.4 = s32[1]{0:T(128)} collective-permute-done((s32[1]{0:T(128)}, s32[1]{0:T(128)}, u32[]{:S(2)}, u32[]{:S(2)}) %collective-permute-start.4) | collective-permute-done | bytes 36 | tf_op jit(solution)/shard_map/ppermute | solution.py:80
  23.5 2.4 %collective-permute-start.5 = (f32[16,2048]{1,0:T(8,128)S(1)}, f32[16,2048]{1,0:T(8,128)S(1)}, u32[]{:S(2)}, u32[]{:S(2)}) collective-permute-start(f32[16,2048]{1,0:T(8,128)S(1)} %constant_dynamic-update-slice_fusion.3), channel_id=1, source_target_pairs={{4,0},{0,4},{12,8},{8,12},{20,16},{16,20},{28,24},{24,28},{5,1},{1... | collective-permute-start | bytes 393224 | tf_op jit(solution)/shard_map/ppermute | solution.py:79
  26.1 3.6 %exponential_convert_fusion.1 = bf16[2048,2048]{1,0:T(8,128)(2,1)S(1)} fusion(bf16[64,2048]{1,0:T(8,128)(2,1)S(1)} %collective-permute-done.3, f32[2048]{0:T(1024)S(1)} %multiply_reduce_fusion.6, f32[2048]{0:T(1024)S(1)} %multiply_reduce_fusion.7, bf16[1,64,2048]{2,1,0:T(8,128)(2,1)S(1)} %all-gather), kind=kOutput, calls=%fused_computation.1 | convolution fusion | flops 557842432 | bytes 8929280 | tf_op jit(solution)/shard_map/dot_general | solution.py:45
  29.7 1.3 %fusion.27 = (f32[16]{0:T(128)S(1)}, f32[16,2048]{1,0:T(8,128)S(1)}) fusion(f32[2048]{0:T(1024)S(1)} %fusion.14, bf16[2048,2048]{1,0:T(8,128)(2,1)S(1)} %exponential_convert_fusion.1, f32[16,2048]{1,0:T(8,128)S(1)} %constant_dynamic-update-slice_fusion.3, f32[2048]{0:T(1024)S(1)} %fusion.13), kind=kOutput, calls=%fused_computation.90 | convolution fusion | flops 134348784 | bytes 8667200 | tf_op jit(solution)/shard_map/dot_general | solution.py:109
  31.2 3.5 %collective-permute-start.6 = (bf16[16,2048]{1,0:T(8,128)(2,1)S(1)}, bf16[16,2048]{1,0:T(8,128)(2,1)S(1)}, u32[]{:S(2)}, u32[]{:S(2)}) collective-permute-start(bf16[16,2048]{1,0:T(8,128)(2,1)S(1)} %get-tuple-element.18), channel_id=1, source_target_pairs={{0,8},{28,20},{1,9},{29,21},{2,10},{30,22},{3,11},{31,23}} | collective-permute-start | bytes 196616 | tf_op jit(solution)/shard_map/ppermute | solution.py:118
  34.7 3.6 %exponential_convert_fusion = bf16[2048,2048]{1,0:T(8,128)(2,1)S(1)} fusion(bf16[64,2048]{1,0:T(8,128)(2,1)S(1)} %collective-permute-done.7, f32[2048]{0:T(1024)S(1)} %multiply_reduce_fusion.7, f32[2048]{0:T(1024)S(1)} %multiply_reduce_fusion.5, bf16[1,64,2048]{2,1,0:T(8,128)(2,1)S(1)} %all-gather), kind=kOutput, calls=%fused_computation | convolution fusion | flops 557842432 | bytes 8929280 | tf_op jit(solution)/shard_map/dot_general | solution.py:45
  38.3 1.3 %fusion.28 = (f32[16]{0:T(128)S(1)}, f32[16,2048]{1,0:T(8,128)S(1)}) fusion(f32[2048]{0:T(1024)S(1)} %fusion.13, bf16[16,2048]{1,0:T(8,128)(2,1)S(1)} %collective-permute-done.6, bf16[2048,2048]{1,0:T(8,128)(2,1)S(1)} %exponential_convert_fusion), kind=kOutput, calls=%fused_computation.91 | convolution fusion | flops 134283248 | bytes 8593472 | tf_op jit(solution)/shard_map/dot_general | solution.py:101
  39.6 1.4 %fusion.29 = (f32[16]{0:T(128)S(1)}, f32[16,2048]{1,0:T(8,128)S(1)}) fusion(f32[2048]{0:T(1024)S(1)} %fusion.14, bf16[2048,2048]{1,0:T(8,128)(2,1)S(1)} %exponential_convert_fusion.1, f32[16,2048]{1,0:T(8,128)S(1)} %constant_dynamic-update-slice_fusion.3, f32[16]{0:T(128)S(1)} %get-tuple-element.42, f32[16,2048]{1,0:T(8,128)S(1)} %get-tuple-element.43, ...), kind=kOutput, calls=%fused_computation.92 | convolution fusion | flops 134414320 | bytes 8790148 | tf_op jit(solution)/shard_map/dot_general | solution.py:109
  41.1 0.8 collective-permute-start.8
  41.9 4.5 %fusion.2 = f32[2048,1024]{1,0:T(8,128)} fusion(bf16[64,2048]{1,0:T(8,128)(2,1)S(1)} %bitcast.45, bf16[1,64,2048]{2,1,0:T(8,128)(2,1)S(1)} %all-gather), kind=kOutput, calls=%fused_computation.29 | convolution fusion | flops 268435456 | bytes 8781824 | tf_op jit(solution)/shard_map/dot_general | solution.py:45
  46.4 1.3 %fusion.30 = (f32[16]{0:T(128)S(1)}, f32[16,2048]{1,0:T(8,128)S(1)}) fusion(f32[2048]{0:T(1024)S(1)} %fusion.13, bf16[16,2048]{1,0:T(8,128)(2,1)S(1)} %collective-permute-done.8, bf16[2048,2048]{1,0:T(8,128)(2,1)S(1)} %exponential_convert_fusion), kind=kOutput, calls=%fused_computation.93 | convolution fusion | flops 134283248 | bytes 8593472 | tf_op jit(solution)/shard_map/dot_general | solution.py:101
  47.7 1.4 %fusion.31 = (f32[16]{0:T(128)S(1)}, f32[16,2048]{1,0:T(8,128)S(1)}) fusion(f32[2048]{0:T(1024)S(1)} %fusion.14, bf16[2048,2048]{1,0:T(8,128)(2,1)S(1)} %exponential_convert_fusion.1, f32[16,2048]{1,0:T(8,128)S(1)} %constant_dynamic-update-slice_fusion.3, f32[16]{0:T(128)S(1)} %get-tuple-element.46, f32[16,2048]{1,0:T(8,128)S(1)} %get-tuple-element.47, ...), kind=kOutput, calls=%fused_computation.94 | convolution fusion | flops 134414320 | bytes 8790148 | tf_op jit(solution)/shard_map/dot_general | solution.py:109
  50.0 1.3 %collective-permute-start.13 = (f32[16,2048]{1,0:T(8,128)S(1)}, f32[16,2048]{1,0:T(8,128)S(1)}, u32[]{:S(2)}, u32[]{:S(2)}) collective-permute-start(f32[16,2048]{1,0:T(8,128)S(1)} %get-tuple-element.19), channel_id=1, source_target_pairs={{0,4},{28,24},{1,5},{29,25},{2,6},{30,26},{3,7},{31,27}} | collective-permute-start | bytes 393224 | tf_op jit(solution)/shard_map/ppermute | solution.py:121
  52.6 1.3 %fusion.32 = (f32[16]{0:T(128)S(1)}, f32[16,2048]{1,0:T(8,128)S(1)}) fusion(f32[2048]{0:T(1024)S(1)} %fusion.13, bf16[16,2048]{1,0:T(8,128)(2,1)S(1)} %collective-permute-done.9, bf16[2048,2048]{1,0:T(8,128)(2,1)S(1)} %exponential_convert_fusion), kind=kOutput, calls=%fused_computation.95 | convolution fusion | flops 134283248 | bytes 8593472 | tf_op jit(solution)/shard_map/dot_general | solution.py:101
  53.9 1.4 %fusion.33 = (f32[16]{0:T(128)S(1)}, f32[16,2048]{1,0:T(8,128)S(1)}) fusion(f32[2048]{0:T(1024)S(1)} %fusion.14, bf16[2048,2048]{1,0:T(8,128)(2,1)S(1)} %exponential_convert_fusion.1, f32[16,2048]{1,0:T(8,128)S(1)} %constant_dynamic-update-slice_fusion.3, f32[16]{0:T(128)S(1)} %get-tuple-element.50, f32[16,2048]{1,0:T(8,128)S(1)} %get-tuple-element.51, ...), kind=kOutput, calls=%fused_computation.96 | convolution fusion | flops 134414320 | bytes 8790148 | tf_op jit(solution)/shard_map/dot_general | solution.py:109
  55.4 1.3 %collective-permute-start.10 = (f32[16,2048]{1,0:T(8,128)S(1)}, f32[16,2048]{1,0:T(8,128)S(1)}, u32[]{:S(2)}, u32[]{:S(2)}) collective-permute-start(f32[16,2048]{1,0:T(8,128)S(1)} %multiply_divide_fusion), channel_id=1, source_target_pairs={{24,28},{4,0},{25,29},{5,1},{26,30},{6,2},{27,31},{7,3}} | collective-permute-start | bytes 393224 | tf_op jit(solution)/shard_map/ppermute | solution.py:121
  57.5 5.7 %collective-permute-done.10 = f32[16,2048]{1,0:T(8,128)S(1)} collective-permute-done((f32[16,2048]{1,0:T(8,128)S(1)}, f32[16,2048]{1,0:T(8,128)S(1)}, u32[]{:S(2)}, u32[]{:S(2)}) %collective-permute-start.10) | collective-permute-done | bytes 131104 | tf_op jit(solution)/shard_map/ppermute | solution.py:121
  63.4 1.2 %collective-permute-start.18 = (f32[1,2048]{1,0:T(1,128)S(1)}, f32[1,2048]{1,0:T(1,128)S(1)}, u32[]{:S(2)}, u32[]{:S(2)}) collective-permute-start(f32[1,2048]{1,0:T(1,128)S(1)} %bitcast.48), channel_id=1, source_target_pairs={{0,2},{1,3},{2,0},{3,1},{4,6},{5,7},{6,4},{7,5},{8,10},{9,11},{10,... | collective-permute-start | bytes 24584 | tf_op jit(solution)/shard_map/ppermute | solution.py:22
  64.6 1.4 %collective-permute-start.19 = (f32[1,2048]{1,0:T(1,128)S(1)}, f32[1,2048]{1,0:T(1,128)S(1)}, u32[]{:S(2)}, u32[]{:S(2)}) collective-permute-start(f32[1,2048]{1,0:T(1,128)S(1)} %bitcast.49), channel_id=1, source_target_pairs={{0,3},{1,0},{2,1},{3,2},{4,7},{5,4},{6,5},{7,6},{8,11},{9,8},{10,9... | collective-permute-start | bytes 24584 | tf_op jit(solution)/shard_map/ppermute | solution.py:22
  68.1 6.9 %multiply_reduce_fusion.1 = (f32[1024]{0:T(1024)S(1)}, f32[1024]{0:T(1024)S(1)}, f32[2048,1024]{1,0:T(8,128)S(1)}) fusion(f32[1024]{0:T(1024)S(1)} %get-tuple-element.39, f32[2048]{0:T(1024)S(1)} %get-tuple-element.10, f32[2048]{0:T(1024)S(1)} %multiply_reduce_fusion.7, f32[2048,1024]{1,0:T(8,128)} %fusion.2, f32[1024]{0:T(1024)S(1)} %get-tuple-element.38, ...), kind=kOutput, calls=%fused_computation.3 | convolution fusion | flops 293599232 | bytes 17203200 | tf_op jit(solution)/shard_map/dot_general | solution.py:45
  75.7 6.4 %multiply_reduce_fusion = (f32[2048]{0:T(1024)S(1)}, f32[2048]{0:T(1024)S(1)}) fusion(f32[2048,1024]{1,0:T(8,128)S(1)} %get-tuple-element.54, f32[1024]{0:T(1024)S(1)} %get-tuple-element.37, f32[1024]{0:T(1024)S(1)} %get-tuple-element.39, f32[2048]{0:T(1024)S(1)} %multiply_reduce_fusion.7, f32[1024]{0:T(1024)S(1)} %get-tuple-element.36, ...), kind=kLoop, calls=%fused_computation.2 | loop fusion | flops 25161728 | bytes 16818176 | tf_op jit(solution)/shard_map/reduce_sum | solution.py:158
  82.3 1.0 %collective-permute-start.20 = (f32[512]{0:T(512)S(1)}, f32[512]{0:T(512)S(1)}, u32[]{:S(2)}, u32[]{:S(2)}) collective-permute-start(f32[512]{0:T(512)S(1)} %get-tuple-element.34), channel_id=1, source_target_pairs={{0,1},{1,2},{2,3},{3,0},{4,5},{5,6},{6,7},{7,4},{8,9},{9,10},{10,1... | collective-permute-start | bytes 6152 | tf_op jit(solution)/shard_map/ppermute | solution.py:22
  83.3 1.1 %collective-permute-start.21 = (f32[512]{0:T(512)S(1)}, f32[512]{0:T(512)S(1)}, u32[]{:S(2)}, u32[]{:S(2)}) collective-permute-start(f32[512]{0:T(512)S(1)} %get-tuple-element.33), channel_id=1, source_target_pairs={{0,2},{1,3},{2,0},{3,1},{4,6},{5,7},{6,4},{7,5},{8,10},{9,11},{10,... | collective-permute-start | bytes 6152 | tf_op jit(solution)/shard_map/ppermute | solution.py:22
  85.0 1.0 %collective-permute-start.15 = (f32[2,16,512]{2,1,0:T(8,128)S(1)}, f32[2,16,512]{2,1,0:T(8,128)S(1)}, u32[]{:S(2)}, u32[]{:S(2)}) collective-permute-start(f32[2,16,512]{2,1,0:T(8,128)S(1)} %get-tuple-element.25), channel_id=1, source_target_pairs={{0,2},{1,3},{2,0},{3,1},{4,6},{5,7},{6,4},{7,5},{8,10},{9,11},{10,... | collective-permute-start | bytes 196616 | tf_op jit(solution)/shard_map/ppermute | solution.py:22
  86.0 1.4 %collective-permute-start.16 = (f32[2,16,512]{2,1,0:T(8,128)S(1)}, f32[2,16,512]{2,1,0:T(8,128)S(1)}, u32[]{:S(2)}, u32[]{:S(2)}) collective-permute-start(f32[2,16,512]{2,1,0:T(8,128)S(1)} %get-tuple-element.22), channel_id=1, source_target_pairs={{0,3},{1,0},{2,1},{3,2},{4,7},{5,4},{6,5},{7,6},{8,11},{9,8},{10,9... | collective-permute-start | bytes 196616 | tf_op jit(solution)/shard_map/ppermute | solution.py:22
  88.7 1.3 %collective-permute-done.15 = f32[2,16,512]{2,1,0:T(8,128)S(1)} collective-permute-done((f32[2,16,512]{2,1,0:T(8,128)S(1)}, f32[2,16,512]{2,1,0:T(8,128)S(1)}, u32[]{:S(2)}, u32[]{:S(2)}) %collective-permute-start.15) | collective-permute-done | bytes 65568 | tf_op jit(solution)/shard_map/ppermute | solution.py:22
  90.1 0.7 fusion.24
  (72 shorter events, 10.1 us)
Async XLA Ops:
  8.1 17.9 %collective-permute-start.3 = (bf16[64,2048]{1,0:T(8,128)(2,1)S(1)}, bf16[64,2048]{1,0:T(8,128)(2,1)S(1)}, u32[]{:S(2)}, u32[]{:S(2)}) collective-permute-start(bf16[64,2048]{1,0:T(8,128)(2,1)S(1)} %bitcast.43), channel_id=1, source_target_pairs={{4,0},{0,4},{12,8},{8,12},{20,16},{16,20},{28,24},{24,28},{5,1},{1... | collective-permute-start | bytes 786440 | tf_op jit(solution)/shard_map/ppermute | solution.py:75
  9.6 21.5 %collective-permute-start.7 = (bf16[64,2048]{1,0:T(8,128)(2,1)S(1)}, bf16[64,2048]{1,0:T(8,128)(2,1)S(1)}, u32[]{:S(2)}, u32[]{:S(2)}) collective-permute-start(bf16[64,2048]{1,0:T(8,128)(2,1)S(1)} %bitcast.44), channel_id=1, source_target_pairs={{8,4},{4,8},{16,12},{12,16},{24,20},{20,24},{9,5},{5,9},{17,13},{1... | collective-permute-start | bytes 786440 | tf_op jit(solution)/shard_map/ppermute | solution.py:83
  11.3 12.0 %collective-permute-start = (f32[16,512]{1,0:T(8,128)S(1)}, f32[16,512]{1,0:T(8,128)S(1)}, u32[]{:S(2)}, u32[]{:S(2)}) collective-permute-start(f32[16,512]{1,0:T(8,128)S(1)} %get-tuple-element.30), channel_id=1, source_target_pairs={{0,1},{1,2},{2,3},{3,0},{4,5},{5,6},{6,7},{7,4},{8,9},{9,10},{10,1... | collective-permute-start | bytes 98312 | tf_op jit(solution)/shard_map/ppermute | solution.py:22
  11.4 11.9 %collective-permute-start.1 = (f32[16,512]{1,0:T(8,128)S(1)}, f32[16,512]{1,0:T(8,128)S(1)}, u32[]{:S(2)}, u32[]{:S(2)}) collective-permute-start(f32[16,512]{1,0:T(8,128)S(1)} %get-tuple-element.29), channel_id=1, source_target_pairs={{0,2},{1,3},{2,0},{3,1},{4,6},{5,7},{6,4},{7,5},{8,10},{9,11},{10,... | collective-permute-start | bytes 98312 | tf_op jit(solution)/shard_map/ppermute | solution.py:22
  13.0 8.4 %collective-permute-start.4 = (s32[1]{0:T(128)}, s32[1]{0:T(128)}, u32[]{:S(2)}, u32[]{:S(2)}) collective-permute-start(s32[1]{0:T(128)} %param.10), channel_id=1, source_target_pairs={{4,0},{0,4},{12,8},{8,12},{20,16},{16,20},{28,24},{24,28},{5,1},{1... | collective-permute-start | bytes 20 | tf_op jit(solution)/shard_map/ppermute | solution.py:80
  21.3 2.2 %collective-permute-start.2 = (f32[16,512]{1,0:T(8,128)S(1)}, f32[16,512]{1,0:T(8,128)S(1)}, u32[]{:S(2)}, u32[]{:S(2)}) collective-permute-start(f32[16,512]{1,0:T(8,128)S(1)} %get-tuple-element.28), channel_id=1, source_target_pairs={{0,3},{1,0},{2,1},{3,2},{4,7},{5,4},{6,5},{7,6},{8,11},{9,8},{10,9... | collective-permute-start | bytes 98312 | tf_op jit(solution)/shard_map/ppermute | solution.py:22
  23.5 7.4 %collective-permute-start.5 = (f32[16,2048]{1,0:T(8,128)S(1)}, f32[16,2048]{1,0:T(8,128)S(1)}, u32[]{:S(2)}, u32[]{:S(2)}) collective-permute-start(f32[16,2048]{1,0:T(8,128)S(1)} %constant_dynamic-update-slice_fusion.3), channel_id=1, source_target_pairs={{4,0},{0,4},{12,8},{8,12},{20,16},{16,20},{28,24},{24,28},{5,1},{1... | collective-permute-start | bytes 393224 | tf_op jit(solution)/shard_map/ppermute | solution.py:79
  31.2 7.1 %collective-permute-start.6 = (bf16[16,2048]{1,0:T(8,128)(2,1)S(1)}, bf16[16,2048]{1,0:T(8,128)(2,1)S(1)}, u32[]{:S(2)}, u32[]{:S(2)}) collective-permute-start(bf16[16,2048]{1,0:T(8,128)(2,1)S(1)} %get-tuple-element.18), channel_id=1, source_target_pairs={{0,8},{28,20},{1,9},{29,21},{2,10},{30,22},{3,11},{31,23}} | collective-permute-start | bytes 196616 | tf_op jit(solution)/shard_map/ppermute | solution.py:118
  38.3 3.7 %copy-start = (bf16[1,64,2048]{2,1,0:T(8,128)(2,1)S(1)}, bf16[1,64,2048]{2,1,0:T(8,128)(2,1)}, u32[]{:S(2)}) copy-start(bf16[1,64,2048]{2,1,0:T(8,128)(2,1)} %param.7) | copy-start | bytes 786436
  41.1 5.4 %collective-permute-start.8 = (bf16[16,2048]{1,0:T(8,128)(2,1)S(1)}, bf16[16,2048]{1,0:T(8,128)(2,1)S(1)}, u32[]{:S(2)}, u32[]{:S(2)}) collective-permute-start(bf16[16,2048]{1,0:T(8,128)(2,1)S(1)} %get-tuple-element.16), channel_id=1, source_target_pairs={{8,16},{20,12},{9,17},{21,13},{10,18},{22,14},{11,19},{23,15}} | collective-permute-start | bytes 196616 | tf_op jit(solution)/shard_map/ppermute | solution.py:118
  49.2 3.4 %collective-permute-start.9 = (bf16[16,2048]{1,0:T(8,128)(2,1)S(1)}, bf16[16,2048]{1,0:T(8,128)(2,1)S(1)}, u32[]{:S(2)}, u32[]{:S(2)}) collective-permute-start(bf16[16,2048]{1,0:T(8,128)(2,1)S(1)} %get-tuple-element.14), channel_id=1, source_target_pairs={{16,24},{12,4},{17,25},{13,5},{18,26},{14,6},{19,27},{15,7}} | collective-permute-start | bytes 196616 | tf_op jit(solution)/shard_map/ppermute | solution.py:118
  50.0 7.5 %collective-permute-start.13 = (f32[16,2048]{1,0:T(8,128)S(1)}, f32[16,2048]{1,0:T(8,128)S(1)}, u32[]{:S(2)}, u32[]{:S(2)}) collective-permute-start(f32[16,2048]{1,0:T(8,128)S(1)} %get-tuple-element.19), channel_id=1, source_target_pairs={{0,4},{28,24},{1,5},{29,25},{2,6},{30,26},{3,7},{31,27}} | collective-permute-start | bytes 393224 | tf_op jit(solution)/shard_map/ppermute | solution.py:121
  51.3 6.2 %collective-permute-start.12 = (f32[16,2048]{1,0:T(8,128)S(1)}, f32[16,2048]{1,0:T(8,128)S(1)}, u32[]{:S(2)}, u32[]{:S(2)}) collective-permute-start(f32[16,2048]{1,0:T(8,128)S(1)} %get-tuple-element.17), channel_id=1, source_target_pairs={{8,12},{20,16},{9,13},{21,17},{10,14},{22,18},{11,15},{23,19}} | collective-permute-start | bytes 393224 | tf_op jit(solution)/shard_map/ppermute | solution.py:121
  51.9 5.6 %collective-permute-start.11 = (f32[16,2048]{1,0:T(8,128)S(1)}, f32[16,2048]{1,0:T(8,128)S(1)}, u32[]{:S(2)}, u32[]{:S(2)}) collective-permute-start(f32[16,2048]{1,0:T(8,128)S(1)} %get-tuple-element.15), channel_id=1, source_target_pairs={{16,20},{12,8},{17,21},{13,9},{18,22},{14,10},{19,23},{15,11}} | collective-permute-start | bytes 393224 | tf_op jit(solution)/shard_map/ppermute | solution.py:121
  55.4 7.8 %collective-permute-start.10 = (f32[16,2048]{1,0:T(8,128)S(1)}, f32[16,2048]{1,0:T(8,128)S(1)}, u32[]{:S(2)}, u32[]{:S(2)}) collective-permute-start(f32[16,2048]{1,0:T(8,128)S(1)} %multiply_divide_fusion), channel_id=1, source_target_pairs={{24,28},{4,0},{25,29},{5,1},{26,30},{6,2},{27,31},{7,3}} | collective-permute-start | bytes 393224 | tf_op jit(solution)/shard_map/ppermute | solution.py:121
  63.3 3.1 %collective-permute-start.17 = (f32[1,2048]{1,0:T(1,128)S(1)}, f32[1,2048]{1,0:T(1,128)S(1)}, u32[]{:S(2)}, u32[]{:S(2)}) collective-permute-start(f32[1,2048]{1,0:T(1,128)S(1)} %bitcast.47), channel_id=1, source_target_pairs={{0,1},{1,2},{2,3},{3,0},{4,5},{5,6},{6,7},{7,4},{8,9},{9,10},{10,1... | collective-permute-start | bytes 24584 | tf_op jit(solution)/shard_map/ppermute | solution.py:22
  63.4 3.7 %collective-permute-start.18 = (f32[1,2048]{1,0:T(1,128)S(1)}, f32[1,2048]{1,0:T(1,128)S(1)}, u32[]{:S(2)}, u32[]{:S(2)}) collective-permute-start(f32[1,2048]{1,0:T(1,128)S(1)} %bitcast.48), channel_id=1, source_target_pairs={{0,2},{1,3},{2,0},{3,1},{4,6},{5,7},{6,4},{7,5},{8,10},{9,11},{10,... | collective-permute-start | bytes 24584 | tf_op jit(solution)/shard_map/ppermute | solution.py:22
  64.6 2.8 %collective-permute-start.19 = (f32[1,2048]{1,0:T(1,128)S(1)}, f32[1,2048]{1,0:T(1,128)S(1)}, u32[]{:S(2)}, u32[]{:S(2)}) collective-permute-start(f32[1,2048]{1,0:T(1,128)S(1)} %bitcast.49), channel_id=1, source_target_pairs={{0,3},{1,0},{2,1},{3,2},{4,7},{5,4},{6,5},{7,6},{8,11},{9,8},{10,9... | collective-permute-start | bytes 24584 | tf_op jit(solution)/shard_map/ppermute | solution.py:22
  82.3 3.7 %collective-permute-start.20 = (f32[512]{0:T(512)S(1)}, f32[512]{0:T(512)S(1)}, u32[]{:S(2)}, u32[]{:S(2)}) collective-permute-start(f32[512]{0:T(512)S(1)} %get-tuple-element.34), channel_id=1, source_target_pairs={{0,1},{1,2},{2,3},{3,0},{4,5},{5,6},{6,7},{7,4},{8,9},{9,10},{10,1... | collective-permute-start | bytes 6152 | tf_op jit(solution)/shard_map/ppermute | solution.py:22
  83.3 4.3 %collective-permute-start.21 = (f32[512]{0:T(512)S(1)}, f32[512]{0:T(512)S(1)}, u32[]{:S(2)}, u32[]{:S(2)}) collective-permute-start(f32[512]{0:T(512)S(1)} %get-tuple-element.33), channel_id=1, source_target_pairs={{0,2},{1,3},{2,0},{3,1},{4,6},{5,7},{6,4},{7,5},{8,10},{9,11},{10,... | collective-permute-start | bytes 6152 | tf_op jit(solution)/shard_map/ppermute | solution.py:22
  84.4 3.4 %collective-permute-start.22 = (f32[512]{0:T(512)S(1)}, f32[512]{0:T(512)S(1)}, u32[]{:S(2)}, u32[]{:S(2)}) collective-permute-start(f32[512]{0:T(512)S(1)} %get-tuple-element.32), channel_id=1, source_target_pairs={{0,3},{1,0},{2,1},{3,2},{4,7},{5,4},{6,5},{7,6},{8,11},{9,8},{10,9... | collective-permute-start | bytes 6152 | tf_op jit(solution)/shard_map/ppermute | solution.py:22
  84.9 3.8 %collective-permute-start.14 = (f32[2,16,512]{2,1,0:T(8,128)S(1)}, f32[2,16,512]{2,1,0:T(8,128)S(1)}, u32[]{:S(2)}, u32[]{:S(2)}) collective-permute-start(f32[2,16,512]{2,1,0:T(8,128)S(1)} %get-tuple-element.24), channel_id=1, source_target_pairs={{0,1},{1,2},{2,3},{3,0},{4,5},{5,6},{6,7},{7,4},{8,9},{9,10},{10,1... | collective-permute-start | bytes 196616 | tf_op jit(solution)/shard_map/ppermute | solution.py:22
  85.0 5.0 %collective-permute-start.15 = (f32[2,16,512]{2,1,0:T(8,128)S(1)}, f32[2,16,512]{2,1,0:T(8,128)S(1)}, u32[]{:S(2)}, u32[]{:S(2)}) collective-permute-start(f32[2,16,512]{2,1,0:T(8,128)S(1)} %get-tuple-element.25), channel_id=1, source_target_pairs={{0,2},{1,3},{2,0},{3,1},{4,6},{5,7},{6,4},{7,5},{8,10},{9,11},{10,... | collective-permute-start | bytes 196616 | tf_op jit(solution)/shard_map/ppermute | solution.py:22
  86.0 4.0 %collective-permute-start.16 = (f32[2,16,512]{2,1,0:T(8,128)S(1)}, f32[2,16,512]{2,1,0:T(8,128)S(1)}, u32[]{:S(2)}, u32[]{:S(2)}) collective-permute-start(f32[2,16,512]{2,1,0:T(8,128)S(1)} %get-tuple-element.22), channel_id=1, source_target_pairs={{0,3},{1,0},{2,1},{3,2},{4,7},{5,4},{6,5},{7,6},{8,11},{9,8},{10,9... | collective-permute-start | bytes 196616 | tf_op jit(solution)/shard_map/ppermute | solution.py:22

commit v18 on v17

--- a/solution.py
+++ b/solution.py
@@ -146,9 +146,10 @@
     cell_live = (pt_rank * own_slots + jnp.arange(own_slots, dtype=jnp.int32) < cell_total).astype(
         jnp.float32
     )
-    cell_span = own_slots // 2
+    cell_parts = 4
+    cell_span = own_slots // cell_parts
     ratio_rows = 0.0
-    for part in range(2):
+    for part in range(cell_parts):
         part_cells = lax.slice_in_dim(own_cells, part * cell_span, (part + 1) * cell_span, axis=1)
         part_norm = lax.slice_in_dim(cell_norm, part * cell_span, (part + 1) * cell_span)
         fit_kernel = jnp.exp(-squared_dist(day_pts, day_norm, part_cells, part_norm))

time: 91.2 us -> 88.6 us (0.971)
  other arithmetic: 10.8 us -> 6.85 us
  waiting for transfers between devices: 11.5 us -> 7.62 us
  matrix products: 28 us -> 31.1 us
  local copies, waits for them, and re-layouts: 2.07 us -> 3.98 us
    reduce_sum x1 -> x2, other arithmetic: 6.38 us -> 1.27 us  [shards(): ratio_rows = ratio_rows + jnp.sum(fit_kernel * inverse[None, :], axis=1)]
    dot_general x4 -> x6, matrix products: 18.6 us -> 21.8 us  [squared_dist(): lax.dot_general(left_pts, right_pts, (((0,), (0,)), ((), ())), preferred_...]
    ppermute x4, waiting for transfers between devices: 5.68 us -> 2.84 us  [shards(): lax.ppermute(following, 'day', [(forward_day, forward_day + 1), (backward...]
    unnamed x2 -> x8, local copies, waits for them, and re-layouts: 0.01 us -> 1.91 us
    ppermute x1, waiting for transfers between devices: 3.34 us -> 2.3 us  [shards(): other_count = lax.ppermute(support_count, 'day', pair_route)[0]]
    reduce_sum x4, other arithmetic: 0.28 us -> 1.23 us  [norm_of(): return jnp.sum(wide * wide, axis=0)]
  transfers between devices with their start and end apart: 23 -> 23, of which waited for: 7 -> 7; matrix products, arithmetic and copies ran while one was open for 21% -> 28% of each run, Pallas kernels for 0% -> 0%
where the time goes in v18:
time: 88.6 us; the launch traced here: 87.9 us
  matrix products  31.1 us (35%)
  starting transfers between devices  27.7 us (31%)
  waiting for transfers between devices  7.62 us (9%)
  blocking collectives  7.46 us (8%)
  other arithmetic  6.85 us (8%)
  local copies, waits for them, and re-layouts  3.98 us (4%)
  between operations  3.2 us (4%)
    dot_general x6, matrix products, squared_dist(): lax.dot_general(left_pts, right_pts, (((0,), (0,)), ((), ())), preferred_...  21.8 us
    ppermute x12, starting transfers between devices, swap_blocks(): lax.ppermute(piece, 'pt', [(i, (i + shift) % count) for i in range(count)])  9.92 us
    all_gather x1, blocking collectives, shards(): day_pts = lax.all_gather(own_pts, 'pt', axis=1, tiled=True)  7.46 us
    dot_general x4, matrix products, shards(): jnp.dot(sent, other_kernel, preferred_element_type=jnp.float32)  5.39 us
    ppermute x3, starting transfers between devices, shards(): lax.ppermute(outgoing, 'day', [(forward_day, forward_day + 2), (backward_...  4.98 us
    ppermute x1, starting transfers between devices, shards(): other_count = lax.ppermute(support_count, 'day', pair_route)[0]  4.27 us
    dot_general x3, matrix products, shards(): jnp.dot(incoming, link_kernel, preferred_element_type=jnp.float32)  3.92 us
    ppermute x4, starting transfers between devices, shards(): lax.ppermute(following, 'day', [(forward_day, forward_day + 1), (backward...  3.92 us
  transfers between devices with their start and end apart: 23, of which 7 were waited for; matrix products, arithmetic and copies ran while one was open for 28% of the time, Pallas kernels for 0%

profile of v18, /device:TPU:0, one launch (start us, length us, event | category | flops | bytes accessed | tf_op | source)
XLA Modules:
  0.0 87.9 jit_solution(2921349865121922479)
XLA Ops:
  0.6 7.5 %all-gather = bf16[1,64,2048]{2,1,0:T(8,128)(2,1)S(1)} all-gather(bf16[1,64,512]{2,1,0:T(8,128)(2,1)} %param.6), channel_id=2, replica_groups=mesh['day'=8,'pt'=4] {'pt'}, dimensions={2}, use_global_device_ids=true | all-gather | bytes 327680 | tf_op jit(solution)/shard_map/all_gather | solution.py:57
  8.1 1.5 %collective-permute-start.3 = (bf16[64,2048]{1,0:T(8,128)(2,1)S(1)}, bf16[64,2048]{1,0:T(8,128)(2,1)S(1)}, u32[]{:S(2)}, u32[]{:S(2)}) collective-permute-start(bf16[64,2048]{1,0:T(8,128)(2,1)S(1)} %bitcast.47), channel_id=1, source_target_pairs={{4,0},{0,4},{12,8},{8,12},{20,16},{16,20},{28,24},{24,28},{5,1},{1... | collective-permute-start | bytes 786440 | tf_op jit(solution)/shard_map/ppermute | solution.py:75
  11.4 1.5 %collective-permute-start.1 = (f32[16,512]{1,0:T(8,128)S(1)}, f32[16,512]{1,0:T(8,128)S(1)}, u32[]{:S(2)}, u32[]{:S(2)}) collective-permute-start(f32[16,512]{1,0:T(8,128)S(1)} %get-tuple-element.29), channel_id=1, source_target_pairs={{0,2},{1,3},{2,0},{3,1},{4,6},{5,7},{6,4},{7,5},{8,10},{9,11},{10,... | collective-permute-start | bytes 98312 | tf_op jit(solution)/shard_map/ppermute | solution.py:22
  13.0 4.3 %collective-permute-start.4 = (s32[1]{0:T(128)}, s32[1]{0:T(128)}, u32[]{:S(2)}, u32[]{:S(2)}) collective-permute-start(s32[1]{0:T(128)} %param.10), channel_id=1, source_target_pairs={{4,0},{0,4},{12,8},{8,12},{20,16},{16,20},{28,24},{24,28},{5,1},{1... | collective-permute-start | bytes 20 | tf_op jit(solution)/shard_map/ppermute | solution.py:80
  18.0 1.0 %multiply_reduce_fusion.8 = f32[2048]{0:T(1024)S(1)} fusion(bf16[1,64,2048]{2,1,0:T(8,128)(2,1)} %param.7), kind=kLoop, calls=%fused_computation.21 | loop fusion | flops 391168 | bytes 270336 | tf_op jit(solution)/shard_map/reduce_sum | solution.py:41
  19.0 2.3 %collective-permute-done.4 = s32[1]{0:T(128)} collective-permute-done((s32[1]{0:T(128)}, s32[1]{0:T(128)}, u32[]{:S(2)}, u32[]{:S(2)}) %collective-permute-start.4) | collective-permute-done | bytes 36 | tf_op jit(solution)/shard_map/ppermute | solution.py:80
  23.5 2.4 %collective-permute-start.5 = (f32[16,2048]{1,0:T(8,128)S(1)}, f32[16,2048]{1,0:T(8,128)S(1)}, u32[]{:S(2)}, u32[]{:S(2)}) collective-permute-start(f32[16,2048]{1,0:T(8,128)S(1)} %constant_dynamic-update-slice_fusion.3), channel_id=1, source_target_pairs={{4,0},{0,4},{12,8},{8,12},{20,16},{16,20},{28,24},{24,28},{5,1},{1... | collective-permute-start | bytes 393224 | tf_op jit(solution)/shard_map/ppermute | solution.py:79
  26.1 3.6 %exponential_convert_fusion.1 = bf16[2048,2048]{1,0:T(8,128)(2,1)S(1)} fusion(bf16[64,2048]{1,0:T(8,128)(2,1)S(1)} %collective-permute-done.3, f32[2048]{0:T(1024)S(1)} %multiply_reduce_fusion.10, f32[2048]{0:T(1024)S(1)} %multiply_reduce_fusion.11, bf16[1,64,2048]{2,1,0:T(8,128)(2,1)S(1)} %all-gather), kind=kOutput, calls=%fused_computation.1 | convolution fusion | flops 557842432 | bytes 8929280 | tf_op jit(solution)/shard_map/dot_general | solution.py:45
  29.7 1.3 %fusion.31 = (f32[16]{0:T(128)S(1)}, f32[16,2048]{1,0:T(8,128)S(1)}) fusion(f32[2048]{0:T(1024)S(1)} %fusion.14, bf16[2048,2048]{1,0:T(8,128)(2,1)S(1)} %exponential_convert_fusion.1, f32[16,2048]{1,0:T(8,128)S(1)} %constant_dynamic-update-slice_fusion.3, f32[2048]{0:T(1024)S(1)} %fusion.13), kind=kOutput, calls=%fused_computation.103 | convolution fusion | flops 134348784 | bytes 8667200 | tf_op jit(solution)/shard_map/dot_general | solution.py:109
  31.2 3.5 %collective-permute-start.6 = (bf16[16,2048]{1,0:T(8,128)(2,1)S(1)}, bf16[16,2048]{1,0:T(8,128)(2,1)S(1)}, u32[]{:S(2)}, u32[]{:S(2)}) collective-permute-start(bf16[16,2048]{1,0:T(8,128)(2,1)S(1)} %get-tuple-element.18), channel_id=1, source_target_pairs={{0,8},{28,20},{1,9},{29,21},{2,10},{30,22},{3,11},{31,23}} | collective-permute-start | bytes 196616 | tf_op jit(solution)/shard_map/ppermute | solution.py:118
  34.7 3.6 %exponential_convert_fusion = bf16[2048,2048]{1,0:T(8,128)(2,1)S(1)} fusion(bf16[64,2048]{1,0:T(8,128)(2,1)S(1)} %collective-permute-done.7, f32[2048]{0:T(1024)S(1)} %multiply_reduce_fusion.11, f32[2048]{0:T(1024)S(1)} %multiply_reduce_fusion.9, bf16[1,64,2048]{2,1,0:T(8,128)(2,1)S(1)} %all-gather), kind=kOutput, calls=%fused_computation | convolution fusion | flops 557842432 | bytes 8929280 | tf_op jit(solution)/shard_map/dot_general | solution.py:45
  38.3 1.3 %fusion.32 = (f32[16]{0:T(128)S(1)}, f32[16,2048]{1,0:T(8,128)S(1)}) fusion(f32[2048]{0:T(1024)S(1)} %fusion.13, bf16[16,2048]{1,0:T(8,128)(2,1)S(1)} %collective-permute-done.6, bf16[2048,2048]{1,0:T(8,128)(2,1)S(1)} %exponential_convert_fusion), kind=kOutput, calls=%fused_computation.104 | convolution fusion | flops 134283248 | bytes 8593472 | tf_op jit(solution)/shard_map/dot_general | solution.py:101
  39.6 1.4 %fusion.33 = (f32[16]{0:T(128)S(1)}, f32[16,2048]{1,0:T(8,128)S(1)}) fusion(f32[2048]{0:T(1024)S(1)} %fusion.14, bf16[2048,2048]{1,0:T(8,128)(2,1)S(1)} %exponential_convert_fusion.1, f32[16,2048]{1,0:T(8,128)S(1)} %constant_dynamic-update-slice_fusion.3, f32[16]{0:T(128)S(1)} %get-tuple-element.46, f32[16,2048]{1,0:T(8,128)S(1)} %get-tuple-element.47, ...), kind=kOutput, calls=%fused_computation.105 | convolution fusion | flops 134414320 | bytes 8790148 | tf_op jit(solution)/shard_map/dot_general | solution.py:109
  41.9 2.9 %negate_exponential_fusion = f32[2048,512]{1,0:T(8,128)} fusion(f32[512]{0:T(512)S(1)} %get-tuple-element.41, f32[2048]{0:T(1024)S(1)} %multiply_reduce_fusion.11, bf16[64,2048]{1,0:T(8,128)(2,1)S(1)} %bitcast.49, bf16[1,64,2048]{2,1,0:T(8,128)(2,1)S(1)} %all-gather), kind=kOutput, calls=%fused_computation.4 | convolution fusion | flops 138412032 | bytes 4532224 | tf_op jit(solution)/shard_map/dot_general | solution.py:45
  44.8 1.3 %fusion.34 = (f32[16]{0:T(128)S(1)}, f32[16,2048]{1,0:T(8,128)S(1)}) fusion(f32[2048]{0:T(1024)S(1)} %fusion.13, bf16[16,2048]{1,0:T(8,128)(2,1)S(1)} %collective-permute-done.8, bf16[2048,2048]{1,0:T(8,128)(2,1)S(1)} %exponential_convert_fusion), kind=kOutput, calls=%fused_computation.106 | convolution fusion | flops 134283248 | bytes 8593472 | tf_op jit(solution)/shard_map/dot_general | solution.py:101
  46.1 1.4 %fusion.35 = (f32[16]{0:T(128)S(1)}, f32[16,2048]{1,0:T(8,128)S(1)}) fusion(f32[2048]{0:T(1024)S(1)} %fusion.14, bf16[2048,2048]{1,0:T(8,128)(2,1)S(1)} %exponential_convert_fusion.1, f32[16,2048]{1,0:T(8,128)S(1)} %constant_dynamic-update-slice_fusion.3, f32[16]{0:T(128)S(1)} %get-tuple-element.50, f32[16,2048]{1,0:T(8,128)S(1)} %get-tuple-element.51, ...), kind=kOutput, calls=%fused_computation.107 | convolution fusion | flops 134414320 | bytes 8790148 | tf_op jit(solution)/shard_map/dot_general | solution.py:109
  48.2 2.9 %negate_exponential_fusion.1 = f32[2048,512]{1,0:T(8,128)} fusion(f32[512]{0:T(512)S(1)} %get-tuple-element.42, f32[2048]{0:T(1024)S(1)} %multiply_reduce_fusion.11, bf16[64,2048]{1,0:T(8,128)(2,1)S(1)} %bitcast.50, bf16[1,64,2048]{2,1,0:T(8,128)(2,1)S(1)} %all-gather), kind=kOutput, calls=%fused_computation.7 | convolution fusion | flops 138412032 | bytes 4532224 | tf_op jit(solution)/shard_map/dot_general | solution.py:45
  51.1 1.3 %collective-permute-start.13 = (f32[16,2048]{1,0:T(8,128)S(1)}, f32[16,2048]{1,0:T(8,128)S(1)}, u32[]{:S(2)}, u32[]{:S(2)}) collective-permute-start(f32[16,2048]{1,0:T(8,128)S(1)} %get-tuple-element.19), channel_id=1, source_target_pairs={{0,4},{28,24},{1,5},{29,25},{2,6},{30,26},{3,7},{31,27}} | collective-permute-start | bytes 393224 | tf_op jit(solution)/shard_map/ppermute | solution.py:121
  53.8 1.3 %fusion.36 = (f32[16]{0:T(128)S(1)}, f32[16,2048]{1,0:T(8,128)S(1)}) fusion(f32[2048]{0:T(1024)S(1)} %fusion.13, bf16[16,2048]{1,0:T(8,128)(2,1)S(1)} %collective-permute-done.9, bf16[2048,2048]{1,0:T(8,128)(2,1)S(1)} %exponential_convert_fusion), kind=kOutput, calls=%fused_computation.108 | convolution fusion | flops 134283248 | bytes 8593472 | tf_op jit(solution)/shard_map/dot_general | solution.py:101
  55.1 1.4 %fusion.37 = (f32[16]{0:T(128)S(1)}, f32[16,2048]{1,0:T(8,128)S(1)}) fusion(f32[2048]{0:T(1024)S(1)} %fusion.14, bf16[2048,2048]{1,0:T(8,128)(2,1)S(1)} %exponential_convert_fusion.1, f32[16,2048]{1,0:T(8,128)S(1)} %constant_dynamic-update-slice_fusion.3, f32[16]{0:T(128)S(1)} %get-tuple-element.54, f32[16,2048]{1,0:T(8,128)S(1)} %get-tuple-element.55, ...), kind=kOutput, calls=%fused_computation.109 | convolution fusion | flops 134414320 | bytes 8790148 | tf_op jit(solution)/shard_map/dot_general | solution.py:109
  56.6 1.3 %collective-permute-start.10 = (f32[16,2048]{1,0:T(8,128)S(1)}, f32[16,2048]{1,0:T(8,128)S(1)}, u32[]{:S(2)}, u32[]{:S(2)}) collective-permute-start(f32[16,2048]{1,0:T(8,128)S(1)} %multiply_divide_fusion), channel_id=1, source_target_pairs={{24,28},{4,0},{25,29},{5,1},{26,30},{6,2},{27,31},{7,3}} | collective-permute-start | bytes 393224 | tf_op jit(solution)/shard_map/ppermute | solution.py:121
  57.9 2.9 %negate_exponential_fusion.3 = f32[2048,512]{1,0:T(8,128)} fusion(f32[512]{0:T(512)S(1)} %get-tuple-element.40, f32[2048]{0:T(1024)S(1)} %multiply_reduce_fusion.11, bf16[64,2048]{1,0:T(8,128)(2,1)S(1)} %bitcast.51, bf16[1,64,2048]{2,1,0:T(8,128)(2,1)S(1)} %all-gather), kind=kOutput, calls=%fused_computation.13 | convolution fusion | flops 138412032 | bytes 4532224 | tf_op jit(solution)/shard_map/dot_general | solution.py:45
  61.5 2.8 %collective-permute-done.10 = f32[16,2048]{1,0:T(8,128)S(1)} collective-permute-done((f32[16,2048]{1,0:T(8,128)S(1)}, f32[16,2048]{1,0:T(8,128)S(1)}, u32[]{:S(2)}, u32[]{:S(2)}) %collective-permute-start.10) | collective-permute-done | bytes 131104 | tf_op jit(solution)/shard_map/ppermute | solution.py:121
  64.6 1.2 %collective-permute-start.18 = (f32[1,2048]{1,0:T(1,128)S(1)}, f32[1,2048]{1,0:T(1,128)S(1)}, u32[]{:S(2)}, u32[]{:S(2)}) collective-permute-start(f32[1,2048]{1,0:T(1,128)S(1)} %bitcast.54), channel_id=1, source_target_pairs={{0,2},{1,3},{2,0},{3,1},{4,6},{5,7},{6,4},{7,5},{8,10},{9,11},{10,... | collective-permute-start | bytes 24584 | tf_op jit(solution)/shard_map/ppermute | solution.py:22
  65.7 1.4 %collective-permute-start.19 = (f32[1,2048]{1,0:T(1,128)S(1)}, f32[1,2048]{1,0:T(1,128)S(1)}, u32[]{:S(2)}, u32[]{:S(2)}) collective-permute-start(f32[1,2048]{1,0:T(1,128)S(1)} %bitcast.55), channel_id=1, source_target_pairs={{0,3},{1,0},{2,1},{3,2},{4,7},{5,4},{6,5},{7,6},{8,11},{9,8},{10,9... | collective-permute-start | bytes 24584 | tf_op jit(solution)/shard_map/ppermute | solution.py:22
  69.2 5.9 %multiply_reduce_fusion.5 = (f32[512]{0:T(512)S(1)}, f32[512]{0:T(512)S(1)}, f32[512]{0:T(512)S(1)}, f32[512]{0:T(512)S(1)}, f32[2048,512]{1,0:T(8,128)S(1)}) fusion(f32[2048]{0:T(1024)S(1)} %get-tuple-element.10, f32[2048,512]{1,0:T(8,128)} %negate_exponential_fusion.1, f32[2048,512]{1,0:T(8,128)} %negate_exponential_fusion, ...), kind=kOutput, calls=%fused_computation.9 | convolution fusion | flops 146798592 | bytes 17131520 | tf_op jit(solution)/shard_map/dot_general | solution.py:45
  77.0 1.6 %copy-done.2 = f32[2048,512]{1,0:T(8,128)S(1)} copy-done((f32[2048,512]{1,0:T(8,128)S(1)}, f32[2048,512]{1,0:T(8,128)}, u32[]{:S(2)}) %copy-start.2) | copy-done | bytes 4194328
  79.4 1.0 %collective-permute-start.20 = (f32[512]{0:T(512)S(1)}, f32[512]{0:T(512)S(1)}, u32[]{:S(2)}, u32[]{:S(2)}) collective-permute-start(f32[512]{0:T(512)S(1)} %get-tuple-element.34), channel_id=1, source_target_pairs={{0,1},{1,2},{2,3},{3,0},{4,5},{5,6},{6,7},{7,4},{8,9},{9,10},{10,1... | collective-permute-start | bytes 6152 | tf_op jit(solution)/shard_map/ppermute | solution.py:22
  80.4 1.1 %collective-permute-start.21 = (f32[512]{0:T(512)S(1)}, f32[512]{0:T(512)S(1)}, u32[]{:S(2)}, u32[]{:S(2)}) collective-permute-start(f32[512]{0:T(512)S(1)} %get-tuple-element.33), channel_id=1, source_target_pairs={{0,2},{1,3},{2,0},{3,1},{4,6},{5,7},{6,4},{7,5},{8,10},{9,11},{10,... | collective-permute-start | bytes 6152 | tf_op jit(solution)/shard_map/ppermute | solution.py:22
  82.1 1.0 %collective-permute-start.15 = (f32[2,16,512]{2,1,0:T(8,128)S(1)}, f32[2,16,512]{2,1,0:T(8,128)S(1)}, u32[]{:S(2)}, u32[]{:S(2)}) collective-permute-start(f32[2,16,512]{2,1,0:T(8,128)S(1)} %get-tuple-element.25), channel_id=1, source_target_pairs={{0,2},{1,3},{2,0},{3,1},{4,6},{5,7},{6,4},{7,5},{8,10},{9,11},{10,... | collective-permute-start | bytes 196616 | tf_op jit(solution)/shard_map/ppermute | solution.py:22
  83.1 1.4 %collective-permute-start.16 = (f32[2,16,512]{2,1,0:T(8,128)S(1)}, f32[2,16,512]{2,1,0:T(8,128)S(1)}, u32[]{:S(2)}, u32[]{:S(2)}) collective-permute-start(f32[2,16,512]{2,1,0:T(8,128)S(1)} %get-tuple-element.22), channel_id=1, source_target_pairs={{0,3},{1,0},{2,1},{3,2},{4,7},{5,4},{6,5},{7,6},{8,11},{9,8},{10,9... | collective-permute-start | bytes 196616 | tf_op jit(solution)/shard_map/ppermute | solution.py:22
  85.8 1.3 %collective-permute-done.15 = f32[2,16,512]{2,1,0:T(8,128)S(1)} collective-permute-done((f32[2,16,512]{2,1,0:T(8,128)S(1)}, f32[2,16,512]{2,1,0:T(8,128)S(1)}, u32[]{:S(2)}, u32[]{:S(2)}) %collective-permute-start.15) | collective-permute-done | bytes 65568 | tf_op jit(solution)/shard_map/ppermute | solution.py:22
  (81 shorter events, 14.3 us)
Async XLA Ops:
  8.1 17.9 %collective-permute-start.3 = (bf16[64,2048]{1,0:T(8,128)(2,1)S(1)}, bf16[64,2048]{1,0:T(8,128)(2,1)S(1)}, u32[]{:S(2)}, u32[]{:S(2)}) collective-permute-start(bf16[64,2048]{1,0:T(8,128)(2,1)S(1)} %bitcast.47), channel_id=1, source_target_pairs={{4,0},{0,4},{12,8},{8,12},{20,16},{16,20},{28,24},{24,28},{5,1},{1... | collective-permute-start | bytes 786440 | tf_op jit(solution)/shard_map/ppermute | solution.py:75
  9.6 21.5 %collective-permute-start.7 = (bf16[64,2048]{1,0:T(8,128)(2,1)S(1)}, bf16[64,2048]{1,0:T(8,128)(2,1)S(1)}, u32[]{:S(2)}, u32[]{:S(2)}) collective-permute-start(bf16[64,2048]{1,0:T(8,128)(2,1)S(1)} %bitcast.48), channel_id=1, source_target_pairs={{8,4},{4,8},{16,12},{12,16},{24,20},{20,24},{9,5},{5,9},{17,13},{1... | collective-permute-start | bytes 786440 | tf_op jit(solution)/shard_map/ppermute | solution.py:83
  11.3 12.0 %collective-permute-start = (f32[16,512]{1,0:T(8,128)S(1)}, f32[16,512]{1,0:T(8,128)S(1)}, u32[]{:S(2)}, u32[]{:S(2)}) collective-permute-start(f32[16,512]{1,0:T(8,128)S(1)} %get-tuple-element.30), channel_id=1, source_target_pairs={{0,1},{1,2},{2,3},{3,0},{4,5},{5,6},{6,7},{7,4},{8,9},{9,10},{10,1... | collective-permute-start | bytes 98312 | tf_op jit(solution)/shard_map/ppermute | solution.py:22
  11.4 11.9 %collective-permute-start.1 = (f32[16,512]{1,0:T(8,128)S(1)}, f32[16,512]{1,0:T(8,128)S(1)}, u32[]{:S(2)}, u32[]{:S(2)}) collective-permute-start(f32[16,512]{1,0:T(8,128)S(1)} %get-tuple-element.29), channel_id=1, source_target_pairs={{0,2},{1,3},{2,0},{3,1},{4,6},{5,7},{6,4},{7,5},{8,10},{9,11},{10,... | collective-permute-start | bytes 98312 | tf_op jit(solution)/shard_map/ppermute | solution.py:22
  13.0 8.4 %collective-permute-start.4 = (s32[1]{0:T(128)}, s32[1]{0:T(128)}, u32[]{:S(2)}, u32[]{:S(2)}) collective-permute-start(s32[1]{0:T(128)} %param.10), channel_id=1, source_target_pairs={{4,0},{0,4},{12,8},{8,12},{20,16},{16,20},{28,24},{24,28},{5,1},{1... | collective-permute-start | bytes 20 | tf_op jit(solution)/shard_map/ppermute | solution.py:80
  21.3 2.2 %collective-permute-start.2 = (f32[16,512]{1,0:T(8,128)S(1)}, f32[16,512]{1,0:T(8,128)S(1)}, u32[]{:S(2)}, u32[]{:S(2)}) collective-permute-start(f32[16,512]{1,0:T(8,128)S(1)} %get-tuple-element.28), channel_id=1, source_target_pairs={{0,3},{1,0},{2,1},{3,2},{4,7},{5,4},{6,5},{7,6},{8,11},{9,8},{10,9... | collective-permute-start | bytes 98312 | tf_op jit(solution)/shard_map/ppermute | solution.py:22
  23.5 7.4 %collective-permute-start.5 = (f32[16,2048]{1,0:T(8,128)S(1)}, f32[16,2048]{1,0:T(8,128)S(1)}, u32[]{:S(2)}, u32[]{:S(2)}) collective-permute-start(f32[16,2048]{1,0:T(8,128)S(1)} %constant_dynamic-update-slice_fusion.3), channel_id=1, source_target_pairs={{4,0},{0,4},{12,8},{8,12},{20,16},{16,20},{28,24},{24,28},{5,1},{1... | collective-permute-start | bytes 393224 | tf_op jit(solution)/shard_map/ppermute | solution.py:79
  31.2 7.1 %collective-permute-start.6 = (bf16[16,2048]{1,0:T(8,128)(2,1)S(1)}, bf16[16,2048]{1,0:T(8,128)(2,1)S(1)}, u32[]{:S(2)}, u32[]{:S(2)}) collective-permute-start(bf16[16,2048]{1,0:T(8,128)(2,1)S(1)} %get-tuple-element.18), channel_id=1, source_target_pairs={{0,8},{28,20},{1,9},{29,21},{2,10},{30,22},{3,11},{31,23}} | collective-permute-start | bytes 196616 | tf_op jit(solution)/shard_map/ppermute | solution.py:118
  39.6 2.3 %copy-start.3 = (bf16[1,64,2048]{2,1,0:T(8,128)(2,1)S(1)}, bf16[1,64,2048]{2,1,0:T(8,128)(2,1)}, u32[]{:S(2)}) copy-start(bf16[1,64,2048]{2,1,0:T(8,128)(2,1)} %param.7) | copy-start | bytes 786436
  41.0 3.7 %collective-permute-start.8 = (bf16[16,2048]{1,0:T(8,128)(2,1)S(1)}, bf16[16,2048]{1,0:T(8,128)(2,1)S(1)}, u32[]{:S(2)}, u32[]{:S(2)}) collective-permute-start(bf16[16,2048]{1,0:T(8,128)(2,1)S(1)} %get-tuple-element.16), channel_id=1, source_target_pairs={{8,16},{20,12},{9,17},{21,13},{10,18},{22,14},{11,19},{23,15}} | collective-permute-start | bytes 196616 | tf_op jit(solution)/shard_map/ppermute | solution.py:118
  47.6 6.2 %collective-permute-start.9 = (bf16[16,2048]{1,0:T(8,128)(2,1)S(1)}, bf16[16,2048]{1,0:T(8,128)(2,1)S(1)}, u32[]{:S(2)}, u32[]{:S(2)}) collective-permute-start(bf16[16,2048]{1,0:T(8,128)(2,1)S(1)} %get-tuple-element.14), channel_id=1, source_target_pairs={{16,24},{12,4},{17,25},{13,5},{18,26},{14,6},{19,27},{15,7}} | collective-permute-start | bytes 196616 | tf_op jit(solution)/shard_map/ppermute | solution.py:118
  51.1 10.4 %collective-permute-start.13 = (f32[16,2048]{1,0:T(8,128)S(1)}, f32[16,2048]{1,0:T(8,128)S(1)}, u32[]{:S(2)}, u32[]{:S(2)}) collective-permute-start(f32[16,2048]{1,0:T(8,128)S(1)} %get-tuple-element.19), channel_id=1, source_target_pairs={{0,4},{28,24},{1,5},{29,25},{2,6},{30,26},{3,7},{31,27}} | collective-permute-start | bytes 393224 | tf_op jit(solution)/shard_map/ppermute | solution.py:121
  52.4 9.1 %collective-permute-start.12 = (f32[16,2048]{1,0:T(8,128)S(1)}, f32[16,2048]{1,0:T(8,128)S(1)}, u32[]{:S(2)}, u32[]{:S(2)}) collective-permute-start(f32[16,2048]{1,0:T(8,128)S(1)} %get-tuple-element.17), channel_id=1, source_target_pairs={{8,12},{20,16},{9,13},{21,17},{10,14},{22,18},{11,15},{23,19}} | collective-permute-start | bytes 393224 | tf_op jit(solution)/shard_map/ppermute | solution.py:121
  53.1 8.4 %collective-permute-start.11 = (f32[16,2048]{1,0:T(8,128)S(1)}, f32[16,2048]{1,0:T(8,128)S(1)}, u32[]{:S(2)}, u32[]{:S(2)}) collective-permute-start(f32[16,2048]{1,0:T(8,128)S(1)} %get-tuple-element.15), channel_id=1, source_target_pairs={{16,20},{12,8},{17,21},{13,9},{18,22},{14,10},{19,23},{15,11}} | collective-permute-start | bytes 393224 | tf_op jit(solution)/shard_map/ppermute | solution.py:121
  56.6 7.8 %collective-permute-start.10 = (f32[16,2048]{1,0:T(8,128)S(1)}, f32[16,2048]{1,0:T(8,128)S(1)}, u32[]{:S(2)}, u32[]{:S(2)}) collective-permute-start(f32[16,2048]{1,0:T(8,128)S(1)} %multiply_divide_fusion), channel_id=1, source_target_pairs={{24,28},{4,0},{25,29},{5,1},{26,30},{6,2},{27,31},{7,3}} | collective-permute-start | bytes 393224 | tf_op jit(solution)/shard_map/ppermute | solution.py:121
  64.5 3.1 %collective-permute-start.17 = (f32[1,2048]{1,0:T(1,128)S(1)}, f32[1,2048]{1,0:T(1,128)S(1)}, u32[]{:S(2)}, u32[]{:S(2)}) collective-permute-start(f32[1,2048]{1,0:T(1,128)S(1)} %bitcast.53), channel_id=1, source_target_pairs={{0,1},{1,2},{2,3},{3,0},{4,5},{5,6},{6,7},{7,4},{8,9},{9,10},{10,1... | collective-permute-start | bytes 24584 | tf_op jit(solution)/shard_map/ppermute | solution.py:22
  64.6 3.7 %collective-permute-start.18 = (f32[1,2048]{1,0:T(1,128)S(1)}, f32[1,2048]{1,0:T(1,128)S(1)}, u32[]{:S(2)}, u32[]{:S(2)}) collective-permute-start(f32[1,2048]{1,0:T(1,128)S(1)} %bitcast.54), channel_id=1, source_target_pairs={{0,2},{1,3},{2,0},{3,1},{4,6},{5,7},{6,4},{7,5},{8,10},{9,11},{10,... | collective-permute-start | bytes 24584 | tf_op jit(solution)/shard_map/ppermute | solution.py:22
  65.7 2.8 %collective-permute-start.19 = (f32[1,2048]{1,0:T(1,128)S(1)}, f32[1,2048]{1,0:T(1,128)S(1)}, u32[]{:S(2)}, u32[]{:S(2)}) collective-permute-start(f32[1,2048]{1,0:T(1,128)S(1)} %bitcast.55), channel_id=1, source_target_pairs={{0,3},{1,0},{2,1},{3,2},{4,7},{5,4},{6,5},{7,6},{8,11},{9,8},{10,9... | collective-permute-start | bytes 24584 | tf_op jit(solution)/shard_map/ppermute | solution.py:22
  69.2 6.8 %copy-start = (f32[2048,512]{1,0:T(8,128)S(1)}, f32[2048,512]{1,0:T(8,128)}, u32[]{:S(2)}) copy-start(f32[2048,512]{1,0:T(8,128)} %negate_exponential_fusion) | copy-start | bytes 12582916
  69.2 7.1 %copy-start.1 = (f32[2048,512]{1,0:T(8,128)S(1)}, f32[2048,512]{1,0:T(8,128)}, u32[]{:S(2)}) copy-start(f32[2048,512]{1,0:T(8,128)} %negate_exponential_fusion.1) | copy-start | bytes 12582916
  76.3 2.2 %copy-start.2 = (f32[2048,512]{1,0:T(8,128)S(1)}, f32[2048,512]{1,0:T(8,128)}, u32[]{:S(2)}) copy-start(f32[2048,512]{1,0:T(8,128)} %negate_exponential_fusion.3) | copy-start | bytes 12582916
  79.4 3.7 %collective-permute-start.20 = (f32[512]{0:T(512)S(1)}, f32[512]{0:T(512)S(1)}, u32[]{:S(2)}, u32[]{:S(2)}) collective-permute-start(f32[512]{0:T(512)S(1)} %get-tuple-element.34), channel_id=1, source_target_pairs={{0,1},{1,2},{2,3},{3,0},{4,5},{5,6},{6,7},{7,4},{8,9},{9,10},{10,1... | collective-permute-start | bytes 6152 | tf_op jit(solution)/shard_map/ppermute | solution.py:22
  80.4 4.3 %collective-permute-start.21 = (f32[512]{0:T(512)S(1)}, f32[512]{0:T(512)S(1)}, u32[]{:S(2)}, u32[]{:S(2)}) collective-permute-start(f32[512]{0:T(512)S(1)} %get-tuple-element.33), channel_id=1, source_target_pairs={{0,2},{1,3},{2,0},{3,1},{4,6},{5,7},{6,4},{7,5},{8,10},{9,11},{10,... | collective-permute-start | bytes 6152 | tf_op jit(solution)/shard_map/ppermute | solution.py:22
  81.5 3.4 %collective-permute-start.22 = (f32[512]{0:T(512)S(1)}, f32[512]{0:T(512)S(1)}, u32[]{:S(2)}, u32[]{:S(2)}) collective-permute-start(f32[512]{0:T(512)S(1)} %get-tuple-element.32), channel_id=1, source_target_pairs={{0,3},{1,0},{2,1},{3,2},{4,7},{5,4},{6,5},{7,6},{8,11},{9,8},{10,9... | collective-permute-start | bytes 6152 | tf_op jit(solution)/shard_map/ppermute | solution.py:22
  82.0 3.8 %collective-permute-start.14 = (f32[2,16,512]{2,1,0:T(8,128)S(1)}, f32[2,16,512]{2,1,0:T(8,128)S(1)}, u32[]{:S(2)}, u32[]{:S(2)}) collective-permute-start(f32[2,16,512]{2,1,0:T(8,128)S(1)} %get-tuple-element.24), channel_id=1, source_target_pairs={{0,1},{1,2},{2,3},{3,0},{4,5},{5,6},{6,7},{7,4},{8,9},{9,10},{10,1... | collective-permute-start | bytes 196616 | tf_op jit(solution)/shard_map/ppermute | solution.py:22
  82.1 5.0 %collective-permute-start.15 = (f32[2,16,512]{2,1,0:T(8,128)S(1)}, f32[2,16,512]{2,1,0:T(8,128)S(1)}, u32[]{:S(2)}, u32[]{:S(2)}) collective-permute-start(f32[2,16,512]{2,1,0:T(8,128)S(1)} %get-tuple-element.25), channel_id=1, source_target_pairs={{0,2},{1,3},{2,0},{3,1},{4,6},{5,7},{6,4},{7,5},{8,10},{9,11},{10,... | collective-permute-start | bytes 196616 | tf_op jit(solution)/shard_map/ppermute | solution.py:22
  83.1 4.0 %collective-permute-start.16 = (f32[2,16,512]{2,1,0:T(8,128)S(1)}, f32[2,16,512]{2,1,0:T(8,128)S(1)}, u32[]{:S(2)}, u32[]{:S(2)}) collective-permute-start(f32[2,16,512]{2,1,0:T(8,128)S(1)} %get-tuple-element.22), channel_id=1, source_target_pairs={{0,3},{1,0},{2,1},{3,2},{4,7},{5,4},{6,5},{7,6},{8,11},{9,8},{10,9... | collective-permute-start | bytes 196616 | tf_op jit(solution)/shard_map/ppermute | solution.py:22

commit v19 on v18

--- a/solution.py
+++ b/solution.py
@@ -146,7 +146,7 @@
     cell_live = (pt_rank * own_slots + jnp.arange(own_slots, dtype=jnp.int32) < cell_total).astype(
         jnp.float32
     )
-    cell_parts = 4
+    cell_parts = 8
     cell_span = own_slots // cell_parts
     ratio_rows = 0.0
     for part in range(cell_parts):

time: 88.6 us -> 98.6 us (1.11)
  the two profiles are of different devices: /device:TPU:0 before, /device:TPU:11 now
where the time goes in v19:
time: 98.6 us; the launch traced here: 98.1 us
  matrix products  35.3 us (36%)
  starting transfers between devices  27.4 us (28%)
  other arithmetic  10.7 us (11%)
  waiting for transfers between devices  8.77 us (9%)
  blocking collectives  6.5 us (7%)
  local copies, waits for them, and re-layouts  6.29 us (6%)
  between operations  3.2 us (3%)
    dot_general x10, matrix products, squared_dist(): lax.dot_general(left_pts, right_pts, (((0,), (0,)), ((), ())), preferred_...  26 us
    ppermute x12, starting transfers between devices, swap_blocks(): lax.ppermute(piece, 'pt', [(i, (i + shift) % count) for i in range(count)])  9.65 us
    ppermute x4, starting transfers between devices, shards(): lax.ppermute(following, 'day', [(forward_day, forward_day + 1), (backward...  8.52 us
    ppermute x12, waiting for transfers between devices, swap_blocks(): lax.ppermute(piece, 'pt', [(i, (i + shift) % count) for i in range(count)])  6.83 us
    all_gather x1, blocking collectives, shards(): day_pts = lax.all_gather(own_pts, 'pt', axis=1, tiled=True)  6.5 us
    dot_general x4, matrix products, shards(): jnp.dot(sent, other_kernel, preferred_element_type=jnp.float32)  5.37 us
    ppermute x1, starting transfers between devices, shards(): link_pts = lax.ppermute(day_pts, 'day', link_route)  4.12 us
    dot_general x3, matrix products, shards(): jnp.dot(incoming, link_kernel, preferred_element_type=jnp.float32)  3.92 us
  transfers between devices with their start and end apart: 23, of which 6 were waited for; matrix products, arithmetic and copies ran while one was open for 31% of the time, Pallas kernels for 0%

profile of v19, /device:TPU:11, one launch (start us, length us, event | category | flops | bytes accessed | tf_op | source)
XLA Modules:
  0.0 98.1 jit_solution(14672451141517571371)
XLA Ops:
  0.6 6.5 %all-gather = bf16[1,64,2048]{2,1,0:T(8,128)(2,1)S(1)} all-gather(bf16[1,64,512]{2,1,0:T(8,128)(2,1)} %param.6), channel_id=2, replica_groups=mesh['day'=8,'pt'=4] {'pt'}, dimensions={2}, use_global_device_ids=true | all-gather | bytes 327680 | tf_op jit(solution)/shard_map/all_gather | solution.py:57
  7.4 4.1 %collective-permute-start.7 = (bf16[64,2048]{1,0:T(8,128)(2,1)S(1)}, bf16[64,2048]{1,0:T(8,128)(2,1)S(1)}, u32[]{:S(2)}, u32[]{:S(2)}) collective-permute-start(bf16[64,2048]{1,0:T(8,128)(2,1)S(1)} %bitcast.56), channel_id=1, source_target_pairs={{8,4},{4,8},{16,12},{12,16},{24,20},{20,24},{9,5},{5,9},{17,13},{1... | collective-permute-start | bytes 786440 | tf_op jit(solution)/shard_map/ppermute | solution.py:83
  12.6 1.9 %collective-permute-start = (f32[16,512]{1,0:T(8,128)S(1)}, f32[16,512]{1,0:T(8,128)S(1)}, u32[]{:S(2)}, u32[]{:S(2)}) collective-permute-start(f32[16,512]{1,0:T(8,128)S(1)} %get-tuple-element.34), channel_id=1, source_target_pairs={{0,1},{1,2},{2,3},{3,0},{4,5},{5,6},{6,7},{7,4},{8,9},{9,10},{10,1... | collective-permute-start | bytes 98312 | tf_op jit(solution)/shard_map/ppermute | solution.py:22
  17.1 2.7 %fusion.11 = f32[2048,256]{1,0:T(8,128)} fusion(f32[256]{0:T(256)S(1)} %get-tuple-element.52, f32[2048]{0:T(1024)S(1)} %multiply_reduce_fusion.19, bf16[64,2048]{1,0:T(8,128)(2,1)} %bitcast.57, bf16[1,64,2048]{2,1,0:T(8,128)(2,1)S(1)} %all-gather), kind=kOutput, calls=%fused_computation.17 | convolution fusion | flops 69206016 | bytes 2401280 | tf_op jit(solution)/shard_map/dot_general | solution.py:45
  19.8 2.0 %fusion.14 = f32[2048,256]{1,0:T(8,128)} fusion(f32[256]{0:T(256)S(1)} %get-tuple-element.53, f32[2048]{0:T(1024)S(1)} %multiply_reduce_fusion.19, bf16[64,2048]{1,0:T(8,128)(2,1)S(1)} %bitcast.58, bf16[1,64,2048]{2,1,0:T(8,128)(2,1)S(1)} %all-gather), kind=kOutput, calls=%fused_computation.21 | convolution fusion | flops 69206016 | bytes 2401280 | tf_op jit(solution)/shard_map/dot_general | solution.py:45
  21.8 2.0 %fusion.17 = f32[2048,256]{1,0:T(8,128)} fusion(f32[256]{0:T(256)S(1)} %get-tuple-element.54, f32[2048]{0:T(1024)S(1)} %multiply_reduce_fusion.19, bf16[64,2048]{1,0:T(8,128)(2,1)S(1)} %bitcast.59, bf16[1,64,2048]{2,1,0:T(8,128)(2,1)S(1)} %all-gather), kind=kOutput, calls=%fused_computation.25 | convolution fusion | flops 69206016 | bytes 2401280 | tf_op jit(solution)/shard_map/dot_general | solution.py:45
  26.0 1.8 %collective-permute-done.2 = f32[16,512]{1,0:T(8,128)S(1)} collective-permute-done((f32[16,512]{1,0:T(8,128)S(1)}, f32[16,512]{1,0:T(8,128)S(1)}, u32[]{:S(2)}, u32[]{:S(2)}) %collective-permute-start.2) | collective-permute-done | bytes 32800 | tf_op jit(solution)/shard_map/ppermute | solution.py:22
  27.8 1.5 %collective-permute-start.5 = (f32[16,2048]{1,0:T(8,128)S(1)}, f32[16,2048]{1,0:T(8,128)S(1)}, u32[]{:S(2)}, u32[]{:S(2)}) collective-permute-start(f32[16,2048]{1,0:T(8,128)S(1)} %constant_dynamic-update-slice_fusion.3), channel_id=1, source_target_pairs={{4,0},{0,4},{12,8},{8,12},{20,16},{16,20},{28,24},{24,28},{5,1},{1... | collective-permute-start | bytes 393224 | tf_op jit(solution)/shard_map/ppermute | solution.py:79
  29.3 3.6 %exponential_convert_fusion.1 = bf16[2048,2048]{1,0:T(8,128)(2,1)S(1)} fusion(bf16[64,2048]{1,0:T(8,128)(2,1)S(1)} %collective-permute-done.3, f32[2048]{0:T(1024)S(1)} %multiply_reduce_fusion.18, f32[2048]{0:T(1024)S(1)} %multiply_reduce_fusion.19, bf16[1,64,2048]{2,1,0:T(8,128)(2,1)S(1)} %all-gather), kind=kOutput, calls=%fused_computation.1 | convolution fusion | flops 557842432 | bytes 8929280 | tf_op jit(solution)/shard_map/dot_general | solution.py:45
  32.9 1.3 %fusion.67 = (f32[16]{0:T(128)S(1)}, f32[16,2048]{1,0:T(8,128)S(1)}) fusion(f32[2048]{0:T(1024)S(1)} %fusion.42, bf16[2048,2048]{1,0:T(8,128)(2,1)S(1)} %exponential_convert_fusion.1, f32[16,2048]{1,0:T(8,128)S(1)} %constant_dynamic-update-slice_fusion.3, f32[2048]{0:T(1024)S(1)} %fusion.41), kind=kOutput, calls=%fused_computation.155 | convolution fusion | flops 134348784 | bytes 8667200 | tf_op jit(solution)/shard_map/dot_general | solution.py:109
  35.1 3.6 %exponential_convert_fusion = bf16[2048,2048]{1,0:T(8,128)(2,1)S(1)} fusion(bf16[64,2048]{1,0:T(8,128)(2,1)S(1)} %collective-permute-done.7, f32[2048]{0:T(1024)S(1)} %multiply_reduce_fusion.19, f32[2048]{0:T(1024)S(1)} %multiply_reduce_fusion.17, bf16[1,64,2048]{2,1,0:T(8,128)(2,1)S(1)} %all-gather), kind=kOutput, calls=%fused_computation | convolution fusion | flops 557842432 | bytes 8929280 | tf_op jit(solution)/shard_map/dot_general | solution.py:45
  38.7 1.3 %fusion.68 = (f32[16]{0:T(128)S(1)}, f32[16,2048]{1,0:T(8,128)S(1)}) fusion(f32[2048]{0:T(1024)S(1)} %fusion.41, bf16[16,2048]{1,0:T(8,128)(2,1)S(1)} %collective-permute-done.6, bf16[2048,2048]{1,0:T(8,128)(2,1)S(1)} %exponential_convert_fusion), kind=kOutput, calls=%fused_computation.156 | convolution fusion | flops 134283248 | bytes 8593472 | tf_op jit(solution)/shard_map/dot_general | solution.py:101
  40.0 1.4 %fusion.69 = (f32[16]{0:T(128)S(1)}, f32[16,2048]{1,0:T(8,128)S(1)}) fusion(f32[2048]{0:T(1024)S(1)} %fusion.42, bf16[2048,2048]{1,0:T(8,128)(2,1)S(1)} %exponential_convert_fusion.1, f32[16,2048]{1,0:T(8,128)S(1)} %constant_dynamic-update-slice_fusion.3, f32[16]{0:T(128)S(1)} %get-tuple-element.58, f32[16,2048]{1,0:T(8,128)S(1)} %get-tuple-element.59, ...), kind=kOutput, calls=%fused_computation.157 | convolution fusion | flops 134414320 | bytes 8790148 | tf_op jit(solution)/shard_map/dot_general | solution.py:109
  41.5 1.5 %collective-permute-start.8 = (bf16[16,2048]{1,0:T(8,128)(2,1)S(1)}, bf16[16,2048]{1,0:T(8,128)(2,1)S(1)}, u32[]{:S(2)}, u32[]{:S(2)}) collective-permute-start(bf16[16,2048]{1,0:T(8,128)(2,1)S(1)} %get-tuple-element.20), channel_id=1, source_target_pairs={{8,16},{20,12},{9,17},{21,13},{10,18},{22,14},{11,19},{23,15}} | collective-permute-start | bytes 196616 | tf_op jit(solution)/shard_map/ppermute | solution.py:118
  43.0 1.9 %fusion.23 = f32[2048,256]{1,0:T(8,128)} fusion(f32[256]{0:T(256)S(1)} %get-tuple-element.48, f32[2048]{0:T(1024)S(1)} %multiply_reduce_fusion.19, bf16[64,2048]{1,0:T(8,128)(2,1)S(1)} %bitcast.61, bf16[1,64,2048]{2,1,0:T(8,128)(2,1)S(1)} %all-gather), kind=kOutput, calls=%fused_computation.33 | convolution fusion | flops 69206016 | bytes 2401280 | tf_op jit(solution)/shard_map/dot_general | solution.py:45
  44.9 1.9 %collective-permute-done.8 = bf16[16,2048]{1,0:T(8,128)(2,1)S(1)} collective-permute-done((bf16[16,2048]{1,0:T(8,128)(2,1)S(1)}, bf16[16,2048]{1,0:T(8,128)(2,1)S(1)}, u32[]{:S(2)}, u32[]{:S(2)}) %collective-permute-start.8) | collective-permute-done | bytes 65568 | tf_op jit(solution)/shard_map/ppermute | solution.py:118
  46.8 1.3 %fusion.70 = (f32[16]{0:T(128)S(1)}, f32[16,2048]{1,0:T(8,128)S(1)}) fusion(f32[2048]{0:T(1024)S(1)} %fusion.41, bf16[16,2048]{1,0:T(8,128)(2,1)S(1)} %collective-permute-done.8, bf16[2048,2048]{1,0:T(8,128)(2,1)S(1)} %exponential_convert_fusion), kind=kOutput, calls=%fused_computation.158 | convolution fusion | flops 134283248 | bytes 8593472 | tf_op jit(solution)/shard_map/dot_general | solution.py:101
  48.1 1.4 %fusion.71 = (f32[16]{0:T(128)S(1)}, f32[16,2048]{1,0:T(8,128)S(1)}) fusion(f32[2048]{0:T(1024)S(1)} %fusion.42, bf16[2048,2048]{1,0:T(8,128)(2,1)S(1)} %exponential_convert_fusion.1, f32[16,2048]{1,0:T(8,128)S(1)} %constant_dynamic-update-slice_fusion.3, f32[16]{0:T(128)S(1)} %get-tuple-element.62, f32[16,2048]{1,0:T(8,128)S(1)} %get-tuple-element.63, ...), kind=kOutput, calls=%fused_computation.159 | convolution fusion | flops 134414320 | bytes 8790148 | tf_op jit(solution)/shard_map/dot_general | solution.py:109
  50.2 1.3 %collective-permute-start.9 = (bf16[16,2048]{1,0:T(8,128)(2,1)S(1)}, bf16[16,2048]{1,0:T(8,128)(2,1)S(1)}, u32[]{:S(2)}, u32[]{:S(2)}) collective-permute-start(bf16[16,2048]{1,0:T(8,128)(2,1)S(1)} %get-tuple-element.18), channel_id=1, source_target_pairs={{16,24},{12,4},{17,25},{13,5},{18,26},{14,6},{19,27},{15,7}} | collective-permute-start | bytes 196616 | tf_op jit(solution)/shard_map/ppermute | solution.py:118
  51.5 2.0 %fusion.5 = f32[2048,256]{1,0:T(8,128)} fusion(f32[256]{0:T(256)S(1)} %get-tuple-element.50, f32[2048]{0:T(1024)S(1)} %multiply_reduce_fusion.19, bf16[64,2048]{1,0:T(8,128)(2,1)S(1)} %bitcast.62, bf16[1,64,2048]{2,1,0:T(8,128)(2,1)S(1)} %all-gather), kind=kOutput, calls=%fused_computation.9 | convolution fusion | flops 69206016 | bytes 2401280 | tf_op jit(solution)/shard_map/dot_general | solution.py:45
  54.2 1.3 %collective-permute-start.12 = (f32[16,2048]{1,0:T(8,128)S(1)}, f32[16,2048]{1,0:T(8,128)}, u32[]{:S(2)}, u32[]{:S(2)}) collective-permute-start(f32[16,2048]{1,0:T(8,128)S(1)} %get-tuple-element.21), channel_id=1, source_target_pairs={{8,12},{20,16},{9,13},{21,17},{10,14},{22,18},{11,15},{23,19}} | collective-permute-start | bytes 393224 | tf_op jit(solution)/shard_map/ppermute | solution.py:121
  55.5 5.3 %collective-permute-start.11 = (f32[16,2048]{1,0:T(8,128)}, f32[16,2048]{1,0:T(8,128)}, u32[]{:S(2)}, u32[]{:S(2)}) collective-permute-start(f32[16,2048]{1,0:T(8,128)} %get-tuple-element.19), channel_id=1, source_target_pairs={{16,20},{12,8},{17,21},{13,9},{18,22},{14,10},{19,23},{15,11}} | collective-permute-start | bytes 393224 | tf_op jit(solution)/shard_map/ppermute | solution.py:121
  60.8 1.3 %fusion.72 = (f32[16]{0:T(128)S(1)}, f32[16,2048]{1,0:T(8,128)S(1)}) fusion(f32[2048]{0:T(1024)S(1)} %fusion.41, bf16[16,2048]{1,0:T(8,128)(2,1)S(1)} %collective-permute-done.9, bf16[2048,2048]{1,0:T(8,128)(2,1)S(1)} %exponential_convert_fusion), kind=kOutput, calls=%fused_computation.160 | convolution fusion | flops 134283248 | bytes 8593472 | tf_op jit(solution)/shard_map/dot_general | solution.py:101
  62.1 1.4 %fusion.73 = (f32[16]{0:T(128)S(1)}, f32[16,2048]{1,0:T(8,128)S(1)}) fusion(f32[2048]{0:T(1024)S(1)} %fusion.42, bf16[2048,2048]{1,0:T(8,128)(2,1)S(1)} %exponential_convert_fusion.1, f32[16,2048]{1,0:T(8,128)S(1)} %constant_dynamic-update-slice_fusion.3, f32[16]{0:T(128)S(1)} %get-tuple-element.66, f32[16,2048]{1,0:T(8,128)S(1)} %get-tuple-element.67, ...), kind=kOutput, calls=%fused_computation.161 | convolution fusion | flops 134414320 | bytes 8790148 | tf_op jit(solution)/shard_map/dot_general | solution.py:109
  64.2 1.3 %collective-permute-start.10 = (f32[16,2048]{1,0:T(8,128)}, f32[16,2048]{1,0:T(8,128)}, u32[]{:S(2)}, u32[]{:S(2)}) collective-permute-start(f32[16,2048]{1,0:T(8,128)} %multiply_divide_fusion), channel_id=1, source_target_pairs={{24,28},{4,0},{25,29},{5,1},{26,30},{6,2},{27,31},{7,3}} | collective-permute-start | bytes 393224 | tf_op jit(solution)/shard_map/ppermute | solution.py:121
  65.5 1.9 %fusion.8 = f32[2048,256]{1,0:T(8,128)} fusion(f32[256]{0:T(256)S(1)} %copy-done.14, f32[2048]{0:T(1024)S(1)} %copy-done.8, bf16[64,2048]{1,0:T(8,128)(2,1)S(1)} %bitcast.63, bf16[1,64,2048]{2,1,0:T(8,128)(2,1)S(1)} %all-gather), kind=kOutput, calls=%fused_computation.13 | convolution fusion | flops 69206016 | bytes 2401280 | tf_op jit(solution)/shard_map/dot_general | solution.py:45
  68.8 1.1 %multiply_reduce_fusion.20 = (f32[2048]{0:T(1024)S(1)}, f32[16,2048]{1,0:T(8,128)S(1)}, f32[16,2048]{1,0:T(8,128)S(1)}) fusion(f32[16,2048]{1,0:T(8,128)S(1)} %constant_dynamic-update-slice_fusion.3, pred[]{:T(512)S(6)} %eq.67, f32[16,2048]{1,0:T(8,128)} %collective-permute-done.10, f32[16,2048]{1,0:T(8,128)} %collective-permute-done.11, ...), kind=kLoop, calls=%fused_computation.70 | loop fusion | flops 587776 | bytes 1327305 | tf_op jit(solution)/shard_map/reduce_sum | solution.py:137
  69.8 3.1 %collective-permute-start.17 = (f32[1,2048]{1,0:T(1,128)S(1)}, f32[1,2048]{1,0:T(1,128)S(1)}, u32[]{:S(2)}, u32[]{:S(2)}) collective-permute-start(f32[1,2048]{1,0:T(1,128)S(1)} %bitcast.65), channel_id=1, source_target_pairs={{0,1},{1,2},{2,3},{3,0},{4,5},{5,6},{6,7},{7,4},{8,9},{9,10},{10,1... | collective-permute-start | bytes 24584 | tf_op jit(solution)/shard_map/ppermute | solution.py:22
  74.0 1.7 %collective-permute-done.18 = f32[1,2048]{1,0:T(1,128)S(1)} collective-permute-done((f32[1,2048]{1,0:T(1,128)S(1)}, f32[1,2048]{1,0:T(1,128)S(1)}, u32[]{:S(2)}, u32[]{:S(2)}) %collective-permute-start.18) | collective-permute-done | bytes 8224 | tf_op jit(solution)/shard_map/ppermute | solution.py:22
  77.5 5.7 %multiply_reduce_fusion.13 = (f32[256]{0:T(256)S(1)}, f32[256]{0:T(256)S(1)}, f32[256]{0:T(256)S(1)}, f32[256]{0:T(256)S(1)}, f32[256]{0:T(256)S(1)}, /*index=5*...) fusion(f32[2048]{0:T(1024)S(1)} %get-tuple-element.14, f32[2048,256]{1,0:T(8,128)} %fusion.17, ...), kind=kOutput, calls=%fused_computation.54 | convolution fusion | flops 77592576 | bytes 17097728 | tf_op jit(solution)/shard_map/dot_general | solution.py:45
  91.8 1.1 %collective-permute-start.14 = (f32[2,16,512]{2,1,0:T(8,128)S(1)}, f32[2,16,512]{2,1,0:T(8,128)S(1)}, u32[]{:S(2)}, u32[]{:S(2)}) collective-permute-start(f32[2,16,512]{2,1,0:T(8,128)S(1)} %get-tuple-element.28), channel_id=1, source_target_pairs={{0,1},{1,2},{2,3},{3,0},{4,5},{5,6},{6,7},{7,4},{8,9},{9,10},{10,1... | collective-permute-start | bytes 196616 | tf_op jit(solution)/shard_map/ppermute | solution.py:22
  95.0 1.9 %collective-permute-done.15 = f32[2,16,512]{2,1,0:T(8,128)S(1)} collective-permute-done((f32[2,16,512]{2,1,0:T(8,128)S(1)}, f32[2,16,512]{2,1,0:T(8,128)S(1)}, u32[]{:S(2)}, u32[]{:S(2)}) %collective-permute-start.15) | collective-permute-done | bytes 65568 | tf_op jit(solution)/shard_map/ppermute | solution.py:22
  (109 shorter events, 23.0 us)
Async XLA Ops:
  7.1 22.1 %collective-permute-start.3 = (bf16[64,2048]{1,0:T(8,128)(2,1)S(1)}, bf16[64,2048]{1,0:T(8,128)(2,1)S(1)}, u32[]{:S(2)}, u32[]{:S(2)}) collective-permute-start(bf16[64,2048]{1,0:T(8,128)(2,1)S(1)} %bitcast.55), channel_id=1, source_target_pairs={{4,0},{0,4},{12,8},{8,12},{20,16},{16,20},{28,24},{24,28},{5,1},{1... | collective-permute-start | bytes 786440 | tf_op jit(solution)/shard_map/ppermute | solution.py:75
  7.4 26.9 %collective-permute-start.7 = (bf16[64,2048]{1,0:T(8,128)(2,1)S(1)}, bf16[64,2048]{1,0:T(8,128)(2,1)S(1)}, u32[]{:S(2)}, u32[]{:S(2)}) collective-permute-start(bf16[64,2048]{1,0:T(8,128)(2,1)S(1)} %bitcast.56), channel_id=1, source_target_pairs={{8,4},{4,8},{16,12},{12,16},{24,20},{20,24},{9,5},{5,9},{17,13},{1... | collective-permute-start | bytes 786440 | tf_op jit(solution)/shard_map/ppermute | solution.py:83
  11.6 8.2 %copy-start.6 = (bf16[1,64,2048]{2,1,0:T(8,128)(2,1)S(1)}, bf16[1,64,2048]{2,1,0:T(8,128)(2,1)}, u32[]{:S(2)}) copy-start(bf16[1,64,2048]{2,1,0:T(8,128)(2,1)} %param.7) | copy-start | bytes 786436
  12.6 13.3 %collective-permute-start = (f32[16,512]{1,0:T(8,128)S(1)}, f32[16,512]{1,0:T(8,128)S(1)}, u32[]{:S(2)}, u32[]{:S(2)}) collective-permute-start(f32[16,512]{1,0:T(8,128)S(1)} %get-tuple-element.34), channel_id=1, source_target_pairs={{0,1},{1,2},{2,3},{3,0},{4,5},{5,6},{6,7},{7,4},{8,9},{9,10},{10,1... | collective-permute-start | bytes 98312 | tf_op jit(solution)/shard_map/ppermute | solution.py:22
  14.5 11.4 %collective-permute-start.1 = (f32[16,512]{1,0:T(8,128)S(1)}, f32[16,512]{1,0:T(8,128)S(1)}, u32[]{:S(2)}, u32[]{:S(2)}) collective-permute-start(f32[16,512]{1,0:T(8,128)S(1)} %get-tuple-element.33), channel_id=1, source_target_pairs={{0,2},{1,3},{2,0},{3,1},{4,6},{5,7},{6,4},{7,5},{8,10},{9,11},{10,... | collective-permute-start | bytes 98312 | tf_op jit(solution)/shard_map/ppermute | solution.py:22
  14.7 9.6 %collective-permute-start.4 = (s32[1]{0:T(128)}, s32[1]{0:T(128)}, u32[]{:S(2)}, u32[]{:S(2)}) collective-permute-start(s32[1]{0:T(128)} %param.10), channel_id=1, source_target_pairs={{4,0},{0,4},{12,8},{8,12},{20,16},{16,20},{28,24},{24,28},{5,1},{1... | collective-permute-start | bytes 20 | tf_op jit(solution)/shard_map/ppermute | solution.py:80
  14.8 36.7 %copy-start.7 = (f32[2048]{0:T(1024)}, f32[2048]{0:T(1024)S(1)}, u32[]{:S(2)}) copy-start(f32[2048]{0:T(1024)S(1)} %multiply_reduce_fusion.19) | copy-start | bytes 24580
  24.4 3.4 %collective-permute-start.2 = (f32[16,512]{1,0:T(8,128)S(1)}, f32[16,512]{1,0:T(8,128)S(1)}, u32[]{:S(2)}, u32[]{:S(2)}) collective-permute-start(f32[16,512]{1,0:T(8,128)S(1)} %get-tuple-element.32), channel_id=1, source_target_pairs={{0,3},{1,0},{2,1},{3,2},{4,7},{5,4},{6,5},{7,6},{8,11},{9,8},{10,9... | collective-permute-start | bytes 98312 | tf_op jit(solution)/shard_map/ppermute | solution.py:22
  27.8 6.4 %collective-permute-start.5 = (f32[16,2048]{1,0:T(8,128)S(1)}, f32[16,2048]{1,0:T(8,128)S(1)}, u32[]{:S(2)}, u32[]{:S(2)}) collective-permute-start(f32[16,2048]{1,0:T(8,128)S(1)} %constant_dynamic-update-slice_fusion.3), channel_id=1, source_target_pairs={{4,0},{0,4},{12,8},{8,12},{20,16},{16,20},{28,24},{24,28},{5,1},{1... | collective-permute-start | bytes 393224 | tf_op jit(solution)/shard_map/ppermute | solution.py:79
  34.4 4.3 %collective-permute-start.6 = (bf16[16,2048]{1,0:T(8,128)(2,1)S(1)}, bf16[16,2048]{1,0:T(8,128)(2,1)S(1)}, u32[]{:S(2)}, u32[]{:S(2)}) collective-permute-start(bf16[16,2048]{1,0:T(8,128)(2,1)S(1)} %get-tuple-element.22), channel_id=1, source_target_pairs={{0,8},{28,20},{1,9},{29,21},{2,10},{30,22},{3,11},{31,23}} | collective-permute-start | bytes 196616 | tf_op jit(solution)/shard_map/ppermute | solution.py:118
  41.5 5.3 %collective-permute-start.8 = (bf16[16,2048]{1,0:T(8,128)(2,1)S(1)}, bf16[16,2048]{1,0:T(8,128)(2,1)S(1)}, u32[]{:S(2)}, u32[]{:S(2)}) collective-permute-start(bf16[16,2048]{1,0:T(8,128)(2,1)S(1)} %get-tuple-element.20), channel_id=1, source_target_pairs={{8,16},{20,12},{9,17},{21,13},{10,18},{22,14},{11,19},{23,15}} | collective-permute-start | bytes 196616 | tf_op jit(solution)/shard_map/ppermute | solution.py:118
  50.2 10.5 %collective-permute-start.9 = (bf16[16,2048]{1,0:T(8,128)(2,1)S(1)}, bf16[16,2048]{1,0:T(8,128)(2,1)S(1)}, u32[]{:S(2)}, u32[]{:S(2)}) collective-permute-start(bf16[16,2048]{1,0:T(8,128)(2,1)S(1)} %get-tuple-element.18), channel_id=1, source_target_pairs={{16,24},{12,4},{17,25},{13,5},{18,26},{14,6},{19,27},{15,7}} | collective-permute-start | bytes 196616 | tf_op jit(solution)/shard_map/ppermute | solution.py:118
  53.5 15.2 %collective-permute-start.13 = (f32[16,2048]{1,0:T(8,128)S(1)}, f32[16,2048]{1,0:T(8,128)S(1)}, u32[]{:S(2)}, u32[]{:S(2)}) collective-permute-start(f32[16,2048]{1,0:T(8,128)S(1)} %get-tuple-element.23), channel_id=1, source_target_pairs={{0,4},{28,24},{1,5},{29,25},{2,6},{30,26},{3,7},{31,27}} | collective-permute-start | bytes 393224 | tf_op jit(solution)/shard_map/ppermute | solution.py:121
  54.2 14.5 %collective-permute-start.12 = (f32[16,2048]{1,0:T(8,128)S(1)}, f32[16,2048]{1,0:T(8,128)}, u32[]{:S(2)}, u32[]{:S(2)}) collective-permute-start(f32[16,2048]{1,0:T(8,128)S(1)} %get-tuple-element.21), channel_id=1, source_target_pairs={{8,12},{20,16},{9,13},{21,17},{10,14},{22,18},{11,15},{23,19}} | collective-permute-start | bytes 393224 | tf_op jit(solution)/shard_map/ppermute | solution.py:121
  55.5 13.3 %collective-permute-start.11 = (f32[16,2048]{1,0:T(8,128)}, f32[16,2048]{1,0:T(8,128)}, u32[]{:S(2)}, u32[]{:S(2)}) collective-permute-start(f32[16,2048]{1,0:T(8,128)} %get-tuple-element.19), channel_id=1, source_target_pairs={{16,20},{12,8},{17,21},{13,9},{18,22},{14,10},{19,23},{15,11}} | collective-permute-start | bytes 393224 | tf_op jit(solution)/shard_map/ppermute | solution.py:121
  62.1 3.4 %copy-start.8 = (f32[2048]{0:T(1024)S(1)}, f32[2048]{0:T(1024)}, u32[]{:S(2)}) copy-start(f32[2048]{0:T(1024)} %copy-done.7) | copy-start | bytes 24580
  62.1 3.4 %copy-start.14 = (f32[256]{0:T(256)S(1)}, f32[256]{0:T(256)}, u32[]{:S(2)}) copy-start(f32[256]{0:T(256)} %get-tuple-element.51) | copy-start | bytes 3076
  64.2 4.5 %collective-permute-start.10 = (f32[16,2048]{1,0:T(8,128)}, f32[16,2048]{1,0:T(8,128)}, u32[]{:S(2)}, u32[]{:S(2)}) collective-permute-start(f32[16,2048]{1,0:T(8,128)} %multiply_divide_fusion), channel_id=1, source_target_pairs={{24,28},{4,0},{25,29},{5,1},{26,30},{6,2},{27,31},{7,3}} | collective-permute-start | bytes 393224 | tf_op jit(solution)/shard_map/ppermute | solution.py:121
  65.5 12.0 %copy-start.9 = (f32[2048]{0:T(1024)S(1)}, f32[2048]{0:T(1024)}, u32[]{:S(2)}) copy-start(f32[2048]{0:T(1024)} %copy-done.7) | copy-start | bytes 24580
  69.8 4.1 %collective-permute-start.17 = (f32[1,2048]{1,0:T(1,128)S(1)}, f32[1,2048]{1,0:T(1,128)S(1)}, u32[]{:S(2)}, u32[]{:S(2)}) collective-permute-start(f32[1,2048]{1,0:T(1,128)S(1)} %bitcast.65), channel_id=1, source_target_pairs={{0,1},{1,2},{2,3},{3,0},{4,5},{5,6},{6,7},{7,4},{8,9},{9,10},{10,1... | collective-permute-start | bytes 24584 | tf_op jit(solution)/shard_map/ppermute | solution.py:22
  73.0 2.8 %collective-permute-start.18 = (f32[1,2048]{1,0:T(1,128)S(1)}, f32[1,2048]{1,0:T(1,128)S(1)}, u32[]{:S(2)}, u32[]{:S(2)}) collective-permute-start(f32[1,2048]{1,0:T(1,128)S(1)} %bitcast.66), channel_id=1, source_target_pairs={{0,2},{1,3},{2,0},{3,1},{4,6},{5,7},{6,4},{7,5},{8,10},{9,11},{10,... | collective-permute-start | bytes 24584 | tf_op jit(solution)/shard_map/ppermute | solution.py:22
  73.7 3.1 %collective-permute-start.19 = (f32[1,2048]{1,0:T(1,128)S(1)}, f32[1,2048]{1,0:T(1,128)S(1)}, u32[]{:S(2)}, u32[]{:S(2)}) collective-permute-start(f32[1,2048]{1,0:T(1,128)S(1)} %bitcast.67), channel_id=1, source_target_pairs={{0,3},{1,0},{2,1},{3,2},{4,7},{5,4},{6,5},{7,6},{8,11},{9,8},{10,9... | collective-permute-start | bytes 24584 | tf_op jit(solution)/shard_map/ppermute | solution.py:22
  77.5 5.7 %copy-start.10 = (f32[2048]{0:T(1024)S(1)}, f32[2048]{0:T(1024)}, u32[]{:S(2)}) copy-start(f32[2048]{0:T(1024)} %fusion.43) | copy-start | bytes 24580
  77.5 6.4 %copy-start.1 = (f32[2048,256]{1,0:T(8,128)S(1)}, f32[2048,256]{1,0:T(8,128)}, u32[]{:S(2)}) copy-start(f32[2048,256]{1,0:T(8,128)} %fusion.14) | copy-start | bytes 6291460
  77.5 6.4 %copy-start.2 = (f32[2048,256]{1,0:T(8,128)S(1)}, f32[2048,256]{1,0:T(8,128)}, u32[]{:S(2)}) copy-start(f32[2048,256]{1,0:T(8,128)} %fusion.17) | copy-start | bytes 6291460
  84.0 2.2 %copy-start.5 = (f32[2048,256]{1,0:T(8,128)S(1)}, f32[2048,256]{1,0:T(8,128)}, u32[]{:S(2)}) copy-start(f32[2048,256]{1,0:T(8,128)} %fusion.8) | copy-start | bytes 6291460
  90.2 3.4 %collective-permute-start.20 = (f32[512]{0:T(512)S(1)}, f32[512]{0:T(512)S(1)}, u32[]{:S(2)}, u32[]{:S(2)}) collective-permute-start(f32[512]{0:T(512)S(1)} %get-tuple-element.38), channel_id=1, source_target_pairs={{0,1},{1,2},{2,3},{3,0},{4,5},{5,6},{6,7},{7,4},{8,9},{9,10},{10,1... | collective-permute-start | bytes 6152 | tf_op jit(solution)/shard_map/ppermute | solution.py:22
  90.2 3.6 %collective-permute-start.21 = (f32[512]{0:T(512)S(1)}, f32[512]{0:T(512)S(1)}, u32[]{:S(2)}, u32[]{:S(2)}) collective-permute-start(f32[512]{0:T(512)S(1)} %get-tuple-element.37), channel_id=1, source_target_pairs={{0,2},{1,3},{2,0},{3,1},{4,6},{5,7},{6,4},{7,5},{8,10},{9,11},{10,... | collective-permute-start | bytes 6152 | tf_op jit(solution)/shard_map/ppermute | solution.py:22
  91.0 3.1 %collective-permute-start.22 = (f32[512]{0:T(512)S(1)}, f32[512]{0:T(512)S(1)}, u32[]{:S(2)}, u32[]{:S(2)}) collective-permute-start(f32[512]{0:T(512)S(1)} %get-tuple-element.36), channel_id=1, source_target_pairs={{0,3},{1,0},{2,1},{3,2},{4,7},{5,4},{6,5},{7,6},{8,11},{9,8},{10,9... | collective-permute-start | bytes 6152 | tf_op jit(solution)/shard_map/ppermute | solution.py:22
  91.8 3.2 %collective-permute-start.14 = (f32[2,16,512]{2,1,0:T(8,128)S(1)}, f32[2,16,512]{2,1,0:T(8,128)S(1)}, u32[]{:S(2)}, u32[]{:S(2)}) collective-permute-start(f32[2,16,512]{2,1,0:T(8,128)S(1)} %get-tuple-element.28), channel_id=1, source_target_pairs={{0,1},{1,2},{2,3},{3,0},{4,5},{5,6},{6,7},{7,4},{8,9},{9,10},{10,1... | collective-permute-start | bytes 196616 | tf_op jit(solution)/shard_map/ppermute | solution.py:22
  92.9 4.0 %collective-permute-start.15 = (f32[2,16,512]{2,1,0:T(8,128)S(1)}, f32[2,16,512]{2,1,0:T(8,128)S(1)}, u32[]{:S(2)}, u32[]{:S(2)}) collective-permute-start(f32[2,16,512]{2,1,0:T(8,128)S(1)} %get-tuple-element.29), channel_id=1, source_target_pairs={{0,2},{1,3},{2,0},{3,1},{4,6},{5,7},{6,4},{7,5},{8,10},{9,11},{10,... | collective-permute-start | bytes 196616 | tf_op jit(solution)/shard_map/ppermute | solution.py:22
  93.6 3.8 %collective-permute-start.16 = (f32[2,16,512]{2,1,0:T(8,128)S(1)}, f32[2,16,512]{2,1,0:T(8,128)S(1)}, u32[]{:S(2)}, u32[]{:S(2)}) collective-permute-start(f32[2,16,512]{2,1,0:T(8,128)S(1)} %get-tuple-element.26), channel_id=1, source_target_pairs={{0,3},{1,0},{2,1},{3,2},{4,7},{5,4},{6,5},{7,6},{8,11},{9,8},{10,9... | collective-permute-start | bytes 196616 | tf_op jit(solution)/shard_map/ppermute | solution.py:22
  (6 other events, 8.9 us)

commit v20 on v18

--- a/solution.py
+++ b/solution.py
@@ -136,6 +136,9 @@
     backward_out = both_out[1]
     mass_part = jnp.sum(forward_rows * block_weight * backward_rows, axis=0)
     full_mass = live_all * sum_over_pt(mass_part)
+    full_mass, both_out = lax.optimization_barrier((full_mass, both_out))
+    forward_out = both_out[0]
+    backward_out = both_out[1]
     mass_total = jnp.sum(full_mass)
 
     cell_total = cell_count[0]

time: 88.6 us -> 89.1 us (level)
  transfers between devices with their start and end apart: 23 -> 23, of which waited for: 7 -> 6; matrix products, arithmetic and copies ran while one was open for 28% -> 28% of each run, Pallas kernels for 0% -> 0%
where the time goes in v20:
time: 89.1 us; the launch traced here: 88.5 us
  matrix products  31.1 us (35%)
  starting transfers between devices  27.5 us (31%)
  waiting for transfers between devices  8.4 us (9%)
  blocking collectives  7.46 us (8%)
  other arithmetic  6.85 us (8%)
  local copies, waits for them, and re-layouts  3.99 us (4%)
  between operations  3.24 us (4%)
    dot_general x6, matrix products, squared_dist(): lax.dot_general(left_pts, right_pts, (((0,), (0,)), ((), ())), preferred_...  21.7 us
    ppermute x12, starting transfers between devices, swap_blocks(): lax.ppermute(piece, 'pt', [(i, (i + shift) % count) for i in range(count)])  9.72 us
    all_gather x1, blocking collectives, shards(): day_pts = lax.all_gather(own_pts, 'pt', axis=1, tiled=True)  7.46 us
    dot_general x4, matrix products, shards(): jnp.dot(sent, other_kernel, preferred_element_type=jnp.float32)  5.39 us
    ppermute x3, starting transfers between devices, shards(): lax.ppermute(outgoing, 'day', [(forward_day, forward_day + 2), (backward_...  4.98 us
    ppermute x1, starting transfers between devices, shards(): other_count = lax.ppermute(support_count, 'day', pair_route)[0]  4.27 us
    dot_general x3, matrix products, shards(): jnp.dot(incoming, link_kernel, preferred_element_type=jnp.float32)  3.92 us
    ppermute x4, starting transfers between devices, shards(): lax.ppermute(following, 'day', [(forward_day, forward_day + 1), (backward...  3.92 us
  transfers between devices with their start and end apart: 23, of which 6 were waited for; matrix products, arithmetic and copies ran while one was open for 28% of the time, Pallas kernels for 0%

profile of v20, /device:TPU:0, one launch (start us, length us, event | category | flops | bytes accessed | tf_op | source)
XLA Modules:
  0.0 88.5 jit_solution(59398012628714327)
XLA Ops:
  0.6 7.5 %all-gather = bf16[1,64,2048]{2,1,0:T(8,128)(2,1)S(1)} all-gather(bf16[1,64,512]{2,1,0:T(8,128)(2,1)} %param.6), channel_id=2, replica_groups=mesh['day'=8,'pt'=4] {'pt'}, dimensions={2}, use_global_device_ids=true | all-gather | bytes 327680 | tf_op jit(solution)/shard_map/all_gather | solution.py:57
  8.1 1.5 %collective-permute-start.3 = (bf16[64,2048]{1,0:T(8,128)(2,1)S(1)}, bf16[64,2048]{1,0:T(8,128)(2,1)S(1)}, u32[]{:S(2)}, u32[]{:S(2)}) collective-permute-start(bf16[64,2048]{1,0:T(8,128)(2,1)S(1)} %bitcast.47), channel_id=1, source_target_pairs={{4,0},{0,4},{12,8},{8,12},{20,16},{16,20},{28,24},{24,28},{5,1},{1... | collective-permute-start | bytes 786440 | tf_op jit(solution)/shard_map/ppermute | solution.py:75
  11.4 1.5 %collective-permute-start.1 = (f32[16,512]{1,0:T(8,128)S(1)}, f32[16,512]{1,0:T(8,128)S(1)}, u32[]{:S(2)}, u32[]{:S(2)}) collective-permute-start(f32[16,512]{1,0:T(8,128)S(1)} %get-tuple-element.31), channel_id=1, source_target_pairs={{0,2},{1,3},{2,0},{3,1},{4,6},{5,7},{6,4},{7,5},{8,10},{9,11},{10,... | collective-permute-start | bytes 98312 | tf_op jit(solution)/shard_map/ppermute | solution.py:22
  13.0 4.3 %collective-permute-start.4 = (s32[1]{0:T(128)}, s32[1]{0:T(128)}, u32[]{:S(2)}, u32[]{:S(2)}) collective-permute-start(s32[1]{0:T(128)} %param.10), channel_id=1, source_target_pairs={{4,0},{0,4},{12,8},{8,12},{20,16},{16,20},{28,24},{24,28},{5,1},{1... | collective-permute-start | bytes 20 | tf_op jit(solution)/shard_map/ppermute | solution.py:80
  18.0 1.0 %multiply_reduce_fusion.8 = f32[2048]{0:T(1024)S(1)} fusion(bf16[1,64,2048]{2,1,0:T(8,128)(2,1)} %param.7), kind=kLoop, calls=%fused_computation.21 | loop fusion | flops 391168 | bytes 270336 | tf_op jit(solution)/shard_map/reduce_sum | solution.py:41
  19.0 2.3 %collective-permute-done.4 = s32[1]{0:T(128)} collective-permute-done((s32[1]{0:T(128)}, s32[1]{0:T(128)}, u32[]{:S(2)}, u32[]{:S(2)}) %collective-permute-start.4) | collective-permute-done | bytes 36 | tf_op jit(solution)/shard_map/ppermute | solution.py:80
  23.5 2.4 %collective-permute-start.5 = (f32[16,2048]{1,0:T(8,128)S(1)}, f32[16,2048]{1,0:T(8,128)S(1)}, u32[]{:S(2)}, u32[]{:S(2)}) collective-permute-start(f32[16,2048]{1,0:T(8,128)S(1)} %constant_dynamic-update-slice_fusion.2), channel_id=1, source_target_pairs={{4,0},{0,4},{12,8},{8,12},{20,16},{16,20},{28,24},{24,28},{5,1},{1... | collective-permute-start | bytes 393224 | tf_op jit(solution)/shard_map/ppermute | solution.py:79
  26.1 3.6 %exponential_convert_fusion.1 = bf16[2048,2048]{1,0:T(8,128)(2,1)S(1)} fusion(bf16[64,2048]{1,0:T(8,128)(2,1)S(1)} %collective-permute-done.3, f32[2048]{0:T(1024)S(1)} %multiply_reduce_fusion.10, f32[2048]{0:T(1024)S(1)} %multiply_reduce_fusion.11, bf16[1,64,2048]{2,1,0:T(8,128)(2,1)S(1)} %all-gather), kind=kOutput, calls=%fused_computation.1 | convolution fusion | flops 557842432 | bytes 8929280 | tf_op jit(solution)/shard_map/dot_general | solution.py:45
  29.7 1.3 %fusion.29 = (f32[16]{0:T(128)S(1)}, f32[16,2048]{1,0:T(8,128)S(1)}) fusion(f32[2048]{0:T(1024)S(1)} %fusion.14, bf16[2048,2048]{1,0:T(8,128)(2,1)S(1)} %exponential_convert_fusion.1, f32[16,2048]{1,0:T(8,128)S(1)} %constant_dynamic-update-slice_fusion.2, f32[2048]{0:T(1024)S(1)} %fusion.13), kind=kOutput, calls=%fused_computation.102 | convolution fusion | flops 134348784 | bytes 8667200 | tf_op jit(solution)/shard_map/dot_general | solution.py:109
  31.2 3.5 %collective-permute-start.6 = (bf16[16,2048]{1,0:T(8,128)(2,1)S(1)}, bf16[16,2048]{1,0:T(8,128)(2,1)S(1)}, u32[]{:S(2)}, u32[]{:S(2)}) collective-permute-start(bf16[16,2048]{1,0:T(8,128)(2,1)S(1)} %get-tuple-element.20), channel_id=1, source_target_pairs={{0,8},{28,20},{1,9},{29,21},{2,10},{30,22},{3,11},{31,23}} | collective-permute-start | bytes 196616 | tf_op jit(solution)/shard_map/ppermute | solution.py:118
  34.7 3.6 %exponential_convert_fusion = bf16[2048,2048]{1,0:T(8,128)(2,1)S(1)} fusion(bf16[64,2048]{1,0:T(8,128)(2,1)S(1)} %collective-permute-done.7, f32[2048]{0:T(1024)S(1)} %multiply_reduce_fusion.11, f32[2048]{0:T(1024)S(1)} %multiply_reduce_fusion.9, bf16[1,64,2048]{2,1,0:T(8,128)(2,1)S(1)} %all-gather), kind=kOutput, calls=%fused_computation | convolution fusion | flops 557842432 | bytes 8929280 | tf_op jit(solution)/shard_map/dot_general | solution.py:45
  38.3 1.3 %fusion.30 = (f32[16]{0:T(128)S(1)}, f32[16,2048]{1,0:T(8,128)S(1)}) fusion(f32[2048]{0:T(1024)S(1)} %fusion.13, bf16[16,2048]{1,0:T(8,128)(2,1)S(1)} %collective-permute-done.6, bf16[2048,2048]{1,0:T(8,128)(2,1)S(1)} %exponential_convert_fusion), kind=kOutput, calls=%fused_computation.103 | convolution fusion | flops 134283248 | bytes 8593472 | tf_op jit(solution)/shard_map/dot_general | solution.py:101
  39.6 1.4 %fusion.31 = (f32[16]{0:T(128)S(1)}, f32[16,2048]{1,0:T(8,128)S(1)}) fusion(f32[2048]{0:T(1024)S(1)} %fusion.14, bf16[2048,2048]{1,0:T(8,128)(2,1)S(1)} %exponential_convert_fusion.1, f32[16,2048]{1,0:T(8,128)S(1)} %constant_dynamic-update-slice_fusion.2, f32[16]{0:T(128)S(1)} %get-tuple-element.48, f32[16,2048]{1,0:T(8,128)S(1)} %get-tuple-element.49, ...), kind=kOutput, calls=%fused_computation.104 | convolution fusion | flops 134414320 | bytes 8790148 | tf_op jit(solution)/shard_map/dot_general | solution.py:109
  41.9 2.9 %negate_exponential_fusion = f32[2048,512]{1,0:T(8,128)} fusion(f32[512]{0:T(512)S(1)} %get-tuple-element.43, f32[2048]{0:T(1024)S(1)} %multiply_reduce_fusion.11, bf16[64,2048]{1,0:T(8,128)(2,1)S(1)} %bitcast.49, bf16[1,64,2048]{2,1,0:T(8,128)(2,1)S(1)} %all-gather), kind=kOutput, calls=%fused_computation.4 | convolution fusion | flops 138412032 | bytes 4532224 | tf_op jit(solution)/shard_map/dot_general | solution.py:45
  44.8 1.3 %fusion.32 = (f32[16]{0:T(128)S(1)}, f32[16,2048]{1,0:T(8,128)S(1)}) fusion(f32[2048]{0:T(1024)S(1)} %fusion.13, bf16[16,2048]{1,0:T(8,128)(2,1)S(1)} %collective-permute-done.8, bf16[2048,2048]{1,0:T(8,128)(2,1)S(1)} %exponential_convert_fusion), kind=kOutput, calls=%fused_computation.105 | convolution fusion | flops 134283248 | bytes 8593472 | tf_op jit(solution)/shard_map/dot_general | solution.py:101
  46.1 1.4 %fusion.33 = (f32[16]{0:T(128)S(1)}, f32[16,2048]{1,0:T(8,128)S(1)}) fusion(f32[2048]{0:T(1024)S(1)} %fusion.14, bf16[2048,2048]{1,0:T(8,128)(2,1)S(1)} %exponential_convert_fusion.1, f32[16,2048]{1,0:T(8,128)S(1)} %constant_dynamic-update-slice_fusion.2, f32[16]{0:T(128)S(1)} %get-tuple-element.52, f32[16,2048]{1,0:T(8,128)S(1)} %get-tuple-element.53, ...), kind=kOutput, calls=%fused_computation.106 | convolution fusion | flops 134414320 | bytes 8790148 | tf_op jit(solution)/shard_map/dot_general | solution.py:109
  48.2 2.9 %negate_exponential_fusion.1 = f32[2048,512]{1,0:T(8,128)} fusion(f32[512]{0:T(512)S(1)} %get-tuple-element.44, f32[2048]{0:T(1024)S(1)} %multiply_reduce_fusion.11, bf16[64,2048]{1,0:T(8,128)(2,1)S(1)} %bitcast.50, bf16[1,64,2048]{2,1,0:T(8,128)(2,1)S(1)} %all-gather), kind=kOutput, calls=%fused_computation.7 | convolution fusion | flops 138412032 | bytes 4532224 | tf_op jit(solution)/shard_map/dot_general | solution.py:45
  51.1 1.3 %collective-permute-start.13 = (f32[16,2048]{1,0:T(8,128)S(1)}, f32[16,2048]{1,0:T(8,128)S(1)}, u32[]{:S(2)}, u32[]{:S(2)}) collective-permute-start(f32[16,2048]{1,0:T(8,128)S(1)} %get-tuple-element.21), channel_id=1, source_target_pairs={{0,4},{28,24},{1,5},{29,25},{2,6},{30,26},{3,7},{31,27}} | collective-permute-start | bytes 393224 | tf_op jit(solution)/shard_map/ppermute | solution.py:121
  53.8 1.3 %fusion.34 = (f32[16]{0:T(128)S(1)}, f32[16,2048]{1,0:T(8,128)S(1)}) fusion(f32[2048]{0:T(1024)S(1)} %fusion.13, bf16[16,2048]{1,0:T(8,128)(2,1)S(1)} %collective-permute-done.9, bf16[2048,2048]{1,0:T(8,128)(2,1)S(1)} %exponential_convert_fusion), kind=kOutput, calls=%fused_computation.107 | convolution fusion | flops 134283248 | bytes 8593472 | tf_op jit(solution)/shard_map/dot_general | solution.py:101
  55.1 1.4 %fusion.35 = (f32[16]{0:T(128)S(1)}, f32[16,2048]{1,0:T(8,128)S(1)}) fusion(f32[2048]{0:T(1024)S(1)} %fusion.14, bf16[2048,2048]{1,0:T(8,128)(2,1)S(1)} %exponential_convert_fusion.1, f32[16,2048]{1,0:T(8,128)S(1)} %constant_dynamic-update-slice_fusion.2, f32[16]{0:T(128)S(1)} %get-tuple-element.56, f32[16,2048]{1,0:T(8,128)S(1)} %get-tuple-element.57, ...), kind=kOutput, calls=%fused_computation.108 | convolution fusion | flops 134414320 | bytes 8790148 | tf_op jit(solution)/shard_map/dot_general | solution.py:109
  56.5 1.3 %collective-permute-start.10 = (f32[16,2048]{1,0:T(8,128)S(1)}, f32[16,2048]{1,0:T(8,128)S(1)}, u32[]{:S(2)}, u32[]{:S(2)}) collective-permute-start(f32[16,2048]{1,0:T(8,128)S(1)} %multiply_divide_fusion), channel_id=1, source_target_pairs={{24,28},{4,0},{25,29},{5,1},{26,30},{6,2},{27,31},{7,3}} | collective-permute-start | bytes 393224 | tf_op jit(solution)/shard_map/ppermute | solution.py:121
  57.8 2.9 %negate_exponential_fusion.3 = f32[2048,512]{1,0:T(8,128)} fusion(f32[512]{0:T(512)S(1)} %get-tuple-element.42, f32[2048]{0:T(1024)S(1)} %multiply_reduce_fusion.11, bf16[64,2048]{1,0:T(8,128)(2,1)S(1)} %bitcast.51, bf16[1,64,2048]{2,1,0:T(8,128)(2,1)S(1)} %all-gather), kind=kOutput, calls=%fused_computation.13 | convolution fusion | flops 138412032 | bytes 4532224 | tf_op jit(solution)/shard_map/dot_general | solution.py:45
  61.5 2.9 %collective-permute-done.10 = f32[16,2048]{1,0:T(8,128)S(1)} collective-permute-done((f32[16,2048]{1,0:T(8,128)S(1)}, f32[16,2048]{1,0:T(8,128)S(1)}, u32[]{:S(2)}, u32[]{:S(2)}) %collective-permute-start.10) | collective-permute-done | bytes 131104 | tf_op jit(solution)/shard_map/ppermute | solution.py:121
  64.6 1.1 %collective-permute-start.15 = (f32[1,2048]{1,0:T(1,128)S(1)}, f32[1,2048]{1,0:T(1,128)S(1)}, u32[]{:S(2)}, u32[]{:S(2)}) collective-permute-start(f32[1,2048]{1,0:T(1,128)S(1)} %bitcast.54), channel_id=1, source_target_pairs={{0,2},{1,3},{2,0},{3,1},{4,6},{5,7},{6,4},{7,5},{8,10},{9,11},{10,... | collective-permute-start | bytes 24584 | tf_op jit(solution)/shard_map/ppermute | solution.py:22
  65.8 1.4 %collective-permute-start.16 = (f32[1,2048]{1,0:T(1,128)S(1)}, f32[1,2048]{1,0:T(1,128)S(1)}, u32[]{:S(2)}, u32[]{:S(2)}) collective-permute-start(f32[1,2048]{1,0:T(1,128)S(1)} %bitcast.55), channel_id=1, source_target_pairs={{0,3},{1,0},{2,1},{3,2},{4,7},{5,4},{6,5},{7,6},{8,11},{9,8},{10,9... | collective-permute-start | bytes 24584 | tf_op jit(solution)/shard_map/ppermute | solution.py:22
  67.3 1.0 %collective-permute-start.18 = (f32[2,16,512]{2,1,0:T(8,128)S(1)}, f32[2,16,512]{2,1,0:T(8,128)S(1)}, u32[]{:S(2)}, u32[]{:S(2)}) collective-permute-start(f32[2,16,512]{2,1,0:T(8,128)S(1)} %get-tuple-element.27), channel_id=1, source_target_pairs={{0,2},{1,3},{2,0},{3,1},{4,6},{5,7},{6,4},{7,5},{8,10},{9,11},{10,... | collective-permute-start | bytes 196616 | tf_op jit(solution)/shard_map/ppermute | solution.py:22
  68.4 1.4 %collective-permute-start.19 = (f32[2,16,512]{2,1,0:T(8,128)S(1)}, f32[2,16,512]{2,1,0:T(8,128)S(1)}, u32[]{:S(2)}, u32[]{:S(2)}) collective-permute-start(f32[2,16,512]{2,1,0:T(8,128)S(1)} %get-tuple-element.24), channel_id=1, source_target_pairs={{0,3},{1,0},{2,1},{3,2},{4,7},{5,4},{6,5},{7,6},{8,11},{9,8},{10,9... | collective-permute-start | bytes 196616 | tf_op jit(solution)/shard_map/ppermute | solution.py:22
  71.0 1.3 %collective-permute-done.18 = f32[2,16,512]{2,1,0:T(8,128)S(1)} collective-permute-done((f32[2,16,512]{2,1,0:T(8,128)S(1)}, f32[2,16,512]{2,1,0:T(8,128)S(1)}, u32[]{:S(2)}, u32[]{:S(2)}) %collective-permute-start.18) | collective-permute-done | bytes 65568 | tf_op jit(solution)/shard_map/ppermute | solution.py:22
  73.0 5.9 %multiply_reduce_fusion.5 = (f32[512]{0:T(512)S(1)}, f32[512]{0:T(512)S(1)}, f32[512]{0:T(512)S(1)}, f32[512]{0:T(512)S(1)}, f32[2048,512]{1,0:T(8,128)S(1)}) fusion(f32[2048]{0:T(1024)S(1)} %fusion.12, f32[2048,512]{1,0:T(8,128)} %negate_exponential_fusion.1, f32[2048,512]{1,0:T(8,128)} %negate_exponential_fusion, ...), kind=kOutput, calls=%fused_computation.9 | convolution fusion | flops 146798592 | bytes 17131520 | tf_op jit(solution)/shard_map/dot_general | solution.py:45
  80.7 1.6 %copy-done.2 = f32[2048,512]{1,0:T(8,128)S(1)} copy-done((f32[2048,512]{1,0:T(8,128)S(1)}, f32[2048,512]{1,0:T(8,128)}, u32[]{:S(2)}) %copy-start.2) | copy-done | bytes 4194328
  83.8 0.9 %collective-permute-start.21 = (f32[512]{0:T(512)S(1)}, f32[512]{0:T(512)S(1)}, u32[]{:S(2)}, u32[]{:S(2)}) collective-permute-start(f32[512]{0:T(512)S(1)} %get-tuple-element.35), channel_id=1, source_target_pairs={{0,2},{1,3},{2,0},{3,1},{4,6},{5,7},{6,4},{7,5},{8,10},{9,11},{10,... | collective-permute-start | bytes 6152 | tf_op jit(solution)/shard_map/ppermute | solution.py:22
  86.4 1.0 %collective-permute-done.21 = f32[512]{0:T(512)S(1)} collective-permute-done((f32[512]{0:T(512)S(1)}, f32[512]{0:T(512)S(1)}, u32[]{:S(2)}, u32[]{:S(2)}) %collective-permute-start.21) | collective-permute-done | bytes 2080 | tf_op jit(solution)/shard_map/ppermute | solution.py:22
  (82 shorter events, 14.9 us)
Async XLA Ops:
  8.1 17.9 %collective-permute-start.3 = (bf16[64,2048]{1,0:T(8,128)(2,1)S(1)}, bf16[64,2048]{1,0:T(8,128)(2,1)S(1)}, u32[]{:S(2)}, u32[]{:S(2)}) collective-permute-start(bf16[64,2048]{1,0:T(8,128)(2,1)S(1)} %bitcast.47), channel_id=1, source_target_pairs={{4,0},{0,4},{12,8},{8,12},{20,16},{16,20},{28,24},{24,28},{5,1},{1... | collective-permute-start | bytes 786440 | tf_op jit(solution)/shard_map/ppermute | solution.py:75
  9.6 21.5 %collective-permute-start.7 = (bf16[64,2048]{1,0:T(8,128)(2,1)S(1)}, bf16[64,2048]{1,0:T(8,128)(2,1)S(1)}, u32[]{:S(2)}, u32[]{:S(2)}) collective-permute-start(bf16[64,2048]{1,0:T(8,128)(2,1)S(1)} %bitcast.48), channel_id=1, source_target_pairs={{8,4},{4,8},{16,12},{12,16},{24,20},{20,24},{9,5},{5,9},{17,13},{1... | collective-permute-start | bytes 786440 | tf_op jit(solution)/shard_map/ppermute | solution.py:83
  11.3 12.0 %collective-permute-start = (f32[16,512]{1,0:T(8,128)S(1)}, f32[16,512]{1,0:T(8,128)S(1)}, u32[]{:S(2)}, u32[]{:S(2)}) collective-permute-start(f32[16,512]{1,0:T(8,128)S(1)} %get-tuple-element.32), channel_id=1, source_target_pairs={{0,1},{1,2},{2,3},{3,0},{4,5},{5,6},{6,7},{7,4},{8,9},{9,10},{10,1... | collective-permute-start | bytes 98312 | tf_op jit(solution)/shard_map/ppermute | solution.py:22
  11.4 11.9 %collective-permute-start.1 = (f32[16,512]{1,0:T(8,128)S(1)}, f32[16,512]{1,0:T(8,128)S(1)}, u32[]{:S(2)}, u32[]{:S(2)}) collective-permute-start(f32[16,512]{1,0:T(8,128)S(1)} %get-tuple-element.31), channel_id=1, source_target_pairs={{0,2},{1,3},{2,0},{3,1},{4,6},{5,7},{6,4},{7,5},{8,10},{9,11},{10,... | collective-permute-start | bytes 98312 | tf_op jit(solution)/shard_map/ppermute | solution.py:22
  13.0 8.4 %collective-permute-start.4 = (s32[1]{0:T(128)}, s32[1]{0:T(128)}, u32[]{:S(2)}, u32[]{:S(2)}) collective-permute-start(s32[1]{0:T(128)} %param.10), channel_id=1, source_target_pairs={{4,0},{0,4},{12,8},{8,12},{20,16},{16,20},{28,24},{24,28},{5,1},{1... | collective-permute-start | bytes 20 | tf_op jit(solution)/shard_map/ppermute | solution.py:80
  21.3 2.2 %collective-permute-start.2 = (f32[16,512]{1,0:T(8,128)S(1)}, f32[16,512]{1,0:T(8,128)S(1)}, u32[]{:S(2)}, u32[]{:S(2)}) collective-permute-start(f32[16,512]{1,0:T(8,128)S(1)} %get-tuple-element.30), channel_id=1, source_target_pairs={{0,3},{1,0},{2,1},{3,2},{4,7},{5,4},{6,5},{7,6},{8,11},{9,8},{10,9... | collective-permute-start | bytes 98312 | tf_op jit(solution)/shard_map/ppermute | solution.py:22
  23.5 7.5 %collective-permute-start.5 = (f32[16,2048]{1,0:T(8,128)S(1)}, f32[16,2048]{1,0:T(8,128)S(1)}, u32[]{:S(2)}, u32[]{:S(2)}) collective-permute-start(f32[16,2048]{1,0:T(8,128)S(1)} %constant_dynamic-update-slice_fusion.2), channel_id=1, source_target_pairs={{4,0},{0,4},{12,8},{8,12},{20,16},{16,20},{28,24},{24,28},{5,1},{1... | collective-permute-start | bytes 393224 | tf_op jit(solution)/shard_map/ppermute | solution.py:79
  31.2 7.1 %collective-permute-start.6 = (bf16[16,2048]{1,0:T(8,128)(2,1)S(1)}, bf16[16,2048]{1,0:T(8,128)(2,1)S(1)}, u32[]{:S(2)}, u32[]{:S(2)}) collective-permute-start(bf16[16,2048]{1,0:T(8,128)(2,1)S(1)} %get-tuple-element.20), channel_id=1, source_target_pairs={{0,8},{28,20},{1,9},{29,21},{2,10},{30,22},{3,11},{31,23}} | collective-permute-start | bytes 196616 | tf_op jit(solution)/shard_map/ppermute | solution.py:118
  39.6 2.3 %copy-start.3 = (bf16[1,64,2048]{2,1,0:T(8,128)(2,1)S(1)}, bf16[1,64,2048]{2,1,0:T(8,128)(2,1)}, u32[]{:S(2)}) copy-start(bf16[1,64,2048]{2,1,0:T(8,128)(2,1)} %param.7) | copy-start | bytes 786436
  41.0 3.7 %collective-permute-start.8 = (bf16[16,2048]{1,0:T(8,128)(2,1)S(1)}, bf16[16,2048]{1,0:T(8,128)(2,1)S(1)}, u32[]{:S(2)}, u32[]{:S(2)}) collective-permute-start(bf16[16,2048]{1,0:T(8,128)(2,1)S(1)} %get-tuple-element.18), channel_id=1, source_target_pairs={{8,16},{20,12},{9,17},{21,13},{10,18},{22,14},{11,19},{23,15}} | collective-permute-start | bytes 196616 | tf_op jit(solution)/shard_map/ppermute | solution.py:118
  47.5 6.2 %collective-permute-start.9 = (bf16[16,2048]{1,0:T(8,128)(2,1)S(1)}, bf16[16,2048]{1,0:T(8,128)(2,1)S(1)}, u32[]{:S(2)}, u32[]{:S(2)}) collective-permute-start(bf16[16,2048]{1,0:T(8,128)(2,1)S(1)} %get-tuple-element.16), channel_id=1, source_target_pairs={{16,24},{12,4},{17,25},{13,5},{18,26},{14,6},{19,27},{15,7}} | collective-permute-start | bytes 196616 | tf_op jit(solution)/shard_map/ppermute | solution.py:118
  51.1 10.3 %collective-permute-start.13 = (f32[16,2048]{1,0:T(8,128)S(1)}, f32[16,2048]{1,0:T(8,128)S(1)}, u32[]{:S(2)}, u32[]{:S(2)}) collective-permute-start(f32[16,2048]{1,0:T(8,128)S(1)} %get-tuple-element.21), channel_id=1, source_target_pairs={{0,4},{28,24},{1,5},{29,25},{2,6},{30,26},{3,7},{31,27}} | collective-permute-start | bytes 393224 | tf_op jit(solution)/shard_map/ppermute | solution.py:121
  52.4 9.1 %collective-permute-start.12 = (f32[16,2048]{1,0:T(8,128)S(1)}, f32[16,2048]{1,0:T(8,128)S(1)}, u32[]{:S(2)}, u32[]{:S(2)}) collective-permute-start(f32[16,2048]{1,0:T(8,128)S(1)} %get-tuple-element.19), channel_id=1, source_target_pairs={{8,12},{20,16},{9,13},{21,17},{10,14},{22,18},{11,15},{23,19}} | collective-permute-start | bytes 393224 | tf_op jit(solution)/shard_map/ppermute | solution.py:121
  53.1 8.4 %collective-permute-start.11 = (f32[16,2048]{1,0:T(8,128)S(1)}, f32[16,2048]{1,0:T(8,128)S(1)}, u32[]{:S(2)}, u32[]{:S(2)}) collective-permute-start(f32[16,2048]{1,0:T(8,128)S(1)} %get-tuple-element.17), channel_id=1, source_target_pairs={{16,20},{12,8},{17,21},{13,9},{18,22},{14,10},{19,23},{15,11}} | collective-permute-start | bytes 393224 | tf_op jit(solution)/shard_map/ppermute | solution.py:121
  56.5 7.8 %collective-permute-start.10 = (f32[16,2048]{1,0:T(8,128)S(1)}, f32[16,2048]{1,0:T(8,128)S(1)}, u32[]{:S(2)}, u32[]{:S(2)}) collective-permute-start(f32[16,2048]{1,0:T(8,128)S(1)} %multiply_divide_fusion), channel_id=1, source_target_pairs={{24,28},{4,0},{25,29},{5,1},{26,30},{6,2},{27,31},{7,3}} | collective-permute-start | bytes 393224 | tf_op jit(solution)/shard_map/ppermute | solution.py:121
  64.5 3.9 %collective-permute-start.14 = (f32[1,2048]{1,0:T(1,128)S(1)}, f32[1,2048]{1,0:T(1,128)S(1)}, u32[]{:S(2)}, u32[]{:S(2)}) collective-permute-start(f32[1,2048]{1,0:T(1,128)S(1)} %bitcast.53), channel_id=1, source_target_pairs={{0,1},{1,2},{2,3},{3,0},{4,5},{5,6},{6,7},{7,4},{8,9},{9,10},{10,1... | collective-permute-start | bytes 24584 | tf_op jit(solution)/shard_map/ppermute | solution.py:22
  64.6 5.4 %collective-permute-start.15 = (f32[1,2048]{1,0:T(1,128)S(1)}, f32[1,2048]{1,0:T(1,128)S(1)}, u32[]{:S(2)}, u32[]{:S(2)}) collective-permute-start(f32[1,2048]{1,0:T(1,128)S(1)} %bitcast.54), channel_id=1, source_target_pairs={{0,2},{1,3},{2,0},{3,1},{4,6},{5,7},{6,4},{7,5},{8,10},{9,11},{10,... | collective-permute-start | bytes 24584 | tf_op jit(solution)/shard_map/ppermute | solution.py:22
  65.8 4.4 %collective-permute-start.16 = (f32[1,2048]{1,0:T(1,128)S(1)}, f32[1,2048]{1,0:T(1,128)S(1)}, u32[]{:S(2)}, u32[]{:S(2)}) collective-permute-start(f32[1,2048]{1,0:T(1,128)S(1)} %bitcast.55), channel_id=1, source_target_pairs={{0,3},{1,0},{2,1},{3,2},{4,7},{5,4},{6,5},{7,6},{8,11},{9,8},{10,9... | collective-permute-start | bytes 24584 | tf_op jit(solution)/shard_map/ppermute | solution.py:22
  67.2 3.8 %collective-permute-start.17 = (f32[2,16,512]{2,1,0:T(8,128)S(1)}, f32[2,16,512]{2,1,0:T(8,128)S(1)}, u32[]{:S(2)}, u32[]{:S(2)}) collective-permute-start(f32[2,16,512]{2,1,0:T(8,128)S(1)} %get-tuple-element.26), channel_id=1, source_target_pairs={{0,1},{1,2},{2,3},{3,0},{4,5},{5,6},{6,7},{7,4},{8,9},{9,10},{10,1... | collective-permute-start | bytes 196616 | tf_op jit(solution)/shard_map/ppermute | solution.py:22
  67.3 5.0 %collective-permute-start.18 = (f32[2,16,512]{2,1,0:T(8,128)S(1)}, f32[2,16,512]{2,1,0:T(8,128)S(1)}, u32[]{:S(2)}, u32[]{:S(2)}) collective-permute-start(f32[2,16,512]{2,1,0:T(8,128)S(1)} %get-tuple-element.27), channel_id=1, source_target_pairs={{0,2},{1,3},{2,0},{3,1},{4,6},{5,7},{6,4},{7,5},{8,10},{9,11},{10,... | collective-permute-start | bytes 196616 | tf_op jit(solution)/shard_map/ppermute | solution.py:22
  68.4 3.9 %collective-permute-start.19 = (f32[2,16,512]{2,1,0:T(8,128)S(1)}, f32[2,16,512]{2,1,0:T(8,128)S(1)}, u32[]{:S(2)}, u32[]{:S(2)}) collective-permute-start(f32[2,16,512]{2,1,0:T(8,128)S(1)} %get-tuple-element.24), channel_id=1, source_target_pairs={{0,3},{1,0},{2,1},{3,2},{4,7},{5,4},{6,5},{7,6},{8,11},{9,8},{10,9... | collective-permute-start | bytes 196616 | tf_op jit(solution)/shard_map/ppermute | solution.py:22
  72.9 6.8 %copy-start = (f32[2048,512]{1,0:T(8,128)S(1)}, f32[2048,512]{1,0:T(8,128)}, u32[]{:S(2)}) copy-start(f32[2048,512]{1,0:T(8,128)} %negate_exponential_fusion) | copy-start | bytes 12582916
  73.0 7.1 %copy-start.1 = (f32[2048,512]{1,0:T(8,128)S(1)}, f32[2048,512]{1,0:T(8,128)}, u32[]{:S(2)}) copy-start(f32[2048,512]{1,0:T(8,128)} %negate_exponential_fusion.1) | copy-start | bytes 12582916
  80.1 2.2 %copy-start.2 = (f32[2048,512]{1,0:T(8,128)S(1)}, f32[2048,512]{1,0:T(8,128)}, u32[]{:S(2)}) copy-start(f32[2048,512]{1,0:T(8,128)} %negate_exponential_fusion.3) | copy-start | bytes 12582916
  83.1 3.1 %collective-permute-start.20 = (f32[512]{0:T(512)S(1)}, f32[512]{0:T(512)S(1)}, u32[]{:S(2)}, u32[]{:S(2)}) collective-permute-start(f32[512]{0:T(512)S(1)} %get-tuple-element.36), channel_id=1, source_target_pairs={{0,1},{1,2},{2,3},{3,0},{4,5},{5,6},{6,7},{7,4},{8,9},{9,10},{10,1... | collective-permute-start | bytes 6152 | tf_op jit(solution)/shard_map/ppermute | solution.py:22
  83.8 3.6 %collective-permute-start.21 = (f32[512]{0:T(512)S(1)}, f32[512]{0:T(512)S(1)}, u32[]{:S(2)}, u32[]{:S(2)}) collective-permute-start(f32[512]{0:T(512)S(1)} %get-tuple-element.35), channel_id=1, source_target_pairs={{0,2},{1,3},{2,0},{3,1},{4,6},{5,7},{6,4},{7,5},{8,10},{9,11},{10,... | collective-permute-start | bytes 6152 | tf_op jit(solution)/shard_map/ppermute | solution.py:22
  84.7 2.8 %collective-permute-start.22 = (f32[512]{0:T(512)S(1)}, f32[512]{0:T(512)S(1)}, u32[]{:S(2)}, u32[]{:S(2)}) collective-permute-start(f32[512]{0:T(512)S(1)} %get-tuple-element.34), channel_id=1, source_target_pairs={{0,3},{1,0},{2,1},{3,2},{4,7},{5,4},{6,5},{7,6},{8,11},{9,8},{10,9... | collective-permute-start | bytes 6152 | tf_op jit(solution)/shard_map/ppermute | solution.py:22

commit v21 on v18

--- a/solution.py
+++ b/solution.py
@@ -111,7 +111,6 @@
             other_total,
         )
         if round_index == 0:
-            link_pts = lax.optimization_barrier((link_pts, following))[0]
             link_kernel = chain_kernel(link_pts)
         if round_index < half - 1:
             outgoing = (following * other_weight).astype(jnp.bfloat16)

time: 88.6 us -> 88.6 us (level)
  no operation moved by 1% of the time
where the time goes in v21:
time: 88.6 us; the launch traced here: 87.9 us
  matrix products  31.1 us (35%)
  starting transfers between devices  27.7 us (31%)
  waiting for transfers between devices  7.62 us (9%)
  blocking collectives  7.46 us (8%)
  other arithmetic  6.85 us (8%)
  local copies, waits for them, and re-layouts  3.98 us (4%)
  between operations  3.2 us (4%)
    dot_general x6, matrix products, squared_dist(): lax.dot_general(left_pts, right_pts, (((0,), (0,)), ((), ())), preferred_...  21.8 us
    ppermute x12, starting transfers between devices, swap_blocks(): lax.ppermute(piece, 'pt', [(i, (i + shift) % count) for i in range(count)])  9.92 us
    all_gather x1, blocking collectives, shards(): day_pts = lax.all_gather(own_pts, 'pt', axis=1, tiled=True)  7.46 us
    dot_general x4, matrix products, shards(): jnp.dot(sent, other_kernel, preferred_element_type=jnp.float32)  5.39 us
    ppermute x3, starting transfers between devices, shards(): lax.ppermute(outgoing, 'day', [(forward_day, forward_day + 2), (backward_...  4.98 us
    ppermute x1, starting transfers between devices, shards(): other_count = lax.ppermute(support_count, 'day', pair_route)[0]  4.27 us
    dot_general x3, matrix products, shards(): jnp.dot(incoming, link_kernel, preferred_element_type=jnp.float32)  3.92 us
    ppermute x4, starting transfers between devices, shards(): lax.ppermute(following, 'day', [(forward_day, forward_day + 1), (backward...  3.92 us
  transfers between devices with their start and end apart: 23, of which 7 were waited for; matrix products, arithmetic and copies ran while one was open for 28% of the time, Pallas kernels for 0%

profile of v21, /device:TPU:0, one launch (start us, length us, event | category | flops | bytes accessed | tf_op | source)
XLA Modules:
  0.0 87.9 jit_solution(10244133573843841732)
XLA Ops:
  0.6 7.5 %all-gather = bf16[1,64,2048]{2,1,0:T(8,128)(2,1)S(1)} all-gather(bf16[1,64,512]{2,1,0:T(8,128)(2,1)} %param.6), channel_id=2, replica_groups=mesh['day'=8,'pt'=4] {'pt'}, dimensions={2}, use_global_device_ids=true | all-gather | bytes 327680 | tf_op jit(solution)/shard_map/all_gather | solution.py:57
  8.1 1.5 %collective-permute-start.3 = (bf16[64,2048]{1,0:T(8,128)(2,1)S(1)}, bf16[64,2048]{1,0:T(8,128)(2,1)S(1)}, u32[]{:S(2)}, u32[]{:S(2)}) collective-permute-start(bf16[64,2048]{1,0:T(8,128)(2,1)S(1)} %bitcast.47), channel_id=1, source_target_pairs={{4,0},{0,4},{12,8},{8,12},{20,16},{16,20},{28,24},{24,28},{5,1},{1... | collective-permute-start | bytes 786440 | tf_op jit(solution)/shard_map/ppermute | solution.py:75
  11.4 1.5 %collective-permute-start.1 = (f32[16,512]{1,0:T(8,128)S(1)}, f32[16,512]{1,0:T(8,128)S(1)}, u32[]{:S(2)}, u32[]{:S(2)}) collective-permute-start(f32[16,512]{1,0:T(8,128)S(1)} %get-tuple-element.27), channel_id=1, source_target_pairs={{0,2},{1,3},{2,0},{3,1},{4,6},{5,7},{6,4},{7,5},{8,10},{9,11},{10,... | collective-permute-start | bytes 98312 | tf_op jit(solution)/shard_map/ppermute | solution.py:22
  13.0 4.3 %collective-permute-start.4 = (s32[1]{0:T(128)}, s32[1]{0:T(128)}, u32[]{:S(2)}, u32[]{:S(2)}) collective-permute-start(s32[1]{0:T(128)} %param.10), channel_id=1, source_target_pairs={{4,0},{0,4},{12,8},{8,12},{20,16},{16,20},{28,24},{24,28},{5,1},{1... | collective-permute-start | bytes 20 | tf_op jit(solution)/shard_map/ppermute | solution.py:80
  18.0 1.0 %multiply_reduce_fusion.8 = f32[2048]{0:T(1024)S(1)} fusion(bf16[1,64,2048]{2,1,0:T(8,128)(2,1)} %param.7), kind=kLoop, calls=%fused_computation.21 | loop fusion | flops 391168 | bytes 270336 | tf_op jit(solution)/shard_map/reduce_sum | solution.py:41
  19.0 2.3 %collective-permute-done.4 = s32[1]{0:T(128)} collective-permute-done((s32[1]{0:T(128)}, s32[1]{0:T(128)}, u32[]{:S(2)}, u32[]{:S(2)}) %collective-permute-start.4) | collective-permute-done | bytes 36 | tf_op jit(solution)/shard_map/ppermute | solution.py:80
  23.5 2.4 %collective-permute-start.5 = (f32[16,2048]{1,0:T(8,128)S(1)}, f32[16,2048]{1,0:T(8,128)S(1)}, u32[]{:S(2)}, u32[]{:S(2)}) collective-permute-start(f32[16,2048]{1,0:T(8,128)S(1)} %constant_dynamic-update-slice_fusion.3), channel_id=1, source_target_pairs={{4,0},{0,4},{12,8},{8,12},{20,16},{16,20},{28,24},{24,28},{5,1},{1... | collective-permute-start | bytes 393224 | tf_op jit(solution)/shard_map/ppermute | solution.py:79
  26.1 3.6 %exponential_convert_fusion.1 = bf16[2048,2048]{1,0:T(8,128)(2,1)S(1)} fusion(bf16[64,2048]{1,0:T(8,128)(2,1)S(1)} %collective-permute-done.3, f32[2048]{0:T(1024)S(1)} %multiply_reduce_fusion.10, f32[2048]{0:T(1024)S(1)} %multiply_reduce_fusion.11, bf16[1,64,2048]{2,1,0:T(8,128)(2,1)S(1)} %all-gather), kind=kOutput, calls=%fused_computation.1 | convolution fusion | flops 557842432 | bytes 8929280 | tf_op jit(solution)/shard_map/dot_general | solution.py:45
  29.7 1.3 %fusion.31 = (f32[16]{0:T(128)S(1)}, f32[16,2048]{1,0:T(8,128)S(1)}) fusion(f32[2048]{0:T(1024)S(1)} %fusion.14, bf16[2048,2048]{1,0:T(8,128)(2,1)S(1)} %exponential_convert_fusion.1, f32[16,2048]{1,0:T(8,128)S(1)} %constant_dynamic-update-slice_fusion.3, f32[2048]{0:T(1024)S(1)} %fusion.13), kind=kOutput, calls=%fused_computation.103 | convolution fusion | flops 134348784 | bytes 8667200 | tf_op jit(solution)/shard_map/dot_general | solution.py:109
  31.1 3.5 %collective-permute-start.6 = (bf16[16,2048]{1,0:T(8,128)(2,1)S(1)}, bf16[16,2048]{1,0:T(8,128)(2,1)S(1)}, u32[]{:S(2)}, u32[]{:S(2)}) collective-permute-start(bf16[16,2048]{1,0:T(8,128)(2,1)S(1)} %get-tuple-element.16), channel_id=1, source_target_pairs={{0,8},{28,20},{1,9},{29,21},{2,10},{30,22},{3,11},{31,23}} | collective-permute-start | bytes 196616 | tf_op jit(solution)/shard_map/ppermute | solution.py:117
  34.7 3.6 %exponential_convert_fusion = bf16[2048,2048]{1,0:T(8,128)(2,1)S(1)} fusion(bf16[64,2048]{1,0:T(8,128)(2,1)S(1)} %collective-permute-done.7, f32[2048]{0:T(1024)S(1)} %multiply_reduce_fusion.11, f32[2048]{0:T(1024)S(1)} %multiply_reduce_fusion.9, bf16[1,64,2048]{2,1,0:T(8,128)(2,1)S(1)} %all-gather), kind=kOutput, calls=%fused_computation | convolution fusion | flops 557842432 | bytes 8929280 | tf_op jit(solution)/shard_map/dot_general | solution.py:45
  38.3 1.3 %fusion.32 = (f32[16]{0:T(128)S(1)}, f32[16,2048]{1,0:T(8,128)S(1)}) fusion(f32[2048]{0:T(1024)S(1)} %fusion.13, bf16[16,2048]{1,0:T(8,128)(2,1)S(1)} %collective-permute-done.6, bf16[2048,2048]{1,0:T(8,128)(2,1)S(1)} %exponential_convert_fusion), kind=kOutput, calls=%fused_computation.104 | convolution fusion | flops 134283248 | bytes 8593472 | tf_op jit(solution)/shard_map/dot_general | solution.py:101
  39.6 1.4 %fusion.33 = (f32[16]{0:T(128)S(1)}, f32[16,2048]{1,0:T(8,128)S(1)}) fusion(f32[2048]{0:T(1024)S(1)} %fusion.14, bf16[2048,2048]{1,0:T(8,128)(2,1)S(1)} %exponential_convert_fusion.1, f32[16,2048]{1,0:T(8,128)S(1)} %constant_dynamic-update-slice_fusion.3, f32[16]{0:T(128)S(1)} %get-tuple-element.44, f32[16,2048]{1,0:T(8,128)S(1)} %get-tuple-element.45, ...), kind=kOutput, calls=%fused_computation.105 | convolution fusion | flops 134414320 | bytes 8790148 | tf_op jit(solution)/shard_map/dot_general | solution.py:109
  41.9 2.9 %negate_exponential_fusion = f32[2048,512]{1,0:T(8,128)} fusion(f32[512]{0:T(512)S(1)} %get-tuple-element.39, f32[2048]{0:T(1024)S(1)} %multiply_reduce_fusion.11, bf16[64,2048]{1,0:T(8,128)(2,1)S(1)} %bitcast.49, bf16[1,64,2048]{2,1,0:T(8,128)(2,1)S(1)} %all-gather), kind=kOutput, calls=%fused_computation.4 | convolution fusion | flops 138412032 | bytes 4532224 | tf_op jit(solution)/shard_map/dot_general | solution.py:45
  44.8 1.3 %fusion.34 = (f32[16]{0:T(128)S(1)}, f32[16,2048]{1,0:T(8,128)S(1)}) fusion(f32[2048]{0:T(1024)S(1)} %fusion.13, bf16[16,2048]{1,0:T(8,128)(2,1)S(1)} %collective-permute-done.8, bf16[2048,2048]{1,0:T(8,128)(2,1)S(1)} %exponential_convert_fusion), kind=kOutput, calls=%fused_computation.106 | convolution fusion | flops 134283248 | bytes 8593472 | tf_op jit(solution)/shard_map/dot_general | solution.py:101
  46.1 1.4 %fusion.35 = (f32[16]{0:T(128)S(1)}, f32[16,2048]{1,0:T(8,128)S(1)}) fusion(f32[2048]{0:T(1024)S(1)} %fusion.14, bf16[2048,2048]{1,0:T(8,128)(2,1)S(1)} %exponential_convert_fusion.1, f32[16,2048]{1,0:T(8,128)S(1)} %constant_dynamic-update-slice_fusion.3, f32[16]{0:T(128)S(1)} %get-tuple-element.48, f32[16,2048]{1,0:T(8,128)S(1)} %get-tuple-element.49, ...), kind=kOutput, calls=%fused_computation.107 | convolution fusion | flops 134414320 | bytes 8790148 | tf_op jit(solution)/shard_map/dot_general | solution.py:109
  48.2 2.9 %negate_exponential_fusion.1 = f32[2048,512]{1,0:T(8,128)} fusion(f32[512]{0:T(512)S(1)} %get-tuple-element.40, f32[2048]{0:T(1024)S(1)} %multiply_reduce_fusion.11, bf16[64,2048]{1,0:T(8,128)(2,1)S(1)} %bitcast.50, bf16[1,64,2048]{2,1,0:T(8,128)(2,1)S(1)} %all-gather), kind=kOutput, calls=%fused_computation.7 | convolution fusion | flops 138412032 | bytes 4532224 | tf_op jit(solution)/shard_map/dot_general | solution.py:45
  51.1 1.3 %collective-permute-start.13 = (f32[16,2048]{1,0:T(8,128)S(1)}, f32[16,2048]{1,0:T(8,128)S(1)}, u32[]{:S(2)}, u32[]{:S(2)}) collective-permute-start(f32[16,2048]{1,0:T(8,128)S(1)} %get-tuple-element.17), channel_id=1, source_target_pairs={{0,4},{28,24},{1,5},{29,25},{2,6},{30,26},{3,7},{31,27}} | collective-permute-start | bytes 393224 | tf_op jit(solution)/shard_map/ppermute | solution.py:120
  53.8 1.3 %fusion.36 = (f32[16]{0:T(128)S(1)}, f32[16,2048]{1,0:T(8,128)S(1)}) fusion(f32[2048]{0:T(1024)S(1)} %fusion.13, bf16[16,2048]{1,0:T(8,128)(2,1)S(1)} %collective-permute-done.9, bf16[2048,2048]{1,0:T(8,128)(2,1)S(1)} %exponential_convert_fusion), kind=kOutput, calls=%fused_computation.108 | convolution fusion | flops 134283248 | bytes 8593472 | tf_op jit(solution)/shard_map/dot_general | solution.py:101
  55.1 1.4 %fusion.37 = (f32[16]{0:T(128)S(1)}, f32[16,2048]{1,0:T(8,128)S(1)}) fusion(f32[2048]{0:T(1024)S(1)} %fusion.14, bf16[2048,2048]{1,0:T(8,128)(2,1)S(1)} %exponential_convert_fusion.1, f32[16,2048]{1,0:T(8,128)S(1)} %constant_dynamic-update-slice_fusion.3, f32[16]{0:T(128)S(1)} %get-tuple-element.52, f32[16,2048]{1,0:T(8,128)S(1)} %get-tuple-element.53, ...), kind=kOutput, calls=%fused_computation.109 | convolution fusion | flops 134414320 | bytes 8790148 | tf_op jit(solution)/shard_map/dot_general | solution.py:109
  56.6 1.3 %collective-permute-start.10 = (f32[16,2048]{1,0:T(8,128)S(1)}, f32[16,2048]{1,0:T(8,128)S(1)}, u32[]{:S(2)}, u32[]{:S(2)}) collective-permute-start(f32[16,2048]{1,0:T(8,128)S(1)} %multiply_divide_fusion), channel_id=1, source_target_pairs={{24,28},{4,0},{25,29},{5,1},{26,30},{6,2},{27,31},{7,3}} | collective-permute-start | bytes 393224 | tf_op jit(solution)/shard_map/ppermute | solution.py:120
  57.9 2.9 %negate_exponential_fusion.3 = f32[2048,512]{1,0:T(8,128)} fusion(f32[512]{0:T(512)S(1)} %get-tuple-element.38, f32[2048]{0:T(1024)S(1)} %multiply_reduce_fusion.11, bf16[64,2048]{1,0:T(8,128)(2,1)S(1)} %bitcast.51, bf16[1,64,2048]{2,1,0:T(8,128)(2,1)S(1)} %all-gather), kind=kOutput, calls=%fused_computation.13 | convolution fusion | flops 138412032 | bytes 4532224 | tf_op jit(solution)/shard_map/dot_general | solution.py:45
  61.5 2.8 %collective-permute-done.10 = f32[16,2048]{1,0:T(8,128)S(1)} collective-permute-done((f32[16,2048]{1,0:T(8,128)S(1)}, f32[16,2048]{1,0:T(8,128)S(1)}, u32[]{:S(2)}, u32[]{:S(2)}) %collective-permute-start.10) | collective-permute-done | bytes 131104 | tf_op jit(solution)/shard_map/ppermute | solution.py:120
  64.6 1.2 %collective-permute-start.18 = (f32[1,2048]{1,0:T(1,128)S(1)}, f32[1,2048]{1,0:T(1,128)S(1)}, u32[]{:S(2)}, u32[]{:S(2)}) collective-permute-start(f32[1,2048]{1,0:T(1,128)S(1)} %bitcast.54), channel_id=1, source_target_pairs={{0,2},{1,3},{2,0},{3,1},{4,6},{5,7},{6,4},{7,5},{8,10},{9,11},{10,... | collective-permute-start | bytes 24584 | tf_op jit(solution)/shard_map/ppermute | solution.py:22
  65.7 1.4 %collective-permute-start.19 = (f32[1,2048]{1,0:T(1,128)S(1)}, f32[1,2048]{1,0:T(1,128)S(1)}, u32[]{:S(2)}, u32[]{:S(2)}) collective-permute-start(f32[1,2048]{1,0:T(1,128)S(1)} %bitcast.55), channel_id=1, source_target_pairs={{0,3},{1,0},{2,1},{3,2},{4,7},{5,4},{6,5},{7,6},{8,11},{9,8},{10,9... | collective-permute-start | bytes 24584 | tf_op jit(solution)/shard_map/ppermute | solution.py:22
  69.2 5.9 %multiply_reduce_fusion.5 = (f32[512]{0:T(512)S(1)}, f32[512]{0:T(512)S(1)}, f32[512]{0:T(512)S(1)}, f32[512]{0:T(512)S(1)}, f32[2048,512]{1,0:T(8,128)S(1)}) fusion(f32[2048]{0:T(1024)S(1)} %get-tuple-element.8, f32[2048,512]{1,0:T(8,128)} %negate_exponential_fusion.1, f32[2048,512]{1,0:T(8,128)} %negate_exponential_fusion, ...), kind=kOutput, calls=%fused_computation.9 | convolution fusion | flops 146798592 | bytes 17131520 | tf_op jit(solution)/shard_map/dot_general | solution.py:45
  77.0 1.6 %copy-done.2 = f32[2048,512]{1,0:T(8,128)S(1)} copy-done((f32[2048,512]{1,0:T(8,128)S(1)}, f32[2048,512]{1,0:T(8,128)}, u32[]{:S(2)}) %copy-start.2) | copy-done | bytes 4194328
  79.4 1.0 %collective-permute-start.20 = (f32[512]{0:T(512)S(1)}, f32[512]{0:T(512)S(1)}, u32[]{:S(2)}, u32[]{:S(2)}) collective-permute-start(f32[512]{0:T(512)S(1)} %get-tuple-element.32), channel_id=1, source_target_pairs={{0,1},{1,2},{2,3},{3,0},{4,5},{5,6},{6,7},{7,4},{8,9},{9,10},{10,1... | collective-permute-start | bytes 6152 | tf_op jit(solution)/shard_map/ppermute | solution.py:22
  80.4 1.1 %collective-permute-start.21 = (f32[512]{0:T(512)S(1)}, f32[512]{0:T(512)S(1)}, u32[]{:S(2)}, u32[]{:S(2)}) collective-permute-start(f32[512]{0:T(512)S(1)} %get-tuple-element.31), channel_id=1, source_target_pairs={{0,2},{1,3},{2,0},{3,1},{4,6},{5,7},{6,4},{7,5},{8,10},{9,11},{10,... | collective-permute-start | bytes 6152 | tf_op jit(solution)/shard_map/ppermute | solution.py:22
  82.1 1.0 %collective-permute-start.15 = (f32[2,16,512]{2,1,0:T(8,128)S(1)}, f32[2,16,512]{2,1,0:T(8,128)S(1)}, u32[]{:S(2)}, u32[]{:S(2)}) collective-permute-start(f32[2,16,512]{2,1,0:T(8,128)S(1)} %get-tuple-element.23), channel_id=1, source_target_pairs={{0,2},{1,3},{2,0},{3,1},{4,6},{5,7},{6,4},{7,5},{8,10},{9,11},{10,... | collective-permute-start | bytes 196616 | tf_op jit(solution)/shard_map/ppermute | solution.py:22
  83.1 1.4 %collective-permute-start.16 = (f32[2,16,512]{2,1,0:T(8,128)S(1)}, f32[2,16,512]{2,1,0:T(8,128)S(1)}, u32[]{:S(2)}, u32[]{:S(2)}) collective-permute-start(f32[2,16,512]{2,1,0:T(8,128)S(1)} %get-tuple-element.20), channel_id=1, source_target_pairs={{0,3},{1,0},{2,1},{3,2},{4,7},{5,4},{6,5},{7,6},{8,11},{9,8},{10,9... | collective-permute-start | bytes 196616 | tf_op jit(solution)/shard_map/ppermute | solution.py:22
  85.8 1.3 %collective-permute-done.15 = f32[2,16,512]{2,1,0:T(8,128)S(1)} collective-permute-done((f32[2,16,512]{2,1,0:T(8,128)S(1)}, f32[2,16,512]{2,1,0:T(8,128)S(1)}, u32[]{:S(2)}, u32[]{:S(2)}) %collective-permute-start.15) | collective-permute-done | bytes 65568 | tf_op jit(solution)/shard_map/ppermute | solution.py:22
  (81 shorter events, 14.3 us)
Async XLA Ops:
  8.1 17.9 %collective-permute-start.3 = (bf16[64,2048]{1,0:T(8,128)(2,1)S(1)}, bf16[64,2048]{1,0:T(8,128)(2,1)S(1)}, u32[]{:S(2)}, u32[]{:S(2)}) collective-permute-start(bf16[64,2048]{1,0:T(8,128)(2,1)S(1)} %bitcast.47), channel_id=1, source_target_pairs={{4,0},{0,4},{12,8},{8,12},{20,16},{16,20},{28,24},{24,28},{5,1},{1... | collective-permute-start | bytes 786440 | tf_op jit(solution)/shard_map/ppermute | solution.py:75
  9.6 25.0 %collective-permute-start.7 = (bf16[64,2048]{1,0:T(8,128)(2,1)S(1)}, bf16[64,2048]{1,0:T(8,128)(2,1)S(1)}, u32[]{:S(2)}, u32[]{:S(2)}) collective-permute-start(bf16[64,2048]{1,0:T(8,128)(2,1)S(1)} %bitcast.48), channel_id=1, source_target_pairs={{8,4},{4,8},{16,12},{12,16},{24,20},{20,24},{9,5},{5,9},{17,13},{1... | collective-permute-start | bytes 786440 | tf_op jit(solution)/shard_map/ppermute | solution.py:83
  11.3 12.0 %collective-permute-start = (f32[16,512]{1,0:T(8,128)S(1)}, f32[16,512]{1,0:T(8,128)S(1)}, u32[]{:S(2)}, u32[]{:S(2)}) collective-permute-start(f32[16,512]{1,0:T(8,128)S(1)} %get-tuple-element.28), channel_id=1, source_target_pairs={{0,1},{1,2},{2,3},{3,0},{4,5},{5,6},{6,7},{7,4},{8,9},{9,10},{10,1... | collective-permute-start | bytes 98312 | tf_op jit(solution)/shard_map/ppermute | solution.py:22
  11.4 11.9 %collective-permute-start.1 = (f32[16,512]{1,0:T(8,128)S(1)}, f32[16,512]{1,0:T(8,128)S(1)}, u32[]{:S(2)}, u32[]{:S(2)}) collective-permute-start(f32[16,512]{1,0:T(8,128)S(1)} %get-tuple-element.27), channel_id=1, source_target_pairs={{0,2},{1,3},{2,0},{3,1},{4,6},{5,7},{6,4},{7,5},{8,10},{9,11},{10,... | collective-permute-start | bytes 98312 | tf_op jit(solution)/shard_map/ppermute | solution.py:22
  13.0 8.4 %collective-permute-start.4 = (s32[1]{0:T(128)}, s32[1]{0:T(128)}, u32[]{:S(2)}, u32[]{:S(2)}) collective-permute-start(s32[1]{0:T(128)} %param.10), channel_id=1, source_target_pairs={{4,0},{0,4},{12,8},{8,12},{20,16},{16,20},{28,24},{24,28},{5,1},{1... | collective-permute-start | bytes 20 | tf_op jit(solution)/shard_map/ppermute | solution.py:80
  21.3 2.2 %collective-permute-start.2 = (f32[16,512]{1,0:T(8,128)S(1)}, f32[16,512]{1,0:T(8,128)S(1)}, u32[]{:S(2)}, u32[]{:S(2)}) collective-permute-start(f32[16,512]{1,0:T(8,128)S(1)} %get-tuple-element.26), channel_id=1, source_target_pairs={{0,3},{1,0},{2,1},{3,2},{4,7},{5,4},{6,5},{7,6},{8,11},{9,8},{10,9... | collective-permute-start | bytes 98312 | tf_op jit(solution)/shard_map/ppermute | solution.py:22
  23.5 7.4 %collective-permute-start.5 = (f32[16,2048]{1,0:T(8,128)S(1)}, f32[16,2048]{1,0:T(8,128)S(1)}, u32[]{:S(2)}, u32[]{:S(2)}) collective-permute-start(f32[16,2048]{1,0:T(8,128)S(1)} %constant_dynamic-update-slice_fusion.3), channel_id=1, source_target_pairs={{4,0},{0,4},{12,8},{8,12},{20,16},{16,20},{28,24},{24,28},{5,1},{1... | collective-permute-start | bytes 393224 | tf_op jit(solution)/shard_map/ppermute | solution.py:79
  31.1 7.2 %collective-permute-start.6 = (bf16[16,2048]{1,0:T(8,128)(2,1)S(1)}, bf16[16,2048]{1,0:T(8,128)(2,1)S(1)}, u32[]{:S(2)}, u32[]{:S(2)}) collective-permute-start(bf16[16,2048]{1,0:T(8,128)(2,1)S(1)} %get-tuple-element.16), channel_id=1, source_target_pairs={{0,8},{28,20},{1,9},{29,21},{2,10},{30,22},{3,11},{31,23}} | collective-permute-start | bytes 196616 | tf_op jit(solution)/shard_map/ppermute | solution.py:117
  39.6 2.3 %copy-start.3 = (bf16[1,64,2048]{2,1,0:T(8,128)(2,1)S(1)}, bf16[1,64,2048]{2,1,0:T(8,128)(2,1)}, u32[]{:S(2)}) copy-start(bf16[1,64,2048]{2,1,0:T(8,128)(2,1)} %param.7) | copy-start | bytes 786436
  41.0 3.7 %collective-permute-start.8 = (bf16[16,2048]{1,0:T(8,128)(2,1)S(1)}, bf16[16,2048]{1,0:T(8,128)(2,1)S(1)}, u32[]{:S(2)}, u32[]{:S(2)}) collective-permute-start(bf16[16,2048]{1,0:T(8,128)(2,1)S(1)} %get-tuple-element.14), channel_id=1, source_target_pairs={{8,16},{20,12},{9,17},{21,13},{10,18},{22,14},{11,19},{23,15}} | collective-permute-start | bytes 196616 | tf_op jit(solution)/shard_map/ppermute | solution.py:117
  47.6 6.2 %collective-permute-start.9 = (bf16[16,2048]{1,0:T(8,128)(2,1)S(1)}, bf16[16,2048]{1,0:T(8,128)(2,1)S(1)}, u32[]{:S(2)}, u32[]{:S(2)}) collective-permute-start(bf16[16,2048]{1,0:T(8,128)(2,1)S(1)} %get-tuple-element.12), channel_id=1, source_target_pairs={{16,24},{12,4},{17,25},{13,5},{18,26},{14,6},{19,27},{15,7}} | collective-permute-start | bytes 196616 | tf_op jit(solution)/shard_map/ppermute | solution.py:117
  51.1 10.4 %collective-permute-start.13 = (f32[16,2048]{1,0:T(8,128)S(1)}, f32[16,2048]{1,0:T(8,128)S(1)}, u32[]{:S(2)}, u32[]{:S(2)}) collective-permute-start(f32[16,2048]{1,0:T(8,128)S(1)} %get-tuple-element.17), channel_id=1, source_target_pairs={{0,4},{28,24},{1,5},{29,25},{2,6},{30,26},{3,7},{31,27}} | collective-permute-start | bytes 393224 | tf_op jit(solution)/shard_map/ppermute | solution.py:120
  52.4 9.1 %collective-permute-start.12 = (f32[16,2048]{1,0:T(8,128)S(1)}, f32[16,2048]{1,0:T(8,128)S(1)}, u32[]{:S(2)}, u32[]{:S(2)}) collective-permute-start(f32[16,2048]{1,0:T(8,128)S(1)} %get-tuple-element.15), channel_id=1, source_target_pairs={{8,12},{20,16},{9,13},{21,17},{10,14},{22,18},{11,15},{23,19}} | collective-permute-start | bytes 393224 | tf_op jit(solution)/shard_map/ppermute | solution.py:120
  53.1 8.4 %collective-permute-start.11 = (f32[16,2048]{1,0:T(8,128)S(1)}, f32[16,2048]{1,0:T(8,128)S(1)}, u32[]{:S(2)}, u32[]{:S(2)}) collective-permute-start(f32[16,2048]{1,0:T(8,128)S(1)} %get-tuple-element.13), channel_id=1, source_target_pairs={{16,20},{12,8},{17,21},{13,9},{18,22},{14,10},{19,23},{15,11}} | collective-permute-start | bytes 393224 | tf_op jit(solution)/shard_map/ppermute | solution.py:120
  56.6 7.8 %collective-permute-start.10 = (f32[16,2048]{1,0:T(8,128)S(1)}, f32[16,2048]{1,0:T(8,128)S(1)}, u32[]{:S(2)}, u32[]{:S(2)}) collective-permute-start(f32[16,2048]{1,0:T(8,128)S(1)} %multiply_divide_fusion), channel_id=1, source_target_pairs={{24,28},{4,0},{25,29},{5,1},{26,30},{6,2},{27,31},{7,3}} | collective-permute-start | bytes 393224 | tf_op jit(solution)/shard_map/ppermute | solution.py:120
  64.5 3.1 %collective-permute-start.17 = (f32[1,2048]{1,0:T(1,128)S(1)}, f32[1,2048]{1,0:T(1,128)S(1)}, u32[]{:S(2)}, u32[]{:S(2)}) collective-permute-start(f32[1,2048]{1,0:T(1,128)S(1)} %bitcast.53), channel_id=1, source_target_pairs={{0,1},{1,2},{2,3},{3,0},{4,5},{5,6},{6,7},{7,4},{8,9},{9,10},{10,1... | collective-permute-start | bytes 24584 | tf_op jit(solution)/shard_map/ppermute | solution.py:22
  64.6 3.7 %collective-permute-start.18 = (f32[1,2048]{1,0:T(1,128)S(1)}, f32[1,2048]{1,0:T(1,128)S(1)}, u32[]{:S(2)}, u32[]{:S(2)}) collective-permute-start(f32[1,2048]{1,0:T(1,128)S(1)} %bitcast.54), channel_id=1, source_target_pairs={{0,2},{1,3},{2,0},{3,1},{4,6},{5,7},{6,4},{7,5},{8,10},{9,11},{10,... | collective-permute-start | bytes 24584 | tf_op jit(solution)/shard_map/ppermute | solution.py:22
  65.7 2.8 %collective-permute-start.19 = (f32[1,2048]{1,0:T(1,128)S(1)}, f32[1,2048]{1,0:T(1,128)S(1)}, u32[]{:S(2)}, u32[]{:S(2)}) collective-permute-start(f32[1,2048]{1,0:T(1,128)S(1)} %bitcast.55), channel_id=1, source_target_pairs={{0,3},{1,0},{2,1},{3,2},{4,7},{5,4},{6,5},{7,6},{8,11},{9,8},{10,9... | collective-permute-start | bytes 24584 | tf_op jit(solution)/shard_map/ppermute | solution.py:22
  69.2 6.8 %copy-start = (f32[2048,512]{1,0:T(8,128)S(1)}, f32[2048,512]{1,0:T(8,128)}, u32[]{:S(2)}) copy-start(f32[2048,512]{1,0:T(8,128)} %negate_exponential_fusion) | copy-start | bytes 12582916
  69.2 7.1 %copy-start.1 = (f32[2048,512]{1,0:T(8,128)S(1)}, f32[2048,512]{1,0:T(8,128)}, u32[]{:S(2)}) copy-start(f32[2048,512]{1,0:T(8,128)} %negate_exponential_fusion.1) | copy-start | bytes 12582916
  76.3 2.2 %copy-start.2 = (f32[2048,512]{1,0:T(8,128)S(1)}, f32[2048,512]{1,0:T(8,128)}, u32[]{:S(2)}) copy-start(f32[2048,512]{1,0:T(8,128)} %negate_exponential_fusion.3) | copy-start | bytes 12582916
  79.4 3.7 %collective-permute-start.20 = (f32[512]{0:T(512)S(1)}, f32[512]{0:T(512)S(1)}, u32[]{:S(2)}, u32[]{:S(2)}) collective-permute-start(f32[512]{0:T(512)S(1)} %get-tuple-element.32), channel_id=1, source_target_pairs={{0,1},{1,2},{2,3},{3,0},{4,5},{5,6},{6,7},{7,4},{8,9},{9,10},{10,1... | collective-permute-start | bytes 6152 | tf_op jit(solution)/shard_map/ppermute | solution.py:22
  80.4 4.3 %collective-permute-start.21 = (f32[512]{0:T(512)S(1)}, f32[512]{0:T(512)S(1)}, u32[]{:S(2)}, u32[]{:S(2)}) collective-permute-start(f32[512]{0:T(512)S(1)} %get-tuple-element.31), channel_id=1, source_target_pairs={{0,2},{1,3},{2,0},{3,1},{4,6},{5,7},{6,4},{7,5},{8,10},{9,11},{10,... | collective-permute-start | bytes 6152 | tf_op jit(solution)/shard_map/ppermute | solution.py:22
  81.5 3.4 %collective-permute-start.22 = (f32[512]{0:T(512)S(1)}, f32[512]{0:T(512)S(1)}, u32[]{:S(2)}, u32[]{:S(2)}) collective-permute-start(f32[512]{0:T(512)S(1)} %get-tuple-element.30), channel_id=1, source_target_pairs={{0,3},{1,0},{2,1},{3,2},{4,7},{5,4},{6,5},{7,6},{8,11},{9,8},{10,9... | collective-permute-start | bytes 6152 | tf_op jit(solution)/shard_map/ppermute | solution.py:22
  82.0 3.8 %collective-permute-start.14 = (f32[2,16,512]{2,1,0:T(8,128)S(1)}, f32[2,16,512]{2,1,0:T(8,128)S(1)}, u32[]{:S(2)}, u32[]{:S(2)}) collective-permute-start(f32[2,16,512]{2,1,0:T(8,128)S(1)} %get-tuple-element.22), channel_id=1, source_target_pairs={{0,1},{1,2},{2,3},{3,0},{4,5},{5,6},{6,7},{7,4},{8,9},{9,10},{10,1... | collective-permute-start | bytes 196616 | tf_op jit(solution)/shard_map/ppermute | solution.py:22
  82.1 5.0 %collective-permute-start.15 = (f32[2,16,512]{2,1,0:T(8,128)S(1)}, f32[2,16,512]{2,1,0:T(8,128)S(1)}, u32[]{:S(2)}, u32[]{:S(2)}) collective-permute-start(f32[2,16,512]{2,1,0:T(8,128)S(1)} %get-tuple-element.23), channel_id=1, source_target_pairs={{0,2},{1,3},{2,0},{3,1},{4,6},{5,7},{6,4},{7,5},{8,10},{9,11},{10,... | collective-permute-start | bytes 196616 | tf_op jit(solution)/shard_map/ppermute | solution.py:22
  83.1 4.0 %collective-permute-start.16 = (f32[2,16,512]{2,1,0:T(8,128)S(1)}, f32[2,16,512]{2,1,0:T(8,128)S(1)}, u32[]{:S(2)}, u32[]{:S(2)}) collective-permute-start(f32[2,16,512]{2,1,0:T(8,128)S(1)} %get-tuple-element.20), channel_id=1, source_target_pairs={{0,3},{1,0},{2,1},{3,2},{4,7},{5,4},{6,5},{7,6},{8,11},{9,8},{10,9... | collective-permute-start | bytes 196616 | tf_op jit(solution)/shard_map/ppermute | solution.py:22

commit v22 on v21

--- a/solution.py
+++ b/solution.py
@@ -21,6 +21,22 @@
         if shift:
             piece = lax.ppermute(piece, "pt", [(i, (i + shift) % count) for i in range(count)])
         out = lax.dynamic_update_slice_in_dim(out, piece, ((rank - shift) % count) * put, put_axis)
+    return out
+
+
+def gather_over_pt(x, axis):
+    count = lax.axis_size("pt")
+    rank = lax.axis_index("pt")
+    shape = list(x.shape)
+    shape[axis] *= count
+    out = jnp.zeros(shape, x.dtype)
+    for shift in range(count):
+        piece = x if shift == 0 else lax.ppermute(
+            x, "pt", [((i + shift) % count, i) for i in range(count)]
+        )
+        out = lax.dynamic_update_slice_in_dim(
+            out, piece, ((rank + shift) % count) * x.shape[axis], axis
+        )
     return out
 
 
@@ -54,7 +70,7 @@
     day_count = lax.axis_size("day")
     own_pts = points[0]
     per_device = own_pts.shape[1]
-    day_pts = lax.all_gather(own_pts, "pt", axis=1, tiled=True)
+    day_pts = gather_over_pt(own_pts, 1)
     support_total = day_pts.shape[1]
     own_weight = clone_weight[0] * potential[0][None, :]
     block_rows = own_weight.shape[0] // lax.axis_size("pt")

time: 88.6 us -> 90.2 us (1.018)
  blocking collectives: 7.46 us -> 0 us
  waiting for transfers between devices: 7.62 us -> 12.7 us
  starting transfers between devices: 27.7 us -> 30.8 us
  local copies, waits for them, and re-layouts: 3.98 us -> 4.92 us
    all_gather x1 -> x0, blocking collectives: 7.46 us -> none  [shards(): day_pts = lax.all_gather(own_pts, 'pt', axis=1, tiled=True)]
    ppermute x1, waiting for transfers between devices: 0.01 us -> 6.3 us  [shards(): other_pts = lax.ppermute(day_pts, 'day', pair_route)]
    ppermute x3, starting transfers between devices: 4.98 us -> 10.1 us  [shards(): lax.ppermute(outgoing, 'day', [(forward_day, forward_day + 2), (backward_...]
    ppermute x0 -> x3, starting transfers between devices: none -> 3.28 us  [gather_over_pt(): lax.ppermute(x, 'pt', [((i + shift) % count, i) for i in range(count)])]
    ppermute x1, starting transfers between devices: 4.27 us -> 1.49 us  [shards(): other_count = lax.ppermute(support_count, 'day', pair_route)[0]]
    ppermute x1, waiting for transfers between devices: 2.3 us -> 0.01 us  [shards(): other_count = lax.ppermute(support_count, 'day', pair_route)[0]]
    ppermute x1, starting transfers between devices: 2.45 us -> 0.68 us  [shards(): other_weight = lax.ppermute(block_weight, 'day', pair_route)]
  transfers between devices with their start and end apart: 23 -> 26, of which waited for: 7 -> 8; matrix products, arithmetic and copies ran while one was open for 28% -> 28% of each run, Pallas kernels for 0% -> 0%
where the time goes in v22:
time: 90.2 us; the launch traced here: 89.7 us
  matrix products  31.1 us (34%)
  starting transfers between devices  30.8 us (34%)
  waiting for transfers between devices  12.7 us (14%)
  other arithmetic  6.86 us (8%)
  local copies, waits for them, and re-layouts  4.92 us (5%)
  between operations  3.3 us (4%)
    dot_general x6, matrix products, squared_dist(): lax.dot_general(left_pts, right_pts, (((0,), (0,)), ((), ())), preferred_...  21.7 us
    ppermute x12, starting transfers between devices, swap_blocks(): lax.ppermute(piece, 'pt', [(i, (i + shift) % count) for i in range(count)])  10.1 us
    ppermute x3, starting transfers between devices, shards(): lax.ppermute(outgoing, 'day', [(forward_day, forward_day + 2), (backward_...  10.1 us
    ppermute x1, waiting for transfers between devices, shards(): other_pts = lax.ppermute(day_pts, 'day', pair_route)  6.3 us
    dot_general x4, matrix products, shards(): jnp.dot(sent, other_kernel, preferred_element_type=jnp.float32)  5.4 us
    dot_general x3, matrix products, shards(): jnp.dot(incoming, link_kernel, preferred_element_type=jnp.float32)  3.92 us
    ppermute x4, starting transfers between devices, shards(): lax.ppermute(following, 'day', [(forward_day, forward_day + 1), (backward...  3.92 us
    ppermute x3, starting transfers between devices, gather_over_pt(): lax.ppermute(x, 'pt', [((i + shift) % count, i) for i in range(count)])  3.28 us
  transfers between devices with their start and end apart: 26, of which 8 were waited for; matrix products, arithmetic and copies ran while one was open for 28% of the time, Pallas kernels for 0%

profile of v22, /device:TPU:0, one launch (start us, length us, event | category | flops | bytes accessed | tf_op | source)
XLA Modules:
  0.0 89.7 jit_solution(13599034784484387736)
XLA Ops:
  0.6 2.5 %collective-permute-start.3 = (bf16[64,512]{1,0:T(8,128)(2,1)}, bf16[64,512]{1,0:T(8,128)(2,1)S(1)}, u32[]{:S(2)}, u32[]{:S(2)}) collective-permute-start(bf16[64,512]{1,0:T(8,128)(2,1)} %bitcast.43), channel_id=1, source_target_pairs={{1,0},{2,1},{3,2},{0,3},{5,4},{6,5},{7,6},{4,7},{9,8},{10,9},{11,1... | collective-permute-start | bytes 196616 | tf_op jit(solution)/shard_map/ppermute | solution.py:34
  3.9 0.9 %bitcast_multiply_fusion = f32[64,512]{1,0:T(8,128)S(1)} fusion(f32[1,64,512]{2,1,0:T(8,128)} %param.8, f32[512]{0:T(512)} %bitcast.50), kind=kLoop, calls=%fused_computation.33 | loop fusion | flops 32768 | bytes 264192 | tf_op jit(solution)/shard_map/mul | solution.py:75
  4.9 1.4 %collective-permute-start = (f32[16,512]{1,0:T(8,128)S(1)}, f32[16,512]{1,0:T(8,128)S(1)}, u32[]{:S(2)}, u32[]{:S(2)}) collective-permute-start(f32[16,512]{1,0:T(8,128)S(1)} %get-tuple-element.28), channel_id=1, source_target_pairs={{0,1},{1,2},{2,3},{3,0},{4,5},{5,6},{6,7},{7,4},{8,9},{9,10},{10,1... | collective-permute-start | bytes 98312 | tf_op jit(solution)/shard_map/ppermute | solution.py:22
  6.3 1.5 %collective-permute-start.7 = (s32[1]{0:T(128)}, s32[1]{0:T(128)}, u32[]{:S(2)}, u32[]{:S(2)}) collective-permute-start(s32[1]{0:T(128)} %param.10), channel_id=1, source_target_pairs={{4,0},{0,4},{12,8},{8,12},{20,16},{16,20},{28,24},{24,28},{5,1},{1... | collective-permute-start | bytes 20 | tf_op jit(solution)/shard_map/ppermute | solution.py:96
  8.5 0.9 constant_dynamic-update-slice_fusion.6
  9.4 1.0 %multiply_reduce_fusion.8 = f32[2048]{0:T(1024)S(1)} fusion(bf16[1,64,2048]{2,1,0:T(8,128)(2,1)} %param.7), kind=kLoop, calls=%fused_computation.21 | loop fusion | flops 391168 | bytes 270336 | tf_op jit(solution)/shard_map/reduce_sum | solution.py:57
  16.9 6.3 %collective-permute-done.6 = bf16[64,2048]{1,0:T(8,128)(2,1)S(1)} collective-permute-done((bf16[64,2048]{1,0:T(8,128)(2,1)S(1)}, bf16[64,2048]{1,0:T(8,128)(2,1)S(1)}, u32[]{:S(2)}, u32[]{:S(2)}) %collective-permute-start.6) | collective-permute-done | bytes 262176 | tf_op jit(solution)/shard_map/ppermute | solution.py:91
  23.3 3.6 %exponential_convert_fusion.1 = bf16[2048,2048]{1,0:T(8,128)(2,1)S(1)} fusion(bf16[64,2048]{1,0:T(8,128)(2,1)S(1)} %constant_dynamic-update-slice_fusion.3, bf16[64,2048]{1,0:T(8,128)(2,1)S(1)} %collective-permute-done.6, f32[2048]{0:T(1024)S(1)} %multiply_reduce_fusion.10, f32[2048]{0:T(1024)S(1)} %multiply_reduce_fusion.11), kind=kOutput, calls=%fused_computation.1 | convolution fusion | flops 557842432 | bytes 8929280 | tf_op jit(solution)/shard_map/dot_general | solution.py:61
  26.9 1.3 %fusion.25 = (f32[16]{0:T(128)S(1)}, f32[16,2048]{1,0:T(8,128)S(1)}) fusion(f32[2048]{0:T(1024)S(1)} %fusion.14, bf16[2048,2048]{1,0:T(8,128)(2,1)S(1)} %exponential_convert_fusion.1, f32[16,2048]{1,0:T(8,128)S(1)} %constant_dynamic-update-slice_fusion.7, f32[2048]{0:T(1024)S(1)} %fusion.13), kind=kOutput, calls=%fused_computation.101 | convolution fusion | flops 134348784 | bytes 8667200 | tf_op jit(solution)/shard_map/dot_general | solution.py:125
  28.8 8.6 %collective-permute-start.9 = (bf16[16,2048]{1,0:T(8,128)(2,1)S(1)}, bf16[16,2048]{1,0:T(8,128)(2,1)S(1)}, u32[]{:S(2)}, u32[]{:S(2)}) collective-permute-start(bf16[16,2048]{1,0:T(8,128)(2,1)S(1)} %get-tuple-element.16), channel_id=1, source_target_pairs={{0,8},{28,20},{1,9},{29,21},{2,10},{30,22},{3,11},{31,23}} | collective-permute-start | bytes 196616 | tf_op jit(solution)/shard_map/ppermute | solution.py:133
  37.5 3.6 %exponential_convert_fusion = bf16[2048,2048]{1,0:T(8,128)(2,1)S(1)} fusion(bf16[64,2048]{1,0:T(8,128)(2,1)S(1)} %collective-permute-done.10, bf16[64,2048]{1,0:T(8,128)(2,1)S(1)} %constant_dynamic-update-slice_fusion.3, f32[2048]{0:T(1024)S(1)} %multiply_reduce_fusion.11, f32[2048]{0:T(1024)S(1)} %multiply_reduce_fusion.9), kind=kOutput, calls=%fused_computation | convolution fusion | flops 557842432 | bytes 8929280 | tf_op jit(solution)/shard_map/dot_general | solution.py:61
  41.1 1.3 %fusion.26 = (f32[16]{0:T(128)S(1)}, f32[16,2048]{1,0:T(8,128)S(1)}) fusion(f32[2048]{0:T(1024)S(1)} %fusion.13, bf16[16,2048]{1,0:T(8,128)(2,1)S(1)} %collective-permute-done.9, bf16[2048,2048]{1,0:T(8,128)(2,1)S(1)} %exponential_convert_fusion), kind=kOutput, calls=%fused_computation.102 | convolution fusion | flops 134283248 | bytes 8593472 | tf_op jit(solution)/shard_map/dot_general | solution.py:117
  42.5 1.4 %fusion.27 = (f32[16]{0:T(128)S(1)}, f32[16,2048]{1,0:T(8,128)S(1)}) fusion(f32[2048]{0:T(1024)S(1)} %fusion.14, bf16[2048,2048]{1,0:T(8,128)(2,1)S(1)} %exponential_convert_fusion.1, f32[16,2048]{1,0:T(8,128)S(1)} %constant_dynamic-update-slice_fusion.7, f32[16]{0:T(128)S(1)} %get-tuple-element.44, f32[16,2048]{1,0:T(8,128)S(1)} %get-tuple-element.45, ...), kind=kOutput, calls=%fused_computation.103 | convolution fusion | flops 134414320 | bytes 8790148 | tf_op jit(solution)/shard_map/dot_general | solution.py:125
  44.8 2.9 %negate_exponential_fusion = f32[2048,512]{1,0:T(8,128)} fusion(bf16[64,2048]{1,0:T(8,128)(2,1)S(1)} %constant_dynamic-update-slice_fusion.3, f32[512]{0:T(512)S(1)} %get-tuple-element.39, f32[2048]{0:T(1024)S(1)} %multiply_reduce_fusion.11, bf16[64,2048]{1,0:T(8,128)(2,1)S(1)} %bitcast.39), kind=kOutput, calls=%fused_computation.4 | convolution fusion | flops 138412032 | bytes 4532224 | tf_op jit(solution)/shard_map/dot_general | solution.py:61
  47.6 1.3 %fusion.28 = (f32[16]{0:T(128)S(1)}, f32[16,2048]{1,0:T(8,128)S(1)}) fusion(f32[2048]{0:T(1024)S(1)} %fusion.13, bf16[16,2048]{1,0:T(8,128)(2,1)S(1)} %collective-permute-done.11, bf16[2048,2048]{1,0:T(8,128)(2,1)S(1)} %exponential_convert_fusion), kind=kOutput, calls=%fused_computation.104 | convolution fusion | flops 134283248 | bytes 8593472 | tf_op jit(solution)/shard_map/dot_general | solution.py:117
  48.9 1.4 %fusion.29 = (f32[16]{0:T(128)S(1)}, f32[16,2048]{1,0:T(8,128)S(1)}) fusion(f32[2048]{0:T(1024)S(1)} %fusion.14, bf16[2048,2048]{1,0:T(8,128)(2,1)S(1)} %exponential_convert_fusion.1, f32[16,2048]{1,0:T(8,128)S(1)} %constant_dynamic-update-slice_fusion.7, f32[16]{0:T(128)S(1)} %get-tuple-element.48, f32[16,2048]{1,0:T(8,128)S(1)} %get-tuple-element.49, ...), kind=kOutput, calls=%fused_computation.105 | convolution fusion | flops 134414320 | bytes 8790148 | tf_op jit(solution)/shard_map/dot_general | solution.py:125
  51.1 2.9 %negate_exponential_fusion.1 = f32[2048,512]{1,0:T(8,128)} fusion(bf16[64,2048]{1,0:T(8,128)(2,1)S(1)} %constant_dynamic-update-slice_fusion.3, f32[512]{0:T(512)S(1)} %get-tuple-element.40, f32[2048]{0:T(1024)S(1)} %multiply_reduce_fusion.11, bf16[64,2048]{1,0:T(8,128)(2,1)S(1)} %bitcast.40), kind=kOutput, calls=%fused_computation.7 | convolution fusion | flops 138412032 | bytes 4532224 | tf_op jit(solution)/shard_map/dot_general | solution.py:61
  54.0 1.3 %collective-permute-start.16 = (f32[16,2048]{1,0:T(8,128)S(1)}, f32[16,2048]{1,0:T(8,128)S(1)}, u32[]{:S(2)}, u32[]{:S(2)}) collective-permute-start(f32[16,2048]{1,0:T(8,128)S(1)} %get-tuple-element.17), channel_id=1, source_target_pairs={{0,4},{28,24},{1,5},{29,25},{2,6},{30,26},{3,7},{31,27}} | collective-permute-start | bytes 393224 | tf_op jit(solution)/shard_map/ppermute | solution.py:136
  56.7 1.3 %fusion.30 = (f32[16]{0:T(128)S(1)}, f32[16,2048]{1,0:T(8,128)S(1)}) fusion(f32[2048]{0:T(1024)S(1)} %fusion.13, bf16[16,2048]{1,0:T(8,128)(2,1)S(1)} %collective-permute-done.12, bf16[2048,2048]{1,0:T(8,128)(2,1)S(1)} %exponential_convert_fusion), kind=kOutput, calls=%fused_computation.106 | convolution fusion | flops 134283248 | bytes 8593472 | tf_op jit(solution)/shard_map/dot_general | solution.py:117
  58.0 1.4 %fusion.31 = (f32[16]{0:T(128)S(1)}, f32[16,2048]{1,0:T(8,128)S(1)}) fusion(f32[2048]{0:T(1024)S(1)} %fusion.14, bf16[2048,2048]{1,0:T(8,128)(2,1)S(1)} %exponential_convert_fusion.1, f32[16,2048]{1,0:T(8,128)S(1)} %constant_dynamic-update-slice_fusion.7, f32[16]{0:T(128)S(1)} %get-tuple-element.52, f32[16,2048]{1,0:T(8,128)S(1)} %get-tuple-element.53, ...), kind=kOutput, calls=%fused_computation.107 | convolution fusion | flops 134414320 | bytes 8790148 | tf_op jit(solution)/shard_map/dot_general | solution.py:125
  59.4 1.3 %collective-permute-start.13 = (f32[16,2048]{1,0:T(8,128)S(1)}, f32[16,2048]{1,0:T(8,128)S(1)}, u32[]{:S(2)}, u32[]{:S(2)}) collective-permute-start(f32[16,2048]{1,0:T(8,128)S(1)} %multiply_divide_fusion), channel_id=1, source_target_pairs={{24,28},{4,0},{25,29},{5,1},{26,30},{6,2},{27,31},{7,3}} | collective-permute-start | bytes 393224 | tf_op jit(solution)/shard_map/ppermute | solution.py:136
  60.7 2.9 %negate_exponential_fusion.3 = f32[2048,512]{1,0:T(8,128)} fusion(bf16[64,2048]{1,0:T(8,128)(2,1)S(1)} %constant_dynamic-update-slice_fusion.3, f32[512]{0:T(512)S(1)} %get-tuple-element.38, f32[2048]{0:T(1024)S(1)} %multiply_reduce_fusion.11, bf16[64,2048]{1,0:T(8,128)(2,1)S(1)} %bitcast.41), kind=kOutput, calls=%fused_computation.13 | convolution fusion | flops 138412032 | bytes 4532224 | tf_op jit(solution)/shard_map/dot_general | solution.py:61
  63.6 2.7 %collective-permute-done.13 = f32[16,2048]{1,0:T(8,128)S(1)} collective-permute-done((f32[16,2048]{1,0:T(8,128)S(1)}, f32[16,2048]{1,0:T(8,128)S(1)}, u32[]{:S(2)}, u32[]{:S(2)}) %collective-permute-start.13) | collective-permute-done | bytes 131104 | tf_op jit(solution)/shard_map/ppermute | solution.py:136
  66.5 1.0 %collective-permute-start.21 = (f32[1,2048]{1,0:T(1,128)S(1)}, f32[1,2048]{1,0:T(1,128)S(1)}, u32[]{:S(2)}, u32[]{:S(2)}) collective-permute-start(f32[1,2048]{1,0:T(1,128)S(1)} %bitcast.47), channel_id=1, source_target_pairs={{0,2},{1,3},{2,0},{3,1},{4,6},{5,7},{6,4},{7,5},{8,10},{9,11},{10,... | collective-permute-start | bytes 24584 | tf_op jit(solution)/shard_map/ppermute | solution.py:22
  67.5 1.4 %collective-permute-start.22 = (f32[1,2048]{1,0:T(1,128)S(1)}, f32[1,2048]{1,0:T(1,128)S(1)}, u32[]{:S(2)}, u32[]{:S(2)}) collective-permute-start(f32[1,2048]{1,0:T(1,128)S(1)} %bitcast.48), channel_id=1, source_target_pairs={{0,3},{1,0},{2,1},{3,2},{4,7},{5,4},{6,5},{7,6},{8,11},{9,8},{10,9... | collective-permute-start | bytes 24584 | tf_op jit(solution)/shard_map/ppermute | solution.py:22
  71.2 5.9 %multiply_reduce_fusion.5 = (f32[512]{0:T(512)S(1)}, f32[512]{0:T(512)S(1)}, f32[512]{0:T(512)S(1)}, f32[512]{0:T(512)S(1)}, f32[2048,512]{1,0:T(8,128)S(1)}) fusion(f32[2048]{0:T(1024)S(1)} %get-tuple-element.8, f32[2048,512]{1,0:T(8,128)} %negate_exponential_fusion.1, f32[2048,512]{1,0:T(8,128)} %negate_exponential_fusion, ...), kind=kOutput, calls=%fused_computation.9 | convolution fusion | flops 146798592 | bytes 17131520 | tf_op jit(solution)/shard_map/dot_general | solution.py:61
  78.9 1.6 %copy-done.2 = f32[2048,512]{1,0:T(8,128)S(1)} copy-done((f32[2048,512]{1,0:T(8,128)S(1)}, f32[2048,512]{1,0:T(8,128)}, u32[]{:S(2)}) %copy-start.2) | copy-done | bytes 4194328
  81.3 1.0 %collective-permute-start.23 = (f32[512]{0:T(512)S(1)}, f32[512]{0:T(512)S(1)}, u32[]{:S(2)}, u32[]{:S(2)}) collective-permute-start(f32[512]{0:T(512)S(1)} %get-tuple-element.32), channel_id=1, source_target_pairs={{0,1},{1,2},{2,3},{3,0},{4,5},{5,6},{6,7},{7,4},{8,9},{9,10},{10,1... | collective-permute-start | bytes 6152 | tf_op jit(solution)/shard_map/ppermute | solution.py:22
  82.3 0.9 %collective-permute-start.24 = (f32[512]{0:T(512)S(1)}, f32[512]{0:T(512)S(1)}, u32[]{:S(2)}, u32[]{:S(2)}) collective-permute-start(f32[512]{0:T(512)S(1)} %get-tuple-element.31), channel_id=1, source_target_pairs={{0,2},{1,3},{2,0},{3,1},{4,6},{5,7},{6,4},{7,5},{8,10},{9,11},{10,... | collective-permute-start | bytes 6152 | tf_op jit(solution)/shard_map/ppermute | solution.py:22
  83.9 1.1 %collective-permute-start.18 = (f32[2,16,512]{2,1,0:T(8,128)S(1)}, f32[2,16,512]{2,1,0:T(8,128)S(1)}, u32[]{:S(2)}, u32[]{:S(2)}) collective-permute-start(f32[2,16,512]{2,1,0:T(8,128)S(1)} %get-tuple-element.23), channel_id=1, source_target_pairs={{0,2},{1,3},{2,0},{3,1},{4,6},{5,7},{6,4},{7,5},{8,10},{9,11},{10,... | collective-permute-start | bytes 196616 | tf_op jit(solution)/shard_map/ppermute | solution.py:22
  85.0 1.4 %collective-permute-start.19 = (f32[2,16,512]{2,1,0:T(8,128)S(1)}, f32[2,16,512]{2,1,0:T(8,128)S(1)}, u32[]{:S(2)}, u32[]{:S(2)}) collective-permute-start(f32[2,16,512]{2,1,0:T(8,128)S(1)} %get-tuple-element.20), channel_id=1, source_target_pairs={{0,3},{1,0},{2,1},{3,2},{4,7},{5,4},{6,5},{7,6},{8,11},{9,8},{10,9... | collective-permute-start | bytes 196616 | tf_op jit(solution)/shard_map/ppermute | solution.py:22
  87.8 1.1 %collective-permute-done.18 = f32[2,16,512]{2,1,0:T(8,128)S(1)} collective-permute-done((f32[2,16,512]{2,1,0:T(8,128)S(1)}, f32[2,16,512]{2,1,0:T(8,128)S(1)}, u32[]{:S(2)}, u32[]{:S(2)}) %collective-permute-start.18) | collective-permute-done | bytes 65568 | tf_op jit(solution)/shard_map/ppermute | solution.py:22
  (91 shorter events, 17.6 us)
Async XLA Ops:
  0.6 13.3 %collective-permute-start.3 = (bf16[64,512]{1,0:T(8,128)(2,1)}, bf16[64,512]{1,0:T(8,128)(2,1)S(1)}, u32[]{:S(2)}, u32[]{:S(2)}) collective-permute-start(bf16[64,512]{1,0:T(8,128)(2,1)} %bitcast.43), channel_id=1, source_target_pairs={{1,0},{2,1},{3,2},{0,3},{5,4},{6,5},{7,6},{4,7},{9,8},{10,9},{11,1... | collective-permute-start | bytes 196616 | tf_op jit(solution)/shard_map/ppermute | solution.py:34
  3.1 10.8 %collective-permute-start.4 = (bf16[64,512]{1,0:T(8,128)(2,1)}, bf16[64,512]{1,0:T(8,128)(2,1)S(1)}, u32[]{:S(2)}, u32[]{:S(2)}) collective-permute-start(bf16[64,512]{1,0:T(8,128)(2,1)} %bitcast.44), channel_id=1, source_target_pairs={{2,0},{3,1},{0,2},{1,3},{6,4},{7,5},{4,6},{5,7},{10,8},{11,9},{8,1... | collective-permute-start | bytes 196616 | tf_op jit(solution)/shard_map/ppermute | solution.py:34
  3.8 10.2 %collective-permute-start.5 = (bf16[64,512]{1,0:T(8,128)(2,1)}, bf16[64,512]{1,0:T(8,128)(2,1)S(1)}, u32[]{:S(2)}, u32[]{:S(2)}) collective-permute-start(bf16[64,512]{1,0:T(8,128)(2,1)} %bitcast.45), channel_id=1, source_target_pairs={{3,0},{0,1},{1,2},{2,3},{7,4},{4,5},{5,6},{6,7},{11,8},{8,9},{9,10... | collective-permute-start | bytes 196616 | tf_op jit(solution)/shard_map/ppermute | solution.py:34
  4.9 8.5 %collective-permute-start = (f32[16,512]{1,0:T(8,128)S(1)}, f32[16,512]{1,0:T(8,128)S(1)}, u32[]{:S(2)}, u32[]{:S(2)}) collective-permute-start(f32[16,512]{1,0:T(8,128)S(1)} %get-tuple-element.28), channel_id=1, source_target_pairs={{0,1},{1,2},{2,3},{3,0},{4,5},{5,6},{6,7},{7,4},{8,9},{9,10},{10,1... | collective-permute-start | bytes 98312 | tf_op jit(solution)/shard_map/ppermute | solution.py:22
  6.3 4.9 %collective-permute-start.7 = (s32[1]{0:T(128)}, s32[1]{0:T(128)}, u32[]{:S(2)}, u32[]{:S(2)}) collective-permute-start(s32[1]{0:T(128)} %param.10), channel_id=1, source_target_pairs={{4,0},{0,4},{12,8},{8,12},{20,16},{16,20},{28,24},{24,28},{5,1},{1... | collective-permute-start | bytes 20 | tf_op jit(solution)/shard_map/ppermute | solution.py:96
  11.2 4.0 %collective-permute-start.1 = (f32[16,512]{1,0:T(8,128)S(1)}, f32[16,512]{1,0:T(8,128)S(1)}, u32[]{:S(2)}, u32[]{:S(2)}) collective-permute-start(f32[16,512]{1,0:T(8,128)S(1)} %get-tuple-element.27), channel_id=1, source_target_pairs={{0,2},{1,3},{2,0},{3,1},{4,6},{5,7},{6,4},{7,5},{8,10},{9,11},{10,... | collective-permute-start | bytes 98312 | tf_op jit(solution)/shard_map/ppermute | solution.py:22
  13.3 2.2 %collective-permute-start.2 = (f32[16,512]{1,0:T(8,128)S(1)}, f32[16,512]{1,0:T(8,128)S(1)}, u32[]{:S(2)}, u32[]{:S(2)}) collective-permute-start(f32[16,512]{1,0:T(8,128)S(1)} %get-tuple-element.26), channel_id=1, source_target_pairs={{0,3},{1,0},{2,1},{3,2},{4,7},{5,4},{6,5},{7,6},{8,11},{9,8},{10,9... | collective-permute-start | bytes 98312 | tf_op jit(solution)/shard_map/ppermute | solution.py:22
  14.0 9.2 %collective-permute-start.6 = (bf16[64,2048]{1,0:T(8,128)(2,1)S(1)}, bf16[64,2048]{1,0:T(8,128)(2,1)S(1)}, u32[]{:S(2)}, u32[]{:S(2)}) collective-permute-start(bf16[64,2048]{1,0:T(8,128)(2,1)S(1)} %constant_dynamic-update-slice_fusion.3), channel_id=1, source_target_pairs={{4,0},{0,4},{12,8},{8,12},{20,16},{16,20},{28,24},{24,28},{5,1},{1... | collective-permute-start | bytes 786440 | tf_op jit(solution)/shard_map/ppermute | solution.py:91
  15.5 13.2 %collective-permute-start.8 = (f32[16,2048]{1,0:T(8,128)S(1)}, f32[16,2048]{1,0:T(8,128)S(1)}, u32[]{:S(2)}, u32[]{:S(2)}) collective-permute-start(f32[16,2048]{1,0:T(8,128)S(1)} %constant_dynamic-update-slice_fusion.7), channel_id=1, source_target_pairs={{4,0},{0,4},{12,8},{8,12},{20,16},{16,20},{28,24},{24,28},{5,1},{1... | collective-permute-start | bytes 393224 | tf_op jit(solution)/shard_map/ppermute | solution.py:95
  16.2 21.2 %collective-permute-start.10 = (bf16[64,2048]{1,0:T(8,128)(2,1)S(1)}, bf16[64,2048]{1,0:T(8,128)(2,1)S(1)}, u32[]{:S(2)}, u32[]{:S(2)}) collective-permute-start(bf16[64,2048]{1,0:T(8,128)(2,1)S(1)} %constant_dynamic-update-slice_fusion.3), channel_id=1, source_target_pairs={{8,4},{4,8},{16,12},{12,16},{24,20},{20,24},{9,5},{5,9},{17,13},{1... | collective-permute-start | bytes 786440 | tf_op jit(solution)/shard_map/ppermute | solution.py:99
  28.8 12.3 %collective-permute-start.9 = (bf16[16,2048]{1,0:T(8,128)(2,1)S(1)}, bf16[16,2048]{1,0:T(8,128)(2,1)S(1)}, u32[]{:S(2)}, u32[]{:S(2)}) collective-permute-start(bf16[16,2048]{1,0:T(8,128)(2,1)S(1)} %get-tuple-element.16), channel_id=1, source_target_pairs={{0,8},{28,20},{1,9},{29,21},{2,10},{30,22},{3,11},{31,23}} | collective-permute-start | bytes 196616 | tf_op jit(solution)/shard_map/ppermute | solution.py:133
  42.4 2.3 %copy-start.3 = (bf16[1,64,2048]{2,1,0:T(8,128)(2,1)S(1)}, bf16[1,64,2048]{2,1,0:T(8,128)(2,1)}, u32[]{:S(2)}) copy-start(bf16[1,64,2048]{2,1,0:T(8,128)(2,1)} %param.7) | copy-start | bytes 786436
  43.9 3.7 %collective-permute-start.11 = (bf16[16,2048]{1,0:T(8,128)(2,1)S(1)}, bf16[16,2048]{1,0:T(8,128)(2,1)S(1)}, u32[]{:S(2)}, u32[]{:S(2)}) collective-permute-start(bf16[16,2048]{1,0:T(8,128)(2,1)S(1)} %get-tuple-element.14), channel_id=1, source_target_pairs={{8,16},{20,12},{9,17},{21,13},{10,18},{22,14},{11,19},{23,15}} | collective-permute-start | bytes 196616 | tf_op jit(solution)/shard_map/ppermute | solution.py:133
  50.4 6.2 %collective-permute-start.12 = (bf16[16,2048]{1,0:T(8,128)(2,1)S(1)}, bf16[16,2048]{1,0:T(8,128)(2,1)S(1)}, u32[]{:S(2)}, u32[]{:S(2)}) collective-permute-start(bf16[16,2048]{1,0:T(8,128)(2,1)S(1)} %get-tuple-element.12), channel_id=1, source_target_pairs={{16,24},{12,4},{17,25},{13,5},{18,26},{14,6},{19,27},{15,7}} | collective-permute-start | bytes 196616 | tf_op jit(solution)/shard_map/ppermute | solution.py:133
  54.0 9.6 %collective-permute-start.16 = (f32[16,2048]{1,0:T(8,128)S(1)}, f32[16,2048]{1,0:T(8,128)S(1)}, u32[]{:S(2)}, u32[]{:S(2)}) collective-permute-start(f32[16,2048]{1,0:T(8,128)S(1)} %get-tuple-element.17), channel_id=1, source_target_pairs={{0,4},{28,24},{1,5},{29,25},{2,6},{30,26},{3,7},{31,27}} | collective-permute-start | bytes 393224 | tf_op jit(solution)/shard_map/ppermute | solution.py:136
  55.3 8.3 %collective-permute-start.15 = (f32[16,2048]{1,0:T(8,128)S(1)}, f32[16,2048]{1,0:T(8,128)S(1)}, u32[]{:S(2)}, u32[]{:S(2)}) collective-permute-start(f32[16,2048]{1,0:T(8,128)S(1)} %get-tuple-element.15), channel_id=1, source_target_pairs={{8,12},{20,16},{9,13},{21,17},{10,14},{22,18},{11,15},{23,19}} | collective-permute-start | bytes 393224 | tf_op jit(solution)/shard_map/ppermute | solution.py:136
  56.0 7.7 %collective-permute-start.14 = (f32[16,2048]{1,0:T(8,128)S(1)}, f32[16,2048]{1,0:T(8,128)S(1)}, u32[]{:S(2)}, u32[]{:S(2)}) collective-permute-start(f32[16,2048]{1,0:T(8,128)S(1)} %get-tuple-element.13), channel_id=1, source_target_pairs={{16,20},{12,8},{17,21},{13,9},{18,22},{14,10},{19,23},{15,11}} | collective-permute-start | bytes 393224 | tf_op jit(solution)/shard_map/ppermute | solution.py:136
  59.4 6.9 %collective-permute-start.13 = (f32[16,2048]{1,0:T(8,128)S(1)}, f32[16,2048]{1,0:T(8,128)S(1)}, u32[]{:S(2)}, u32[]{:S(2)}) collective-permute-start(f32[16,2048]{1,0:T(8,128)S(1)} %multiply_divide_fusion), channel_id=1, source_target_pairs={{24,28},{4,0},{25,29},{5,1},{26,30},{6,2},{27,31},{7,3}} | collective-permute-start | bytes 393224 | tf_op jit(solution)/shard_map/ppermute | solution.py:136
  66.4 3.1 %collective-permute-start.20 = (f32[1,2048]{1,0:T(1,128)S(1)}, f32[1,2048]{1,0:T(1,128)S(1)}, u32[]{:S(2)}, u32[]{:S(2)}) collective-permute-start(f32[1,2048]{1,0:T(1,128)S(1)} %bitcast.46), channel_id=1, source_target_pairs={{0,1},{1,2},{2,3},{3,0},{4,5},{5,6},{6,7},{7,4},{8,9},{9,10},{10,1... | collective-permute-start | bytes 24584 | tf_op jit(solution)/shard_map/ppermute | solution.py:22
  66.5 3.8 %collective-permute-start.21 = (f32[1,2048]{1,0:T(1,128)S(1)}, f32[1,2048]{1,0:T(1,128)S(1)}, u32[]{:S(2)}, u32[]{:S(2)}) collective-permute-start(f32[1,2048]{1,0:T(1,128)S(1)} %bitcast.47), channel_id=1, source_target_pairs={{0,2},{1,3},{2,0},{3,1},{4,6},{5,7},{6,4},{7,5},{8,10},{9,11},{10,... | collective-permute-start | bytes 24584 | tf_op jit(solution)/shard_map/ppermute | solution.py:22
  67.5 2.9 %collective-permute-start.22 = (f32[1,2048]{1,0:T(1,128)S(1)}, f32[1,2048]{1,0:T(1,128)S(1)}, u32[]{:S(2)}, u32[]{:S(2)}) collective-permute-start(f32[1,2048]{1,0:T(1,128)S(1)} %bitcast.48), channel_id=1, source_target_pairs={{0,3},{1,0},{2,1},{3,2},{4,7},{5,4},{6,5},{7,6},{8,11},{9,8},{10,9... | collective-permute-start | bytes 24584 | tf_op jit(solution)/shard_map/ppermute | solution.py:22
  71.2 6.8 %copy-start = (f32[2048,512]{1,0:T(8,128)S(1)}, f32[2048,512]{1,0:T(8,128)}, u32[]{:S(2)}) copy-start(f32[2048,512]{1,0:T(8,128)} %negate_exponential_fusion) | copy-start | bytes 12582916
  71.2 7.1 %copy-start.1 = (f32[2048,512]{1,0:T(8,128)S(1)}, f32[2048,512]{1,0:T(8,128)}, u32[]{:S(2)}) copy-start(f32[2048,512]{1,0:T(8,128)} %negate_exponential_fusion.1) | copy-start | bytes 12582916
  78.3 2.2 %copy-start.2 = (f32[2048,512]{1,0:T(8,128)S(1)}, f32[2048,512]{1,0:T(8,128)}, u32[]{:S(2)}) copy-start(f32[2048,512]{1,0:T(8,128)} %negate_exponential_fusion.3) | copy-start | bytes 12582916
  81.3 3.7 %collective-permute-start.23 = (f32[512]{0:T(512)S(1)}, f32[512]{0:T(512)S(1)}, u32[]{:S(2)}, u32[]{:S(2)}) collective-permute-start(f32[512]{0:T(512)S(1)} %get-tuple-element.32), channel_id=1, source_target_pairs={{0,1},{1,2},{2,3},{3,0},{4,5},{5,6},{6,7},{7,4},{8,9},{9,10},{10,1... | collective-permute-start | bytes 6152 | tf_op jit(solution)/shard_map/ppermute | solution.py:22
  82.3 4.3 %collective-permute-start.24 = (f32[512]{0:T(512)S(1)}, f32[512]{0:T(512)S(1)}, u32[]{:S(2)}, u32[]{:S(2)}) collective-permute-start(f32[512]{0:T(512)S(1)} %get-tuple-element.31), channel_id=1, source_target_pairs={{0,2},{1,3},{2,0},{3,1},{4,6},{5,7},{6,4},{7,5},{8,10},{9,11},{10,... | collective-permute-start | bytes 6152 | tf_op jit(solution)/shard_map/ppermute | solution.py:22
  83.2 3.6 %collective-permute-start.25 = (f32[512]{0:T(512)S(1)}, f32[512]{0:T(512)S(1)}, u32[]{:S(2)}, u32[]{:S(2)}) collective-permute-start(f32[512]{0:T(512)S(1)} %get-tuple-element.30), channel_id=1, source_target_pairs={{0,3},{1,0},{2,1},{3,2},{4,7},{5,4},{6,5},{7,6},{8,11},{9,8},{10,9... | collective-permute-start | bytes 6152 | tf_op jit(solution)/shard_map/ppermute | solution.py:22
  83.8 3.9 %collective-permute-start.17 = (f32[2,16,512]{2,1,0:T(8,128)S(1)}, f32[2,16,512]{2,1,0:T(8,128)S(1)}, u32[]{:S(2)}, u32[]{:S(2)}) collective-permute-start(f32[2,16,512]{2,1,0:T(8,128)S(1)} %get-tuple-element.22), channel_id=1, source_target_pairs={{0,1},{1,2},{2,3},{3,0},{4,5},{5,6},{6,7},{7,4},{8,9},{9,10},{10,1... | collective-permute-start | bytes 196616 | tf_op jit(solution)/shard_map/ppermute | solution.py:22
  83.9 5.0 %collective-permute-start.18 = (f32[2,16,512]{2,1,0:T(8,128)S(1)}, f32[2,16,512]{2,1,0:T(8,128)S(1)}, u32[]{:S(2)}, u32[]{:S(2)}) collective-permute-start(f32[2,16,512]{2,1,0:T(8,128)S(1)} %get-tuple-element.23), channel_id=1, source_target_pairs={{0,2},{1,3},{2,0},{3,1},{4,6},{5,7},{6,4},{7,5},{8,10},{9,11},{10,... | collective-permute-start | bytes 196616 | tf_op jit(solution)/shard_map/ppermute | solution.py:22
  85.0 3.9 %collective-permute-start.19 = (f32[2,16,512]{2,1,0:T(8,128)S(1)}, f32[2,16,512]{2,1,0:T(8,128)S(1)}, u32[]{:S(2)}, u32[]{:S(2)}) collective-permute-start(f32[2,16,512]{2,1,0:T(8,128)S(1)} %get-tuple-element.20), channel_id=1, source_target_pairs={{0,3},{1,0},{2,1},{3,2},{4,7},{5,4},{6,5},{7,6},{8,11},{9,8},{10,9... | collective-permute-start | bytes 196616 | tf_op jit(solution)/shard_map/ppermute | solution.py:22
